TPU v7x, 32 devices: a whole 2x2x4 slice. The times are simulated.
32 devices in a mesh: row: 4 (over y, x), col: 8 (over z, core).
Axes of the slice: x: 2, y: 2, z: 4, core: 2. Of those that a mesh axis runs over, the one named last changes fastest.
Arguments:
- density: float32 [2048, 2048], P('row', 'col'), as said below
- pattern: int32 [16, 16], replicated, may hold values from 0 to 1, as said below
Outputs:
- purified: float32 [2048, 2048], P('row', 'col')
Inputs may be any that keep to these rules, and one draw needn't show every extreme that they name: density is symmetric and zero outside the blocks that pattern allows. pattern is symmetric with ones on its diagonal, and every block row holds exactly 7 ones.
All inputs are finite; a program needn't handle non-finite values.
Results may differ from a plain program's by a relative error of at most 0.0061.
Values may be sent and summed in bfloat16 or wider, within the bound.
No kernel may reach another device: no remote copies, remote signals or barrier semaphores. Data moves between devices by JAX's collectives and lax.ppermute only.
A program may use at most 64 MiB of HBM per device.

v0:
```python
import jax
import jax.numpy as jnp
from jax import lax
from jax.sharding import PartitionSpec as P

BS = 128
STEPS = 2


def allowed_blocks(pattern):
    count = pattern.shape[0]
    index = lax.iota(jnp.int32, count)
    eye = (index[:, None] == index[None, :]).astype(jnp.int32)
    return jnp.maximum(jnp.maximum(pattern, pattern.T), eye)


def apply_mask(values, blocks):
    row_blocks, col_blocks = blocks.shape
    shaped = values.reshape(row_blocks, BS, col_blocks, BS) * blocks[:, None, :, None]
    return shaped.reshape(row_blocks * BS, col_blocks * BS)


def on_device(density, pattern):
    rows, cols = density.shape
    row_blocks = rows // BS
    col_blocks = cols // BS
    allowed = allowed_blocks(pattern)
    first_row = lax.axis_index("row") * row_blocks
    first_col = lax.axis_index("col") * col_blocks
    blocks = lax.dynamic_slice(allowed, (first_row, first_col), (row_blocks, col_blocks)).astype(
        jnp.float32
    )
    current = apply_mask(density, blocks)
    for step in range(STEPS):
        xb = current.astype(jnp.bfloat16)
        x_panel = lax.all_gather(xb, "row", axis=0, tiled=True)
        square = jnp.dot(
            lax.all_gather(xb, "col", axis=1, tiled=True),
            x_panel,
            preferred_element_type=jnp.float32,
        )
        square = apply_mask(square, blocks)
        qb = square.astype(jnp.bfloat16)
        q_panel = lax.all_gather(qb, "row", axis=0, tiled=True)
        total = jnp.dot(
            lax.all_gather(qb, "col", axis=1, tiled=True),
            x_panel,
            preferred_element_type=jnp.float32,
        )
        jordan = total + jnp.dot(
            lax.all_gather(xb, "col", axis=1, tiled=True),
            q_panel,
            preferred_element_type=jnp.float32,
        )
        current = apply_mask(3.0 * square - jordan, blocks)
    return current


def solution(mesh):
    placed = (P("row", "col"), P())
    return jax.shard_map(
        on_device, mesh=mesh, in_specs=placed, out_specs=P("row", "col"), check_vma=False
    )
```

profile of v0, /device:TPU:1, one launch (start us, length us, event | category | flops | bytes accessed | tf_op | source)
XLA Modules:
  0.0 264.7 jit_solution(4661226299853887989)
XLA Ops:
  6.5 0.0 all-gather.11.cloned.1.call-start
  6.5 0.8 copy.3
  7.3 0.8 fusion.7
  8.1 0.2 mul.53
  8.3 1.8 fusion.5
  10.1 0.0 all-gather.11.cloned.1.call-update
  10.1 0.0 all-gather.9.cloned.1.call-start
  10.2 0.7 all-gather.9.cloned.1.call-update
  10.9 0.0 all-gather.13.cloned.1.call-start
  10.9 28.1 %all-gather.11.cloned.1.call-done = bf16[2048,256]{1,0:T(8,128)(2,1)} async-done(((bf16[512,256]{1,0:T(8,128)(2,1)}), bf16[2048,256]{1,0:T(8,128)(2,1)}) %all-gather.11.cloned.1.call-update) | async-done | bytes 1048592 | tf_op jit(solution)/shard_map/all_gather | solution.py:36
  39.0 32.9 %all-gather.9.cloned.1.call-done = bf16[512,2048]{1,0:T(8,128)(2,1)} async-done(((bf16[512,256]{1,0:T(8,128)(2,1)}), bf16[512,2048]{1,0:T(8,128)(2,1)}) %all-gather.9.cloned.1.call-update) | async-done | bytes 2097168 | tf_op jit(solution)/shard_map/all_gather | solution.py:38
  71.8 3.3 %fusion.8 = (bf16[512,256]{1,0:T(8,128)(2,1)}, f32[512,256]{1,0:T(8,128)S(1)}) fusion(f32[64,8,2,128]{3,2,1,0:T(2,128)S(1)} %bitcast.24, bf16[512,2048]{1,0:T(8,128)(2,1)} %all-gather.9.cloned.1.call-done, bf16[2048,256]{1,0:T(8,128)(2,1)} %all-gather.11.cloned.1.call-done), kind=kOutput, calls=%fused_computation.15 | convolution fusion | flops 537133056 | bytes 4456448 | tf_op jit(solution)/shard_map/dot_general | solution.py:37
  75.1 0.0 all-gather.13.cloned.1.call-update
  75.1 0.0 copy-start.1
  75.1 0.0 all-gather.15.cloned.1.call-start
  75.2 0.5 all-gather.15.cloned.1.call-update
  75.7 0.0 all-gather.19.cloned.1.call-start
  75.8 29.4 %all-gather.13.cloned.1.call-done = bf16[512,2048]{1,0:T(8,128)(2,1)} async-done(((bf16[512,256]{1,0:T(8,128)(2,1)}), bf16[512,2048]{1,0:T(8,128)(2,1)}) %all-gather.13.cloned.1.call-update) | async-done | bytes 2097168 | tf_op jit(solution)/shard_map/all_gather | solution.py:46
  105.2 3.4 %fusion.10 = f32[512,256]{1,0:T(8,128)} fusion(bf16[512,2048]{1,0:T(8,128)(2,1)} %all-gather.13.cloned.1.call-done, bf16[2048,256]{1,0:T(8,128)(2,1)} %all-gather.11.cloned.1.call-done), kind=kOutput, calls=%fused_computation.17 | convolution fusion | flops 536870912 | bytes 3670016 | tf_op jit(solution)/shard_map/dot_general | solution.py:45
  108.6 23.7 %all-gather.15.cloned.1.call-done = bf16[2048,256]{1,0:T(8,128)(2,1)} async-done(((bf16[512,256]{1,0:T(8,128)(2,1)}), bf16[2048,256]{1,0:T(8,128)(2,1)}) %all-gather.15.cloned.1.call-update) | async-done | bytes 1048592 | tf_op jit(solution)/shard_map/all_gather | solution.py:44
  132.2 0.0 copy-done.1
  132.2 2.8 %fusion.4 = bf16[512,256]{1,0:T(8,128)(2,1)} fusion(f32[512,256]{1,0:T(8,128)} %fusion.10, bf16[512,2048]{1,0:T(8,128)(2,1)S(1)} %copy-done.1, bf16[2048,256]{1,0:T(8,128)(2,1)} %all-gather.15.cloned.1.call-done, f32[512,256]{1,0:T(8,128)S(1)} %get-tuple-element.6, f32[64,8,2,128]{3,2,1,0:T(2,128)S(1)} %bitcast.25), kind=kOutput, calls=%fused_computation.8 | convolution fusion | flops 537526272 | bytes 4980736 | tf_op jit(solution)/shard_map/dot_general | solution.py:50
  135.0 0.0 all-gather.19.cloned.1.call-update
  135.0 0.0 all-gather.17.cloned.1.call-start
  135.0 0.5 all-gather.17.cloned.1.call-update
  135.6 0.0 all-gather.21.cloned.1.call-start
  135.6 26.1 %all-gather.19.cloned.1.call-done = bf16[2048,256]{1,0:T(8,128)(2,1)} async-done(((bf16[512,256]{1,0:T(8,128)(2,1)}), bf16[2048,256]{1,0:T(8,128)(2,1)}) %all-gather.19.cloned.1.call-update) | async-done | bytes 1048592 | tf_op jit(solution)/shard_map/all_gather | solution.py:36
  161.8 32.7 %all-gather.17.cloned.1.call-done = bf16[512,2048]{1,0:T(8,128)(2,1)} async-done(((bf16[512,256]{1,0:T(8,128)(2,1)}), bf16[512,2048]{1,0:T(8,128)(2,1)}) %all-gather.17.cloned.1.call-update) | async-done | bytes 2097168 | tf_op jit(solution)/shard_map/all_gather | solution.py:38
  194.5 3.3 %fusion.9 = (bf16[512,256]{1,0:T(8,128)(2,1)}, f32[512,256]{1,0:T(8,128)S(1)}) fusion(f32[64,8,2,128]{3,2,1,0:T(2,128)S(1)} %bitcast.26, bf16[512,2048]{1,0:T(8,128)(2,1)} %all-gather.17.cloned.1.call-done, bf16[2048,256]{1,0:T(8,128)(2,1)} %all-gather.19.cloned.1.call-done), kind=kOutput, calls=%fused_computation.16 | convolution fusion | flops 537133056 | bytes 4456448 | tf_op jit(solution)/shard_map/dot_general | solution.py:37
  197.8 0.0 all-gather.21.cloned.1.call-update
  197.8 0.0 copy-start
  197.8 0.0 all-gather.23.cloned.1.call-start
  197.8 0.7 all-gather.23.cloned.1.call-update
  198.6 29.3 %all-gather.21.cloned.1.call-done = bf16[512,2048]{1,0:T(8,128)(2,1)} async-done(((bf16[512,256]{1,0:T(8,128)(2,1)}), bf16[512,2048]{1,0:T(8,128)(2,1)}) %all-gather.21.cloned.1.call-update) | async-done | bytes 2097168 | tf_op jit(solution)/shard_map/all_gather | solution.py:46
  227.9 3.4 %fusion.11 = f32[512,256]{1,0:T(8,128)} fusion(bf16[512,2048]{1,0:T(8,128)(2,1)} %all-gather.21.cloned.1.call-done, bf16[2048,256]{1,0:T(8,128)(2,1)} %all-gather.19.cloned.1.call-done), kind=kOutput, calls=%fused_computation.18 | convolution fusion | flops 536870912 | bytes 3670016 | tf_op jit(solution)/shard_map/dot_general | solution.py:45
  231.2 23.8 %all-gather.23.cloned.1.call-done = bf16[2048,256]{1,0:T(8,128)(2,1)} async-done(((bf16[512,256]{1,0:T(8,128)(2,1)}), bf16[2048,256]{1,0:T(8,128)(2,1)}) %all-gather.23.cloned.1.call-update) | async-done | bytes 1048592 | tf_op jit(solution)/shard_map/all_gather | solution.py:44
  255.0 0.0 copy-done
  255.0 2.9 %fusion.3 = f32[512,256]{1,0:T(8,128)} fusion(f32[512,256]{1,0:T(8,128)} %fusion.11, bf16[512,2048]{1,0:T(8,128)(2,1)S(1)} %copy-done, bf16[2048,256]{1,0:T(8,128)(2,1)} %all-gather.23.cloned.1.call-done, f32[512,256]{1,0:T(8,128)S(1)} %get-tuple-element.8, f32[64,8,2,128]{3,2,1,0:T(2,128)S(1)} %bitcast.27), kind=kOutput, calls=%fused_computation.7 | convolution fusion | flops 537395200 | bytes 5242880 | tf_op jit(solution)/shard_map/dot_general | solution.py:50
Async XLA Ops:
  6.5 32.4 %all-gather.11.cloned.1.call-start = ((), (), s32[]{:S(2)}) async-start(), calls=%async_computation.1 | async-start | bytes 1310720 | tf_op jit(solution)/shard_map/all_gather | solution.py:36
  10.1 61.7 %all-gather.9.cloned.1.call-start = ((), (), s32[]{:S(2)}) async-start(), calls=%async_computation | async-start | bytes 2359296 | tf_op jit(solution)/shard_map/all_gather | solution.py:38
  10.9 94.3 %all-gather.13.cloned.1.call-start = ((), (), s32[]{:S(2)}) async-start(), calls=%async_computation.2 | async-start | bytes 2359296 | tf_op jit(solution)/shard_map/all_gather | solution.py:46
  75.1 57.1 %copy-start.1 = (bf16[512,2048]{1,0:T(8,128)(2,1)S(1)}, bf16[512,2048]{1,0:T(8,128)(2,1)}, u32[]{:S(2)}) copy-start(bf16[512,2048]{1,0:T(8,128)(2,1)} %all-gather.9.cloned.1.call-done) | copy-start | bytes 6291460
  75.1 57.1 %all-gather.15.cloned.1.call-start = ((), (), s32[]{:S(2)}) async-start(), calls=%async_computation.3 | async-start | bytes 1310720 | tf_op jit(solution)/shard_map/all_gather | solution.py:44
  75.7 86.1 %all-gather.19.cloned.1.call-start = ((), (), s32[]{:S(2)}) async-start(), calls=%async_computation.5 | async-start | bytes 1310720 | tf_op jit(solution)/shard_map/all_gather | solution.py:36
  135.0 59.5 %all-gather.17.cloned.1.call-start = ((), (), s32[]{:S(2)}) async-start(), calls=%async_computation.4 | async-start | bytes 2359296 | tf_op jit(solution)/shard_map/all_gather | solution.py:38
  135.6 92.3 %all-gather.21.cloned.1.call-start = ((), (), s32[]{:S(2)}) async-start(), calls=%async_computation.6 | async-start | bytes 2359296 | tf_op jit(solution)/shard_map/all_gather | solution.py:46
  197.8 57.2 %copy-start = (bf16[512,2048]{1,0:T(8,128)(2,1)S(1)}, bf16[512,2048]{1,0:T(8,128)(2,1)}, u32[]{:S(2)}) copy-start(bf16[512,2048]{1,0:T(8,128)(2,1)} %all-gather.17.cloned.1.call-done) | copy-start | bytes 6291460
  197.8 57.2 %all-gather.23.cloned.1.call-start = ((), (), s32[]{:S(2)}) async-start(), calls=%async_computation.7 | async-start | bytes 1310720 | tf_op jit(solution)/shard_map/all_gather | solution.py:44
Sparse Core Ops, SparseCore 0:
  10.2 28.6 all-gather.10
  40.6 31.2 all-gather.8
  75.2 29.8 all-gather.12
  106.9 25.2 all-gather.14
  135.1 26.6 all-gather.18
  163.2 31.2 all-gather.16
  197.9 29.8 all-gather.20
  229.7 25.2 all-gather.22
where the time goes:
time: 266 us; the launch traced here: 265 us
  waiting for transfers between devices  228 us (86%)
  matrix products  18.9 us (7%)
  between operations  13.5 us (5%)
    all_gather x2, waiting for transfers between devices, on_device(): lax.all_gather(xb, 'col', axis=1, tiled=True)  65.6 us
    all_gather x2, waiting for transfers between devices, on_device(): lax.all_gather(qb, 'col', axis=1, tiled=True)  58.7 us
    all_gather x2, waiting for transfers between devices, on_device(): x_panel = lax.all_gather(xb, 'row', axis=0, tiled=True)  54.2 us
    all_gather x2, waiting for transfers between devices, on_device(): q_panel = lax.all_gather(qb, 'row', axis=0, tiled=True)  47.4 us
    dot_general x2, matrix products, on_device(): jnp.dot(lax.all_gather(qb, 'col', axis=1, tiled=True), x_panel, preferred...  6.72 us
    dot_general x2, matrix products, on_device(): jnp.dot(lax.all_gather(xb, 'col', axis=1, tiled=True), x_panel, preferred...  6.54 us
    dot_general x2, matrix products, on_device(): jnp.dot(lax.all_gather(xb, 'col', axis=1, tiled=True), q_panel, preferred...  5.63 us
  transfers between devices with their start and end apart: 8, of which 8 were waited for; matrix products, arithmetic and copies ran while one was open for 3% of the time, Pallas kernels for 0%

commit v1 on v0

v1 whole, which is shorter than its diff:
```python
import jax
import jax.numpy as jnp
from jax import lax
from jax.sharding import PartitionSpec as P

BS = 128
STEPS = 2


def allowed_blocks(pattern):
    count = pattern.shape[0]
    index = lax.iota(jnp.int32, count)
    eye = (index[:, None] == index[None, :]).astype(jnp.int32)
    return jnp.maximum(jnp.maximum(pattern, pattern.T), eye)


def apply_mask(values, blocks):
    row_blocks, col_blocks = blocks.shape
    shaped = values.reshape(row_blocks, BS, col_blocks, BS) * blocks[:, None, :, None]
    return shaped.reshape(row_blocks * BS, col_blocks * BS)


def xor_permute(x, axis, size, s):
    return lax.ppermute(x, axis, perm=[(i, i ^ s) for i in range(size)])


def exchange(xb, n_row, n_col):
    col_pieces = [xb] + [xor_permute(xb, "row", n_row, t) for t in range(1, n_row)]
    chips = n_col // 2
    same_core = [xb] + [xor_permute(xb, "col", n_col, 2 * s) for s in range(1, chips)]
    partner_own = xor_permute(xb, "col", n_col, 1)
    relayed = xor_permute(jnp.stack(same_core[1:]), "col", n_col, 1)
    row_pieces = []
    for s in range(chips):
        row_pieces.append(same_core[s])
        row_pieces.append(partner_own if s == 0 else relayed[s - 1])
    return jnp.stack(row_pieces), jnp.stack(col_pieces)


def ordered_k_blocks(col_pieces, me_row, me_col, n_col):
    n_row, rows, cols = col_pieces.shape
    per = rows // cols
    split = col_pieces.reshape(n_row * per, cols, cols)
    s = lax.iota(jnp.int32, n_col)
    owner = jnp.bitwise_xor(s, me_col)
    index = jnp.bitwise_xor(owner // per, me_row) * per + owner % per
    return jnp.take(split, index, axis=0)


def contract(row_pieces, k_blocks):
    return jnp.einsum("sik,skj->ij", row_pieces, k_blocks, preferred_element_type=jnp.float32)


def on_device(density, pattern):
    rows, cols = density.shape
    row_blocks = rows // BS
    col_blocks = cols // BS
    n_row = lax.axis_size("row")
    n_col = lax.axis_size("col")
    me_row = lax.axis_index("row")
    me_col = lax.axis_index("col")
    allowed = allowed_blocks(pattern)
    blocks = lax.dynamic_slice(
        allowed, (me_row * row_blocks, me_col * col_blocks), (row_blocks, col_blocks)
    ).astype(jnp.float32)
    current = apply_mask(density, blocks)
    for step in range(STEPS):
        xb = current.astype(jnp.bfloat16)
        x_row, x_col = exchange(xb, n_row, n_col)
        x_k = ordered_k_blocks(x_col, me_row, me_col, n_col)
        square = apply_mask(contract(x_row, x_k), blocks)
        qb = square.astype(jnp.bfloat16)
        q_row, q_col = exchange(qb, n_row, n_col)
        q_k = ordered_k_blocks(q_col, me_row, me_col, n_col)
        jordan = contract(q_row, x_k) + contract(x_row, q_k)
        current = apply_mask(3.0 * square - jordan, blocks)
    return current


def solution(mesh):
    placed = (P("row", "col"), P())
    return jax.shard_map(
        on_device, mesh=mesh, in_specs=placed, out_specs=P("row", "col"), check_vma=False
    )
```

time: 266 us -> 158 us (0.59)
  waiting for transfers between devices: 228 us -> 69.7 us
  starting transfers between devices: 0.28 us -> 33.4 us
  local copies, waits for them, and re-layouts: 0.98 us -> 29.9 us
  between operations: 13.5 us -> 0.29 us
  other arithmetic: 2.56 us -> 9.13 us
  matrix products: 18.9 us -> 14.9 us
    all_gather x8 -> x0, waiting for transfers between devices: 226 us -> none  [the longest x2 65.6 us: on_device(): lax.all_gather(xb, 'col', axis=1, tiled=True)]
    ppermute x0 -> x32, waiting for transfers between devices: none -> 69.7 us  [xor_permute(): return lax.ppermute(x, axis, perm=[(i, i ^ s) for i in range(size)])]
    ppermute x0 -> x32, starting transfers between devices: none -> 33.4 us  [xor_permute(): return lax.ppermute(x, axis, perm=[(i, i ^ s) for i in range(size)])]
    unnamed x5 -> x37, local copies, waits for them, and re-layouts: 0.77 us -> 21.8 us
    another operation x0 -> x8, other arithmetic: none -> 6.46 us  [the longest x4 4.33 us: exchange(): return (jnp.stack(row_pieces), jnp.stack(col_pieces))]
    gather x0 -> x4, local copies, waits for them, and re-layouts: none -> 4.48 us  [ordered_k_blocks(): return jnp.take(split, index, axis=0)]
    dot_general x6, matrix products: 18.9 us -> 14.9 us  [contract(): jnp.einsum('sik,skj->ij', row_pieces, k_blocks, preferred_element_type=jn...]
    another operation x0 -> x4, local copies, waits for them, and re-layouts: none -> 3.38 us  [exchange(): return (jnp.stack(row_pieces), jnp.stack(col_pieces))]
  transfers between devices with their start and end apart: 8 -> 32, of which waited for: 8 -> 11; matrix products, arithmetic and copies ran while one was open for 3% -> 16% of each run, Pallas kernels for 0% -> 0%
where the time goes in v1:
time: 158 us; the launch traced here: 157 us
  waiting for transfers between devices  69.7 us (44%)
  starting transfers between devices  33.4 us (21%)
  local copies, waits for them, and re-layouts  29.9 us (19%)
  matrix products  14.9 us (9%)
  other arithmetic  9.13 us (6%)
    ppermute x32, waiting for transfers between devices, xor_permute(): return lax.ppermute(x, axis, perm=[(i, i ^ s) for i in range(size)])  69.7 us
    ppermute x32, starting transfers between devices, xor_permute(): return lax.ppermute(x, axis, perm=[(i, i ^ s) for i in range(size)])  33.4 us
    unnamed x37, local copies, waits for them, and re-layouts  21.8 us
    dot_general x6, matrix products, contract(): jnp.einsum('sik,skj->ij', row_pieces, k_blocks, preferred_element_type=jn...  14.9 us
    gather x4, local copies, waits for them, and re-layouts, ordered_k_blocks(): return jnp.take(split, index, axis=0)  4.48 us
    another operation x4, other arithmetic, exchange(): return (jnp.stack(row_pieces), jnp.stack(col_pieces))  4.33 us
    another operation x4, local copies, waits for them, and re-layouts, exchange(): return (jnp.stack(row_pieces), jnp.stack(col_pieces))  3.38 us
  transfers between devices with their start and end apart: 32, of which 11 were waited for; matrix products, arithmetic and copies ran while one was open for 16% of the time, Pallas kernels for 0%

profile of v1, /device:TPU:1, one launch (start us, length us, event | category | flops | bytes accessed | tf_op | source)
XLA Modules:
  0.0 157.3 jit_solution(5055429105224537333)
XLA Ops:
  1.7 1.9 %constant_dynamic-update-slice_fusion.3 = (bf16[8,512,256]{2,1,0:T(8,128)(2,1)}, bf16[512,256]{1,0:T(8,128)(2,1)}) fusion(f32[512,256]{1,0:T(8,128)} %param.4, f32[64,8,2,128]{3,2,1,0:T(2,128)S(1)} %bitcast.104), kind=kLoop, calls=%fused_computation.54 | loop fusion | flops 262143 | bytes 1572864
  3.6 4.2 %collective-permute-start.3 = (bf16[512,256]{1,0:T(8,128)(2,1)}, bf16[512,256]{1,0:T(8,128)(2,1)S(1)}, u32[]{:S(2)}, u32[]{:S(2)}) collective-permute-start(bf16[512,256]{1,0:T(8,128)(2,1)} %get-tuple-element.13), channel_id=1, source_target_pairs={{0,6},{1,7},{2,4},{3,5},{4,2},{5,3},{6,0},{7,1},{8,14},{9,15},{10,... | collective-permute-start | bytes 786440 | tf_op jit(solution)/shard_map/ppermute | solution.py:24
  8.1 2.2 %collective-permute-start.7 = (bf16[512,256]{1,0:T(8,128)(2,1)}, bf16[512,256]{1,0:T(8,128)(2,1)S(1)}, u32[]{:S(2)}, u32[]{:S(2)}) collective-permute-start(bf16[512,256]{1,0:T(8,128)(2,1)} %get-tuple-element.13), channel_id=1, source_target_pairs={{0,24},{8,16},{16,8},{24,0},{1,25},{9,17},{17,9},{25,1},{2,26},{10... | collective-permute-start | bytes 786440 | tf_op jit(solution)/shard_map/ppermute | solution.py:24
  10.5 3.6 %collective-permute-done.3 = bf16[512,256]{1,0:T(8,128)(2,1)S(1)} collective-permute-done((bf16[512,256]{1,0:T(8,128)(2,1)}, bf16[512,256]{1,0:T(8,128)(2,1)S(1)}, u32[]{:S(2)}, u32[]{:S(2)}) %collective-permute-start.3) | collective-permute-done | bytes 262176 | tf_op jit(solution)/shard_map/ppermute | solution.py:24
  14.1 1.0 collective-permute-start.5
  15.1 14.8 %collective-permute-done.2 = bf16[512,256]{1,0:T(8,128)(2,1)S(1)} collective-permute-done((bf16[512,256]{1,0:T(8,128)(2,1)}, bf16[512,256]{1,0:T(8,128)(2,1)S(1)}, u32[]{:S(2)}, u32[]{:S(2)}) %collective-permute-start.2) | collective-permute-done | bytes 262176 | tf_op jit(solution)/shard_map/ppermute | solution.py:24
  29.9 1.4 collective-permute-start
  32.3 1.1 pad_maximum_fusion
  34.0 1.7 %bitcast_dynamic-update-slice_fusion.3 = bf16[8,512,256]{2,1,0:T(8,128)(2,1)} fusion(bf16[8,512,256]{2,1,0:T(8,128)(2,1)} %get-tuple-element.12, bf16[512,256]{1,0:T(8,128)(2,1)} %collective-permute-done), kind=kLoop, calls=%fused_computation.50 | loop fusion | bytes 524288
  36.4 1.7 %slice_dynamic-update-slice_fusion.11 = bf16[8,512,256]{2,1,0:T(8,128)(2,1)} fusion(bf16[8,512,256]{2,1,0:T(8,128)(2,1)} %constant_dynamic-update-slice_fusion.2, bf16[3,512,256]{2,1,0:T(8,128)(2,1)} %collective-permute-done.4), kind=kLoop, calls=%fused_computation.46 | loop fusion | bytes 524288
  38.8 1.7 %slice_dynamic-update-slice_fusion.10 = bf16[8,512,256]{2,1,0:T(8,128)(2,1)} fusion(bf16[8,512,256]{2,1,0:T(8,128)(2,1)} %constant_dynamic-update-slice_fusion.1, bf16[3,512,256]{2,1,0:T(8,128)(2,1)} %collective-permute-done.4), kind=kLoop, calls=%fused_computation.45 | loop fusion | bytes 524288
  41.2 1.7 %slice_dynamic-update-slice_fusion.9 = bf16[8,512,256]{2,1,0:T(8,128)(2,1)} fusion(bf16[8,512,256]{2,1,0:T(8,128)(2,1)} %constant_dynamic-update-slice_fusion, bf16[3,512,256]{2,1,0:T(8,128)(2,1)} %collective-permute-done.4), kind=kLoop, calls=%fused_computation.44 | loop fusion | bytes 524288 | tf_op jit(solution)/shard_map/stack | solution.py:37
  42.9 3.3 %constant_dynamic-update-slice_fusion.7 = (bf16[8,512,256]{2,1,0:T(8,128)(2,1)}, bf16[512,256]{1,0:T(8,128)(2,1)}, f32[512,256]{1,0:T(8,128)}) fusion(f32[64,8,2,128]{3,2,1,0:T(2,128)S(1)} %bitcast.105, bf16[8,512,256]{2,1,0:T(8,128)(2,1)} %slice_dynamic-update-slice_fusion.9, bf16[8,256,256]{2,1,0:T(8,128)(2,1)S(1)} %gather_fusion, ...), kind=kOutput, calls=%fused_computation.58 | convolution fusion | flops 537657344 | bytes 4718600 | tf_op jit(solution)/shard_map/sik,skj->ij/dot_general | solution.py:51
  46.2 2.2 %collective-permute-start.15 = (bf16[512,256]{1,0:T(8,128)(2,1)}, bf16[512,256]{1,0:T(8,128)(2,1)S(1)}, u32[]{:S(2)}, u32[]{:S(2)}) collective-permute-start(bf16[512,256]{1,0:T(8,128)(2,1)} %get-tuple-element.9), channel_id=1, source_target_pairs={{0,24},{8,16},{16,8},{24,0},{1,25},{9,17},{17,9},{25,1},{2,26},{10... | collective-permute-start | bytes 786440 | tf_op jit(solution)/shard_map/ppermute | solution.py:24
  48.9 2.2 %collective-permute-start.11 = (bf16[512,256]{1,0:T(8,128)(2,1)}, bf16[512,256]{1,0:T(8,128)(2,1)S(1)}, u32[]{:S(2)}, u32[]{:S(2)}) collective-permute-start(bf16[512,256]{1,0:T(8,128)(2,1)} %get-tuple-element.9), channel_id=1, source_target_pairs={{0,6},{1,7},{2,4},{3,5},{4,2},{5,3},{6,0},{7,1},{8,14},{9,15},{10,... | collective-permute-start | bytes 786440 | tf_op jit(solution)/shard_map/ppermute | solution.py:24
  51.1 3.7 %collective-permute-done.15 = bf16[512,256]{1,0:T(8,128)(2,1)S(1)} collective-permute-done((bf16[512,256]{1,0:T(8,128)(2,1)}, bf16[512,256]{1,0:T(8,128)(2,1)S(1)}, u32[]{:S(2)}, u32[]{:S(2)}) %collective-permute-start.15) | collective-permute-done | bytes 262176 | tf_op jit(solution)/shard_map/ppermute | solution.py:24
  54.8 6.4 %collective-permute-done.14 = bf16[512,256]{1,0:T(8,128)(2,1)S(1)} collective-permute-done((bf16[512,256]{1,0:T(8,128)(2,1)}, bf16[512,256]{1,0:T(8,128)(2,1)S(1)}, u32[]{:S(2)}, u32[]{:S(2)}) %collective-permute-start.14) | collective-permute-done | bytes 262176 | tf_op jit(solution)/shard_map/ppermute | solution.py:24
  61.7 1.1 pad_maximum_fusion.1
  62.8 1.6 %gather_fusion.1 = bf16[8,256,256]{2,1,0:T(8,128)(2,1)} fusion(bf16[8,256,256]{2,1,0:T(8,128)(2,1)S(1)} %bitcast.102, s32[1024]{0:T(1024)S(1)} %pad_clamp_fusion), kind=kCustom, calls=%fused_computation.1.clone | custom fusion | bytes 2097184 | tf_op jit(solution)/shard_map/jit(_take)/gather | solution.py:47
  64.4 6.3 %collective-permute-done.10 = bf16[512,256]{1,0:T(8,128)(2,1)S(1)} collective-permute-done((bf16[512,256]{1,0:T(8,128)(2,1)}, bf16[512,256]{1,0:T(8,128)(2,1)S(1)}, u32[]{:S(2)}, u32[]{:S(2)}) %collective-permute-start.10) | collective-permute-done | bytes 262176 | tf_op jit(solution)/shard_map/ppermute | solution.py:24
  70.8 3.2 %collective-permute-start.12 = (bf16[3,512,256]{2,1,0:T(8,128)(2,1)S(1)}, bf16[3,512,256]{2,1,0:T(8,128)(2,1)S(1)}, u32[]{:S(2)}, u32[]{:S(2)}) collective-permute-start(bf16[3,512,256]{2,1,0:T(8,128)(2,1)S(1)} %pad_maximum_fusion.5), channel_id=1, source_target_pairs={{0,1},{1,0},{2,3},{3,2},{4,5},{5,4},{6,7},{7,6},{8,9},{9,8},{10,11... | collective-permute-start | bytes 2359304 | tf_op jit(solution)/shard_map/ppermute | solution.py:24
  74.0 1.7 %bitcast_dynamic-update-slice_fusion.2 = bf16[8,512,256]{2,1,0:T(8,128)(2,1)} fusion(bf16[8,512,256]{2,1,0:T(8,128)(2,1)} %get-tuple-element.8, bf16[512,256]{1,0:T(8,128)(2,1)} %collective-permute-done.8), kind=kLoop, calls=%fused_computation.49 | loop fusion | bytes 524288
  76.4 2.5 %convolution_bitcast_fusion.3 = f32[512,256]{1,0:T(8,128)S(1)} fusion(bf16[8,512,256]{2,1,0:T(8,128)(2,1)} %slice_dynamic-update-slice_fusion.9, bf16[8,256,256]{2,1,0:T(8,128)(2,1)S(1)} %copy-done.1, pred[8]{0:T(512)(128)(4,1)S(1)} %get-tuple-element.10), kind=kOutput, calls=%fused_computation.7 | convolution fusion | flops 537395200 | bytes 3670024 | tf_op jit(solution)/shard_map/sik,skj->ij/dot_general | solution.py:51
  80.0 1.6 %constant_dynamic-update-slice_fusion.11 = (bf16[8,512,256]{2,1,0:T(8,128)(2,1)}, bf16[512,256]{1,0:T(8,128)(2,1)}) fusion(f32[64,8,2,128]{3,2,1,0:T(2,128)S(1)} %bitcast.106, f32[512,256]{1,0:T(8,128)S(1)} %convolution_bitcast_fusion.3, bf16[8,512,256]{2,1,0:T(8,128)(2,1)S(1)} %slice_dynamic-update-slice_fusion.6, ...), kind=kOutput, calls=%fused_computation.62 | convolution fusion | flops 538050560 | bytes 5242888 | tf_op jit(solution)/shard_map/sik,skj->ij/dot_general | solution.py:51
  81.6 2.0 %collective-permute-start.19 = (bf16[512,256]{1,0:T(8,128)(2,1)}, bf16[512,256]{1,0:T(8,128)(2,1)S(1)}, u32[]{:S(2)}, u32[]{:S(2)}) collective-permute-start(bf16[512,256]{1,0:T(8,128)(2,1)} %get-tuple-element.16), channel_id=1, source_target_pairs={{0,6},{1,7},{2,4},{3,5},{4,2},{5,3},{6,0},{7,1},{8,14},{9,15},{10,... | collective-permute-start | bytes 786440 | tf_op jit(solution)/shard_map/ppermute | solution.py:24
  83.6 1.6 collective-permute-start.17
  85.1 2.2 %collective-permute-start.23 = (bf16[512,256]{1,0:T(8,128)(2,1)}, bf16[512,256]{1,0:T(8,128)(2,1)S(1)}, u32[]{:S(2)}, u32[]{:S(2)}) collective-permute-start(bf16[512,256]{1,0:T(8,128)(2,1)} %get-tuple-element.16), channel_id=1, source_target_pairs={{0,24},{8,16},{16,8},{24,0},{1,25},{9,17},{17,9},{25,1},{2,26},{10... | collective-permute-start | bytes 786440 | tf_op jit(solution)/shard_map/ppermute | solution.py:24
  87.5 4.1 %collective-permute-done.19 = bf16[512,256]{1,0:T(8,128)(2,1)S(1)} collective-permute-done((bf16[512,256]{1,0:T(8,128)(2,1)}, bf16[512,256]{1,0:T(8,128)(2,1)S(1)}, u32[]{:S(2)}, u32[]{:S(2)}) %collective-permute-start.19) | collective-permute-done | bytes 262176 | tf_op jit(solution)/shard_map/ppermute | solution.py:24
  91.6 1.2 collective-permute-start.21
  92.8 12.7 %collective-permute-done.18 = bf16[512,256]{1,0:T(8,128)(2,1)S(1)} collective-permute-done((bf16[512,256]{1,0:T(8,128)(2,1)}, bf16[512,256]{1,0:T(8,128)(2,1)S(1)}, u32[]{:S(2)}, u32[]{:S(2)}) %collective-permute-start.18) | collective-permute-done | bytes 262176 | tf_op jit(solution)/shard_map/ppermute | solution.py:24
  105.6 1.0 pad_maximum_fusion.6
  107.4 1.1 pad_maximum_fusion.2
  110.0 1.7 %bitcast_dynamic-update-slice_fusion.1 = bf16[8,512,256]{2,1,0:T(8,128)(2,1)} fusion(bf16[8,512,256]{2,1,0:T(8,128)(2,1)} %get-tuple-element.15, bf16[512,256]{1,0:T(8,128)(2,1)} %collective-permute-done.16), kind=kLoop, calls=%fused_computation.48 | loop fusion | bytes 524288
  112.3 1.7 %slice_dynamic-update-slice_fusion.5 = bf16[8,512,256]{2,1,0:T(8,128)(2,1)} fusion(bf16[8,512,256]{2,1,0:T(8,128)(2,1)} %constant_dynamic-update-slice_fusion.10, bf16[3,512,256]{2,1,0:T(8,128)(2,1)} %collective-permute-done.20), kind=kLoop, calls=%fused_computation.40 | loop fusion | bytes 524288
  114.7 1.7 %slice_dynamic-update-slice_fusion.4 = bf16[8,512,256]{2,1,0:T(8,128)(2,1)} fusion(bf16[8,512,256]{2,1,0:T(8,128)(2,1)} %constant_dynamic-update-slice_fusion.9, bf16[3,512,256]{2,1,0:T(8,128)(2,1)} %collective-permute-done.20), kind=kLoop, calls=%fused_computation.39 | loop fusion | bytes 524288
  117.2 1.7 %slice_dynamic-update-slice_fusion.3 = bf16[8,512,256]{2,1,0:T(8,128)(2,1)} fusion(bf16[8,512,256]{2,1,0:T(8,128)(2,1)} %constant_dynamic-update-slice_fusion.8, bf16[3,512,256]{2,1,0:T(8,128)(2,1)} %collective-permute-done.20), kind=kLoop, calls=%fused_computation.38 | loop fusion | bytes 524288 | tf_op jit(solution)/shard_map/stack | solution.py:37
  118.8 3.3 %constant_dynamic-update-slice_fusion.15 = (bf16[8,512,256]{2,1,0:T(8,128)(2,1)}, bf16[512,256]{1,0:T(8,128)(2,1)}, f32[512,256]{1,0:T(8,128)}) fusion(f32[64,8,2,128]{3,2,1,0:T(2,128)S(1)} %bitcast.107, bf16[8,512,256]{2,1,0:T(8,128)(2,1)} %slice_dynamic-update-slice_fusion.3, bf16[8,256,256]{2,1,0:T(8,128)(2,1)S(1)} %gather_fusion.2, ...), kind=kOutput, calls=%fused_computation.66 | convolution fusion | flops 537657344 | bytes 4718600 | tf_op jit(solution)/shard_map/sik,skj->ij/dot_general | solution.py:51
  122.2 2.2 %collective-permute-start.31 = (bf16[512,256]{1,0:T(8,128)(2,1)}, bf16[512,256]{1,0:T(8,128)(2,1)S(1)}, u32[]{:S(2)}, u32[]{:S(2)}) collective-permute-start(bf16[512,256]{1,0:T(8,128)(2,1)} %get-tuple-element.7), channel_id=1, source_target_pairs={{0,24},{8,16},{16,8},{24,0},{1,25},{9,17},{17,9},{25,1},{2,26},{10... | collective-permute-start | bytes 786440 | tf_op jit(solution)/shard_map/ppermute | solution.py:24
  124.8 1.3 collective-permute-start.27
  126.1 4.7 %collective-permute-done.31 = bf16[512,256]{1,0:T(8,128)(2,1)S(1)} collective-permute-done((bf16[512,256]{1,0:T(8,128)(2,1)}, bf16[512,256]{1,0:T(8,128)(2,1)S(1)}, u32[]{:S(2)}, u32[]{:S(2)}) %collective-permute-start.31) | collective-permute-done | bytes 262176 | tf_op jit(solution)/shard_map/ppermute | solution.py:24
  130.8 6.3 %collective-permute-done.30 = bf16[512,256]{1,0:T(8,128)(2,1)S(1)} collective-permute-done((bf16[512,256]{1,0:T(8,128)(2,1)}, bf16[512,256]{1,0:T(8,128)(2,1)S(1)}, u32[]{:S(2)}, u32[]{:S(2)}) %collective-permute-start.30) | collective-permute-done | bytes 262176 | tf_op jit(solution)/shard_map/ppermute | solution.py:24
  137.6 1.1 pad_maximum_fusion.3
  138.7 1.6 %gather_fusion.3 = bf16[8,256,256]{2,1,0:T(8,128)(2,1)} fusion(bf16[8,256,256]{2,1,0:T(8,128)(2,1)S(1)} %bitcast.100, s32[1024]{0:T(1024)S(1)} %pad_clamp_fusion), kind=kCustom, calls=%fused_computation.3.clone | custom fusion | bytes 2097184 | tf_op jit(solution)/shard_map/jit(_take)/gather | solution.py:47
  140.3 6.1 %collective-permute-done.26 = bf16[512,256]{1,0:T(8,128)(2,1)S(1)} collective-permute-done((bf16[512,256]{1,0:T(8,128)(2,1)}, bf16[512,256]{1,0:T(8,128)(2,1)S(1)}, u32[]{:S(2)}, u32[]{:S(2)}) %collective-permute-start.26) | collective-permute-done | bytes 262176 | tf_op jit(solution)/shard_map/ppermute | solution.py:24
  146.5 3.3 %collective-permute-start.28 = (bf16[3,512,256]{2,1,0:T(8,128)(2,1)S(1)}, bf16[3,512,256]{2,1,0:T(8,128)(2,1)S(1)}, u32[]{:S(2)}, u32[]{:S(2)}) collective-permute-start(bf16[3,512,256]{2,1,0:T(8,128)(2,1)S(1)} %pad_maximum_fusion.7), channel_id=1, source_target_pairs={{0,1},{1,0},{2,3},{3,2},{4,5},{5,4},{6,7},{7,6},{8,9},{9,8},{10,11... | collective-permute-start | bytes 2359304 | tf_op jit(solution)/shard_map/ppermute | solution.py:24
  149.8 1.7 %bitcast_dynamic-update-slice_fusion = bf16[8,512,256]{2,1,0:T(8,128)(2,1)} fusion(bf16[8,512,256]{2,1,0:T(8,128)(2,1)} %get-tuple-element.6, bf16[512,256]{1,0:T(8,128)(2,1)} %collective-permute-done.24), kind=kLoop, calls=%fused_computation.47 | loop fusion | bytes 524288
  152.2 2.5 %convolution_bitcast_fusion = f32[512,256]{1,0:T(8,128)S(1)} fusion(bf16[8,512,256]{2,1,0:T(8,128)(2,1)} %slice_dynamic-update-slice_fusion.3, bf16[8,256,256]{2,1,0:T(8,128)(2,1)S(1)} %copy-done, pred[8]{0:T(512)(128)(4,1)S(1)} %get-tuple-element.10), kind=kOutput, calls=%fused_computation.4 | convolution fusion | flops 537395200 | bytes 3670024 | tf_op jit(solution)/shard_map/sik,skj->ij/dot_general | solution.py:51
  155.7 1.6 %bitcast_multiply_fusion = f32[512,256]{1,0:T(8,128)} fusion(f32[512,256]{1,0:T(8,128)S(1)} %copy-done.4, f32[512,256]{1,0:T(8,128)S(1)} %convolution_bitcast_fusion, bf16[8,512,256]{2,1,0:T(8,128)(2,1)S(1)} %slice_dynamic-update-slice_fusion, bf16[8,256,256]{2,1,0:T(8,128)(2,1)S(1)} %gather_fusion.2, pred[8]{0:T(512)(128)(4,1)S(1)} %get-tuple-element.10, ...), kind=kOutput, calls=%fused_computation.28 | convolution fusion | flops 537919488 | bytes 5242888 | tf_op jit(solution)/shard_map/sik,skj->ij/dot_general | solution.py:51
  (80 shorter events, 16.3 us)
Async XLA Ops:
  3.6 10.5 %collective-permute-start.3 = (bf16[512,256]{1,0:T(8,128)(2,1)}, bf16[512,256]{1,0:T(8,128)(2,1)S(1)}, u32[]{:S(2)}, u32[]{:S(2)}) collective-permute-start(bf16[512,256]{1,0:T(8,128)(2,1)} %get-tuple-element.13), channel_id=1, source_target_pairs={{0,6},{1,7},{2,4},{3,5},{4,2},{5,3},{6,0},{7,1},{8,14},{9,15},{10,... | collective-permute-start | bytes 786440 | tf_op jit(solution)/shard_map/ppermute | solution.py:24
  7.8 22.1 %collective-permute-start.2 = (bf16[512,256]{1,0:T(8,128)(2,1)}, bf16[512,256]{1,0:T(8,128)(2,1)S(1)}, u32[]{:S(2)}, u32[]{:S(2)}) collective-permute-start(bf16[512,256]{1,0:T(8,128)(2,1)} %get-tuple-element.13), channel_id=1, source_target_pairs={{0,4},{1,5},{2,6},{3,7},{4,0},{5,1},{6,2},{7,3},{8,12},{9,13},{10,... | collective-permute-start | bytes 786440 | tf_op jit(solution)/shard_map/ppermute | solution.py:24
  7.8 23.5 %collective-permute-start.1 = (bf16[512,256]{1,0:T(8,128)(2,1)}, bf16[512,256]{1,0:T(8,128)(2,1)S(1)}, u32[]{:S(2)}, u32[]{:S(2)}) collective-permute-start(bf16[512,256]{1,0:T(8,128)(2,1)} %get-tuple-element.13), channel_id=1, source_target_pairs={{0,2},{1,3},{2,0},{3,1},{4,6},{5,7},{6,4},{7,5},{8,10},{9,11},{10,... | collective-permute-start | bytes 786440 | tf_op jit(solution)/shard_map/ppermute | solution.py:24
  8.1 24.2 %collective-permute-start.7 = (bf16[512,256]{1,0:T(8,128)(2,1)}, bf16[512,256]{1,0:T(8,128)(2,1)S(1)}, u32[]{:S(2)}, u32[]{:S(2)}) collective-permute-start(bf16[512,256]{1,0:T(8,128)(2,1)} %get-tuple-element.13), channel_id=1, source_target_pairs={{0,24},{8,16},{16,8},{24,0},{1,25},{9,17},{17,9},{25,1},{2,26},{10... | collective-permute-start | bytes 786440 | tf_op jit(solution)/shard_map/ppermute | solution.py:24
  10.2 22.0 %collective-permute-start.6 = (bf16[512,256]{1,0:T(8,128)(2,1)}, bf16[512,256]{1,0:T(8,128)(2,1)S(1)}, u32[]{:S(2)}, u32[]{:S(2)}) collective-permute-start(bf16[512,256]{1,0:T(8,128)(2,1)} %get-tuple-element.13), channel_id=1, source_target_pairs={{0,16},{8,24},{16,0},{24,8},{1,17},{9,25},{17,1},{25,9},{2,18},{10... | collective-permute-start | bytes 786440 | tf_op jit(solution)/shard_map/ppermute | solution.py:24
  14.1 18.2 %collective-permute-start.5 = (bf16[512,256]{1,0:T(8,128)(2,1)}, bf16[512,256]{1,0:T(8,128)(2,1)S(1)}, u32[]{:S(2)}, u32[]{:S(2)}) collective-permute-start(bf16[512,256]{1,0:T(8,128)(2,1)} %get-tuple-element.13), channel_id=1, source_target_pairs={{0,8},{8,0},{16,24},{24,16},{1,9},{9,1},{17,25},{25,17},{2,10},{10... | collective-permute-start | bytes 786440 | tf_op jit(solution)/shard_map/ppermute | solution.py:24
  29.9 4.1 %collective-permute-start = (bf16[512,256]{1,0:T(8,128)(2,1)}, bf16[512,256]{1,0:T(8,128)(2,1)}, u32[]{:S(2)}, u32[]{:S(2)}) collective-permute-start(bf16[512,256]{1,0:T(8,128)(2,1)} %get-tuple-element.13), channel_id=1, source_target_pairs={{0,1},{1,0},{2,3},{3,2},{4,5},{5,4},{6,7},{7,6},{8,9},{9,8},{10,11... | collective-permute-start | bytes 786440 | tf_op jit(solution)/shard_map/ppermute | solution.py:24
  32.2 4.2 %collective-permute-start.4 = (bf16[3,512,256]{2,1,0:T(8,128)(2,1)}, bf16[3,512,256]{2,1,0:T(8,128)(2,1)}, u32[]{:S(2)}, u32[]{:S(2)}) collective-permute-start(bf16[3,512,256]{2,1,0:T(8,128)(2,1)} %pad_maximum_fusion.4), channel_id=1, source_target_pairs={{0,1},{1,0},{2,3},{3,2},{4,5},{5,4},{6,7},{7,6},{8,9},{9,8},{10,11... | collective-permute-start | bytes 2359304 | tf_op jit(solution)/shard_map/ppermute | solution.py:24
  46.2 8.5 %collective-permute-start.15 = (bf16[512,256]{1,0:T(8,128)(2,1)}, bf16[512,256]{1,0:T(8,128)(2,1)S(1)}, u32[]{:S(2)}, u32[]{:S(2)}) collective-permute-start(bf16[512,256]{1,0:T(8,128)(2,1)} %get-tuple-element.9), channel_id=1, source_target_pairs={{0,24},{8,16},{16,8},{24,0},{1,25},{9,17},{17,9},{25,1},{2,26},{10... | collective-permute-start | bytes 786440 | tf_op jit(solution)/shard_map/ppermute | solution.py:24
  48.4 12.8 %collective-permute-start.14 = (bf16[512,256]{1,0:T(8,128)(2,1)}, bf16[512,256]{1,0:T(8,128)(2,1)S(1)}, u32[]{:S(2)}, u32[]{:S(2)}) collective-permute-start(bf16[512,256]{1,0:T(8,128)(2,1)} %get-tuple-element.9), channel_id=1, source_target_pairs={{0,16},{8,24},{16,0},{24,8},{1,17},{9,25},{17,1},{25,9},{2,18},{10... | collective-permute-start | bytes 786440 | tf_op jit(solution)/shard_map/ppermute | solution.py:24
  48.6 13.1 %collective-permute-start.13 = (bf16[512,256]{1,0:T(8,128)(2,1)}, bf16[512,256]{1,0:T(8,128)(2,1)S(1)}, u32[]{:S(2)}, u32[]{:S(2)}) collective-permute-start(bf16[512,256]{1,0:T(8,128)(2,1)} %get-tuple-element.9), channel_id=1, source_target_pairs={{0,8},{8,0},{16,24},{24,16},{1,9},{9,1},{17,25},{25,17},{2,10},{10... | collective-permute-start | bytes 786440 | tf_op jit(solution)/shard_map/ppermute | solution.py:24
  48.9 15.5 %collective-permute-start.11 = (bf16[512,256]{1,0:T(8,128)(2,1)}, bf16[512,256]{1,0:T(8,128)(2,1)S(1)}, u32[]{:S(2)}, u32[]{:S(2)}) collective-permute-start(bf16[512,256]{1,0:T(8,128)(2,1)} %get-tuple-element.9), channel_id=1, source_target_pairs={{0,6},{1,7},{2,4},{3,5},{4,2},{5,3},{6,0},{7,1},{8,14},{9,15},{10,... | collective-permute-start | bytes 786440 | tf_op jit(solution)/shard_map/ppermute | solution.py:24
  51.1 19.6 %collective-permute-start.10 = (bf16[512,256]{1,0:T(8,128)(2,1)}, bf16[512,256]{1,0:T(8,128)(2,1)S(1)}, u32[]{:S(2)}, u32[]{:S(2)}) collective-permute-start(bf16[512,256]{1,0:T(8,128)(2,1)} %get-tuple-element.9), channel_id=1, source_target_pairs={{0,4},{1,5},{2,6},{3,7},{4,0},{5,1},{6,2},{7,3},{8,12},{9,13},{10,... | collective-permute-start | bytes 786440 | tf_op jit(solution)/shard_map/ppermute | solution.py:24
  54.7 16.0 %collective-permute-start.9 = (bf16[512,256]{1,0:T(8,128)(2,1)}, bf16[512,256]{1,0:T(8,128)(2,1)S(1)}, u32[]{:S(2)}, u32[]{:S(2)}) collective-permute-start(bf16[512,256]{1,0:T(8,128)(2,1)} %get-tuple-element.9), channel_id=1, source_target_pairs={{0,2},{1,3},{2,0},{3,1},{4,6},{5,7},{6,4},{7,5},{8,10},{9,11},{10,... | collective-permute-start | bytes 786440 | tf_op jit(solution)/shard_map/ppermute | solution.py:24
  61.2 12.8 %collective-permute-start.8 = (bf16[512,256]{1,0:T(8,128)(2,1)}, bf16[512,256]{1,0:T(8,128)(2,1)}, u32[]{:S(2)}, u32[]{:S(2)}) collective-permute-start(bf16[512,256]{1,0:T(8,128)(2,1)} %get-tuple-element.9), channel_id=1, source_target_pairs={{0,1},{1,0},{2,3},{3,2},{4,5},{5,4},{6,7},{7,6},{8,9},{9,8},{10,11... | collective-permute-start | bytes 786440 | tf_op jit(solution)/shard_map/ppermute | solution.py:24
  64.4 12.0 %copy-start.1 = (bf16[8,256,256]{2,1,0:T(8,128)(2,1)S(1)}, bf16[8,256,256]{2,1,0:T(8,128)(2,1)}, u32[]{:S(2)}) copy-start(bf16[8,256,256]{2,1,0:T(8,128)(2,1)} %gather_fusion.1) | copy-start | bytes 3145732
  70.8 8.2 %collective-permute-start.12 = (bf16[3,512,256]{2,1,0:T(8,128)(2,1)S(1)}, bf16[3,512,256]{2,1,0:T(8,128)(2,1)S(1)}, u32[]{:S(2)}, u32[]{:S(2)}) collective-permute-start(bf16[3,512,256]{2,1,0:T(8,128)(2,1)S(1)} %pad_maximum_fusion.5), channel_id=1, source_target_pairs={{0,1},{1,0},{2,3},{3,2},{4,5},{5,4},{6,7},{7,6},{8,9},{9,8},{10,11... | collective-permute-start | bytes 2359304 | tf_op jit(solution)/shard_map/ppermute | solution.py:24
  76.4 2.6 %copy-start.3 = (bf16[8,512,256]{2,1,0:T(8,128)(2,1)S(1)}, bf16[8,512,256]{2,1,0:T(8,128)(2,1)}, u32[]{:S(2)}) copy-start(bf16[8,512,256]{2,1,0:T(8,128)(2,1)} %constant_dynamic-update-slice_fusion.6) | copy-start | bytes 6291460
  79.0 1.0 copy-start.5
  81.6 10.0 %collective-permute-start.19 = (bf16[512,256]{1,0:T(8,128)(2,1)}, bf16[512,256]{1,0:T(8,128)(2,1)S(1)}, u32[]{:S(2)}, u32[]{:S(2)}) collective-permute-start(bf16[512,256]{1,0:T(8,128)(2,1)} %get-tuple-element.16), channel_id=1, source_target_pairs={{0,6},{1,7},{2,4},{3,5},{4,2},{5,3},{6,0},{7,1},{8,14},{9,15},{10,... | collective-permute-start | bytes 786440 | tf_op jit(solution)/shard_map/ppermute | solution.py:24
  83.6 22.0 %collective-permute-start.18 = (bf16[512,256]{1,0:T(8,128)(2,1)}, bf16[512,256]{1,0:T(8,128)(2,1)S(1)}, u32[]{:S(2)}, u32[]{:S(2)}) collective-permute-start(bf16[512,256]{1,0:T(8,128)(2,1)} %get-tuple-element.16), channel_id=1, source_target_pairs={{0,4},{1,5},{2,6},{3,7},{4,0},{5,1},{6,2},{7,3},{8,12},{9,13},{10,... | collective-permute-start | bytes 786440 | tf_op jit(solution)/shard_map/ppermute | solution.py:24
  83.6 22.0 %collective-permute-start.17 = (bf16[512,256]{1,0:T(8,128)(2,1)}, bf16[512,256]{1,0:T(8,128)(2,1)S(1)}, u32[]{:S(2)}, u32[]{:S(2)}) collective-permute-start(bf16[512,256]{1,0:T(8,128)(2,1)} %get-tuple-element.16), channel_id=1, source_target_pairs={{0,2},{1,3},{2,0},{3,1},{4,6},{5,7},{6,4},{7,5},{8,10},{9,11},{10,... | collective-permute-start | bytes 786440 | tf_op jit(solution)/shard_map/ppermute | solution.py:24
  85.1 22.2 %collective-permute-start.23 = (bf16[512,256]{1,0:T(8,128)(2,1)}, bf16[512,256]{1,0:T(8,128)(2,1)S(1)}, u32[]{:S(2)}, u32[]{:S(2)}) collective-permute-start(bf16[512,256]{1,0:T(8,128)(2,1)} %get-tuple-element.16), channel_id=1, source_target_pairs={{0,24},{8,16},{16,8},{24,0},{1,25},{9,17},{17,9},{25,1},{2,26},{10... | collective-permute-start | bytes 786440 | tf_op jit(solution)/shard_map/ppermute | solution.py:24
  87.3 20.0 %collective-permute-start.22 = (bf16[512,256]{1,0:T(8,128)(2,1)}, bf16[512,256]{1,0:T(8,128)(2,1)S(1)}, u32[]{:S(2)}, u32[]{:S(2)}) collective-permute-start(bf16[512,256]{1,0:T(8,128)(2,1)} %get-tuple-element.16), channel_id=1, source_target_pairs={{0,16},{8,24},{16,0},{24,8},{1,17},{9,25},{17,1},{25,9},{2,18},{10... | collective-permute-start | bytes 786440 | tf_op jit(solution)/shard_map/ppermute | solution.py:24
  91.6 15.8 %collective-permute-start.21 = (bf16[512,256]{1,0:T(8,128)(2,1)}, bf16[512,256]{1,0:T(8,128)(2,1)S(1)}, u32[]{:S(2)}, u32[]{:S(2)}) collective-permute-start(bf16[512,256]{1,0:T(8,128)(2,1)} %get-tuple-element.16), channel_id=1, source_target_pairs={{0,8},{8,0},{16,24},{24,16},{1,9},{9,1},{17,25},{25,17},{2,10},{10... | collective-permute-start | bytes 786440 | tf_op jit(solution)/shard_map/ppermute | solution.py:24
  106.5 5.8 %collective-permute-start.20 = (bf16[3,512,256]{2,1,0:T(8,128)(2,1)}, bf16[3,512,256]{2,1,0:T(8,128)(2,1)}, u32[]{:S(2)}, u32[]{:S(2)}) collective-permute-start(bf16[3,512,256]{2,1,0:T(8,128)(2,1)} %pad_maximum_fusion.6), channel_id=1, source_target_pairs={{0,1},{1,0},{2,3},{3,2},{4,5},{5,4},{6,7},{7,6},{8,9},{9,8},{10,11... | collective-permute-start | bytes 2359304 | tf_op jit(solution)/shard_map/ppermute | solution.py:24
  107.3 2.6 %collective-permute-start.16 = (bf16[512,256]{1,0:T(8,128)(2,1)}, bf16[512,256]{1,0:T(8,128)(2,1)}, u32[]{:S(2)}, u32[]{:S(2)}) collective-permute-start(bf16[512,256]{1,0:T(8,128)(2,1)} %get-tuple-element.16), channel_id=1, source_target_pairs={{0,1},{1,0},{2,3},{3,2},{4,5},{5,4},{6,7},{7,6},{8,9},{9,8},{10,11... | collective-permute-start | bytes 786440 | tf_op jit(solution)/shard_map/ppermute | solution.py:24
  122.2 8.7 %collective-permute-start.31 = (bf16[512,256]{1,0:T(8,128)(2,1)}, bf16[512,256]{1,0:T(8,128)(2,1)S(1)}, u32[]{:S(2)}, u32[]{:S(2)}) collective-permute-start(bf16[512,256]{1,0:T(8,128)(2,1)} %get-tuple-element.7), channel_id=1, source_target_pairs={{0,24},{8,16},{16,8},{24,0},{1,25},{9,17},{17,9},{25,1},{2,26},{10... | collective-permute-start | bytes 786440 | tf_op jit(solution)/shard_map/ppermute | solution.py:24
  124.3 12.8 %collective-permute-start.30 = (bf16[512,256]{1,0:T(8,128)(2,1)}, bf16[512,256]{1,0:T(8,128)(2,1)S(1)}, u32[]{:S(2)}, u32[]{:S(2)}) collective-permute-start(bf16[512,256]{1,0:T(8,128)(2,1)} %get-tuple-element.7), channel_id=1, source_target_pairs={{0,16},{8,24},{16,0},{24,8},{1,17},{9,25},{17,1},{25,9},{2,18},{10... | collective-permute-start | bytes 786440 | tf_op jit(solution)/shard_map/ppermute | solution.py:24
  124.6 13.1 %collective-permute-start.29 = (bf16[512,256]{1,0:T(8,128)(2,1)}, bf16[512,256]{1,0:T(8,128)(2,1)S(1)}, u32[]{:S(2)}, u32[]{:S(2)}) collective-permute-start(bf16[512,256]{1,0:T(8,128)(2,1)} %get-tuple-element.7), channel_id=1, source_target_pairs={{0,8},{8,0},{16,24},{24,16},{1,9},{9,1},{17,25},{25,17},{2,10},{10... | collective-permute-start | bytes 786440 | tf_op jit(solution)/shard_map/ppermute | solution.py:24
  124.8 15.5 %collective-permute-start.27 = (bf16[512,256]{1,0:T(8,128)(2,1)}, bf16[512,256]{1,0:T(8,128)(2,1)S(1)}, u32[]{:S(2)}, u32[]{:S(2)}) collective-permute-start(bf16[512,256]{1,0:T(8,128)(2,1)} %get-tuple-element.7), channel_id=1, source_target_pairs={{0,6},{1,7},{2,4},{3,5},{4,2},{5,3},{6,0},{7,1},{8,14},{9,15},{10,... | collective-permute-start | bytes 786440 | tf_op jit(solution)/shard_map/ppermute | solution.py:24
  126.1 20.3 %collective-permute-start.26 = (bf16[512,256]{1,0:T(8,128)(2,1)}, bf16[512,256]{1,0:T(8,128)(2,1)S(1)}, u32[]{:S(2)}, u32[]{:S(2)}) collective-permute-start(bf16[512,256]{1,0:T(8,128)(2,1)} %get-tuple-element.7), channel_id=1, source_target_pairs={{0,4},{1,5},{2,6},{3,7},{4,0},{5,1},{6,2},{7,3},{8,12},{9,13},{10,... | collective-permute-start | bytes 786440 | tf_op jit(solution)/shard_map/ppermute | solution.py:24
  130.8 15.6 %collective-permute-start.25 = (bf16[512,256]{1,0:T(8,128)(2,1)}, bf16[512,256]{1,0:T(8,128)(2,1)S(1)}, u32[]{:S(2)}, u32[]{:S(2)}) collective-permute-start(bf16[512,256]{1,0:T(8,128)(2,1)} %get-tuple-element.7), channel_id=1, source_target_pairs={{0,2},{1,3},{2,0},{3,1},{4,6},{5,7},{6,4},{7,5},{8,10},{9,11},{10,... | collective-permute-start | bytes 786440 | tf_op jit(solution)/shard_map/ppermute | solution.py:24
  137.1 12.6 %collective-permute-start.24 = (bf16[512,256]{1,0:T(8,128)(2,1)}, bf16[512,256]{1,0:T(8,128)(2,1)}, u32[]{:S(2)}, u32[]{:S(2)}) collective-permute-start(bf16[512,256]{1,0:T(8,128)(2,1)} %get-tuple-element.7), channel_id=1, source_target_pairs={{0,1},{1,0},{2,3},{3,2},{4,5},{5,4},{6,7},{7,6},{8,9},{9,8},{10,11... | collective-permute-start | bytes 786440 | tf_op jit(solution)/shard_map/ppermute | solution.py:24
  140.3 11.8 %copy-start = (bf16[8,256,256]{2,1,0:T(8,128)(2,1)S(1)}, bf16[8,256,256]{2,1,0:T(8,128)(2,1)}, u32[]{:S(2)}) copy-start(bf16[8,256,256]{2,1,0:T(8,128)(2,1)} %gather_fusion.3) | copy-start | bytes 3145732
  146.5 8.2 %collective-permute-start.28 = (bf16[3,512,256]{2,1,0:T(8,128)(2,1)S(1)}, bf16[3,512,256]{2,1,0:T(8,128)(2,1)S(1)}, u32[]{:S(2)}, u32[]{:S(2)}) collective-permute-start(bf16[3,512,256]{2,1,0:T(8,128)(2,1)S(1)} %pad_maximum_fusion.7), channel_id=1, source_target_pairs={{0,1},{1,0},{2,3},{3,2},{4,5},{5,4},{6,7},{7,6},{8,9},{9,8},{10,11... | collective-permute-start | bytes 2359304 | tf_op jit(solution)/shard_map/ppermute | solution.py:24
  152.2 2.6 %copy-start.2 = (bf16[8,512,256]{2,1,0:T(8,128)(2,1)S(1)}, bf16[8,512,256]{2,1,0:T(8,128)(2,1)}, u32[]{:S(2)}) copy-start(bf16[8,512,256]{2,1,0:T(8,128)(2,1)} %constant_dynamic-update-slice_fusion.14) | copy-start | bytes 6291460
  154.7 1.0 copy-start.4

commit v2 on v1

--- a/solution.py
+++ b/solution.py
@@ -34,7 +34,7 @@
     for s in range(chips):
         row_pieces.append(same_core[s])
         row_pieces.append(partner_own if s == 0 else relayed[s - 1])
-    return jnp.stack(row_pieces), jnp.stack(col_pieces)
+    return row_pieces, jnp.stack(col_pieces)
 
 
 def ordered_k_blocks(col_pieces, me_row, me_col, n_col):
@@ -48,7 +48,11 @@
 
 
 def contract(row_pieces, k_blocks):
-    return jnp.einsum("sik,skj->ij", row_pieces, k_blocks, preferred_element_type=jnp.float32)
+    total = None
+    for s, piece in enumerate(row_pieces):
+        part = jnp.dot(piece, k_blocks[s], preferred_element_type=jnp.float32)
+        total = part if total is None else total + part
+    return total
 
 
 def on_device(density, pattern):

time: 158 us -> 156 us (0.987)
  matrix products: 14.9 us -> 40.4 us
  local copies, waits for them, and re-layouts: 29.9 us -> 8.96 us
  waiting for transfers between devices: 69.7 us -> 61.1 us
    dot_general x6 -> x48, matrix products: 14.9 us -> 40.4 us  [contract(): part = jnp.dot(piece, k_blocks[s], preferred_element_type=jnp.float32)]
    unnamed x37 -> x25, local copies, waits for them, and re-layouts: 21.8 us -> 3.85 us
    ppermute x32, waiting for transfers between devices: 69.7 us -> 61.1 us  [xor_permute(): return lax.ppermute(x, axis, perm=[(i, i ^ s) for i in range(size)])]
    another operation x4 -> x0, local copies, waits for them, and re-layouts: 3.38 us -> none  [exchange(): return (jnp.stack(row_pieces), jnp.stack(col_pieces))]
    another operation x4, other arithmetic: 2.12 us -> 4.35 us  [exchange(): relayed = xor_permute(jnp.stack(same_core[1:]), 'col', n_col, 1)]
    unnamed x1 -> x0, other arithmetic: 1.88 us -> none
  transfers between devices with their start and end apart: 32 -> 32, of which waited for: 11 -> 10; matrix products, arithmetic and copies ran while one was open for 16% -> 26% of each run, Pallas kernels for 0% -> 0%
where the time goes in v2:
time: 156 us; the launch traced here: 154 us
  waiting for transfers between devices  61.1 us (39%)
  matrix products  40.4 us (26%)
  starting transfers between devices  33.7 us (22%)
  other arithmetic  9.64 us (6%)
  local copies, waits for them, and re-layouts  8.96 us (6%)
    ppermute x32, waiting for transfers between devices, xor_permute(): return lax.ppermute(x, axis, perm=[(i, i ^ s) for i in range(size)])  61.1 us
    dot_general x48, matrix products, contract(): part = jnp.dot(piece, k_blocks[s], preferred_element_type=jnp.float32)  40.4 us
    ppermute x32, starting transfers between devices, xor_permute(): return lax.ppermute(x, axis, perm=[(i, i ^ s) for i in range(size)])  33.7 us
    gather x4, local copies, waits for them, and re-layouts, ordered_k_blocks(): return jnp.take(split, index, axis=0)  4.9 us
    another operation x4, other arithmetic, exchange(): return (row_pieces, jnp.stack(col_pieces))  4.46 us
    another operation x4, other arithmetic, exchange(): relayed = xor_permute(jnp.stack(same_core[1:]), 'col', n_col, 1)  4.35 us
    unnamed x25, local copies, waits for them, and re-layouts  3.85 us
  transfers between devices with their start and end apart: 32, of which 10 were waited for; matrix products, arithmetic and copies ran while one was open for 26% of the time, Pallas kernels for 0%

profile of v2, /device:TPU:1, one launch (start us, length us, event | category | flops | bytes accessed | tf_op | source)
XLA Modules:
  0.0 154.5 jit_solution(13268229035559185857)
XLA Ops:
  1.2 4.2 %collective-permute-start.6 = (bf16[512,256]{1,0:T(8,128)(2,1)S(1)}, bf16[512,256]{1,0:T(8,128)(2,1)S(1)}, u32[]{:S(2)}, u32[]{:S(2)}) collective-permute-start(bf16[512,256]{1,0:T(8,128)(2,1)S(1)} %fusion.39), channel_id=1, source_target_pairs={{0,6},{1,7},{2,4},{3,5},{4,2},{5,3},{6,0},{7,1},{8,14},{9,15},{10,... | collective-permute-start | bytes 786440 | tf_op jit(solution)/shard_map/ppermute | solution.py:24
  5.7 2.2 %collective-permute-start.2 = (bf16[512,256]{1,0:T(8,128)(2,1)S(1)}, bf16[512,256]{1,0:T(8,128)(2,1)S(1)}, u32[]{:S(2)}, u32[]{:S(2)}) collective-permute-start(bf16[512,256]{1,0:T(8,128)(2,1)S(1)} %fusion.39), channel_id=1, source_target_pairs={{0,24},{8,16},{16,8},{24,0},{1,25},{9,17},{17,9},{25,1},{2,26},{10... | collective-permute-start | bytes 786440 | tf_op jit(solution)/shard_map/ppermute | solution.py:24
  8.1 3.4 %collective-permute-done.6 = bf16[512,256]{1,0:T(8,128)(2,1)S(1)} collective-permute-done((bf16[512,256]{1,0:T(8,128)(2,1)S(1)}, bf16[512,256]{1,0:T(8,128)(2,1)S(1)}, u32[]{:S(2)}, u32[]{:S(2)}) %collective-permute-start.6) | collective-permute-done | bytes 262176 | tf_op jit(solution)/shard_map/ppermute | solution.py:24
  12.5 14.7 %collective-permute-done.5 = bf16[512,256]{1,0:T(8,128)(2,1)S(1)} collective-permute-done((bf16[512,256]{1,0:T(8,128)(2,1)S(1)}, bf16[512,256]{1,0:T(8,128)(2,1)S(1)}, u32[]{:S(2)}, u32[]{:S(2)}) %collective-permute-start.5) | collective-permute-done | bytes 262176 | tf_op jit(solution)/shard_map/ppermute | solution.py:24
  27.3 1.4 collective-permute-start.3
  32.0 1.2 convolution_add_fusion.11
  36.7 1.2 fusion.79
  37.9 2.2 %collective-permute-start.15 = (bf16[512,256]{1,0:T(8,128)(2,1)}, bf16[512,256]{1,0:T(8,128)(2,1)S(1)}, u32[]{:S(2)}, u32[]{:S(2)}) collective-permute-start(bf16[512,256]{1,0:T(8,128)(2,1)} %get-tuple-element.8), channel_id=1, source_target_pairs={{0,24},{8,16},{16,8},{24,0},{1,25},{9,17},{17,9},{25,1},{2,26},{10... | collective-permute-start | bytes 786440 | tf_op jit(solution)/shard_map/ppermute | solution.py:24
  40.6 2.2 %collective-permute-start.11 = (bf16[512,256]{1,0:T(8,128)(2,1)}, bf16[512,256]{1,0:T(8,128)(2,1)}, u32[]{:S(2)}, u32[]{:S(2)}) collective-permute-start(bf16[512,256]{1,0:T(8,128)(2,1)} %get-tuple-element.8), channel_id=1, source_target_pairs={{0,6},{1,7},{2,4},{3,5},{4,2},{5,3},{6,0},{7,1},{8,14},{9,15},{10,... | collective-permute-start | bytes 786440 | tf_op jit(solution)/shard_map/ppermute | solution.py:24
  42.8 2.1 %fusion.64 = f32[512,256]{1,0:T(8,128)} fusion(bf16[512,256]{1,0:T(8,128)(2,1)} %get-tuple-element.8, bf16[8,256,256]{2,1,0:T(8,128)(2,1)S(1)} %broadcast_select_fusion.3), kind=kOutput, calls=%fused_computation.137 | convolution fusion | flops 67108864 | bytes 917504 | tf_op jit(solution)/shard_map/dot_general | solution.py:53
  44.8 1.6 %collective-permute-done.15 = bf16[512,256]{1,0:T(8,128)(2,1)S(1)} collective-permute-done((bf16[512,256]{1,0:T(8,128)(2,1)}, bf16[512,256]{1,0:T(8,128)(2,1)S(1)}, u32[]{:S(2)}, u32[]{:S(2)}) %collective-permute-start.15) | collective-permute-done | bytes 262176 | tf_op jit(solution)/shard_map/ppermute | solution.py:24
  46.5 6.5 %collective-permute-done.14 = bf16[512,256]{1,0:T(8,128)(2,1)S(1)} collective-permute-done((bf16[512,256]{1,0:T(8,128)(2,1)}, bf16[512,256]{1,0:T(8,128)(2,1)S(1)}, u32[]{:S(2)}, u32[]{:S(2)}) %collective-permute-start.14) | collective-permute-done | bytes 262176 | tf_op jit(solution)/shard_map/ppermute | solution.py:24
  53.4 2.1 %pad_maximum_fusion.1 = bf16[4,512,256]{2,1,0:T(8,128)(2,1)} fusion(bf16[1,512,256]{2,1,0:T(8,128)(2,1)S(1)} %bitcast.251, bf16[1,512,256]{2,1,0:T(8,128)(2,1)S(1)} %bitcast.255, bf16[1,512,256]{2,1,0:T(8,128)(2,1)S(1)} %bitcast.257, bf16[1,512,256]{2,1,0:T(8,128)(2,1)} %bitcast.26), kind=kLoop, calls=%fused_computation.56 | loop fusion | flops 1572864 | bytes 2097152 | tf_op jit(solution)/shard_map/stack | solution.py:37
  55.5 1.8 %gather_fusion.1 = bf16[8,256,256]{2,1,0:T(8,128)(2,1)S(1)} fusion(bf16[8,256,256]{2,1,0:T(8,128)(2,1)} %bitcast.238, s32[1024]{0:T(1024)S(1)} %pad_clamp_fusion), kind=kCustom, calls=%fused_computation.1.clone | custom fusion | bytes 2097184 | tf_op jit(solution)/shard_map/jit(_take)/gather | solution.py:47
  57.7 4.3 %collective-permute-done.10 = bf16[512,256]{1,0:T(8,128)(2,1)} collective-permute-done((bf16[512,256]{1,0:T(8,128)(2,1)}, bf16[512,256]{1,0:T(8,128)(2,1)}, u32[]{:S(2)}, u32[]{:S(2)}) %collective-permute-start.10) | collective-permute-done | bytes 262176 | tf_op jit(solution)/shard_map/ppermute | solution.py:24
  62.0 1.2 pad_maximum_fusion.5
  63.2 3.6 %collective-permute-start.12 = (bf16[3,512,256]{2,1,0:T(8,128)(2,1)S(1)}, bf16[3,512,256]{2,1,0:T(8,128)(2,1)S(1)}, u32[]{:S(2)}, u32[]{:S(2)}) collective-permute-start(bf16[3,512,256]{2,1,0:T(8,128)(2,1)S(1)} %pad_maximum_fusion.5), channel_id=1, source_target_pairs={{0,1},{1,0},{2,3},{3,2},{4,5},{5,4},{6,7},{7,6},{8,9},{9,8},{10,11... | collective-permute-start | bytes 2359304 | tf_op jit(solution)/shard_map/ppermute | solution.py:24
  66.8 1.2 fusion.50
  68.2 1.2 fusion.48
  70.9 1.2 convolution_add_fusion.7
  72.1 1.2 fusion.68
  73.2 1.2 fusion.66
  74.5 1.2 convolution_add_fusion.9
  77.5 1.3 fusion.38
  78.8 2.2 %collective-permute-start.22 = (bf16[512,256]{1,0:T(8,128)(2,1)S(1)}, bf16[512,256]{1,0:T(8,128)(2,1)S(1)}, u32[]{:S(2)}, u32[]{:S(2)}) collective-permute-start(bf16[512,256]{1,0:T(8,128)(2,1)S(1)} %fusion.38), channel_id=1, source_target_pairs={{0,6},{1,7},{2,4},{3,5},{4,2},{5,3},{6,0},{7,1},{8,14},{9,15},{10,... | collective-permute-start | bytes 786440 | tf_op jit(solution)/shard_map/ppermute | solution.py:24
  81.0 1.5 collective-permute-start.20
  82.4 2.2 %collective-permute-start.18 = (bf16[512,256]{1,0:T(8,128)(2,1)S(1)}, bf16[512,256]{1,0:T(8,128)(2,1)S(1)}, u32[]{:S(2)}, u32[]{:S(2)}) collective-permute-start(bf16[512,256]{1,0:T(8,128)(2,1)S(1)} %fusion.38), channel_id=1, source_target_pairs={{0,24},{8,16},{16,8},{24,0},{1,25},{9,17},{17,9},{25,1},{2,26},{10... | collective-permute-start | bytes 786440 | tf_op jit(solution)/shard_map/ppermute | solution.py:24
  84.8 3.8 %collective-permute-done.22 = bf16[512,256]{1,0:T(8,128)(2,1)S(1)} collective-permute-done((bf16[512,256]{1,0:T(8,128)(2,1)S(1)}, bf16[512,256]{1,0:T(8,128)(2,1)S(1)}, u32[]{:S(2)}, u32[]{:S(2)}) %collective-permute-start.22) | collective-permute-done | bytes 262176 | tf_op jit(solution)/shard_map/ppermute | solution.py:24
  88.7 1.2 collective-permute-start.16
  89.9 12.7 %collective-permute-done.21 = bf16[512,256]{1,0:T(8,128)(2,1)S(1)} collective-permute-done((bf16[512,256]{1,0:T(8,128)(2,1)S(1)}, bf16[512,256]{1,0:T(8,128)(2,1)S(1)}, u32[]{:S(2)}, u32[]{:S(2)}) %collective-permute-start.21) | collective-permute-done | bytes 262176 | tf_op jit(solution)/shard_map/ppermute | solution.py:24
  106.8 1.2 convolution_add_fusion.5
  111.5 1.2 fusion.80
  112.7 2.2 %collective-permute-start.31 = (bf16[512,256]{1,0:T(8,128)(2,1)}, bf16[512,256]{1,0:T(8,128)(2,1)S(1)}, u32[]{:S(2)}, u32[]{:S(2)}) collective-permute-start(bf16[512,256]{1,0:T(8,128)(2,1)} %get-tuple-element.10), channel_id=1, source_target_pairs={{0,24},{8,16},{16,8},{24,0},{1,25},{9,17},{17,9},{25,1},{2,26},{10... | collective-permute-start | bytes 786440 | tf_op jit(solution)/shard_map/ppermute | solution.py:24
  116.6 2.1 %fusion.70 = f32[512,256]{1,0:T(8,128)} fusion(bf16[512,256]{1,0:T(8,128)(2,1)} %get-tuple-element.10, bf16[8,256,256]{2,1,0:T(8,128)(2,1)S(1)} %broadcast_select_fusion.1), kind=kOutput, calls=%fused_computation.143 | convolution fusion | flops 67108864 | bytes 917504 | tf_op jit(solution)/shard_map/dot_general | solution.py:53
  118.6 2.7 %collective-permute-done.31 = bf16[512,256]{1,0:T(8,128)(2,1)S(1)} collective-permute-done((bf16[512,256]{1,0:T(8,128)(2,1)}, bf16[512,256]{1,0:T(8,128)(2,1)S(1)}, u32[]{:S(2)}, u32[]{:S(2)}) %collective-permute-start.31) | collective-permute-done | bytes 262176 | tf_op jit(solution)/shard_map/ppermute | solution.py:24
  121.3 6.5 %collective-permute-done.30 = bf16[512,256]{1,0:T(8,128)(2,1)S(1)} collective-permute-done((bf16[512,256]{1,0:T(8,128)(2,1)}, bf16[512,256]{1,0:T(8,128)(2,1)S(1)}, u32[]{:S(2)}, u32[]{:S(2)}) %collective-permute-start.30) | collective-permute-done | bytes 262176 | tf_op jit(solution)/shard_map/ppermute | solution.py:24
  128.2 2.1 %pad_maximum_fusion.3 = bf16[4,512,256]{2,1,0:T(8,128)(2,1)} fusion(bf16[1,512,256]{2,1,0:T(8,128)(2,1)S(1)} %bitcast.252, bf16[1,512,256]{2,1,0:T(8,128)(2,1)S(1)} %bitcast.256, bf16[1,512,256]{2,1,0:T(8,128)(2,1)S(1)} %bitcast.258, bf16[1,512,256]{2,1,0:T(8,128)(2,1)} %bitcast.64), kind=kLoop, calls=%fused_computation.58 | loop fusion | flops 1572864 | bytes 2097152 | tf_op jit(solution)/shard_map/stack | solution.py:37
  130.3 1.8 %gather_fusion.3 = bf16[8,256,256]{2,1,0:T(8,128)(2,1)S(1)} fusion(bf16[8,256,256]{2,1,0:T(8,128)(2,1)} %bitcast.236, s32[1024]{0:T(1024)S(1)} %pad_clamp_fusion), kind=kCustom, calls=%fused_computation.3.clone | custom fusion | bytes 2097184 | tf_op jit(solution)/shard_map/jit(_take)/gather | solution.py:47
  132.5 4.7 %collective-permute-done.26 = bf16[512,256]{1,0:T(8,128)(2,1)} collective-permute-done((bf16[512,256]{1,0:T(8,128)(2,1)}, bf16[512,256]{1,0:T(8,128)(2,1)}, u32[]{:S(2)}, u32[]{:S(2)}) %collective-permute-start.26) | collective-permute-done | bytes 262176 | tf_op jit(solution)/shard_map/ppermute | solution.py:24
  137.3 1.2 pad_maximum_fusion.7
  138.5 3.2 %collective-permute-start.28 = (bf16[3,512,256]{2,1,0:T(8,128)(2,1)S(1)}, bf16[3,512,256]{2,1,0:T(8,128)(2,1)S(1)}, u32[]{:S(2)}, u32[]{:S(2)}) collective-permute-start(bf16[3,512,256]{2,1,0:T(8,128)(2,1)S(1)} %pad_maximum_fusion.7), channel_id=1, source_target_pairs={{0,1},{1,0},{2,3},{3,2},{4,5},{5,4},{6,7},{7,6},{8,9},{9,8},{10,11... | collective-permute-start | bytes 2359304 | tf_op jit(solution)/shard_map/ppermute | solution.py:24
  141.7 1.2 fusion.56
  143.1 1.2 fusion.54
  145.8 1.2 convolution_add_fusion.1
  147.0 1.2 fusion.74
  148.1 1.2 fusion.72
  149.4 1.2 convolution_add_fusion.3
  152.4 2.1 %fusion.12 = f32[512,256]{1,0:T(8,128)} fusion(f32[512,256]{1,0:T(8,128)S(1)} %fusion.4, f32[512,256]{1,0:T(8,128)S(1)} %fusion.40, f32[512,256]{1,0:T(8,128)S(1)} %fusion.74, f32[512,256]{1,0:T(8,128)S(1)} %fusion.41, f32[512,256]{1,0:T(8,128)S(1)} %fusion.72, f32[512,256]{1,0:T(8,128)S(1)} %fusion.42, f32[512,256]{1,0:T(8,128)S(1)} %convolution_add_fusion.3, ...), kind=kOutput, calls=%fused_computation.19 | convolution fusion | flops 68419584 | bytes 5636096 | tf_op jit(solution)/shard_map/dot_general | solution.py:53
  (110 shorter events, 27.8 us)
Async XLA Ops:
  0.0 0.7 copy-start.11
  0.0 1.1 copy-start.10
  1.2 10.3 %collective-permute-start.6 = (bf16[512,256]{1,0:T(8,128)(2,1)S(1)}, bf16[512,256]{1,0:T(8,128)(2,1)S(1)}, u32[]{:S(2)}, u32[]{:S(2)}) collective-permute-start(bf16[512,256]{1,0:T(8,128)(2,1)S(1)} %fusion.39), channel_id=1, source_target_pairs={{0,6},{1,7},{2,4},{3,5},{4,2},{5,3},{6,0},{7,1},{8,14},{9,15},{10,... | collective-permute-start | bytes 786440 | tf_op jit(solution)/shard_map/ppermute | solution.py:24
  5.4 21.9 %collective-permute-start.5 = (bf16[512,256]{1,0:T(8,128)(2,1)S(1)}, bf16[512,256]{1,0:T(8,128)(2,1)S(1)}, u32[]{:S(2)}, u32[]{:S(2)}) collective-permute-start(bf16[512,256]{1,0:T(8,128)(2,1)S(1)} %fusion.39), channel_id=1, source_target_pairs={{0,4},{1,5},{2,6},{3,7},{4,0},{5,1},{6,2},{7,3},{8,12},{9,13},{10,... | collective-permute-start | bytes 786440 | tf_op jit(solution)/shard_map/ppermute | solution.py:24
  5.4 23.3 %collective-permute-start.4 = (bf16[512,256]{1,0:T(8,128)(2,1)S(1)}, bf16[512,256]{1,0:T(8,128)(2,1)S(1)}, u32[]{:S(2)}, u32[]{:S(2)}) collective-permute-start(bf16[512,256]{1,0:T(8,128)(2,1)S(1)} %fusion.39), channel_id=1, source_target_pairs={{0,2},{1,3},{2,0},{3,1},{4,6},{5,7},{6,4},{7,5},{8,10},{9,11},{10,... | collective-permute-start | bytes 786440 | tf_op jit(solution)/shard_map/ppermute | solution.py:24
  5.7 23.9 %collective-permute-start.2 = (bf16[512,256]{1,0:T(8,128)(2,1)S(1)}, bf16[512,256]{1,0:T(8,128)(2,1)S(1)}, u32[]{:S(2)}, u32[]{:S(2)}) collective-permute-start(bf16[512,256]{1,0:T(8,128)(2,1)S(1)} %fusion.39), channel_id=1, source_target_pairs={{0,24},{8,16},{16,8},{24,0},{1,25},{9,17},{17,9},{25,1},{2,26},{10... | collective-permute-start | bytes 786440 | tf_op jit(solution)/shard_map/ppermute | solution.py:24
  7.9 21.7 %collective-permute-start.1 = (bf16[512,256]{1,0:T(8,128)(2,1)S(1)}, bf16[512,256]{1,0:T(8,128)(2,1)S(1)}, u32[]{:S(2)}, u32[]{:S(2)}) collective-permute-start(bf16[512,256]{1,0:T(8,128)(2,1)S(1)} %fusion.39), channel_id=1, source_target_pairs={{0,16},{8,24},{16,0},{24,8},{1,17},{9,25},{17,1},{25,9},{2,18},{10... | collective-permute-start | bytes 786440 | tf_op jit(solution)/shard_map/ppermute | solution.py:24
  11.5 18.2 %collective-permute-start = (bf16[512,256]{1,0:T(8,128)(2,1)S(1)}, bf16[512,256]{1,0:T(8,128)(2,1)S(1)}, u32[]{:S(2)}, u32[]{:S(2)}) collective-permute-start(bf16[512,256]{1,0:T(8,128)(2,1)S(1)} %fusion.39), channel_id=1, source_target_pairs={{0,8},{8,0},{16,24},{24,16},{1,9},{9,1},{17,25},{25,17},{2,10},{10... | collective-permute-start | bytes 786440 | tf_op jit(solution)/shard_map/ppermute | solution.py:24
  27.3 2.3 %copy-start = (bf16[512,256]{1,0:T(8,128)(2,1)}, bf16[512,256]{1,0:T(8,128)(2,1)S(1)}, u32[]{:S(2)}) copy-start(bf16[512,256]{1,0:T(8,128)(2,1)S(1)} %collective-permute-done.5) | copy-start | bytes 786436
  27.3 4.7 %collective-permute-start.3 = (bf16[512,256]{1,0:T(8,128)(2,1)S(1)}, bf16[512,256]{1,0:T(8,128)(2,1)}, u32[]{:S(2)}, u32[]{:S(2)}) collective-permute-start(bf16[512,256]{1,0:T(8,128)(2,1)S(1)} %fusion.39), channel_id=1, source_target_pairs={{0,1},{1,0},{2,3},{3,2},{4,5},{5,4},{6,7},{7,6},{8,9},{9,8},{10,11... | collective-permute-start | bytes 786440 | tf_op jit(solution)/shard_map/ppermute | solution.py:24
  29.6 3.6 %collective-permute-start.7 = (bf16[3,512,256]{2,1,0:T(8,128)(2,1)}, bf16[3,512,256]{2,1,0:T(8,128)(2,1)}, u32[]{:S(2)}, u32[]{:S(2)}) collective-permute-start(bf16[3,512,256]{2,1,0:T(8,128)(2,1)} %pad_maximum_fusion.4), channel_id=1, source_target_pairs={{0,1},{1,0},{2,3},{3,2},{4,5},{5,4},{6,7},{7,6},{8,9},{9,8},{10,11... | collective-permute-start | bytes 2359304 | tf_op jit(solution)/shard_map/ppermute | solution.py:24
  30.8 1.0 copy-start.1
  37.9 8.5 %collective-permute-start.15 = (bf16[512,256]{1,0:T(8,128)(2,1)}, bf16[512,256]{1,0:T(8,128)(2,1)S(1)}, u32[]{:S(2)}, u32[]{:S(2)}) collective-permute-start(bf16[512,256]{1,0:T(8,128)(2,1)} %get-tuple-element.8), channel_id=1, source_target_pairs={{0,24},{8,16},{16,8},{24,0},{1,25},{9,17},{17,9},{25,1},{2,26},{10... | collective-permute-start | bytes 786440 | tf_op jit(solution)/shard_map/ppermute | solution.py:24
  40.1 12.9 %collective-permute-start.14 = (bf16[512,256]{1,0:T(8,128)(2,1)}, bf16[512,256]{1,0:T(8,128)(2,1)S(1)}, u32[]{:S(2)}, u32[]{:S(2)}) collective-permute-start(bf16[512,256]{1,0:T(8,128)(2,1)} %get-tuple-element.8), channel_id=1, source_target_pairs={{0,16},{8,24},{16,0},{24,8},{1,17},{9,25},{17,1},{25,9},{2,18},{10... | collective-permute-start | bytes 786440 | tf_op jit(solution)/shard_map/ppermute | solution.py:24
  40.3 13.1 %collective-permute-start.13 = (bf16[512,256]{1,0:T(8,128)(2,1)}, bf16[512,256]{1,0:T(8,128)(2,1)S(1)}, u32[]{:S(2)}, u32[]{:S(2)}) collective-permute-start(bf16[512,256]{1,0:T(8,128)(2,1)} %get-tuple-element.8), channel_id=1, source_target_pairs={{0,8},{8,0},{16,24},{24,16},{1,9},{9,1},{17,25},{25,17},{2,10},{10... | collective-permute-start | bytes 786440 | tf_op jit(solution)/shard_map/ppermute | solution.py:24
  40.6 17.1 %collective-permute-start.11 = (bf16[512,256]{1,0:T(8,128)(2,1)}, bf16[512,256]{1,0:T(8,128)(2,1)}, u32[]{:S(2)}, u32[]{:S(2)}) collective-permute-start(bf16[512,256]{1,0:T(8,128)(2,1)} %get-tuple-element.8), channel_id=1, source_target_pairs={{0,6},{1,7},{2,4},{3,5},{4,2},{5,3},{6,0},{7,1},{8,14},{9,15},{10,... | collective-permute-start | bytes 786440 | tf_op jit(solution)/shard_map/ppermute | solution.py:24
  42.8 19.2 %collective-permute-start.10 = (bf16[512,256]{1,0:T(8,128)(2,1)}, bf16[512,256]{1,0:T(8,128)(2,1)}, u32[]{:S(2)}, u32[]{:S(2)}) collective-permute-start(bf16[512,256]{1,0:T(8,128)(2,1)} %get-tuple-element.8), channel_id=1, source_target_pairs={{0,4},{1,5},{2,6},{3,7},{4,0},{5,1},{6,2},{7,3},{8,12},{9,13},{10,... | collective-permute-start | bytes 786440 | tf_op jit(solution)/shard_map/ppermute | solution.py:24
  46.5 15.5 %collective-permute-start.9 = (bf16[512,256]{1,0:T(8,128)(2,1)}, bf16[512,256]{1,0:T(8,128)(2,1)}, u32[]{:S(2)}, u32[]{:S(2)}) collective-permute-start(bf16[512,256]{1,0:T(8,128)(2,1)} %get-tuple-element.8), channel_id=1, source_target_pairs={{0,2},{1,3},{2,0},{3,1},{4,6},{5,7},{6,4},{7,5},{8,10},{9,11},{10,... | collective-permute-start | bytes 786440 | tf_op jit(solution)/shard_map/ppermute | solution.py:24
  53.0 21.5 %collective-permute-start.8 = (bf16[512,256]{1,0:T(8,128)(2,1)}, bf16[512,256]{1,0:T(8,128)(2,1)}, u32[]{:S(2)}, u32[]{:S(2)}) collective-permute-start(bf16[512,256]{1,0:T(8,128)(2,1)} %get-tuple-element.8), channel_id=1, source_target_pairs={{0,1},{1,0},{2,3},{3,2},{4,5},{5,4},{6,7},{7,6},{8,9},{9,8},{10,11... | collective-permute-start | bytes 786440 | tf_op jit(solution)/shard_map/ppermute | solution.py:24
  63.2 12.8 %collective-permute-start.12 = (bf16[3,512,256]{2,1,0:T(8,128)(2,1)S(1)}, bf16[3,512,256]{2,1,0:T(8,128)(2,1)S(1)}, u32[]{:S(2)}, u32[]{:S(2)}) collective-permute-start(bf16[3,512,256]{2,1,0:T(8,128)(2,1)S(1)} %pad_maximum_fusion.5), channel_id=1, source_target_pairs={{0,1},{1,0},{2,3},{3,2},{4,5},{5,4},{6,7},{7,6},{8,9},{9,8},{10,11... | collective-permute-start | bytes 2359304 | tf_op jit(solution)/shard_map/ppermute | solution.py:24
  68.2 1.2 copy-start.2
  73.2 1.3 copy-start.7
  76.4 1.0 copy-start.9
  78.8 9.9 %collective-permute-start.22 = (bf16[512,256]{1,0:T(8,128)(2,1)S(1)}, bf16[512,256]{1,0:T(8,128)(2,1)S(1)}, u32[]{:S(2)}, u32[]{:S(2)}) collective-permute-start(bf16[512,256]{1,0:T(8,128)(2,1)S(1)} %fusion.38), channel_id=1, source_target_pairs={{0,6},{1,7},{2,4},{3,5},{4,2},{5,3},{6,0},{7,1},{8,14},{9,15},{10,... | collective-permute-start | bytes 786440 | tf_op jit(solution)/shard_map/ppermute | solution.py:24
  81.0 21.7 %collective-permute-start.21 = (bf16[512,256]{1,0:T(8,128)(2,1)S(1)}, bf16[512,256]{1,0:T(8,128)(2,1)S(1)}, u32[]{:S(2)}, u32[]{:S(2)}) collective-permute-start(bf16[512,256]{1,0:T(8,128)(2,1)S(1)} %fusion.38), channel_id=1, source_target_pairs={{0,4},{1,5},{2,6},{3,7},{4,0},{5,1},{6,2},{7,3},{8,12},{9,13},{10,... | collective-permute-start | bytes 786440 | tf_op jit(solution)/shard_map/ppermute | solution.py:24
  81.0 22.5 %collective-permute-start.20 = (bf16[512,256]{1,0:T(8,128)(2,1)S(1)}, bf16[512,256]{1,0:T(8,128)(2,1)S(1)}, u32[]{:S(2)}, u32[]{:S(2)}) collective-permute-start(bf16[512,256]{1,0:T(8,128)(2,1)S(1)} %fusion.38), channel_id=1, source_target_pairs={{0,2},{1,3},{2,0},{3,1},{4,6},{5,7},{6,4},{7,5},{8,10},{9,11},{10,... | collective-permute-start | bytes 786440 | tf_op jit(solution)/shard_map/ppermute | solution.py:24
  82.4 22.0 %collective-permute-start.18 = (bf16[512,256]{1,0:T(8,128)(2,1)S(1)}, bf16[512,256]{1,0:T(8,128)(2,1)S(1)}, u32[]{:S(2)}, u32[]{:S(2)}) collective-permute-start(bf16[512,256]{1,0:T(8,128)(2,1)S(1)} %fusion.38), channel_id=1, source_target_pairs={{0,24},{8,16},{16,8},{24,0},{1,25},{9,17},{17,9},{25,1},{2,26},{10... | collective-permute-start | bytes 786440 | tf_op jit(solution)/shard_map/ppermute | solution.py:24
  84.6 19.9 %collective-permute-start.17 = (bf16[512,256]{1,0:T(8,128)(2,1)S(1)}, bf16[512,256]{1,0:T(8,128)(2,1)S(1)}, u32[]{:S(2)}, u32[]{:S(2)}) collective-permute-start(bf16[512,256]{1,0:T(8,128)(2,1)S(1)} %fusion.38), channel_id=1, source_target_pairs={{0,16},{8,24},{16,0},{24,8},{1,17},{9,25},{17,1},{25,9},{2,18},{10... | collective-permute-start | bytes 786440 | tf_op jit(solution)/shard_map/ppermute | solution.py:24
  88.7 15.8 %collective-permute-start.16 = (bf16[512,256]{1,0:T(8,128)(2,1)S(1)}, bf16[512,256]{1,0:T(8,128)(2,1)S(1)}, u32[]{:S(2)}, u32[]{:S(2)}) collective-permute-start(bf16[512,256]{1,0:T(8,128)(2,1)S(1)} %fusion.38), channel_id=1, source_target_pairs={{0,8},{8,0},{16,24},{24,16},{1,9},{9,1},{17,25},{25,17},{2,10},{10... | collective-permute-start | bytes 786440 | tf_op jit(solution)/shard_map/ppermute | solution.py:24
  102.7 1.8 %copy-start.3 = (bf16[512,256]{1,0:T(8,128)(2,1)}, bf16[512,256]{1,0:T(8,128)(2,1)S(1)}, u32[]{:S(2)}) copy-start(bf16[512,256]{1,0:T(8,128)(2,1)S(1)} %collective-permute-done.21) | copy-start | bytes 786436
  102.7 4.2 %collective-permute-start.19 = (bf16[512,256]{1,0:T(8,128)(2,1)S(1)}, bf16[512,256]{1,0:T(8,128)(2,1)}, u32[]{:S(2)}, u32[]{:S(2)}) collective-permute-start(bf16[512,256]{1,0:T(8,128)(2,1)S(1)} %fusion.38), channel_id=1, source_target_pairs={{0,1},{1,0},{2,3},{3,2},{4,5},{5,4},{6,7},{7,6},{8,9},{9,8},{10,11... | collective-permute-start | bytes 786440 | tf_op jit(solution)/shard_map/ppermute | solution.py:24
  104.4 3.6 %collective-permute-start.23 = (bf16[3,512,256]{2,1,0:T(8,128)(2,1)}, bf16[3,512,256]{2,1,0:T(8,128)(2,1)}, u32[]{:S(2)}, u32[]{:S(2)}) collective-permute-start(bf16[3,512,256]{2,1,0:T(8,128)(2,1)} %pad_maximum_fusion.6), channel_id=1, source_target_pairs={{0,1},{1,0},{2,3},{3,2},{4,5},{5,4},{6,7},{7,6},{8,9},{9,8},{10,11... | collective-permute-start | bytes 2359304 | tf_op jit(solution)/shard_map/ppermute | solution.py:24
  105.6 1.0 copy-start.4
  112.7 8.5 %collective-permute-start.31 = (bf16[512,256]{1,0:T(8,128)(2,1)}, bf16[512,256]{1,0:T(8,128)(2,1)S(1)}, u32[]{:S(2)}, u32[]{:S(2)}) collective-permute-start(bf16[512,256]{1,0:T(8,128)(2,1)} %get-tuple-element.10), channel_id=1, source_target_pairs={{0,24},{8,16},{16,8},{24,0},{1,25},{9,17},{17,9},{25,1},{2,26},{10... | collective-permute-start | bytes 786440 | tf_op jit(solution)/shard_map/ppermute | solution.py:24
  114.9 12.9 %collective-permute-start.30 = (bf16[512,256]{1,0:T(8,128)(2,1)}, bf16[512,256]{1,0:T(8,128)(2,1)S(1)}, u32[]{:S(2)}, u32[]{:S(2)}) collective-permute-start(bf16[512,256]{1,0:T(8,128)(2,1)} %get-tuple-element.10), channel_id=1, source_target_pairs={{0,16},{8,24},{16,0},{24,8},{1,17},{9,25},{17,1},{25,9},{2,18},{10... | collective-permute-start | bytes 786440 | tf_op jit(solution)/shard_map/ppermute | solution.py:24
  115.1 13.1 %collective-permute-start.29 = (bf16[512,256]{1,0:T(8,128)(2,1)}, bf16[512,256]{1,0:T(8,128)(2,1)S(1)}, u32[]{:S(2)}, u32[]{:S(2)}) collective-permute-start(bf16[512,256]{1,0:T(8,128)(2,1)} %get-tuple-element.10), channel_id=1, source_target_pairs={{0,8},{8,0},{16,24},{24,16},{1,9},{9,1},{17,25},{25,17},{2,10},{10... | collective-permute-start | bytes 786440 | tf_op jit(solution)/shard_map/ppermute | solution.py:24
  115.4 17.1 %collective-permute-start.27 = (bf16[512,256]{1,0:T(8,128)(2,1)}, bf16[512,256]{1,0:T(8,128)(2,1)}, u32[]{:S(2)}, u32[]{:S(2)}) collective-permute-start(bf16[512,256]{1,0:T(8,128)(2,1)} %get-tuple-element.10), channel_id=1, source_target_pairs={{0,6},{1,7},{2,4},{3,5},{4,2},{5,3},{6,0},{7,1},{8,14},{9,15},{10,... | collective-permute-start | bytes 786440 | tf_op jit(solution)/shard_map/ppermute | solution.py:24
  116.6 20.7 %collective-permute-start.26 = (bf16[512,256]{1,0:T(8,128)(2,1)}, bf16[512,256]{1,0:T(8,128)(2,1)}, u32[]{:S(2)}, u32[]{:S(2)}) collective-permute-start(bf16[512,256]{1,0:T(8,128)(2,1)} %get-tuple-element.10), channel_id=1, source_target_pairs={{0,4},{1,5},{2,6},{3,7},{4,0},{5,1},{6,2},{7,3},{8,12},{9,13},{10,... | collective-permute-start | bytes 786440 | tf_op jit(solution)/shard_map/ppermute | solution.py:24
  121.3 16.0 %collective-permute-start.25 = (bf16[512,256]{1,0:T(8,128)(2,1)}, bf16[512,256]{1,0:T(8,128)(2,1)}, u32[]{:S(2)}, u32[]{:S(2)}) collective-permute-start(bf16[512,256]{1,0:T(8,128)(2,1)} %get-tuple-element.10), channel_id=1, source_target_pairs={{0,2},{1,3},{2,0},{3,1},{4,6},{5,7},{6,4},{7,5},{8,10},{9,11},{10,... | collective-permute-start | bytes 786440 | tf_op jit(solution)/shard_map/ppermute | solution.py:24
  127.8 21.6 %collective-permute-start.24 = (bf16[512,256]{1,0:T(8,128)(2,1)}, bf16[512,256]{1,0:T(8,128)(2,1)}, u32[]{:S(2)}, u32[]{:S(2)}) collective-permute-start(bf16[512,256]{1,0:T(8,128)(2,1)} %get-tuple-element.10), channel_id=1, source_target_pairs={{0,1},{1,0},{2,3},{3,2},{4,5},{5,4},{6,7},{7,6},{8,9},{9,8},{10,11... | collective-permute-start | bytes 786440 | tf_op jit(solution)/shard_map/ppermute | solution.py:24
  138.5 12.4 %collective-permute-start.28 = (bf16[3,512,256]{2,1,0:T(8,128)(2,1)S(1)}, bf16[3,512,256]{2,1,0:T(8,128)(2,1)S(1)}, u32[]{:S(2)}, u32[]{:S(2)}) collective-permute-start(bf16[3,512,256]{2,1,0:T(8,128)(2,1)S(1)} %pad_maximum_fusion.7), channel_id=1, source_target_pairs={{0,1},{1,0},{2,3},{3,2},{4,5},{5,4},{6,7},{7,6},{8,9},{9,8},{10,11... | collective-permute-start | bytes 2359304 | tf_op jit(solution)/shard_map/ppermute | solution.py:24
  143.1 1.2 copy-start.5
  148.1 1.3 copy-start.6
  151.3 1.0 copy-start.8

commit v3 on v1

--- a/solution.py
+++ b/solution.py
@@ -1,6 +1,10 @@
+import functools
+
 import jax
 import jax.numpy as jnp
 from jax import lax
+from jax.experimental import pallas as pl
+from jax.experimental.pallas import tpu as pltpu
 from jax.sharding import PartitionSpec as P
 
 BS = 128
@@ -34,7 +38,7 @@
     for s in range(chips):
         row_pieces.append(same_core[s])
         row_pieces.append(partner_own if s == 0 else relayed[s - 1])
-    return jnp.stack(row_pieces), jnp.stack(col_pieces)
+    return row_pieces, jnp.stack(col_pieces)
 
 
 def ordered_k_blocks(col_pieces, me_row, me_col, n_col):
@@ -47,8 +51,77 @@
     return jnp.take(split, index, axis=0)
 
 
-def contract(row_pieces, k_blocks):
-    return jnp.einsum("sik,skj->ij", row_pieces, k_blocks, preferred_element_type=jnp.float32)
+def square_kernel(n, *refs):
+    pieces = refs[:n]
+    k_ref, mask_ref, square_ref, qb_ref = refs[n:]
+    acc = jnp.dot(pieces[0][...], k_ref[0], preferred_element_type=jnp.float32)
+    for s in range(1, n):
+        acc = acc + jnp.dot(pieces[s][...], k_ref[s], preferred_element_type=jnp.float32)
+    square = acc * mask_ref[...]
+    square_ref[...] = square
+    qb_ref[...] = square.astype(jnp.bfloat16)
+
+
+def jordan_kernel(n, *refs):
+    q_pieces = refs[:n]
+    x_pieces = refs[n:2 * n]
+    xk_ref, qk_ref, square_ref, mask_ref, current_ref, xb_ref = refs[2 * n:]
+    acc = jnp.dot(q_pieces[0][...], xk_ref[0], preferred_element_type=jnp.float32)
+    acc = acc + jnp.dot(x_pieces[0][...], qk_ref[0], preferred_element_type=jnp.float32)
+    for s in range(1, n):
+        acc = acc + jnp.dot(q_pieces[s][...], xk_ref[s], preferred_element_type=jnp.float32)
+        acc = acc + jnp.dot(x_pieces[s][...], qk_ref[s], preferred_element_type=jnp.float32)
+    current = mask_ref[...] * (3.0 * square_ref[...] - acc)
+    current_ref[...] = current
+    xb_ref[...] = current.astype(jnp.bfloat16)
+
+
+def vmem_spec():
+    return pl.BlockSpec(memory_space=pltpu.VMEM)
+
+
+def square_call(pieces, k_blocks, mask):
+    n = len(pieces)
+    rows, cols = mask.shape
+    out = (
+        jax.ShapeDtypeStruct((rows, cols), jnp.float32),
+        jax.ShapeDtypeStruct((rows, cols), jnp.bfloat16),
+    )
+    cost = pl.CostEstimate(
+        flops=2 * rows * cols * cols * n,
+        transcendentals=0,
+        bytes_accessed=2 * rows * cols * n + 2 * cols * cols * n + 10 * rows * cols,
+    )
+    return pl.pallas_call(
+        functools.partial(square_kernel, n),
+        out_shape=out,
+        in_specs=[vmem_spec()] * (n + 2),
+        out_specs=(vmem_spec(), vmem_spec()),
+        cost_estimate=cost,
+        name="square_panels",
+    )(*pieces, k_blocks, mask)
+
+
+def jordan_call(q_pieces, x_pieces, xk, qk, square, mask):
+    n = len(q_pieces)
+    rows, cols = mask.shape
+    out = (
+        jax.ShapeDtypeStruct((rows, cols), jnp.float32),
+        jax.ShapeDtypeStruct((rows, cols), jnp.bfloat16),
+    )
+    cost = pl.CostEstimate(
+        flops=4 * rows * cols * cols * n,
+        transcendentals=0,
+        bytes_accessed=4 * rows * cols * n + 4 * cols * cols * n + 14 * rows * cols,
+    )
+    return pl.pallas_call(
+        functools.partial(jordan_kernel, n),
+        out_shape=out,
+        in_specs=[vmem_spec()] * (2 * n + 4),
+        out_specs=(vmem_spec(), vmem_spec()),
+        cost_estimate=cost,
+        name="jordan_panels",
+    )(*q_pieces, *x_pieces, xk, qk, square, mask)
 
 
 def on_device(density, pattern):
@@ -63,17 +136,16 @@
     blocks = lax.dynamic_slice(
         allowed, (me_row * row_blocks, me_col * col_blocks), (row_blocks, col_blocks)
     ).astype(jnp.float32)
-    current = apply_mask(density, blocks)
+    mask = apply_mask(jnp.ones((rows, cols), jnp.float32), blocks)
+    current = mask * density
+    xb = current.astype(jnp.bfloat16)
     for step in range(STEPS):
-        xb = current.astype(jnp.bfloat16)
         x_row, x_col = exchange(xb, n_row, n_col)
         x_k = ordered_k_blocks(x_col, me_row, me_col, n_col)
-        square = apply_mask(contract(x_row, x_k), blocks)
-        qb = square.astype(jnp.bfloat16)
+        square, qb = square_call(x_row, x_k, mask)
         q_row, q_col = exchange(qb, n_row, n_col)
         q_k = ordered_k_blocks(q_col, me_row, me_col, n_col)
-        jordan = contract(q_row, x_k) + contract(x_row, q_k)
-        current = apply_mask(3.0 * square - jordan, blocks)
+        current, xb = jordan_call(q_row, x_row, x_k, q_k, square, mask)
     return current
 
 

time: 158 us -> 208 us (1.32); the launches traced: 157 us -> 205 us
  waiting for transfers between devices: 69.7 us -> 110 us
  starting transfers between devices: 33.4 us -> 53 us
  Pallas kernels: 0 us -> 17.6 us
  matrix products: 14.9 us -> 0 us
  local copies, waits for them, and re-layouts: 29.9 us -> 15.2 us
    ppermute x32, waiting for transfers between devices: 69.7 us -> 110 us  [xor_permute(): return lax.ppermute(x, axis, perm=[(i, i ^ s) for i in range(size)])]
    ppermute x32, starting transfers between devices: 33.4 us -> 53 us  [xor_permute(): return lax.ppermute(x, axis, perm=[(i, i ^ s) for i in range(size)])]
    pallas_call x0 -> x4, Pallas kernels: none -> 17.6 us  [the longest x2 10.4 us: jordan_call(): pl.pallas_call(functools.partial(jordan_kernel, n), out_shape=out, in_spe...]
    unnamed x37 -> x46, local copies, waits for them, and re-layouts: 21.8 us -> 4.53 us
    dot_general x6 -> x0, matrix products: 14.9 us -> none  [contract(): jnp.einsum('sik,skj->ij', row_pieces, k_blocks, preferred_element_type=jn...]
    squeeze x0 -> x4, local copies, waits for them, and re-layouts: none -> 8.05 us  [exchange(): row_pieces.append(partner_own if s == 0 else relayed[s - 1])]
    select_n x0 -> x4, other arithmetic: none -> 4.71 us  [ordered_k_blocks(): return jnp.take(split, index, axis=0)]
    another operation x4, other arithmetic: 4.33 us -> 0.53 us  [exchange(): return (row_pieces, jnp.stack(col_pieces))]
  transfers between devices with their start and end apart: 32 -> 32, of which waited for: 11 -> 21; matrix products, arithmetic and copies ran while one was open for 16% -> 8% of each run, Pallas kernels for 0% -> 0%
where the time goes in v3:
time: 208 us; the launch traced here: 205 us
  waiting for transfers between devices  110 us (53%)
  starting transfers between devices  53 us (25%)
  Pallas kernels  17.6 us (8%)
  local copies, waits for them, and re-layouts  15.2 us (7%)
  other arithmetic  9.3 us (4%)
    ppermute x32, waiting for transfers between devices, xor_permute(): return lax.ppermute(x, axis, perm=[(i, i ^ s) for i in range(size)])  110 us
    ppermute x32, starting transfers between devices, xor_permute(): return lax.ppermute(x, axis, perm=[(i, i ^ s) for i in range(size)])  53 us
    pallas_call x2, Pallas kernels, jordan_call(): pl.pallas_call(functools.partial(jordan_kernel, n), out_shape=out, in_spe...  10.4 us
    squeeze x4, local copies, waits for them, and re-layouts, exchange(): row_pieces.append(partner_own if s == 0 else relayed[s - 1])  8.05 us
    pallas_call x2, Pallas kernels, square_call(): pl.pallas_call(functools.partial(square_kernel, n), out_shape=out, in_spe...  7.18 us
    select_n x4, other arithmetic, ordered_k_blocks(): return jnp.take(split, index, axis=0)  4.71 us
    unnamed x46, local copies, waits for them, and re-layouts  4.53 us
  transfers between devices with their start and end apart: 32, of which 21 were waited for; matrix products, arithmetic and copies ran while one was open for 8% of the time, Pallas kernels for 0%

profile of v3, /device:TPU:1, one launch (start us, length us, event | category | flops | bytes accessed | tf_op | source)
XLA Modules:
  0.0 204.8 jit_solution(1514013074875928746)
XLA Ops:
  1.2 2.2 %collective-permute-start.1 = (bf16[512,256]{1,0:T(8,128)(2,1)S(1)}, bf16[512,256]{1,0:T(8,128)(2,1)S(1)}, u32[]{:S(2)}, u32[]{:S(2)}) collective-permute-start(bf16[512,256]{1,0:T(8,128)(2,1)S(1)} %multiply_convert_fusion.refs_0_.refs_8_), channel_id=1, source_target_pairs={{0,2},{1,3},{2,0},{3,1},{4,6},{5,7},{6,4},{7,5},{8,10},{9,11},{10,... | collective-permute-start | bytes 786440 | tf_op jit(solution)/shard_map/ppermute | solution.py:28
  3.4 2.3 %collective-permute-start.2 = (bf16[512,256]{1,0:T(8,128)(2,1)S(1)}, bf16[512,256]{1,0:T(8,128)(2,1)S(1)}, u32[]{:S(2)}, u32[]{:S(2)}) collective-permute-start(bf16[512,256]{1,0:T(8,128)(2,1)S(1)} %multiply_convert_fusion.refs_0_.refs_8_), channel_id=1, source_target_pairs={{0,4},{1,5},{2,6},{3,7},{4,0},{5,1},{6,2},{7,3},{8,12},{9,13},{10,... | collective-permute-start | bytes 786440 | tf_op jit(solution)/shard_map/ppermute | solution.py:28
  5.7 8.6 %collective-permute-done.1.refs_2_.refs_10_ = bf16[512,256]{1,0:T(8,128)(2,1)S(1)} collective-permute-done((bf16[512,256]{1,0:T(8,128)(2,1)S(1)}, bf16[512,256]{1,0:T(8,128)(2,1)S(1)}, u32[]{:S(2)}, u32[]{:S(2)}) %collective-permute-start.1) | collective-permute-done | bytes 262176 | tf_op jit(solution)/shard_map/ppermute | solution.py:28
  14.2 8.3 %collective-permute-done.3.refs_6_.refs_14_ = bf16[512,256]{1,0:T(8,128)(2,1)S(1)} collective-permute-done((bf16[512,256]{1,0:T(8,128)(2,1)S(1)}, bf16[512,256]{1,0:T(8,128)(2,1)S(1)}, u32[]{:S(2)}, u32[]{:S(2)}) %collective-permute-start.3) | collective-permute-done | bytes 262176 | tf_op jit(solution)/shard_map/ppermute | solution.py:28
  23.5 3.3 %collective-permute-start.4 = (bf16[3,512,256]{2,1,0:T(8,128)(2,1)}, bf16[3,512,256]{2,1,0:T(8,128)(2,1)}, u32[]{:S(2)}, u32[]{:S(2)}) collective-permute-start(bf16[3,512,256]{2,1,0:T(8,128)(2,1)} %pad_maximum_fusion.4), channel_id=1, source_target_pairs={{0,1},{1,0},{2,3},{3,2},{4,5},{5,4},{6,7},{7,6},{8,9},{9,8},{10,11... | collective-permute-start | bytes 2359304 | tf_op jit(solution)/shard_map/ppermute | solution.py:28
  26.8 2.2 %collective-permute-start.7 = (bf16[512,256]{1,0:T(8,128)(2,1)S(1)}, bf16[512,256]{1,0:T(8,128)(2,1)S(1)}, u32[]{:S(2)}, u32[]{:S(2)}) collective-permute-start(bf16[512,256]{1,0:T(8,128)(2,1)S(1)} %multiply_convert_fusion.refs_0_.refs_8_), channel_id=1, source_target_pairs={{0,24},{8,16},{16,8},{24,0},{1,25},{9,17},{17,9},{25,1},{2,26},{10... | collective-permute-start | bytes 786440 | tf_op jit(solution)/shard_map/ppermute | solution.py:28
  31.3 4.4 %collective-permute-done.7 = bf16[512,256]{1,0:T(8,128)(2,1)S(1)} collective-permute-done((bf16[512,256]{1,0:T(8,128)(2,1)S(1)}, bf16[512,256]{1,0:T(8,128)(2,1)S(1)}, u32[]{:S(2)}, u32[]{:S(2)}) %collective-permute-start.7) | collective-permute-done | bytes 262176 | tf_op jit(solution)/shard_map/ppermute | solution.py:28
  35.7 5.7 %collective-permute-done.5 = bf16[512,256]{1,0:T(8,128)(2,1)S(1)} collective-permute-done((bf16[512,256]{1,0:T(8,128)(2,1)S(1)}, bf16[512,256]{1,0:T(8,128)(2,1)S(1)}, u32[]{:S(2)}, u32[]{:S(2)}) %collective-permute-start.5) | collective-permute-done | bytes 262176 | tf_op jit(solution)/shard_map/ppermute | solution.py:28
  42.4 1.2 broadcast_select_fusion.3.refs_8_.refs_16_
  43.6 2.0 slice_bitcast_fusion.9
  46.3 3.6 %square_panels.2 = (f32[512,256]{1,0:T(8,128)}, bf16[512,256]{1,0:T(8,128)(2,1)}) custom-call(bf16[512,256]{1,0:T(8,128)(2,1)} %copy-done, bf16[512,256]{1,0:T(8,128)(2,1)} %copy-done.8, bf16[512,256]{1,0:T(8,128)(2,1)} %copy-done.1, bf16[512,256]{1,0:T(8,128)(2,1)} %get-tuple-element.31.refs_3_.refs_11_, bf16[512,256]{1,0:T(8,128)(2,1)} %copy-done.2, ...), custom_call_target="tpu_custom_call" | custom-call | flops 536870912 | bytes 4456448 | tf_op jit(solution)/shard_map/square_panels/pallas_call | solution.py:95
  49.9 4.4 %collective-permute-start.9 = (bf16[512,256]{1,0:T(8,128)(2,1)}, bf16[512,256]{1,0:T(8,128)(2,1)S(1)}, u32[]{:S(2)}, u32[]{:S(2)}) collective-permute-start(bf16[512,256]{1,0:T(8,128)(2,1)} %get-tuple-element.12.refs_0_), channel_id=1, source_target_pairs={{0,2},{1,3},{2,0},{3,1},{4,6},{5,7},{6,4},{7,5},{8,10},{9,11},{10,... | collective-permute-start | bytes 786440 | tf_op jit(solution)/shard_map/ppermute | solution.py:28
  54.3 1.0 collective-permute-start.10
  55.3 1.2 collective-permute-start.11
  56.5 9.0 %collective-permute-done.9.refs_2_ = bf16[512,256]{1,0:T(8,128)(2,1)S(1)} collective-permute-done((bf16[512,256]{1,0:T(8,128)(2,1)}, bf16[512,256]{1,0:T(8,128)(2,1)S(1)}, u32[]{:S(2)}, u32[]{:S(2)}) %collective-permute-start.9) | collective-permute-done | bytes 262176 | tf_op jit(solution)/shard_map/ppermute | solution.py:28
  65.5 8.3 %collective-permute-done.11.refs_6_ = bf16[512,256]{1,0:T(8,128)(2,1)S(1)} collective-permute-done((bf16[512,256]{1,0:T(8,128)(2,1)}, bf16[512,256]{1,0:T(8,128)(2,1)S(1)}, u32[]{:S(2)}, u32[]{:S(2)}) %collective-permute-start.11) | collective-permute-done | bytes 262176 | tf_op jit(solution)/shard_map/ppermute | solution.py:28
  74.7 3.0 %collective-permute-start.12 = (bf16[3,512,256]{2,1,0:T(8,128)(2,1)}, bf16[3,512,256]{2,1,0:T(8,128)(2,1)}, u32[]{:S(2)}, u32[]{:S(2)}) collective-permute-start(bf16[3,512,256]{2,1,0:T(8,128)(2,1)} %pad_maximum_fusion.5), channel_id=1, source_target_pairs={{0,1},{1,0},{2,3},{3,2},{4,5},{5,4},{6,7},{7,6},{8,9},{9,8},{10,11... | collective-permute-start | bytes 2359304 | tf_op jit(solution)/shard_map/ppermute | solution.py:28
  77.8 1.2 collective-permute-start.13
  79.0 1.1 collective-permute-start.14
  81.3 4.3 %collective-permute-done.13 = bf16[512,256]{1,0:T(8,128)(2,1)S(1)} collective-permute-done((bf16[512,256]{1,0:T(8,128)(2,1)S(1)}, bf16[512,256]{1,0:T(8,128)(2,1)S(1)}, u32[]{:S(2)}, u32[]{:S(2)}) %collective-permute-start.13) | collective-permute-done | bytes 262176 | tf_op jit(solution)/shard_map/ppermute | solution.py:28
  86.6 5.6 %collective-permute-done.15 = bf16[512,256]{1,0:T(8,128)(2,1)S(1)} collective-permute-done((bf16[512,256]{1,0:T(8,128)(2,1)S(1)}, bf16[512,256]{1,0:T(8,128)(2,1)S(1)}, u32[]{:S(2)}, u32[]{:S(2)}) %collective-permute-start.15) | collective-permute-done | bytes 262176 | tf_op jit(solution)/shard_map/ppermute | solution.py:28
  92.9 1.2 broadcast_select_fusion.2.refs_17_
  94.1 2.0 slice_bitcast_fusion.6
  96.8 5.2 %jordan_panels.2 = (f32[512,256]{1,0:T(8,128)}, bf16[512,256]{1,0:T(8,128)(2,1)}) custom-call(bf16[512,256]{1,0:T(8,128)(2,1)} %get-tuple-element.12.refs_0_, bf16[512,256]{1,0:T(8,128)(2,1)} %copy-done.20, bf16[512,256]{1,0:T(8,128)(2,1)} %copy-done.11, bf16[512,256]{1,0:T(8,128)(2,1)} %get-tuple-element.28.refs_3_, bf16[512,256]{1,0:T(8,128)(2,1)} %copy-done.13, ...), custom_call_target="tpu_custom_call" | custom-call | flops 1073741824 | bytes 8126464 | tf_op jit(solution)/shard_map/jordan_panels/pallas_call | solution.py:117
  102.0 4.6 %collective-permute-start.17 = (bf16[512,256]{1,0:T(8,128)(2,1)}, bf16[512,256]{1,0:T(8,128)(2,1)S(1)}, u32[]{:S(2)}, u32[]{:S(2)}) collective-permute-start(bf16[512,256]{1,0:T(8,128)(2,1)} %get-tuple-element.14.refs_0_.refs_8_), channel_id=1, source_target_pairs={{0,2},{1,3},{2,0},{3,1},{4,6},{5,7},{6,4},{7,5},{8,10},{9,11},{10,... | collective-permute-start | bytes 786440 | tf_op jit(solution)/shard_map/ppermute | solution.py:28
  106.7 1.1 collective-permute-start.18
  107.8 1.1 collective-permute-start.19
  108.9 8.0 %collective-permute-done.17.refs_2_.refs_10_ = bf16[512,256]{1,0:T(8,128)(2,1)S(1)} collective-permute-done((bf16[512,256]{1,0:T(8,128)(2,1)}, bf16[512,256]{1,0:T(8,128)(2,1)S(1)}, u32[]{:S(2)}, u32[]{:S(2)}) %collective-permute-start.17) | collective-permute-done | bytes 262176 | tf_op jit(solution)/shard_map/ppermute | solution.py:28
  117.2 8.4 %collective-permute-done.19.refs_6_.refs_14_ = bf16[512,256]{1,0:T(8,128)(2,1)S(1)} collective-permute-done((bf16[512,256]{1,0:T(8,128)(2,1)}, bf16[512,256]{1,0:T(8,128)(2,1)S(1)}, u32[]{:S(2)}, u32[]{:S(2)}) %collective-permute-start.19) | collective-permute-done | bytes 262176 | tf_op jit(solution)/shard_map/ppermute | solution.py:28
  126.6 4.1 %collective-permute-start.20 = (bf16[3,512,256]{2,1,0:T(8,128)(2,1)}, bf16[3,512,256]{2,1,0:T(8,128)(2,1)}, u32[]{:S(2)}, u32[]{:S(2)}) collective-permute-start(bf16[3,512,256]{2,1,0:T(8,128)(2,1)} %pad_maximum_fusion.6), channel_id=1, source_target_pairs={{0,1},{1,0},{2,3},{3,2},{4,5},{5,4},{6,7},{7,6},{8,9},{9,8},{10,11... | collective-permute-start | bytes 2359304 | tf_op jit(solution)/shard_map/ppermute | solution.py:28
  132.2 1.2 collective-permute-start.23
  134.3 4.3 %collective-permute-done.21 = bf16[512,256]{1,0:T(8,128)(2,1)S(1)} collective-permute-done((bf16[512,256]{1,0:T(8,128)(2,1)S(1)}, bf16[512,256]{1,0:T(8,128)(2,1)S(1)}, u32[]{:S(2)}, u32[]{:S(2)}) %collective-permute-start.21) | collective-permute-done | bytes 262176 | tf_op jit(solution)/shard_map/ppermute | solution.py:28
  139.2 5.9 %collective-permute-done.23 = bf16[512,256]{1,0:T(8,128)(2,1)S(1)} collective-permute-done((bf16[512,256]{1,0:T(8,128)(2,1)S(1)}, bf16[512,256]{1,0:T(8,128)(2,1)S(1)}, u32[]{:S(2)}, u32[]{:S(2)}) %collective-permute-start.23) | collective-permute-done | bytes 262176 | tf_op jit(solution)/shard_map/ppermute | solution.py:28
  145.9 1.2 broadcast_select_fusion.1.refs_8_.refs_16_
  147.1 2.0 slice_bitcast_fusion.3
  149.8 3.6 %square_panels.3 = (f32[512,256]{1,0:T(8,128)}, bf16[512,256]{1,0:T(8,128)(2,1)}) custom-call(bf16[512,256]{1,0:T(8,128)(2,1)} %get-tuple-element.14.refs_0_.refs_8_, bf16[512,256]{1,0:T(8,128)(2,1)} %copy-done.9, bf16[512,256]{1,0:T(8,128)(2,1)} %copy-done.4, bf16[512,256]{1,0:T(8,128)(2,1)} %get-tuple-element.25.refs_3_.refs_11_, ...), custom_call_target="tpu_custom_call" | custom-call | flops 536870912 | bytes 4456448 | tf_op jit(solution)/shard_map/square_panels/pallas_call | solution.py:95
  153.4 4.0 %collective-permute-start.25 = (bf16[512,256]{1,0:T(8,128)(2,1)}, bf16[512,256]{1,0:T(8,128)(2,1)S(1)}, u32[]{:S(2)}, u32[]{:S(2)}) collective-permute-start(bf16[512,256]{1,0:T(8,128)(2,1)} %get-tuple-element.15.refs_0_), channel_id=1, source_target_pairs={{0,2},{1,3},{2,0},{3,1},{4,6},{5,7},{6,4},{7,5},{8,10},{9,11},{10,... | collective-permute-start | bytes 786440 | tf_op jit(solution)/shard_map/ppermute | solution.py:28
  158.4 1.2 collective-permute-start.27
  159.6 7.8 %collective-permute-done.25.refs_2_ = bf16[512,256]{1,0:T(8,128)(2,1)S(1)} collective-permute-done((bf16[512,256]{1,0:T(8,128)(2,1)}, bf16[512,256]{1,0:T(8,128)(2,1)S(1)}, u32[]{:S(2)}, u32[]{:S(2)}) %collective-permute-start.25) | collective-permute-done | bytes 262176 | tf_op jit(solution)/shard_map/ppermute | solution.py:28
  167.8 8.4 %collective-permute-done.27.refs_6_ = bf16[512,256]{1,0:T(8,128)(2,1)S(1)} collective-permute-done((bf16[512,256]{1,0:T(8,128)(2,1)}, bf16[512,256]{1,0:T(8,128)(2,1)S(1)}, u32[]{:S(2)}, u32[]{:S(2)}) %collective-permute-start.27) | collective-permute-done | bytes 262176 | tf_op jit(solution)/shard_map/ppermute | solution.py:28
  177.3 4.2 %collective-permute-start.28 = (bf16[3,512,256]{2,1,0:T(8,128)(2,1)}, bf16[3,512,256]{2,1,0:T(8,128)(2,1)}, u32[]{:S(2)}, u32[]{:S(2)}) collective-permute-start(bf16[3,512,256]{2,1,0:T(8,128)(2,1)} %pad_maximum_fusion.7), channel_id=1, source_target_pairs={{0,1},{1,0},{2,3},{3,2},{4,5},{5,4},{6,7},{7,6},{8,9},{9,8},{10,11... | collective-permute-start | bytes 2359304 | tf_op jit(solution)/shard_map/ppermute | solution.py:28
  181.8 1.1 collective-permute-start.30
  182.9 1.2 collective-permute-start.31
  185.0 4.3 %collective-permute-done.29 = bf16[512,256]{1,0:T(8,128)(2,1)S(1)} collective-permute-done((bf16[512,256]{1,0:T(8,128)(2,1)S(1)}, bf16[512,256]{1,0:T(8,128)(2,1)S(1)}, u32[]{:S(2)}, u32[]{:S(2)}) %collective-permute-start.29) | collective-permute-done | bytes 262176 | tf_op jit(solution)/shard_map/ppermute | solution.py:28
  189.3 5.7 %collective-permute-done.31 = bf16[512,256]{1,0:T(8,128)(2,1)S(1)} collective-permute-done((bf16[512,256]{1,0:T(8,128)(2,1)S(1)}, bf16[512,256]{1,0:T(8,128)(2,1)S(1)}, u32[]{:S(2)}, u32[]{:S(2)}) %collective-permute-start.31) | collective-permute-done | bytes 262176 | tf_op jit(solution)/shard_map/ppermute | solution.py:28
  195.8 1.2 broadcast_select_fusion.refs_17_
  196.9 2.0 slice_bitcast_fusion
  199.6 5.2 %jordan_panels.3 = (f32[512,256]{1,0:T(8,128)}, bf16[512,256]{1,0:T(8,128)(2,1)}) custom-call(bf16[512,256]{1,0:T(8,128)(2,1)} %get-tuple-element.15.refs_0_, bf16[512,256]{1,0:T(8,128)(2,1)} %copy-done.19, bf16[512,256]{1,0:T(8,128)(2,1)} %copy-done.10, bf16[512,256]{1,0:T(8,128)(2,1)} %get-tuple-element.22.refs_3_, bf16[512,256]{1,0:T(8,128)(2,1)} %copy-done.12, ...), custom_call_target="tpu_custom_call" | custom-call | flops 1073741824 | bytes 8126464 | tf_op jit(solution)/shard_map/jordan_panels/pallas_call | solution.py:117
  (91 shorter events, 21.6 us)
Async XLA Ops:
  0.0 1.1 copy-start.18
  1.2 40.4 %copy-start = (bf16[512,256]{1,0:T(8,128)(2,1)}, bf16[512,256]{1,0:T(8,128)(2,1)S(1)}, u32[]{:S(2)}) copy-start(bf16[512,256]{1,0:T(8,128)(2,1)S(1)} %multiply_convert_fusion.refs_0_.refs_8_) | copy-start | bytes 786436
  1.2 13.1 %collective-permute-start.1 = (bf16[512,256]{1,0:T(8,128)(2,1)S(1)}, bf16[512,256]{1,0:T(8,128)(2,1)S(1)}, u32[]{:S(2)}, u32[]{:S(2)}) collective-permute-start(bf16[512,256]{1,0:T(8,128)(2,1)S(1)} %multiply_convert_fusion.refs_0_.refs_8_), channel_id=1, source_target_pairs={{0,2},{1,3},{2,0},{3,1},{4,6},{5,7},{6,4},{7,5},{8,10},{9,11},{10,... | collective-permute-start | bytes 786440 | tf_op jit(solution)/shard_map/ppermute | solution.py:28
  3.4 10.9 %collective-permute-start.2 = (bf16[512,256]{1,0:T(8,128)(2,1)S(1)}, bf16[512,256]{1,0:T(8,128)(2,1)S(1)}, u32[]{:S(2)}, u32[]{:S(2)}) collective-permute-start(bf16[512,256]{1,0:T(8,128)(2,1)S(1)} %multiply_convert_fusion.refs_0_.refs_8_), channel_id=1, source_target_pairs={{0,4},{1,5},{2,6},{3,7},{4,0},{5,1},{6,2},{7,3},{8,12},{9,13},{10,... | collective-permute-start | bytes 786440 | tf_op jit(solution)/shard_map/ppermute | solution.py:28
  5.7 16.9 %collective-permute-start.3 = (bf16[512,256]{1,0:T(8,128)(2,1)S(1)}, bf16[512,256]{1,0:T(8,128)(2,1)S(1)}, u32[]{:S(2)}, u32[]{:S(2)}) collective-permute-start(bf16[512,256]{1,0:T(8,128)(2,1)S(1)} %multiply_convert_fusion.refs_0_.refs_8_), channel_id=1, source_target_pairs={{0,6},{1,7},{2,4},{3,5},{4,2},{5,3},{6,0},{7,1},{8,14},{9,15},{10,... | collective-permute-start | bytes 786440 | tf_op jit(solution)/shard_map/ppermute | solution.py:28
  14.2 9.3 %copy-start.1 = (bf16[512,256]{1,0:T(8,128)(2,1)}, bf16[512,256]{1,0:T(8,128)(2,1)S(1)}, u32[]{:S(2)}) copy-start(bf16[512,256]{1,0:T(8,128)(2,1)S(1)} %collective-permute-done.1.refs_2_.refs_10_) | copy-start | bytes 786436
  14.2 9.3 %copy-start.2 = (bf16[512,256]{1,0:T(8,128)(2,1)}, bf16[512,256]{1,0:T(8,128)(2,1)S(1)}, u32[]{:S(2)}) copy-start(bf16[512,256]{1,0:T(8,128)(2,1)S(1)} %collective-permute-done.2.refs_4_.refs_12_) | copy-start | bytes 786436
  22.5 1.0 copy-start.3
  23.5 20.0 %collective-permute-start.4 = (bf16[3,512,256]{2,1,0:T(8,128)(2,1)}, bf16[3,512,256]{2,1,0:T(8,128)(2,1)}, u32[]{:S(2)}, u32[]{:S(2)}) collective-permute-start(bf16[3,512,256]{2,1,0:T(8,128)(2,1)} %pad_maximum_fusion.4), channel_id=1, source_target_pairs={{0,1},{1,0},{2,3},{3,2},{4,5},{5,4},{6,7},{7,6},{8,9},{9,8},{10,11... | collective-permute-start | bytes 2359304 | tf_op jit(solution)/shard_map/ppermute | solution.py:28
  26.8 8.8 %collective-permute-start.7 = (bf16[512,256]{1,0:T(8,128)(2,1)S(1)}, bf16[512,256]{1,0:T(8,128)(2,1)S(1)}, u32[]{:S(2)}, u32[]{:S(2)}) collective-permute-start(bf16[512,256]{1,0:T(8,128)(2,1)S(1)} %multiply_convert_fusion.refs_0_.refs_8_), channel_id=1, source_target_pairs={{0,24},{8,16},{16,8},{24,0},{1,25},{9,17},{17,9},{25,1},{2,26},{10... | collective-permute-start | bytes 786440 | tf_op jit(solution)/shard_map/ppermute | solution.py:28
  29.0 12.3 %collective-permute-start.5 = (bf16[512,256]{1,0:T(8,128)(2,1)S(1)}, bf16[512,256]{1,0:T(8,128)(2,1)S(1)}, u32[]{:S(2)}, u32[]{:S(2)}) collective-permute-start(bf16[512,256]{1,0:T(8,128)(2,1)S(1)} %multiply_convert_fusion.refs_0_.refs_8_), channel_id=1, source_target_pairs={{0,8},{8,0},{16,24},{24,16},{1,9},{9,1},{17,25},{25,17},{2,10},{10... | collective-permute-start | bytes 786440 | tf_op jit(solution)/shard_map/ppermute | solution.py:28
  29.3 12.3 %collective-permute-start.6 = (bf16[512,256]{1,0:T(8,128)(2,1)S(1)}, bf16[512,256]{1,0:T(8,128)(2,1)S(1)}, u32[]{:S(2)}, u32[]{:S(2)}) collective-permute-start(bf16[512,256]{1,0:T(8,128)(2,1)S(1)} %multiply_convert_fusion.refs_0_.refs_8_), channel_id=1, source_target_pairs={{0,16},{8,24},{16,0},{24,8},{1,17},{9,25},{17,1},{25,9},{2,18},{10... | collective-permute-start | bytes 786440 | tf_op jit(solution)/shard_map/ppermute | solution.py:28
  29.5 16.1 %collective-permute-start = (bf16[512,256]{1,0:T(8,128)(2,1)S(1)}, bf16[512,256]{1,0:T(8,128)(2,1)S(1)}, u32[]{:S(2)}, u32[]{:S(2)}) collective-permute-start(bf16[512,256]{1,0:T(8,128)(2,1)S(1)} %multiply_convert_fusion.refs_0_.refs_8_), channel_id=1, source_target_pairs={{0,1},{1,0},{2,3},{3,2},{4,5},{5,4},{6,7},{7,6},{8,9},{9,8},{10,11... | collective-permute-start | bytes 786440 | tf_op jit(solution)/shard_map/ppermute | solution.py:28
  49.9 15.6 %collective-permute-start.9 = (bf16[512,256]{1,0:T(8,128)(2,1)}, bf16[512,256]{1,0:T(8,128)(2,1)S(1)}, u32[]{:S(2)}, u32[]{:S(2)}) collective-permute-start(bf16[512,256]{1,0:T(8,128)(2,1)} %get-tuple-element.12.refs_0_), channel_id=1, source_target_pairs={{0,2},{1,3},{2,0},{3,1},{4,6},{5,7},{6,4},{7,5},{8,10},{9,11},{10,... | collective-permute-start | bytes 786440 | tf_op jit(solution)/shard_map/ppermute | solution.py:28
  54.3 11.2 %collective-permute-start.10 = (bf16[512,256]{1,0:T(8,128)(2,1)}, bf16[512,256]{1,0:T(8,128)(2,1)S(1)}, u32[]{:S(2)}, u32[]{:S(2)}) collective-permute-start(bf16[512,256]{1,0:T(8,128)(2,1)} %get-tuple-element.12.refs_0_), channel_id=1, source_target_pairs={{0,4},{1,5},{2,6},{3,7},{4,0},{5,1},{6,2},{7,3},{8,12},{9,13},{10,... | collective-permute-start | bytes 786440 | tf_op jit(solution)/shard_map/ppermute | solution.py:28
  55.3 18.5 %collective-permute-start.11 = (bf16[512,256]{1,0:T(8,128)(2,1)}, bf16[512,256]{1,0:T(8,128)(2,1)S(1)}, u32[]{:S(2)}, u32[]{:S(2)}) collective-permute-start(bf16[512,256]{1,0:T(8,128)(2,1)} %get-tuple-element.12.refs_0_), channel_id=1, source_target_pairs={{0,6},{1,7},{2,4},{3,5},{4,2},{5,3},{6,0},{7,1},{8,14},{9,15},{10,... | collective-permute-start | bytes 786440 | tf_op jit(solution)/shard_map/ppermute | solution.py:28
  65.5 9.2 %copy-start.11 = (bf16[512,256]{1,0:T(8,128)(2,1)}, bf16[512,256]{1,0:T(8,128)(2,1)S(1)}, u32[]{:S(2)}) copy-start(bf16[512,256]{1,0:T(8,128)(2,1)S(1)} %collective-permute-done.9.refs_2_) | copy-start | bytes 786436
  65.5 9.2 %copy-start.13 = (bf16[512,256]{1,0:T(8,128)(2,1)}, bf16[512,256]{1,0:T(8,128)(2,1)S(1)}, u32[]{:S(2)}) copy-start(bf16[512,256]{1,0:T(8,128)(2,1)S(1)} %collective-permute-done.10.refs_4_) | copy-start | bytes 786436
  73.7 1.0 copy-start.15
  73.7 4.0 %copy-start.17 = (bf16[512,256]{1,0:T(8,128)(2,1)S(1)}, bf16[512,256]{1,0:T(8,128)(2,1)}, u32[]{:S(2)}) copy-start(bf16[512,256]{1,0:T(8,128)(2,1)} %get-tuple-element.12.refs_0_) | copy-start | bytes 786436
  74.7 19.4 %collective-permute-start.12 = (bf16[3,512,256]{2,1,0:T(8,128)(2,1)}, bf16[3,512,256]{2,1,0:T(8,128)(2,1)}, u32[]{:S(2)}, u32[]{:S(2)}) collective-permute-start(bf16[3,512,256]{2,1,0:T(8,128)(2,1)} %pad_maximum_fusion.5), channel_id=1, source_target_pairs={{0,1},{1,0},{2,3},{3,2},{4,5},{5,4},{6,7},{7,6},{8,9},{9,8},{10,11... | collective-permute-start | bytes 2359304 | tf_op jit(solution)/shard_map/ppermute | solution.py:28
  77.8 7.9 %collective-permute-start.13 = (bf16[512,256]{1,0:T(8,128)(2,1)S(1)}, bf16[512,256]{1,0:T(8,128)(2,1)S(1)}, u32[]{:S(2)}, u32[]{:S(2)}) collective-permute-start(bf16[512,256]{1,0:T(8,128)(2,1)S(1)} %copy-done.17), channel_id=1, source_target_pairs={{0,8},{8,0},{16,24},{24,16},{1,9},{9,1},{17,25},{25,17},{2,10},{10... | collective-permute-start | bytes 786440 | tf_op jit(solution)/shard_map/ppermute | solution.py:28
  79.0 7.6 %collective-permute-start.14 = (bf16[512,256]{1,0:T(8,128)(2,1)S(1)}, bf16[512,256]{1,0:T(8,128)(2,1)S(1)}, u32[]{:S(2)}, u32[]{:S(2)}) collective-permute-start(bf16[512,256]{1,0:T(8,128)(2,1)S(1)} %copy-done.17), channel_id=1, source_target_pairs={{0,16},{8,24},{16,0},{24,8},{1,17},{9,25},{17,1},{25,9},{2,18},{10... | collective-permute-start | bytes 786440 | tf_op jit(solution)/shard_map/ppermute | solution.py:28
  80.1 12.0 %collective-permute-start.15 = (bf16[512,256]{1,0:T(8,128)(2,1)S(1)}, bf16[512,256]{1,0:T(8,128)(2,1)S(1)}, u32[]{:S(2)}, u32[]{:S(2)}) collective-permute-start(bf16[512,256]{1,0:T(8,128)(2,1)S(1)} %copy-done.17), channel_id=1, source_target_pairs={{0,24},{8,16},{16,8},{24,0},{1,25},{9,17},{17,9},{25,1},{2,26},{10... | collective-permute-start | bytes 786440 | tf_op jit(solution)/shard_map/ppermute | solution.py:28
  80.4 15.7 %collective-permute-start.8 = (bf16[512,256]{1,0:T(8,128)(2,1)S(1)}, bf16[512,256]{1,0:T(8,128)(2,1)S(1)}, u32[]{:S(2)}, u32[]{:S(2)}) collective-permute-start(bf16[512,256]{1,0:T(8,128)(2,1)S(1)} %copy-done.17), channel_id=1, source_target_pairs={{0,1},{1,0},{2,3},{3,2},{4,5},{5,4},{6,7},{7,6},{8,9},{9,8},{10,11... | collective-permute-start | bytes 786440 | tf_op jit(solution)/shard_map/ppermute | solution.py:28
  102.0 14.8 %collective-permute-start.17 = (bf16[512,256]{1,0:T(8,128)(2,1)}, bf16[512,256]{1,0:T(8,128)(2,1)S(1)}, u32[]{:S(2)}, u32[]{:S(2)}) collective-permute-start(bf16[512,256]{1,0:T(8,128)(2,1)} %get-tuple-element.14.refs_0_.refs_8_), channel_id=1, source_target_pairs={{0,2},{1,3},{2,0},{3,1},{4,6},{5,7},{6,4},{7,5},{8,10},{9,11},{10,... | collective-permute-start | bytes 786440 | tf_op jit(solution)/shard_map/ppermute | solution.py:28
  106.7 10.5 %collective-permute-start.18 = (bf16[512,256]{1,0:T(8,128)(2,1)}, bf16[512,256]{1,0:T(8,128)(2,1)S(1)}, u32[]{:S(2)}, u32[]{:S(2)}) collective-permute-start(bf16[512,256]{1,0:T(8,128)(2,1)} %get-tuple-element.14.refs_0_.refs_8_), channel_id=1, source_target_pairs={{0,4},{1,5},{2,6},{3,7},{4,0},{5,1},{6,2},{7,3},{8,12},{9,13},{10,... | collective-permute-start | bytes 786440 | tf_op jit(solution)/shard_map/ppermute | solution.py:28
  107.8 17.9 %collective-permute-start.19 = (bf16[512,256]{1,0:T(8,128)(2,1)}, bf16[512,256]{1,0:T(8,128)(2,1)S(1)}, u32[]{:S(2)}, u32[]{:S(2)}) collective-permute-start(bf16[512,256]{1,0:T(8,128)(2,1)} %get-tuple-element.14.refs_0_.refs_8_), channel_id=1, source_target_pairs={{0,6},{1,7},{2,4},{3,5},{4,2},{5,3},{6,0},{7,1},{8,14},{9,15},{10,... | collective-permute-start | bytes 786440 | tf_op jit(solution)/shard_map/ppermute | solution.py:28
  116.9 9.7 %copy-start.4 = (bf16[512,256]{1,0:T(8,128)(2,1)}, bf16[512,256]{1,0:T(8,128)(2,1)S(1)}, u32[]{:S(2)}) copy-start(bf16[512,256]{1,0:T(8,128)(2,1)S(1)} %collective-permute-done.17.refs_2_.refs_10_) | copy-start | bytes 786436
  117.2 9.4 %copy-start.5 = (bf16[512,256]{1,0:T(8,128)(2,1)}, bf16[512,256]{1,0:T(8,128)(2,1)S(1)}, u32[]{:S(2)}) copy-start(bf16[512,256]{1,0:T(8,128)(2,1)S(1)} %collective-permute-done.18.refs_4_.refs_12_) | copy-start | bytes 786436
  125.6 5.1 %copy-start.7 = (bf16[512,256]{1,0:T(8,128)(2,1)S(1)}, bf16[512,256]{1,0:T(8,128)(2,1)}, u32[]{:S(2)}) copy-start(bf16[512,256]{1,0:T(8,128)(2,1)} %get-tuple-element.14.refs_0_.refs_8_) | copy-start | bytes 786436
  126.6 20.5 %collective-permute-start.20 = (bf16[3,512,256]{2,1,0:T(8,128)(2,1)}, bf16[3,512,256]{2,1,0:T(8,128)(2,1)}, u32[]{:S(2)}, u32[]{:S(2)}) collective-permute-start(bf16[3,512,256]{2,1,0:T(8,128)(2,1)} %pad_maximum_fusion.6), channel_id=1, source_target_pairs={{0,1},{1,0},{2,3},{3,2},{4,5},{5,4},{6,7},{7,6},{8,9},{9,8},{10,11... | collective-permute-start | bytes 2359304 | tf_op jit(solution)/shard_map/ppermute | solution.py:28
  130.7 7.9 %collective-permute-start.21 = (bf16[512,256]{1,0:T(8,128)(2,1)S(1)}, bf16[512,256]{1,0:T(8,128)(2,1)S(1)}, u32[]{:S(2)}, u32[]{:S(2)}) collective-permute-start(bf16[512,256]{1,0:T(8,128)(2,1)S(1)} %copy-done.7), channel_id=1, source_target_pairs={{0,8},{8,0},{16,24},{24,16},{1,9},{9,1},{17,25},{25,17},{2,10},{10... | collective-permute-start | bytes 786440 | tf_op jit(solution)/shard_map/ppermute | solution.py:28
  131.6 7.5 %collective-permute-start.22 = (bf16[512,256]{1,0:T(8,128)(2,1)S(1)}, bf16[512,256]{1,0:T(8,128)(2,1)S(1)}, u32[]{:S(2)}, u32[]{:S(2)}) collective-permute-start(bf16[512,256]{1,0:T(8,128)(2,1)S(1)} %copy-done.7), channel_id=1, source_target_pairs={{0,16},{8,24},{16,0},{24,8},{1,17},{9,25},{17,1},{25,9},{2,18},{10... | collective-permute-start | bytes 786440 | tf_op jit(solution)/shard_map/ppermute | solution.py:28
  132.2 12.9 %collective-permute-start.23 = (bf16[512,256]{1,0:T(8,128)(2,1)S(1)}, bf16[512,256]{1,0:T(8,128)(2,1)S(1)}, u32[]{:S(2)}, u32[]{:S(2)}) collective-permute-start(bf16[512,256]{1,0:T(8,128)(2,1)S(1)} %copy-done.7), channel_id=1, source_target_pairs={{0,24},{8,16},{16,8},{24,0},{1,25},{9,17},{17,9},{25,1},{2,26},{10... | collective-permute-start | bytes 786440 | tf_op jit(solution)/shard_map/ppermute | solution.py:28
  133.3 15.8 %collective-permute-start.16 = (bf16[512,256]{1,0:T(8,128)(2,1)S(1)}, bf16[512,256]{1,0:T(8,128)(2,1)S(1)}, u32[]{:S(2)}, u32[]{:S(2)}) collective-permute-start(bf16[512,256]{1,0:T(8,128)(2,1)S(1)} %copy-done.7), channel_id=1, source_target_pairs={{0,1},{1,0},{2,3},{3,2},{4,5},{5,4},{6,7},{7,6},{8,9},{9,8},{10,11... | collective-permute-start | bytes 786440 | tf_op jit(solution)/shard_map/ppermute | solution.py:28
  153.4 14.0 %collective-permute-start.25 = (bf16[512,256]{1,0:T(8,128)(2,1)}, bf16[512,256]{1,0:T(8,128)(2,1)S(1)}, u32[]{:S(2)}, u32[]{:S(2)}) collective-permute-start(bf16[512,256]{1,0:T(8,128)(2,1)} %get-tuple-element.15.refs_0_), channel_id=1, source_target_pairs={{0,2},{1,3},{2,0},{3,1},{4,6},{5,7},{6,4},{7,5},{8,10},{9,11},{10,... | collective-permute-start | bytes 786440 | tf_op jit(solution)/shard_map/ppermute | solution.py:28
  157.4 10.4 %collective-permute-start.26 = (bf16[512,256]{1,0:T(8,128)(2,1)}, bf16[512,256]{1,0:T(8,128)(2,1)S(1)}, u32[]{:S(2)}, u32[]{:S(2)}) collective-permute-start(bf16[512,256]{1,0:T(8,128)(2,1)} %get-tuple-element.15.refs_0_), channel_id=1, source_target_pairs={{0,4},{1,5},{2,6},{3,7},{4,0},{5,1},{6,2},{7,3},{8,12},{9,13},{10,... | collective-permute-start | bytes 786440 | tf_op jit(solution)/shard_map/ppermute | solution.py:28
  158.4 17.8 %collective-permute-start.27 = (bf16[512,256]{1,0:T(8,128)(2,1)}, bf16[512,256]{1,0:T(8,128)(2,1)S(1)}, u32[]{:S(2)}, u32[]{:S(2)}) collective-permute-start(bf16[512,256]{1,0:T(8,128)(2,1)} %get-tuple-element.15.refs_0_), channel_id=1, source_target_pairs={{0,6},{1,7},{2,4},{3,5},{4,2},{5,3},{6,0},{7,1},{8,14},{9,15},{10,... | collective-permute-start | bytes 786440 | tf_op jit(solution)/shard_map/ppermute | solution.py:28
  167.4 9.8 %copy-start.10 = (bf16[512,256]{1,0:T(8,128)(2,1)}, bf16[512,256]{1,0:T(8,128)(2,1)S(1)}, u32[]{:S(2)}) copy-start(bf16[512,256]{1,0:T(8,128)(2,1)S(1)} %collective-permute-done.25.refs_2_) | copy-start | bytes 786436
  167.8 9.4 %copy-start.12 = (bf16[512,256]{1,0:T(8,128)(2,1)}, bf16[512,256]{1,0:T(8,128)(2,1)S(1)}, u32[]{:S(2)}) copy-start(bf16[512,256]{1,0:T(8,128)(2,1)S(1)} %collective-permute-done.26.refs_4_) | copy-start | bytes 786436
  176.3 1.0 copy-start.14
  176.3 5.2 %copy-start.16 = (bf16[512,256]{1,0:T(8,128)(2,1)S(1)}, bf16[512,256]{1,0:T(8,128)(2,1)}, u32[]{:S(2)}) copy-start(bf16[512,256]{1,0:T(8,128)(2,1)} %get-tuple-element.15.refs_0_) | copy-start | bytes 786436
  177.3 19.6 %collective-permute-start.28 = (bf16[3,512,256]{2,1,0:T(8,128)(2,1)}, bf16[3,512,256]{2,1,0:T(8,128)(2,1)}, u32[]{:S(2)}, u32[]{:S(2)}) collective-permute-start(bf16[3,512,256]{2,1,0:T(8,128)(2,1)} %pad_maximum_fusion.7), channel_id=1, source_target_pairs={{0,1},{1,0},{2,3},{3,2},{4,5},{5,4},{6,7},{7,6},{8,9},{9,8},{10,11... | collective-permute-start | bytes 2359304 | tf_op jit(solution)/shard_map/ppermute | solution.py:28
  181.5 7.9 %collective-permute-start.29 = (bf16[512,256]{1,0:T(8,128)(2,1)S(1)}, bf16[512,256]{1,0:T(8,128)(2,1)S(1)}, u32[]{:S(2)}, u32[]{:S(2)}) collective-permute-start(bf16[512,256]{1,0:T(8,128)(2,1)S(1)} %copy-done.16), channel_id=1, source_target_pairs={{0,8},{8,0},{16,24},{24,16},{1,9},{9,1},{17,25},{25,17},{2,10},{10... | collective-permute-start | bytes 786440 | tf_op jit(solution)/shard_map/ppermute | solution.py:28
  181.8 7.6 %collective-permute-start.30 = (bf16[512,256]{1,0:T(8,128)(2,1)S(1)}, bf16[512,256]{1,0:T(8,128)(2,1)S(1)}, u32[]{:S(2)}, u32[]{:S(2)}) collective-permute-start(bf16[512,256]{1,0:T(8,128)(2,1)S(1)} %copy-done.16), channel_id=1, source_target_pairs={{0,16},{8,24},{16,0},{24,8},{1,17},{9,25},{17,1},{25,9},{2,18},{10... | collective-permute-start | bytes 786440 | tf_op jit(solution)/shard_map/ppermute | solution.py:28
  182.9 12.1 %collective-permute-start.31 = (bf16[512,256]{1,0:T(8,128)(2,1)S(1)}, bf16[512,256]{1,0:T(8,128)(2,1)S(1)}, u32[]{:S(2)}, u32[]{:S(2)}) collective-permute-start(bf16[512,256]{1,0:T(8,128)(2,1)S(1)} %copy-done.16), channel_id=1, source_target_pairs={{0,24},{8,16},{16,8},{24,0},{1,25},{9,17},{17,9},{25,1},{2,26},{10... | collective-permute-start | bytes 786440 | tf_op jit(solution)/shard_map/ppermute | solution.py:28
  184.1 14.8 %collective-permute-start.24 = (bf16[512,256]{1,0:T(8,128)(2,1)S(1)}, bf16[512,256]{1,0:T(8,128)(2,1)S(1)}, u32[]{:S(2)}, u32[]{:S(2)}) collective-permute-start(bf16[512,256]{1,0:T(8,128)(2,1)S(1)} %copy-done.16), channel_id=1, source_target_pairs={{0,1},{1,0},{2,3},{3,2},{4,5},{5,4},{6,7},{7,6},{8,9},{9,8},{10,11... | collective-permute-start | bytes 786440 | tf_op jit(solution)/shard_map/ppermute | solution.py:28
  (6 other events, 4.5 us)

commit v4 on v2

--- a/solution.py
+++ b/solution.py
@@ -27,13 +27,26 @@
 def exchange(xb, n_row, n_col):
     col_pieces = [xb] + [xor_permute(xb, "row", n_row, t) for t in range(1, n_row)]
     chips = n_col // 2
-    same_core = [xb] + [xor_permute(xb, "col", n_col, 2 * s) for s in range(1, chips)]
+    same = {0: xb}
+    for s in [1] + list(range(2, chips, 2)):
+        same[s] = xor_permute(xb, "col", n_col, 2 * s)
     partner_own = xor_permute(xb, "col", n_col, 1)
-    relayed = xor_permute(jnp.stack(same_core[1:]), "col", n_col, 1)
+    first = sorted(s for s in same if s != 0)
+    relay_first = xor_permute(jnp.stack([same[s] for s in first]), "col", n_col, 1)
+    other = {0: partner_own}
+    for i, s in enumerate(first):
+        other[s] = relay_first[i]
+    forward = list(range(2, chips, 2))
+    if forward:
+        sent = xor_permute(jnp.stack([same[s] for s in forward]), "col", n_col, 2)
+        relay_sent = xor_permute(sent, "col", n_col, 1)
+        for i, s in enumerate(forward):
+            same[s ^ 1] = sent[i]
+            other[s ^ 1] = relay_sent[i]
     row_pieces = []
     for s in range(chips):
-        row_pieces.append(same_core[s])
-        row_pieces.append(partner_own if s == 0 else relayed[s - 1])
+        row_pieces.append(same[s])
+        row_pieces.append(other[s])
     return row_pieces, jnp.stack(col_pieces)
 
 

time: 156 us -> 125 us (0.80)
  waiting for transfers between devices: 61.1 us -> 37.7 us
  matrix products: 40.4 us -> 34.5 us
  starting transfers between devices: 33.7 us -> 35.3 us
    ppermute x32 -> x36, waiting for transfers between devices: 61.1 us -> 37.7 us  [xor_permute(): return lax.ppermute(x, axis, perm=[(i, i ^ s) for i in range(size)])]
    dot_general x48, matrix products: 40.4 us -> 34.5 us  [contract(): part = jnp.dot(piece, k_blocks[s], preferred_element_type=jnp.float32)]
    ppermute x32 -> x36, starting transfers between devices: 33.7 us -> 35.3 us  [xor_permute(): return lax.ppermute(x, axis, perm=[(i, i ^ s) for i in range(size)])]
  transfers between devices with their start and end apart: 32 -> 36, of which waited for: 10 -> 10; matrix products, arithmetic and copies ran while one was open for 26% -> 35% of each run, Pallas kernels for 0% -> 0%
where the time goes in v4:
time: 125 us; the launch traced here: 124 us
  waiting for transfers between devices  37.7 us (30%)
  starting transfers between devices  35.3 us (28%)
  matrix products  34.5 us (28%)
  other arithmetic  8.29 us (7%)
  local copies, waits for them, and re-layouts  7.59 us (6%)
    ppermute x36, waiting for transfers between devices, xor_permute(): return lax.ppermute(x, axis, perm=[(i, i ^ s) for i in range(size)])  37.7 us
    ppermute x36, starting transfers between devices, xor_permute(): return lax.ppermute(x, axis, perm=[(i, i ^ s) for i in range(size)])  35.3 us
    dot_general x48, matrix products, contract(): part = jnp.dot(piece, k_blocks[s], preferred_element_type=jnp.float32)  34.5 us
    gather x4, local copies, waits for them, and re-layouts, ordered_k_blocks(): return jnp.take(split, index, axis=0)  4.9 us
    another operation x4, other arithmetic, exchange(): return (row_pieces, jnp.stack(col_pieces))  4.41 us
    another operation x4, other arithmetic, exchange(): jnp.stack([same[s] for s in first])  3.05 us
  transfers between devices with their start and end apart: 36, of which 10 were waited for; matrix products, arithmetic and copies ran while one was open for 35% of the time, Pallas kernels for 0%

profile of v4, /device:TPU:1, one launch (start us, length us, event | category | flops | bytes accessed | tf_op | source)
XLA Modules:
  0.0 124.1 jit_solution(12563015054425129767)
XLA Ops:
  1.2 3.2 %collective-permute-start.5 = (bf16[512,256]{1,0:T(8,128)(2,1)S(1)}, bf16[512,256]{1,0:T(8,128)(2,1)S(1)}, u32[]{:S(2)}, u32[]{:S(2)}) collective-permute-start(bf16[512,256]{1,0:T(8,128)(2,1)S(1)} %fusion.28), channel_id=1, source_target_pairs={{0,4},{1,5},{2,6},{3,7},{4,0},{5,1},{6,2},{7,3},{8,12},{9,13},{10,... | collective-permute-start | bytes 786440 | tf_op jit(solution)/shard_map/ppermute | solution.py:24
  4.4 1.3 %collective-permute-start.4 = (bf16[512,256]{1,0:T(8,128)(2,1)S(1)}, bf16[512,256]{1,0:T(8,128)(2,1)S(1)}, u32[]{:S(2)}, u32[]{:S(2)}) collective-permute-start(bf16[512,256]{1,0:T(8,128)(2,1)S(1)} %fusion.28), channel_id=1, source_target_pairs={{0,2},{1,3},{2,0},{3,1},{4,6},{5,7},{6,4},{7,5},{8,10},{9,11},{10,... | collective-permute-start | bytes 786440 | tf_op jit(solution)/shard_map/ppermute | solution.py:24
  5.7 2.2 %collective-permute-start.2 = (bf16[512,256]{1,0:T(8,128)(2,1)S(1)}, bf16[512,256]{1,0:T(8,128)(2,1)S(1)}, u32[]{:S(2)}, u32[]{:S(2)}) collective-permute-start(bf16[512,256]{1,0:T(8,128)(2,1)S(1)} %fusion.28), channel_id=1, source_target_pairs={{0,24},{8,16},{16,8},{24,0},{1,25},{9,17},{17,9},{25,1},{2,26},{10... | collective-permute-start | bytes 786440 | tf_op jit(solution)/shard_map/ppermute | solution.py:24
  8.3 7.7 %collective-permute-done.5 = bf16[512,256]{1,0:T(8,128)(2,1)S(1)} collective-permute-done((bf16[512,256]{1,0:T(8,128)(2,1)S(1)}, bf16[512,256]{1,0:T(8,128)(2,1)S(1)}, u32[]{:S(2)}, u32[]{:S(2)}) %collective-permute-start.5) | collective-permute-done | bytes 262176 | tf_op jit(solution)/shard_map/ppermute | solution.py:24
  16.1 1.3 %collective-permute-start.3 = (bf16[512,256]{1,0:T(8,128)(2,1)S(1)}, bf16[512,256]{1,0:T(8,128)(2,1)}, u32[]{:S(2)}, u32[]{:S(2)}) collective-permute-start(bf16[512,256]{1,0:T(8,128)(2,1)S(1)} %fusion.28), channel_id=1, source_target_pairs={{0,1},{1,0},{2,3},{3,2},{4,5},{5,4},{6,7},{7,6},{8,9},{9,8},{10,11... | collective-permute-start | bytes 786440 | tf_op jit(solution)/shard_map/ppermute | solution.py:24
  18.5 1.3 %collective-permute-start.6 = (bf16[2,512,256]{2,1,0:T(8,128)(2,1)}, bf16[2,512,256]{2,1,0:T(8,128)(2,1)}, u32[]{:S(2)}, u32[]{:S(2)}) collective-permute-start(bf16[2,512,256]{2,1,0:T(8,128)(2,1)} %pad_maximum_fusion.4), channel_id=1, source_target_pairs={{0,1},{1,0},{2,3},{3,2},{4,5},{5,4},{6,7},{7,6},{8,9},{9,8},{10,11... | collective-permute-start | bytes 1572872 | tf_op jit(solution)/shard_map/ppermute | solution.py:24
  21.8 1.2 convolution_add_fusion.17
  23.0 2.2 %collective-permute-done.7 = bf16[1,512,256]{2,1,0:T(8,128)(2,1)} collective-permute-done((bf16[1,512,256]{2,1,0:T(8,128)(2,1)S(1)}, bf16[1,512,256]{2,1,0:T(8,128)(2,1)}, u32[]{:S(2)}, u32[]{:S(2)}) %collective-permute-start.7) | collective-permute-done | bytes 262176 | tf_op jit(solution)/shard_map/ppermute | solution.py:24
  26.2 1.2 fusion.54
  27.4 1.2 fusion.59
  28.5 1.2 fusion.57
  30.0 1.1 fusion.79
  31.1 2.2 %collective-permute-start.17 = (bf16[512,256]{1,0:T(8,128)(2,1)}, bf16[512,256]{1,0:T(8,128)(2,1)S(1)}, u32[]{:S(2)}, u32[]{:S(2)}) collective-permute-start(bf16[512,256]{1,0:T(8,128)(2,1)} %get-tuple-element.8), channel_id=1, source_target_pairs={{0,24},{8,16},{16,8},{24,0},{1,25},{9,17},{17,9},{25,1},{2,26},{10... | collective-permute-start | bytes 786440 | tf_op jit(solution)/shard_map/ppermute | solution.py:24
  33.8 2.0 %collective-permute-start.11 = (bf16[512,256]{1,0:T(8,128)(2,1)}, bf16[512,256]{1,0:T(8,128)(2,1)}, u32[]{:S(2)}, u32[]{:S(2)}) collective-permute-start(bf16[512,256]{1,0:T(8,128)(2,1)} %get-tuple-element.8), channel_id=1, source_target_pairs={{0,4},{1,5},{2,6},{3,7},{4,0},{5,1},{6,2},{7,3},{8,12},{9,13},{10,... | collective-permute-start | bytes 786440 | tf_op jit(solution)/shard_map/ppermute | solution.py:24
  35.8 1.5 %collective-permute-start.10 = (bf16[512,256]{1,0:T(8,128)(2,1)}, bf16[512,256]{1,0:T(8,128)(2,1)}, u32[]{:S(2)}, u32[]{:S(2)}) collective-permute-start(bf16[512,256]{1,0:T(8,128)(2,1)} %get-tuple-element.8), channel_id=1, source_target_pairs={{0,2},{1,3},{2,0},{3,1},{4,6},{5,7},{6,4},{7,5},{8,10},{9,11},{10,... | collective-permute-start | bytes 786440 | tf_op jit(solution)/shard_map/ppermute | solution.py:24
  37.2 2.0 %fusion.68 = f32[512,256]{1,0:T(8,128)} fusion(bf16[512,256]{1,0:T(8,128)(2,1)} %get-tuple-element.8, bf16[8,256,256]{2,1,0:T(8,128)(2,1)S(1)} %broadcast_select_fusion.3), kind=kOutput, calls=%fused_computation.141 | convolution fusion | flops 67108864 | bytes 917504 | tf_op jit(solution)/shard_map/dot_general | solution.py:66
  40.2 1.2 collective-permute-start.9
  41.4 4.8 %collective-permute-done.16 = bf16[512,256]{1,0:T(8,128)(2,1)S(1)} collective-permute-done((bf16[512,256]{1,0:T(8,128)(2,1)}, bf16[512,256]{1,0:T(8,128)(2,1)S(1)}, u32[]{:S(2)}, u32[]{:S(2)}) %collective-permute-start.16) | collective-permute-done | bytes 262176 | tf_op jit(solution)/shard_map/ppermute | solution.py:24
  46.2 2.1 %pad_maximum_fusion.1 = bf16[4,512,256]{2,1,0:T(8,128)(2,1)} fusion(bf16[1,512,256]{2,1,0:T(8,128)(2,1)S(1)} %bitcast.270, bf16[1,512,256]{2,1,0:T(8,128)(2,1)S(1)} %bitcast.273, bf16[1,512,256]{2,1,0:T(8,128)(2,1)S(1)} %bitcast.276, bf16[1,512,256]{2,1,0:T(8,128)(2,1)} %bitcast.26), kind=kLoop, calls=%fused_computation.51 | loop fusion | flops 1572864 | bytes 2097152 | tf_op jit(solution)/shard_map/stack | solution.py:50
  48.3 1.8 %gather_fusion.1 = bf16[8,256,256]{2,1,0:T(8,128)(2,1)S(1)} fusion(bf16[8,256,256]{2,1,0:T(8,128)(2,1)} %bitcast.256, s32[1024]{0:T(1024)S(1)} %pad_clamp_fusion), kind=kCustom, calls=%fused_computation.1.clone | custom fusion | bytes 2097184 | tf_op jit(solution)/shard_map/jit(_take)/gather | solution.py:60
  52.8 1.2 fusion.52
  54.0 1.2 fusion.58
  55.4 1.2 fusion.56
  56.6 1.2 convolution_add_fusion.11
  59.0 1.2 fusion.70
  60.2 1.2 convolution_add_fusion.14
  62.2 1.3 %fusion.22 = f32[512,256]{1,0:T(8,128)S(1)} fusion(f32[512,256]{1,0:T(8,128)S(1)} %fusion.48, f32[512,256]{1,0:T(8,128)S(1)} %fusion.32, f32[512,256]{1,0:T(8,128)S(1)} %fusion.70, f32[512,256]{1,0:T(8,128)S(1)} %fusion.33, f32[512,256]{1,0:T(8,128)S(1)} %convolution_add_fusion.14, bf16[512,256]{1,0:T(8,128)(2,1)} %collective-permute-done.10, ...), kind=kOutput, calls=%fused_computation.40 | convolution fusion | flops 67764224 | bytes 3538944 | tf_op jit(solution)/shard_map/dot_general | solution.py:66
  63.8 3.2 %collective-permute-start.23 = (bf16[512,256]{1,0:T(8,128)(2,1)S(1)}, bf16[512,256]{1,0:T(8,128)(2,1)S(1)}, u32[]{:S(2)}, u32[]{:S(2)}) collective-permute-start(bf16[512,256]{1,0:T(8,128)(2,1)S(1)} %fusion.29), channel_id=1, source_target_pairs={{0,4},{1,5},{2,6},{3,7},{4,0},{5,1},{6,2},{7,3},{8,12},{9,13},{10,... | collective-permute-start | bytes 786440 | tf_op jit(solution)/shard_map/ppermute | solution.py:24
  66.9 1.4 %collective-permute-start.20 = (bf16[512,256]{1,0:T(8,128)(2,1)S(1)}, bf16[512,256]{1,0:T(8,128)(2,1)S(1)}, u32[]{:S(2)}, u32[]{:S(2)}) collective-permute-start(bf16[512,256]{1,0:T(8,128)(2,1)S(1)} %fusion.29), channel_id=1, source_target_pairs={{0,24},{8,16},{16,8},{24,0},{1,25},{9,17},{17,9},{25,1},{2,26},{10... | collective-permute-start | bytes 786440 | tf_op jit(solution)/shard_map/ppermute | solution.py:24
  69.6 9.6 %collective-permute-done.23 = bf16[512,256]{1,0:T(8,128)(2,1)S(1)} collective-permute-done((bf16[512,256]{1,0:T(8,128)(2,1)S(1)}, bf16[512,256]{1,0:T(8,128)(2,1)S(1)}, u32[]{:S(2)}, u32[]{:S(2)}) %collective-permute-start.23) | collective-permute-done | bytes 262176 | tf_op jit(solution)/shard_map/ppermute | solution.py:24
  79.9 1.8 %collective-permute-done.19 = bf16[512,256]{1,0:T(8,128)(2,1)S(1)} collective-permute-done((bf16[512,256]{1,0:T(8,128)(2,1)S(1)}, bf16[512,256]{1,0:T(8,128)(2,1)S(1)}, u32[]{:S(2)}, u32[]{:S(2)}) %collective-permute-start.19) | collective-permute-done | bytes 262176 | tf_op jit(solution)/shard_map/ppermute | solution.py:24
  82.7 1.7 %collective-permute-start.24 = (bf16[2,512,256]{2,1,0:T(8,128)(2,1)S(1)}, bf16[2,512,256]{2,1,0:T(8,128)(2,1)S(1)}, u32[]{:S(2)}, u32[]{:S(2)}) collective-permute-start(bf16[2,512,256]{2,1,0:T(8,128)(2,1)S(1)} %pad_maximum_fusion.6), channel_id=1, source_target_pairs={{0,1},{1,0},{2,3},{3,2},{4,5},{5,4},{6,7},{7,6},{8,9},{9,8},{10,11... | collective-permute-start | bytes 1572872 | tf_op jit(solution)/shard_map/ppermute | solution.py:24
  84.8 1.2 convolution_add_fusion.8
  86.0 2.4 %collective-permute-done.25 = bf16[1,512,256]{2,1,0:T(8,128)(2,1)} collective-permute-done((bf16[1,512,256]{2,1,0:T(8,128)(2,1)S(1)}, bf16[1,512,256]{2,1,0:T(8,128)(2,1)}, u32[]{:S(2)}, u32[]{:S(2)}) %collective-permute-start.25) | collective-permute-done | bytes 262176 | tf_op jit(solution)/shard_map/ppermute | solution.py:24
  89.4 1.2 fusion.43
  92.8 1.4 %collective-permute-start.35 = (bf16[512,256]{1,0:T(8,128)(2,1)}, bf16[512,256]{1,0:T(8,128)(2,1)S(1)}, u32[]{:S(2)}, u32[]{:S(2)}) collective-permute-start(bf16[512,256]{1,0:T(8,128)(2,1)} %get-tuple-element.10), channel_id=1, source_target_pairs={{0,24},{8,16},{16,8},{24,0},{1,25},{9,17},{17,9},{25,1},{2,26},{10... | collective-permute-start | bytes 786440 | tf_op jit(solution)/shard_map/ppermute | solution.py:24
  95.7 1.5 %collective-permute-start.28 = (bf16[512,256]{1,0:T(8,128)(2,1)}, bf16[512,256]{1,0:T(8,128)(2,1)}, u32[]{:S(2)}, u32[]{:S(2)}) collective-permute-start(bf16[512,256]{1,0:T(8,128)(2,1)} %get-tuple-element.10), channel_id=1, source_target_pairs={{0,2},{1,3},{2,0},{3,1},{4,6},{5,7},{6,4},{7,5},{8,10},{9,11},{10,... | collective-permute-start | bytes 786440 | tf_op jit(solution)/shard_map/ppermute | solution.py:24
  97.2 2.0 %fusion.72 = f32[512,256]{1,0:T(8,128)} fusion(bf16[512,256]{1,0:T(8,128)(2,1)} %get-tuple-element.10, bf16[8,256,256]{2,1,0:T(8,128)(2,1)S(1)} %broadcast_select_fusion.1), kind=kOutput, calls=%fused_computation.145 | convolution fusion | flops 67108864 | bytes 917504 | tf_op jit(solution)/shard_map/dot_general | solution.py:66
  99.2 2.7 %collective-permute-done.35 = bf16[512,256]{1,0:T(8,128)(2,1)S(1)} collective-permute-done((bf16[512,256]{1,0:T(8,128)(2,1)}, bf16[512,256]{1,0:T(8,128)(2,1)S(1)}, u32[]{:S(2)}, u32[]{:S(2)}) %collective-permute-start.35) | collective-permute-done | bytes 262176 | tf_op jit(solution)/shard_map/ppermute | solution.py:24
  101.9 1.2 collective-permute-start.27
  103.1 4.8 %collective-permute-done.34 = bf16[512,256]{1,0:T(8,128)(2,1)S(1)} collective-permute-done((bf16[512,256]{1,0:T(8,128)(2,1)}, bf16[512,256]{1,0:T(8,128)(2,1)S(1)}, u32[]{:S(2)}, u32[]{:S(2)}) %collective-permute-start.34) | collective-permute-done | bytes 262176 | tf_op jit(solution)/shard_map/ppermute | solution.py:24
  107.9 2.1 %pad_maximum_fusion.3 = bf16[4,512,256]{2,1,0:T(8,128)(2,1)} fusion(bf16[1,512,256]{2,1,0:T(8,128)(2,1)S(1)} %bitcast.271, bf16[1,512,256]{2,1,0:T(8,128)(2,1)S(1)} %bitcast.274, bf16[1,512,256]{2,1,0:T(8,128)(2,1)S(1)} %bitcast.277, bf16[1,512,256]{2,1,0:T(8,128)(2,1)} %bitcast.64), kind=kLoop, calls=%fused_computation.53 | loop fusion | flops 1572864 | bytes 2097152 | tf_op jit(solution)/shard_map/stack | solution.py:50
  110.0 1.8 %gather_fusion.3 = bf16[8,256,256]{2,1,0:T(8,128)(2,1)S(1)} fusion(bf16[8,256,256]{2,1,0:T(8,128)(2,1)} %bitcast.254, s32[1024]{0:T(1024)S(1)} %pad_clamp_fusion), kind=kCustom, calls=%fused_computation.3.clone | custom fusion | bytes 2097184 | tf_op jit(solution)/shard_map/jit(_take)/gather | solution.py:60
  113.9 1.2 fusion.41
  115.8 1.2 convolution_add_fusion.2
  118.1 1.2 fusion.74
  119.4 1.2 convolution_add_fusion.5
  121.7 1.3 %fusion.8 = f32[512,256]{1,0:T(8,128)S(1)} fusion(f32[512,256]{1,0:T(8,128)S(1)} %fusion.37, f32[512,256]{1,0:T(8,128)S(1)} %fusion.30, f32[512,256]{1,0:T(8,128)S(1)} %fusion.74, f32[512,256]{1,0:T(8,128)S(1)} %fusion.31, f32[512,256]{1,0:T(8,128)S(1)} %convolution_add_fusion.5, bf16[512,256]{1,0:T(8,128)(2,1)} %collective-permute-done.28, ...), kind=kOutput, calls=%fused_computation.17 | convolution fusion | flops 67764224 | bytes 3538944 | tf_op jit(solution)/shard_map/dot_general | solution.py:66
  (118 shorter events, 26.5 us)
Async XLA Ops:
  0.0 0.7 copy-start.11
  0.0 1.1 copy-start.10
  1.2 14.9 %collective-permute-start.5 = (bf16[512,256]{1,0:T(8,128)(2,1)S(1)}, bf16[512,256]{1,0:T(8,128)(2,1)S(1)}, u32[]{:S(2)}, u32[]{:S(2)}) collective-permute-start(bf16[512,256]{1,0:T(8,128)(2,1)S(1)} %fusion.28), channel_id=1, source_target_pairs={{0,4},{1,5},{2,6},{3,7},{4,0},{5,1},{6,2},{7,3},{8,12},{9,13},{10,... | collective-permute-start | bytes 786440 | tf_op jit(solution)/shard_map/ppermute | solution.py:24
  4.4 13.0 %collective-permute-start.4 = (bf16[512,256]{1,0:T(8,128)(2,1)S(1)}, bf16[512,256]{1,0:T(8,128)(2,1)S(1)}, u32[]{:S(2)}, u32[]{:S(2)}) collective-permute-start(bf16[512,256]{1,0:T(8,128)(2,1)S(1)} %fusion.28), channel_id=1, source_target_pairs={{0,2},{1,3},{2,0},{3,1},{4,6},{5,7},{6,4},{7,5},{8,10},{9,11},{10,... | collective-permute-start | bytes 786440 | tf_op jit(solution)/shard_map/ppermute | solution.py:24
  5.7 12.9 %collective-permute-start.2 = (bf16[512,256]{1,0:T(8,128)(2,1)S(1)}, bf16[512,256]{1,0:T(8,128)(2,1)S(1)}, u32[]{:S(2)}, u32[]{:S(2)}) collective-permute-start(bf16[512,256]{1,0:T(8,128)(2,1)S(1)} %fusion.28), channel_id=1, source_target_pairs={{0,24},{8,16},{16,8},{24,0},{1,25},{9,17},{17,9},{25,1},{2,26},{10... | collective-permute-start | bytes 786440 | tf_op jit(solution)/shard_map/ppermute | solution.py:24
  7.8 12.6 %collective-permute-start.1 = (bf16[512,256]{1,0:T(8,128)(2,1)S(1)}, bf16[512,256]{1,0:T(8,128)(2,1)S(1)}, u32[]{:S(2)}, u32[]{:S(2)}) collective-permute-start(bf16[512,256]{1,0:T(8,128)(2,1)S(1)} %fusion.28), channel_id=1, source_target_pairs={{0,16},{8,24},{16,0},{24,8},{1,17},{9,25},{17,1},{25,9},{2,18},{10... | collective-permute-start | bytes 786440 | tf_op jit(solution)/shard_map/ppermute | solution.py:24
  8.0 12.4 %collective-permute-start = (bf16[512,256]{1,0:T(8,128)(2,1)S(1)}, bf16[512,256]{1,0:T(8,128)(2,1)S(1)}, u32[]{:S(2)}, u32[]{:S(2)}) collective-permute-start(bf16[512,256]{1,0:T(8,128)(2,1)S(1)} %fusion.28), channel_id=1, source_target_pairs={{0,8},{8,0},{16,24},{24,16},{1,9},{9,1},{17,25},{25,17},{2,10},{10... | collective-permute-start | bytes 786440 | tf_op jit(solution)/shard_map/ppermute | solution.py:24
  16.1 5.7 %collective-permute-start.3 = (bf16[512,256]{1,0:T(8,128)(2,1)S(1)}, bf16[512,256]{1,0:T(8,128)(2,1)}, u32[]{:S(2)}, u32[]{:S(2)}) collective-permute-start(bf16[512,256]{1,0:T(8,128)(2,1)S(1)} %fusion.28), channel_id=1, source_target_pairs={{0,1},{1,0},{2,3},{3,2},{4,5},{5,4},{6,7},{7,6},{8,9},{9,8},{10,11... | collective-permute-start | bytes 786440 | tf_op jit(solution)/shard_map/ppermute | solution.py:24
  17.3 7.8 %collective-permute-start.7 = (bf16[1,512,256]{2,1,0:T(8,128)(2,1)S(1)}, bf16[1,512,256]{2,1,0:T(8,128)(2,1)}, u32[]{:S(2)}, u32[]{:S(2)}) collective-permute-start(bf16[1,512,256]{2,1,0:T(8,128)(2,1)S(1)} %bitcast.261), channel_id=1, source_target_pairs={{0,2},{1,3},{2,0},{3,1},{4,6},{5,7},{6,4},{7,5},{8,10},{9,11},{10,... | collective-permute-start | bytes 786440 | tf_op jit(solution)/shard_map/ppermute | solution.py:24
  18.5 8.8 %collective-permute-start.6 = (bf16[2,512,256]{2,1,0:T(8,128)(2,1)}, bf16[2,512,256]{2,1,0:T(8,128)(2,1)}, u32[]{:S(2)}, u32[]{:S(2)}) collective-permute-start(bf16[2,512,256]{2,1,0:T(8,128)(2,1)} %pad_maximum_fusion.4), channel_id=1, source_target_pairs={{0,1},{1,0},{2,3},{3,2},{4,5},{5,4},{6,7},{7,6},{8,9},{9,8},{10,11... | collective-permute-start | bytes 1572872 | tf_op jit(solution)/shard_map/ppermute | solution.py:24
  25.2 4.8 %collective-permute-start.8 = (bf16[1,512,256]{2,1,0:T(8,128)(2,1)}, bf16[1,512,256]{2,1,0:T(8,128)(2,1)S(1)}, u32[]{:S(2)}, u32[]{:S(2)}) collective-permute-start(bf16[1,512,256]{2,1,0:T(8,128)(2,1)} %collective-permute-done.7), channel_id=1, source_target_pairs={{0,1},{1,0},{2,3},{3,2},{4,5},{5,4},{6,7},{7,6},{8,9},{9,8},{10,11... | collective-permute-start | bytes 786440 | tf_op jit(solution)/shard_map/ppermute | solution.py:24
  30.0 1.1 copy-start.8
  31.1 9.1 %collective-permute-start.17 = (bf16[512,256]{1,0:T(8,128)(2,1)}, bf16[512,256]{1,0:T(8,128)(2,1)S(1)}, u32[]{:S(2)}, u32[]{:S(2)}) collective-permute-start(bf16[512,256]{1,0:T(8,128)(2,1)} %get-tuple-element.8), channel_id=1, source_target_pairs={{0,24},{8,16},{16,8},{24,0},{1,25},{9,17},{17,9},{25,1},{2,26},{10... | collective-permute-start | bytes 786440 | tf_op jit(solution)/shard_map/ppermute | solution.py:24
  33.4 12.9 %collective-permute-start.16 = (bf16[512,256]{1,0:T(8,128)(2,1)}, bf16[512,256]{1,0:T(8,128)(2,1)S(1)}, u32[]{:S(2)}, u32[]{:S(2)}) collective-permute-start(bf16[512,256]{1,0:T(8,128)(2,1)} %get-tuple-element.8), channel_id=1, source_target_pairs={{0,16},{8,24},{16,0},{24,8},{1,17},{9,25},{17,1},{25,9},{2,18},{10... | collective-permute-start | bytes 786440 | tf_op jit(solution)/shard_map/ppermute | solution.py:24
  33.6 12.6 %collective-permute-start.15 = (bf16[512,256]{1,0:T(8,128)(2,1)}, bf16[512,256]{1,0:T(8,128)(2,1)S(1)}, u32[]{:S(2)}, u32[]{:S(2)}) collective-permute-start(bf16[512,256]{1,0:T(8,128)(2,1)} %get-tuple-element.8), channel_id=1, source_target_pairs={{0,8},{8,0},{16,24},{24,16},{1,9},{9,1},{17,25},{25,17},{2,10},{10... | collective-permute-start | bytes 786440 | tf_op jit(solution)/shard_map/ppermute | solution.py:24
  33.8 16.5 %collective-permute-start.11 = (bf16[512,256]{1,0:T(8,128)(2,1)}, bf16[512,256]{1,0:T(8,128)(2,1)}, u32[]{:S(2)}, u32[]{:S(2)}) collective-permute-start(bf16[512,256]{1,0:T(8,128)(2,1)} %get-tuple-element.8), channel_id=1, source_target_pairs={{0,4},{1,5},{2,6},{3,7},{4,0},{5,1},{6,2},{7,3},{8,12},{9,13},{10,... | collective-permute-start | bytes 786440 | tf_op jit(solution)/shard_map/ppermute | solution.py:24
  35.8 15.2 %collective-permute-start.10 = (bf16[512,256]{1,0:T(8,128)(2,1)}, bf16[512,256]{1,0:T(8,128)(2,1)}, u32[]{:S(2)}, u32[]{:S(2)}) collective-permute-start(bf16[512,256]{1,0:T(8,128)(2,1)} %get-tuple-element.8), channel_id=1, source_target_pairs={{0,2},{1,3},{2,0},{3,1},{4,6},{5,7},{6,4},{7,5},{8,10},{9,11},{10,... | collective-permute-start | bytes 786440 | tf_op jit(solution)/shard_map/ppermute | solution.py:24
  40.2 20.0 %collective-permute-start.9 = (bf16[512,256]{1,0:T(8,128)(2,1)}, bf16[512,256]{1,0:T(8,128)(2,1)}, u32[]{:S(2)}, u32[]{:S(2)}) collective-permute-start(bf16[512,256]{1,0:T(8,128)(2,1)} %get-tuple-element.8), channel_id=1, source_target_pairs={{0,1},{1,0},{2,3},{3,2},{4,5},{5,4},{6,7},{7,6},{8,9},{9,8},{10,11... | collective-permute-start | bytes 786440 | tf_op jit(solution)/shard_map/ppermute | solution.py:24
  50.3 11.1 %collective-permute-start.13 = (bf16[1,512,256]{2,1,0:T(8,128)(2,1)}, bf16[1,512,256]{2,1,0:T(8,128)(2,1)S(1)}, u32[]{:S(2)}, u32[]{:S(2)}) collective-permute-start(bf16[1,512,256]{2,1,0:T(8,128)(2,1)} %bitcast.21), channel_id=1, source_target_pairs={{0,2},{1,3},{2,0},{3,1},{4,6},{5,7},{6,4},{7,5},{8,10},{9,11},{10,... | collective-permute-start | bytes 786440 | tf_op jit(solution)/shard_map/ppermute | solution.py:24
  52.1 9.7 %collective-permute-start.12 = (bf16[2,512,256]{2,1,0:T(8,128)(2,1)S(1)}, bf16[2,512,256]{2,1,0:T(8,128)(2,1)S(1)}, u32[]{:S(2)}, u32[]{:S(2)}) collective-permute-start(bf16[2,512,256]{2,1,0:T(8,128)(2,1)S(1)} %pad_maximum_fusion.5), channel_id=1, source_target_pairs={{0,1},{1,0},{2,3},{3,2},{4,5},{5,4},{6,7},{7,6},{8,9},{9,8},{10,11... | collective-permute-start | bytes 1572872 | tf_op jit(solution)/shard_map/ppermute | solution.py:24
  57.8 1.0 copy-start.9
  59.0 1.3 %copy-start.5 = (f32[512,256]{1,0:T(8,128)S(1)}, f32[512,256]{1,0:T(8,128)}, u32[]{:S(2)}) copy-start(f32[512,256]{1,0:T(8,128)} %fusion.68) | copy-start | bytes 1572868
  61.4 2.1 %collective-permute-start.14 = (bf16[1,512,256]{2,1,0:T(8,128)(2,1)S(1)}, bf16[1,512,256]{2,1,0:T(8,128)(2,1)S(1)}, u32[]{:S(2)}, u32[]{:S(2)}) collective-permute-start(bf16[1,512,256]{2,1,0:T(8,128)(2,1)S(1)} %collective-permute-done.13), channel_id=1, source_target_pairs={{0,1},{1,0},{2,3},{3,2},{4,5},{5,4},{6,7},{7,6},{8,9},{9,8},{10,11... | collective-permute-start | bytes 786440 | tf_op jit(solution)/shard_map/ppermute | solution.py:24
  62.2 1.3 %copy-start.3 = (f32[512,256]{1,0:T(8,128)S(1)}, f32[512,256]{1,0:T(8,128)}, u32[]{:S(2)}) copy-start(f32[512,256]{1,0:T(8,128)} %get-tuple-element.9) | copy-start | bytes 1572868
  63.8 15.4 %collective-permute-start.23 = (bf16[512,256]{1,0:T(8,128)(2,1)S(1)}, bf16[512,256]{1,0:T(8,128)(2,1)S(1)}, u32[]{:S(2)}, u32[]{:S(2)}) collective-permute-start(bf16[512,256]{1,0:T(8,128)(2,1)S(1)} %fusion.29), channel_id=1, source_target_pairs={{0,4},{1,5},{2,6},{3,7},{4,0},{5,1},{6,2},{7,3},{8,12},{9,13},{10,... | collective-permute-start | bytes 786440 | tf_op jit(solution)/shard_map/ppermute | solution.py:24
  66.9 13.0 %collective-permute-start.20 = (bf16[512,256]{1,0:T(8,128)(2,1)S(1)}, bf16[512,256]{1,0:T(8,128)(2,1)S(1)}, u32[]{:S(2)}, u32[]{:S(2)}) collective-permute-start(bf16[512,256]{1,0:T(8,128)(2,1)S(1)} %fusion.29), channel_id=1, source_target_pairs={{0,24},{8,16},{16,8},{24,0},{1,25},{9,17},{17,9},{25,1},{2,26},{10... | collective-permute-start | bytes 786440 | tf_op jit(solution)/shard_map/ppermute | solution.py:24
  68.3 13.4 %collective-permute-start.19 = (bf16[512,256]{1,0:T(8,128)(2,1)S(1)}, bf16[512,256]{1,0:T(8,128)(2,1)S(1)}, u32[]{:S(2)}, u32[]{:S(2)}) collective-permute-start(bf16[512,256]{1,0:T(8,128)(2,1)S(1)} %fusion.29), channel_id=1, source_target_pairs={{0,16},{8,24},{16,0},{24,8},{1,17},{9,25},{17,1},{25,9},{2,18},{10... | collective-permute-start | bytes 786440 | tf_op jit(solution)/shard_map/ppermute | solution.py:24
  69.3 12.3 %collective-permute-start.18 = (bf16[512,256]{1,0:T(8,128)(2,1)S(1)}, bf16[512,256]{1,0:T(8,128)(2,1)S(1)}, u32[]{:S(2)}, u32[]{:S(2)}) collective-permute-start(bf16[512,256]{1,0:T(8,128)(2,1)S(1)} %fusion.29), channel_id=1, source_target_pairs={{0,8},{8,0},{16,24},{24,16},{1,9},{9,1},{17,25},{25,17},{2,10},{10... | collective-permute-start | bytes 786440 | tf_op jit(solution)/shard_map/ppermute | solution.py:24
  69.6 13.0 %collective-permute-start.22 = (bf16[512,256]{1,0:T(8,128)(2,1)S(1)}, bf16[512,256]{1,0:T(8,128)(2,1)S(1)}, u32[]{:S(2)}, u32[]{:S(2)}) collective-permute-start(bf16[512,256]{1,0:T(8,128)(2,1)S(1)} %fusion.29), channel_id=1, source_target_pairs={{0,2},{1,3},{2,0},{3,1},{4,6},{5,7},{6,4},{7,5},{8,10},{9,11},{10,... | collective-permute-start | bytes 786440 | tf_op jit(solution)/shard_map/ppermute | solution.py:24
  79.2 5.6 %collective-permute-start.21 = (bf16[512,256]{1,0:T(8,128)(2,1)S(1)}, bf16[512,256]{1,0:T(8,128)(2,1)}, u32[]{:S(2)}, u32[]{:S(2)}) collective-permute-start(bf16[512,256]{1,0:T(8,128)(2,1)S(1)} %fusion.29), channel_id=1, source_target_pairs={{0,1},{1,0},{2,3},{3,2},{4,5},{5,4},{6,7},{7,6},{8,9},{9,8},{10,11... | collective-permute-start | bytes 786440 | tf_op jit(solution)/shard_map/ppermute | solution.py:24
  79.9 8.5 %collective-permute-start.25 = (bf16[1,512,256]{2,1,0:T(8,128)(2,1)S(1)}, bf16[1,512,256]{2,1,0:T(8,128)(2,1)}, u32[]{:S(2)}, u32[]{:S(2)}) collective-permute-start(bf16[1,512,256]{2,1,0:T(8,128)(2,1)S(1)} %bitcast.263), channel_id=1, source_target_pairs={{0,2},{1,3},{2,0},{3,1},{4,6},{5,7},{6,4},{7,5},{8,10},{9,11},{10,... | collective-permute-start | bytes 786440 | tf_op jit(solution)/shard_map/ppermute | solution.py:24
  82.7 7.9 %collective-permute-start.24 = (bf16[2,512,256]{2,1,0:T(8,128)(2,1)S(1)}, bf16[2,512,256]{2,1,0:T(8,128)(2,1)S(1)}, u32[]{:S(2)}, u32[]{:S(2)}) collective-permute-start(bf16[2,512,256]{2,1,0:T(8,128)(2,1)S(1)} %pad_maximum_fusion.6), channel_id=1, source_target_pairs={{0,1},{1,0},{2,3},{3,2},{4,5},{5,4},{6,7},{7,6},{8,9},{9,8},{10,11... | collective-permute-start | bytes 1572872 | tf_op jit(solution)/shard_map/ppermute | solution.py:24
  88.4 3.3 %collective-permute-start.26 = (bf16[1,512,256]{2,1,0:T(8,128)(2,1)}, bf16[1,512,256]{2,1,0:T(8,128)(2,1)S(1)}, u32[]{:S(2)}, u32[]{:S(2)}) collective-permute-start(bf16[1,512,256]{2,1,0:T(8,128)(2,1)} %collective-permute-done.25), channel_id=1, source_target_pairs={{0,1},{1,0},{2,3},{3,2},{4,5},{5,4},{6,7},{7,6},{8,9},{9,8},{10,11... | collective-permute-start | bytes 786440 | tf_op jit(solution)/shard_map/ppermute | solution.py:24
  90.6 0.8 copy-start
  91.7 1.1 copy-start.6
  92.8 9.1 %collective-permute-start.35 = (bf16[512,256]{1,0:T(8,128)(2,1)}, bf16[512,256]{1,0:T(8,128)(2,1)S(1)}, u32[]{:S(2)}, u32[]{:S(2)}) collective-permute-start(bf16[512,256]{1,0:T(8,128)(2,1)} %get-tuple-element.10), channel_id=1, source_target_pairs={{0,24},{8,16},{16,8},{24,0},{1,25},{9,17},{17,9},{25,1},{2,26},{10... | collective-permute-start | bytes 786440 | tf_op jit(solution)/shard_map/ppermute | solution.py:24
  94.3 13.7 %collective-permute-start.34 = (bf16[512,256]{1,0:T(8,128)(2,1)}, bf16[512,256]{1,0:T(8,128)(2,1)S(1)}, u32[]{:S(2)}, u32[]{:S(2)}) collective-permute-start(bf16[512,256]{1,0:T(8,128)(2,1)} %get-tuple-element.10), channel_id=1, source_target_pairs={{0,16},{8,24},{16,0},{24,8},{1,17},{9,25},{17,1},{25,9},{2,18},{10... | collective-permute-start | bytes 786440 | tf_op jit(solution)/shard_map/ppermute | solution.py:24
  95.2 12.7 %collective-permute-start.33 = (bf16[512,256]{1,0:T(8,128)(2,1)}, bf16[512,256]{1,0:T(8,128)(2,1)S(1)}, u32[]{:S(2)}, u32[]{:S(2)}) collective-permute-start(bf16[512,256]{1,0:T(8,128)(2,1)} %get-tuple-element.10), channel_id=1, source_target_pairs={{0,8},{8,0},{16,24},{24,16},{1,9},{9,1},{17,25},{25,17},{2,10},{10... | collective-permute-start | bytes 786440 | tf_op jit(solution)/shard_map/ppermute | solution.py:24
  95.5 16.5 %collective-permute-start.29 = (bf16[512,256]{1,0:T(8,128)(2,1)}, bf16[512,256]{1,0:T(8,128)(2,1)}, u32[]{:S(2)}, u32[]{:S(2)}) collective-permute-start(bf16[512,256]{1,0:T(8,128)(2,1)} %get-tuple-element.10), channel_id=1, source_target_pairs={{0,4},{1,5},{2,6},{3,7},{4,0},{5,1},{6,2},{7,3},{8,12},{9,13},{10,... | collective-permute-start | bytes 786440 | tf_op jit(solution)/shard_map/ppermute | solution.py:24
  95.7 16.6 %collective-permute-start.28 = (bf16[512,256]{1,0:T(8,128)(2,1)}, bf16[512,256]{1,0:T(8,128)(2,1)}, u32[]{:S(2)}, u32[]{:S(2)}) collective-permute-start(bf16[512,256]{1,0:T(8,128)(2,1)} %get-tuple-element.10), channel_id=1, source_target_pairs={{0,2},{1,3},{2,0},{3,1},{4,6},{5,7},{6,4},{7,5},{8,10},{9,11},{10,... | collective-permute-start | bytes 786440 | tf_op jit(solution)/shard_map/ppermute | solution.py:24
  101.9 17.4 %collective-permute-start.27 = (bf16[512,256]{1,0:T(8,128)(2,1)}, bf16[512,256]{1,0:T(8,128)(2,1)}, u32[]{:S(2)}, u32[]{:S(2)}) collective-permute-start(bf16[512,256]{1,0:T(8,128)(2,1)} %get-tuple-element.10), channel_id=1, source_target_pairs={{0,1},{1,0},{2,3},{3,2},{4,5},{5,4},{6,7},{7,6},{8,9},{9,8},{10,11... | collective-permute-start | bytes 786440 | tf_op jit(solution)/shard_map/ppermute | solution.py:24
  112.0 8.5 %collective-permute-start.31 = (bf16[1,512,256]{2,1,0:T(8,128)(2,1)}, bf16[1,512,256]{2,1,0:T(8,128)(2,1)S(1)}, u32[]{:S(2)}, u32[]{:S(2)}) collective-permute-start(bf16[1,512,256]{2,1,0:T(8,128)(2,1)} %bitcast.59), channel_id=1, source_target_pairs={{0,2},{1,3},{2,0},{3,1},{4,6},{5,7},{6,4},{7,5},{8,10},{9,11},{10,... | collective-permute-start | bytes 786440 | tf_op jit(solution)/shard_map/ppermute | solution.py:24
  113.4 1.6 %copy-start.1 = (bf16[2,512,256]{2,1,0:T(8,128)(2,1)S(1)}, bf16[2,512,256]{2,1,0:T(8,128)(2,1)}, u32[]{:S(2)}) copy-start(bf16[2,512,256]{2,1,0:T(8,128)(2,1)} %copy-done) | copy-start | bytes 1572868
  113.4 7.8 %collective-permute-start.30 = (bf16[2,512,256]{2,1,0:T(8,128)(2,1)S(1)}, bf16[2,512,256]{2,1,0:T(8,128)(2,1)S(1)}, u32[]{:S(2)}, u32[]{:S(2)}) collective-permute-start(bf16[2,512,256]{2,1,0:T(8,128)(2,1)S(1)} %pad_maximum_fusion.7), channel_id=1, source_target_pairs={{0,1},{1,0},{2,3},{3,2},{4,5},{5,4},{6,7},{7,6},{8,9},{9,8},{10,11... | collective-permute-start | bytes 1572872 | tf_op jit(solution)/shard_map/ppermute | solution.py:24
  116.9 1.0 copy-start.7
  118.1 1.3 %copy-start.4 = (f32[512,256]{1,0:T(8,128)S(1)}, f32[512,256]{1,0:T(8,128)}, u32[]{:S(2)}) copy-start(f32[512,256]{1,0:T(8,128)} %fusion.72) | copy-start | bytes 1572868
  120.6 2.4 %collective-permute-start.32 = (bf16[1,512,256]{2,1,0:T(8,128)(2,1)S(1)}, bf16[1,512,256]{2,1,0:T(8,128)(2,1)S(1)}, u32[]{:S(2)}, u32[]{:S(2)}) collective-permute-start(bf16[1,512,256]{2,1,0:T(8,128)(2,1)S(1)} %collective-permute-done.31), channel_id=1, source_target_pairs={{0,1},{1,0},{2,3},{3,2},{4,5},{5,4},{6,7},{7,6},{8,9},{9,8},{10,11... | collective-permute-start | bytes 786440 | tf_op jit(solution)/shard_map/ppermute | solution.py:24
  121.7 1.3 %copy-start.2 = (f32[512,256]{1,0:T(8,128)S(1)}, f32[512,256]{1,0:T(8,128)}, u32[]{:S(2)}) copy-start(f32[512,256]{1,0:T(8,128)} %get-tuple-element.11) | copy-start | bytes 1572868

commit v5 on v4

--- a/solution.py
+++ b/solution.py
@@ -25,7 +25,9 @@
 
 
 def exchange(xb, n_row, n_col):
-    col_pieces = [xb] + [xor_permute(xb, "row", n_row, t) for t in range(1, n_row)]
+    col_pieces = lax.all_to_all(
+        jnp.broadcast_to(xb[None], (n_row,) + xb.shape), "row", 0, 0, tiled=True
+    )
     chips = n_col // 2
     same = {0: xb}
     for s in [1] + list(range(2, chips, 2)):
@@ -47,16 +49,15 @@
     for s in range(chips):
         row_pieces.append(same[s])
         row_pieces.append(other[s])
-    return row_pieces, jnp.stack(col_pieces)
+    return row_pieces, col_pieces
 
 
 def ordered_k_blocks(col_pieces, me_row, me_col, n_col):
     n_row, rows, cols = col_pieces.shape
-    per = rows // cols
-    split = col_pieces.reshape(n_row * per, cols, cols)
+    split = col_pieces.reshape(n_row * rows // cols, cols, cols)
     s = lax.iota(jnp.int32, n_col)
     owner = jnp.bitwise_xor(s, me_col)
-    index = jnp.bitwise_xor(owner // per, me_row) * per + owner % per
+    index = owner
     return jnp.take(split, index, axis=0)
 
 

time: 125 us -> 156 us (1.25)
  matrix products: 34.5 us -> 47.1 us
  starting transfers between devices: 35.3 us -> 47 us
  local copies, waits for them, and re-layouts: 7.59 us -> 13.3 us
  waiting for transfers between devices: 37.7 us -> 41.4 us
  other arithmetic: 8.29 us -> 5.47 us
    all_to_all x0 -> x4, starting transfers between devices: none -> 14.9 us  [exchange(): lax.all_to_all(jnp.broadcast_to(xb[None], (n_row,) + xb.shape), 'row', 0,...]
    dot_general x48, matrix products: 34.5 us -> 47.1 us  [contract(): part = jnp.dot(piece, k_blocks[s], preferred_element_type=jnp.float32)]
    another operation x4 -> x0, other arithmetic: 4.41 us -> none  [exchange(): return (row_pieces, jnp.stack(col_pieces))]
    broadcast_in_dim x0 -> x4, local copies, waits for them, and re-layouts: none -> 4.3 us  [exchange(): jnp.broadcast_to(xb[None], (n_row,) + xb.shape)]
    ppermute x36 -> x24, waiting for transfers between devices: 37.7 us -> 41.3 us  [xor_permute(): return lax.ppermute(x, axis, perm=[(i, i ^ s) for i in range(size)])]
    ppermute x36 -> x24, starting transfers between devices: 35.3 us -> 32.1 us  [xor_permute(): return lax.ppermute(x, axis, perm=[(i, i ^ s) for i in range(size)])]
    another operation x4, other arithmetic: 3.05 us -> 4.64 us  [exchange(): jnp.stack([same[s] for s in first])]
    unnamed x25 -> x29, local copies, waits for them, and re-layouts: 2.49 us -> 3.88 us
  transfers between devices with their start and end apart: 36 -> 28, of which waited for: 10 -> 8; matrix products, arithmetic and copies ran while one was open for 35% -> 34% of each run, Pallas kernels for 0% -> 0%
where the time goes in v5:
time: 156 us; the launch traced here: 155 us
  matrix products  47.1 us (30%)
  starting transfers between devices  47 us (30%)
  waiting for transfers between devices  41.4 us (27%)
  local copies, waits for them, and re-layouts  13.3 us (9%)
  other arithmetic  5.47 us (4%)
    dot_general x48, matrix products, contract(): part = jnp.dot(piece, k_blocks[s], preferred_element_type=jnp.float32)  47.1 us
    ppermute x24, waiting for transfers between devices, xor_permute(): return lax.ppermute(x, axis, perm=[(i, i ^ s) for i in range(size)])  41.3 us
    ppermute x24, starting transfers between devices, xor_permute(): return lax.ppermute(x, axis, perm=[(i, i ^ s) for i in range(size)])  32.1 us
    all_to_all x4, starting transfers between devices, exchange(): lax.all_to_all(jnp.broadcast_to(xb[None], (n_row,) + xb.shape), 'row', 0,...  14.9 us
    gather x4, local copies, waits for them, and re-layouts, ordered_k_blocks(): return jnp.take(split, index, axis=0)  4.9 us
    another operation x4, other arithmetic, exchange(): jnp.stack([same[s] for s in first])  4.64 us
    broadcast_in_dim x4, local copies, waits for them, and re-layouts, exchange(): jnp.broadcast_to(xb[None], (n_row,) + xb.shape)  4.3 us
    unnamed x29, local copies, waits for them, and re-layouts  3.88 us
  transfers between devices with their start and end apart: 28, of which 8 were waited for; matrix products, arithmetic and copies ran while one was open for 34% of the time, Pallas kernels for 0%

profile of v5, /device:TPU:1, one launch (start us, length us, event | category | flops | bytes accessed | tf_op | source)
XLA Modules:
  0.0 154.9 jit_solution(15129563816599347467)
XLA Ops:
  2.2 4.3 %all-to-all-start = ((bf16[4,512,256]{2,1,0:T(8,128)(2,1)}), bf16[4,512,256]{2,1,0:T(8,128)(2,1)S(1)}, u32[]{:S(2)}, u32[]{:S(2)}) async-start(bf16[4,512,256]{2,1,0:T(8,128)(2,1)} %broadcast_in_dim.17), calls=%async_computation | async-start | bytes 2097152 | tf_op jit(solution)/shard_map/all_to_all | solution.py:28
  6.5 2.5 %collective-permute-start.2 = (bf16[512,256]{1,0:T(8,128)(2,1)S(1)}, bf16[512,256]{1,0:T(8,128)(2,1)S(1)}, u32[]{:S(2)}, u32[]{:S(2)}) collective-permute-start(bf16[512,256]{1,0:T(8,128)(2,1)S(1)} %fusion.28), channel_id=1, source_target_pairs={{0,4},{1,5},{2,6},{3,7},{4,0},{5,1},{6,2},{7,3},{8,12},{9,13},{10,... | collective-permute-start | bytes 786440 | tf_op jit(solution)/shard_map/ppermute | solution.py:24
  9.0 1.3 collective-permute-start.1
  10.3 1.4 collective-permute-start
  11.6 8.7 %collective-permute-done.2 = bf16[512,256]{1,0:T(8,128)(2,1)S(1)} collective-permute-done((bf16[512,256]{1,0:T(8,128)(2,1)S(1)}, bf16[512,256]{1,0:T(8,128)(2,1)S(1)}, u32[]{:S(2)}, u32[]{:S(2)}) %collective-permute-start.2) | collective-permute-done | bytes 262176 | tf_op jit(solution)/shard_map/ppermute | solution.py:24
  20.3 1.5 collective-permute-start.4
  23.4 3.5 %collective-permute-done.4 = bf16[1,512,256]{2,1,0:T(8,128)(2,1)} collective-permute-done((bf16[1,512,256]{2,1,0:T(8,128)(2,1)S(1)}, bf16[1,512,256]{2,1,0:T(8,128)(2,1)}, u32[]{:S(2)}, u32[]{:S(2)}) %collective-permute-start.4) | collective-permute-done | bytes 262176 | tf_op jit(solution)/shard_map/ppermute | solution.py:24
  27.0 2.2 %collective-permute-start.5 = (bf16[1,512,256]{2,1,0:T(8,128)(2,1)}, bf16[1,512,256]{2,1,0:T(8,128)(2,1)}, u32[]{:S(2)}, u32[]{:S(2)}) collective-permute-start(bf16[1,512,256]{2,1,0:T(8,128)(2,1)} %collective-permute-done.4), channel_id=1, source_target_pairs={{0,1},{1,0},{2,3},{3,2},{4,5},{5,4},{6,7},{7,6},{8,9},{9,8},{10,11... | collective-permute-start | bytes 786440 | tf_op jit(solution)/shard_map/ppermute | solution.py:24
  35.4 2.0 %fusion.78 = (bf16[512,256]{1,0:T(8,128)(2,1)S(1)}, f32[512,256]{1,0:T(8,128)}) fusion(f32[64,8,2,128]{3,2,1,0:T(2,128)S(1)} %bitcast.234, f32[512,256]{1,0:T(8,128)S(1)} %fusion.27, bf16[8,256,256]{2,1,0:T(8,128)(2,1)S(1)} %broadcast_select_fusion.3, bf16[1,512,256]{2,1,0:T(8,128)(2,1)} %collective-permute-done.5), kind=kOutput, calls=%fused_computation.152 | convolution fusion | flops 67502080 | bytes 2228224 | tf_op jit(solution)/shard_map/dot_general | solution.py:67
  37.4 3.1 %collective-permute-start.8 = (bf16[512,256]{1,0:T(8,128)(2,1)S(1)}, bf16[512,256]{1,0:T(8,128)(2,1)}, u32[]{:S(2)}, u32[]{:S(2)}) collective-permute-start(bf16[512,256]{1,0:T(8,128)(2,1)S(1)} %get-tuple-element.6), channel_id=1, source_target_pairs={{0,4},{1,5},{2,6},{3,7},{4,0},{5,1},{6,2},{7,3},{8,12},{9,13},{10,... | collective-permute-start | bytes 786440 | tf_op jit(solution)/shard_map/ppermute | solution.py:24
  40.5 1.5 collective-permute-start.7
  43.6 3.5 %all-to-all-start.1 = ((bf16[4,512,256]{2,1,0:T(8,128)(2,1)}), bf16[4,512,256]{2,1,0:T(8,128)(2,1)S(1)}, u32[]{:S(2)}, u32[]{:S(2)}) async-start(bf16[4,512,256]{2,1,0:T(8,128)(2,1)} %broadcast_in_dim.18), calls=%async_computation.1 | async-start | bytes 2097152 | tf_op jit(solution)/shard_map/all_to_all | solution.py:28
  47.4 5.6 %collective-permute-done.8 = bf16[512,256]{1,0:T(8,128)(2,1)} collective-permute-done((bf16[512,256]{1,0:T(8,128)(2,1)S(1)}, bf16[512,256]{1,0:T(8,128)(2,1)}, u32[]{:S(2)}, u32[]{:S(2)}) %collective-permute-start.8) | collective-permute-done | bytes 262176 | tf_op jit(solution)/shard_map/ppermute | solution.py:24
  55.3 1.2 fusion.70
  57.6 2.8 %collective-permute-done.10 = bf16[1,512,256]{2,1,0:T(8,128)(2,1)} collective-permute-done((bf16[1,512,256]{2,1,0:T(8,128)(2,1)}, bf16[1,512,256]{2,1,0:T(8,128)(2,1)}, u32[]{:S(2)}, u32[]{:S(2)}) %collective-permute-start.10) | collective-permute-done | bytes 262176 | tf_op jit(solution)/shard_map/ppermute | solution.py:24
  60.5 1.5 collective-permute-start.11
  63.6 2.0 %fusion.22 = f32[512,256]{1,0:T(8,128)} fusion(f32[512,256]{1,0:T(8,128)S(1)} %fusion.48, f32[512,256]{1,0:T(8,128)S(1)} %fusion.32, f32[512,256]{1,0:T(8,128)S(1)} %fusion.70, f32[512,256]{1,0:T(8,128)S(1)} %fusion.33, f32[512,256]{1,0:T(8,128)S(1)} %convolution_add_fusion.14, bf16[512,256]{1,0:T(8,128)(2,1)} %collective-permute-done.7, ...), kind=kOutput, calls=%fused_computation.40 | convolution fusion | flops 67764224 | bytes 3538944 | tf_op jit(solution)/shard_map/dot_general | solution.py:67
  66.6 1.8 %gather_fusion.1 = bf16[8,256,256]{2,1,0:T(8,128)(2,1)S(1)} fusion(bf16[8,256,256]{2,1,0:T(8,128)(2,1)} %bitcast.238, s32[1024]{0:T(1024)S(1)} %pad_clamp_fusion), kind=kCustom, calls=%fused_computation.1.clone | custom fusion | bytes 2097184 | tf_op jit(solution)/shard_map/jit(_take)/gather | solution.py:61
  70.1 1.2 fusion.58
  72.7 1.2 convolution_add_fusion.11
  74.2 1.3 convolution_add_fusion.9
  75.5 1.2 fusion.29
  77.8 3.6 %all-to-all-start.2 = ((bf16[4,512,256]{2,1,0:T(8,128)(2,1)}), bf16[4,512,256]{2,1,0:T(8,128)(2,1)S(1)}, u32[]{:S(2)}, u32[]{:S(2)}) async-start(bf16[4,512,256]{2,1,0:T(8,128)(2,1)} %broadcast_in_dim.19), calls=%async_computation.2 | async-start | bytes 2097152 | tf_op jit(solution)/shard_map/all_to_all | solution.py:28
  81.3 2.2 %collective-permute-start.14 = (bf16[512,256]{1,0:T(8,128)(2,1)S(1)}, bf16[512,256]{1,0:T(8,128)(2,1)S(1)}, u32[]{:S(2)}, u32[]{:S(2)}) collective-permute-start(bf16[512,256]{1,0:T(8,128)(2,1)S(1)} %fusion.29), channel_id=1, source_target_pairs={{0,4},{1,5},{2,6},{3,7},{4,0},{5,1},{6,2},{7,3},{8,12},{9,13},{10,... | collective-permute-start | bytes 786440 | tf_op jit(solution)/shard_map/ppermute | solution.py:24
  83.5 1.5 collective-permute-start.13
  85.0 10.6 %collective-permute-done.14 = bf16[512,256]{1,0:T(8,128)(2,1)S(1)} collective-permute-done((bf16[512,256]{1,0:T(8,128)(2,1)S(1)}, bf16[512,256]{1,0:T(8,128)(2,1)S(1)}, u32[]{:S(2)}, u32[]{:S(2)}) %collective-permute-start.14) | collective-permute-done | bytes 262176 | tf_op jit(solution)/shard_map/ppermute | solution.py:24
  98.0 4.4 %collective-permute-done.16 = bf16[1,512,256]{2,1,0:T(8,128)(2,1)} collective-permute-done((bf16[1,512,256]{2,1,0:T(8,128)(2,1)S(1)}, bf16[1,512,256]{2,1,0:T(8,128)(2,1)}, u32[]{:S(2)}, u32[]{:S(2)}) %collective-permute-start.16) | collective-permute-done | bytes 262176 | tf_op jit(solution)/shard_map/ppermute | solution.py:24
  102.4 2.0 %collective-permute-start.17 = (bf16[1,512,256]{2,1,0:T(8,128)(2,1)}, bf16[1,512,256]{2,1,0:T(8,128)(2,1)}, u32[]{:S(2)}, u32[]{:S(2)}) collective-permute-start(bf16[1,512,256]{2,1,0:T(8,128)(2,1)} %collective-permute-done.16), channel_id=1, source_target_pairs={{0,1},{1,0},{2,3},{3,2},{4,5},{5,4},{6,7},{7,6},{8,9},{9,8},{10,11... | collective-permute-start | bytes 786440 | tf_op jit(solution)/shard_map/ppermute | solution.py:24
  105.4 1.2 fusion.43
  109.2 1.2 convolution_add_fusion.8
  110.7 2.0 %fusion.79 = (bf16[512,256]{1,0:T(8,128)(2,1)S(1)}, f32[512,256]{1,0:T(8,128)}) fusion(f32[64,8,2,128]{3,2,1,0:T(2,128)S(1)} %bitcast.236, f32[512,256]{1,0:T(8,128)S(1)} %fusion.13, bf16[8,256,256]{2,1,0:T(8,128)(2,1)S(1)} %broadcast_select_fusion.1, bf16[1,512,256]{2,1,0:T(8,128)(2,1)} %collective-permute-done.17), kind=kOutput, calls=%fused_computation.153 | convolution fusion | flops 67502080 | bytes 2228224 | tf_op jit(solution)/shard_map/dot_general | solution.py:67
  112.6 2.5 %collective-permute-start.20 = (bf16[512,256]{1,0:T(8,128)(2,1)S(1)}, bf16[512,256]{1,0:T(8,128)(2,1)}, u32[]{:S(2)}, u32[]{:S(2)}) collective-permute-start(bf16[512,256]{1,0:T(8,128)(2,1)S(1)} %get-tuple-element.8), channel_id=1, source_target_pairs={{0,4},{1,5},{2,6},{3,7},{4,0},{5,1},{6,2},{7,3},{8,12},{9,13},{10,... | collective-permute-start | bytes 786440 | tf_op jit(solution)/shard_map/ppermute | solution.py:24
  115.1 1.5 collective-permute-start.19
  118.2 3.6 %all-to-all-start.3 = ((bf16[4,512,256]{2,1,0:T(8,128)(2,1)}), bf16[4,512,256]{2,1,0:T(8,128)(2,1)S(1)}, u32[]{:S(2)}, u32[]{:S(2)}) async-start(bf16[4,512,256]{2,1,0:T(8,128)(2,1)} %broadcast_in_dim.20), calls=%async_computation.3 | async-start | bytes 2097152 | tf_op jit(solution)/shard_map/all_to_all | solution.py:28
  122.0 5.5 %collective-permute-done.20 = bf16[512,256]{1,0:T(8,128)(2,1)} collective-permute-done((bf16[512,256]{1,0:T(8,128)(2,1)S(1)}, bf16[512,256]{1,0:T(8,128)(2,1)}, u32[]{:S(2)}, u32[]{:S(2)}) %collective-permute-start.20) | collective-permute-done | bytes 262176 | tf_op jit(solution)/shard_map/ppermute | solution.py:24
  128.0 1.9 %pad_maximum_fusion.3 = bf16[2,512,256]{2,1,0:T(8,128)(2,1)} fusion(bf16[1,512,256]{2,1,0:T(8,128)(2,1)} %bitcast.47, bf16[1,512,256]{2,1,0:T(8,128)(2,1)} %bitcast.46), kind=kLoop, calls=%fused_computation.62 | loop fusion | flops 262144 | bytes 1048576 | tf_op jit(solution)/shard_map/stack | solution.py:37
  130.6 2.0 %fusion.74 = f32[512,256]{1,0:T(8,128)} fusion(bf16[512,256]{1,0:T(8,128)(2,1)} %collective-permute-done.20, bf16[8,256,256]{2,1,0:T(8,128)(2,1)S(1)} %broadcast_select_fusion.1), kind=kOutput, calls=%fused_computation.143 | convolution fusion | flops 67108864 | bytes 917504 | tf_op jit(solution)/shard_map/dot_general | solution.py:67
  132.6 2.0 %convolution_add_fusion.5 = f32[512,256]{1,0:T(8,128)} fusion(f32[512,256]{1,0:T(8,128)S(1)} %fusion.72, bf16[512,256]{1,0:T(8,128)(2,1)} %collective-permute-done.18, bf16[8,256,256]{2,1,0:T(8,128)(2,1)S(1)} %broadcast_select_fusion.1), kind=kOutput, calls=%fused_computation.18 | convolution fusion | flops 67239936 | bytes 1441792 | tf_op jit(solution)/shard_map/dot_general | solution.py:67
  134.9 1.6 %collective-permute-start.23 = (bf16[1,512,256]{2,1,0:T(8,128)(2,1)}, bf16[1,512,256]{2,1,0:T(8,128)(2,1)}, u32[]{:S(2)}, u32[]{:S(2)}) collective-permute-start(bf16[1,512,256]{2,1,0:T(8,128)(2,1)} %collective-permute-done.22), channel_id=1, source_target_pairs={{0,1},{1,0},{2,3},{3,2},{4,5},{5,4},{6,7},{7,6},{8,9},{9,8},{10,11... | collective-permute-start | bytes 786440 | tf_op jit(solution)/shard_map/ppermute | solution.py:24
  136.5 2.0 %fusion.37 = f32[512,256]{1,0:T(8,128)} fusion(bf16[1,512,256]{2,1,0:T(8,128)(2,1)} %collective-permute-done.22, bf16[8,256,256]{2,1,0:T(8,128)(2,1)S(1)} %broadcast_select_fusion.1), kind=kOutput, calls=%fused_computation.76 | convolution fusion | flops 67108864 | bytes 917504 | tf_op jit(solution)/shard_map/dot_general | solution.py:67
  139.5 1.8 %gather_fusion.3 = bf16[8,256,256]{2,1,0:T(8,128)(2,1)S(1)} fusion(bf16[8,256,256]{2,1,0:T(8,128)(2,1)} %bitcast.241, s32[1024]{0:T(1024)S(1)} %pad_clamp_fusion), kind=kCustom, calls=%fused_computation.3.clone | custom fusion | bytes 2097184 | tf_op jit(solution)/shard_map/jit(_take)/gather | solution.py:61
  141.7 1.2 fusion.41
  142.9 1.2 fusion.62
  144.4 1.2 fusion.60
  147.9 1.2 convolution_add_fusion.2
  150.5 1.2 fusion.8
  151.7 1.2 convolution_add_fusion
  153.0 2.0 %bitcast_multiply_fusion = f32[512,256]{1,0:T(8,128)} fusion(f32[512,256]{1,0:T(8,128)S(1)} %copy-done.8, f32[64,8,2,128]{3,2,1,0:T(2,128)S(1)} %bitcast.237, f32[512,256]{1,0:T(8,128)S(1)} %convolution_add_fusion, f32[512,256]{1,0:T(8,128)S(1)} %fusion.8, bf16[1,512,256]{2,1,0:T(8,128)(2,1)} %collective-permute-done.23, ...), kind=kOutput, calls=%fused_computation.54 | convolution fusion | flops 67764224 | bytes 3014656 | tf_op jit(solution)/shard_map/dot_general | solution.py:67
  (107 shorter events, 37.3 us)
Async XLA Ops:
  0.0 0.7 copy-start.13
  0.0 1.1 copy-start.12
  2.2 26.9 %all-to-all-start = ((bf16[4,512,256]{2,1,0:T(8,128)(2,1)}), bf16[4,512,256]{2,1,0:T(8,128)(2,1)S(1)}, u32[]{:S(2)}, u32[]{:S(2)}) async-start(bf16[4,512,256]{2,1,0:T(8,128)(2,1)} %broadcast_in_dim.17), calls=%async_computation | async-start | bytes 2097152 | tf_op jit(solution)/shard_map/all_to_all | solution.py:28
  6.5 13.8 %collective-permute-start.2 = (bf16[512,256]{1,0:T(8,128)(2,1)S(1)}, bf16[512,256]{1,0:T(8,128)(2,1)S(1)}, u32[]{:S(2)}, u32[]{:S(2)}) collective-permute-start(bf16[512,256]{1,0:T(8,128)(2,1)S(1)} %fusion.28), channel_id=1, source_target_pairs={{0,4},{1,5},{2,6},{3,7},{4,0},{5,1},{6,2},{7,3},{8,12},{9,13},{10,... | collective-permute-start | bytes 786440 | tf_op jit(solution)/shard_map/ppermute | solution.py:24
  9.0 12.8 %collective-permute-start.1 = (bf16[512,256]{1,0:T(8,128)(2,1)S(1)}, bf16[512,256]{1,0:T(8,128)(2,1)S(1)}, u32[]{:S(2)}, u32[]{:S(2)}) collective-permute-start(bf16[512,256]{1,0:T(8,128)(2,1)S(1)} %fusion.28), channel_id=1, source_target_pairs={{0,2},{1,3},{2,0},{3,1},{4,6},{5,7},{6,4},{7,5},{8,10},{9,11},{10,... | collective-permute-start | bytes 786440 | tf_op jit(solution)/shard_map/ppermute | solution.py:24
  10.3 23.7 %collective-permute-start = (bf16[512,256]{1,0:T(8,128)(2,1)S(1)}, bf16[512,256]{1,0:T(8,128)(2,1)}, u32[]{:S(2)}, u32[]{:S(2)}) collective-permute-start(bf16[512,256]{1,0:T(8,128)(2,1)S(1)} %fusion.28), channel_id=1, source_target_pairs={{0,1},{1,0},{2,3},{3,2},{4,5},{5,4},{6,7},{7,6},{8,9},{9,8},{10,11... | collective-permute-start | bytes 786440 | tf_op jit(solution)/shard_map/ppermute | solution.py:24
  20.3 11.1 %copy-start.2 = (bf16[512,256]{1,0:T(8,128)(2,1)}, bf16[512,256]{1,0:T(8,128)(2,1)S(1)}, u32[]{:S(2)}) copy-start(bf16[512,256]{1,0:T(8,128)(2,1)S(1)} %collective-permute-done.2) | copy-start | bytes 786436
  20.3 6.7 %collective-permute-start.4 = (bf16[1,512,256]{2,1,0:T(8,128)(2,1)S(1)}, bf16[1,512,256]{2,1,0:T(8,128)(2,1)}, u32[]{:S(2)}, u32[]{:S(2)}) collective-permute-start(bf16[1,512,256]{2,1,0:T(8,128)(2,1)S(1)} %bitcast.243), channel_id=1, source_target_pairs={{0,2},{1,3},{2,0},{3,1},{4,6},{5,7},{6,4},{7,5},{8,10},{9,11},{10,... | collective-permute-start | bytes 786440 | tf_op jit(solution)/shard_map/ppermute | solution.py:24
  22.7 8.9 %collective-permute-start.3 = (bf16[2,512,256]{2,1,0:T(8,128)(2,1)}, bf16[2,512,256]{2,1,0:T(8,128)(2,1)}, u32[]{:S(2)}, u32[]{:S(2)}) collective-permute-start(bf16[2,512,256]{2,1,0:T(8,128)(2,1)} %pad_maximum_fusion), channel_id=1, source_target_pairs={{0,1},{1,0},{2,3},{3,2},{4,5},{5,4},{6,7},{7,6},{8,9},{9,8},{10,11... | collective-permute-start | bytes 1572872 | tf_op jit(solution)/shard_map/ppermute | solution.py:24
  27.0 8.4 %collective-permute-start.5 = (bf16[1,512,256]{2,1,0:T(8,128)(2,1)}, bf16[1,512,256]{2,1,0:T(8,128)(2,1)}, u32[]{:S(2)}, u32[]{:S(2)}) collective-permute-start(bf16[1,512,256]{2,1,0:T(8,128)(2,1)} %collective-permute-done.4), channel_id=1, source_target_pairs={{0,1},{1,0},{2,3},{3,2},{4,5},{5,4},{6,7},{7,6},{8,9},{9,8},{10,11... | collective-permute-start | bytes 786440 | tf_op jit(solution)/shard_map/ppermute | solution.py:24
  37.4 15.5 %collective-permute-start.8 = (bf16[512,256]{1,0:T(8,128)(2,1)S(1)}, bf16[512,256]{1,0:T(8,128)(2,1)}, u32[]{:S(2)}, u32[]{:S(2)}) collective-permute-start(bf16[512,256]{1,0:T(8,128)(2,1)S(1)} %get-tuple-element.6), channel_id=1, source_target_pairs={{0,4},{1,5},{2,6},{3,7},{4,0},{5,1},{6,2},{7,3},{8,12},{9,13},{10,... | collective-permute-start | bytes 786440 | tf_op jit(solution)/shard_map/ppermute | solution.py:24
  40.5 12.9 %collective-permute-start.7 = (bf16[512,256]{1,0:T(8,128)(2,1)S(1)}, bf16[512,256]{1,0:T(8,128)(2,1)}, u32[]{:S(2)}, u32[]{:S(2)}) collective-permute-start(bf16[512,256]{1,0:T(8,128)(2,1)S(1)} %get-tuple-element.6), channel_id=1, source_target_pairs={{0,2},{1,3},{2,0},{3,1},{4,6},{5,7},{6,4},{7,5},{8,10},{9,11},{10,... | collective-permute-start | bytes 786440 | tf_op jit(solution)/shard_map/ppermute | solution.py:24
  42.0 14.5 %collective-permute-start.6 = (bf16[512,256]{1,0:T(8,128)(2,1)S(1)}, bf16[512,256]{1,0:T(8,128)(2,1)}, u32[]{:S(2)}, u32[]{:S(2)}) collective-permute-start(bf16[512,256]{1,0:T(8,128)(2,1)S(1)} %get-tuple-element.6), channel_id=1, source_target_pairs={{0,1},{1,0},{2,3},{3,2},{4,5},{5,4},{6,7},{7,6},{8,9},{9,8},{10,11... | collective-permute-start | bytes 786440 | tf_op jit(solution)/shard_map/ppermute | solution.py:24
  43.6 22.0 %all-to-all-start.1 = ((bf16[4,512,256]{2,1,0:T(8,128)(2,1)}), bf16[4,512,256]{2,1,0:T(8,128)(2,1)S(1)}, u32[]{:S(2)}, u32[]{:S(2)}) async-start(bf16[4,512,256]{2,1,0:T(8,128)(2,1)} %broadcast_in_dim.18), calls=%async_computation.1 | async-start | bytes 2097152 | tf_op jit(solution)/shard_map/all_to_all | solution.py:28
  52.9 7.5 %collective-permute-start.10 = (bf16[1,512,256]{2,1,0:T(8,128)(2,1)}, bf16[1,512,256]{2,1,0:T(8,128)(2,1)}, u32[]{:S(2)}, u32[]{:S(2)}) collective-permute-start(bf16[1,512,256]{2,1,0:T(8,128)(2,1)} %bitcast.17), channel_id=1, source_target_pairs={{0,2},{1,3},{2,0},{3,1},{4,6},{5,7},{6,4},{7,5},{8,10},{9,11},{10,... | collective-permute-start | bytes 786440 | tf_op jit(solution)/shard_map/ppermute | solution.py:24
  54.5 8.7 %collective-permute-start.9 = (bf16[2,512,256]{2,1,0:T(8,128)(2,1)S(1)}, bf16[2,512,256]{2,1,0:T(8,128)(2,1)S(1)}, u32[]{:S(2)}, u32[]{:S(2)}) collective-permute-start(bf16[2,512,256]{2,1,0:T(8,128)(2,1)S(1)} %pad_maximum_fusion.1), channel_id=1, source_target_pairs={{0,1},{1,0},{2,3},{3,2},{4,5},{5,4},{6,7},{7,6},{8,9},{9,8},{10,11... | collective-permute-start | bytes 1572872 | tf_op jit(solution)/shard_map/ppermute | solution.py:24
  60.5 15.0 %collective-permute-start.11 = (bf16[1,512,256]{2,1,0:T(8,128)(2,1)}, bf16[1,512,256]{2,1,0:T(8,128)(2,1)}, u32[]{:S(2)}, u32[]{:S(2)}) collective-permute-start(bf16[1,512,256]{2,1,0:T(8,128)(2,1)} %collective-permute-done.10), channel_id=1, source_target_pairs={{0,1},{1,0},{2,3},{3,2},{4,5},{5,4},{6,7},{7,6},{8,9},{9,8},{10,11... | collective-permute-start | bytes 786440 | tf_op jit(solution)/shard_map/ppermute | solution.py:24
  65.6 1.0 copy-start
  70.0 1.2 copy-start.3
  74.1 1.3 copy-start.9
  74.2 1.3 copy-start.11
  77.8 26.6 %all-to-all-start.2 = ((bf16[4,512,256]{2,1,0:T(8,128)(2,1)}), bf16[4,512,256]{2,1,0:T(8,128)(2,1)S(1)}, u32[]{:S(2)}, u32[]{:S(2)}) async-start(bf16[4,512,256]{2,1,0:T(8,128)(2,1)} %broadcast_in_dim.19), calls=%async_computation.2 | async-start | bytes 2097152 | tf_op jit(solution)/shard_map/all_to_all | solution.py:28
  81.3 14.3 %collective-permute-start.14 = (bf16[512,256]{1,0:T(8,128)(2,1)S(1)}, bf16[512,256]{1,0:T(8,128)(2,1)S(1)}, u32[]{:S(2)}, u32[]{:S(2)}) collective-permute-start(bf16[512,256]{1,0:T(8,128)(2,1)S(1)} %fusion.29), channel_id=1, source_target_pairs={{0,4},{1,5},{2,6},{3,7},{4,0},{5,1},{6,2},{7,3},{8,12},{9,13},{10,... | collective-permute-start | bytes 786440 | tf_op jit(solution)/shard_map/ppermute | solution.py:24
  83.5 13.6 %collective-permute-start.13 = (bf16[512,256]{1,0:T(8,128)(2,1)S(1)}, bf16[512,256]{1,0:T(8,128)(2,1)S(1)}, u32[]{:S(2)}, u32[]{:S(2)}) collective-permute-start(bf16[512,256]{1,0:T(8,128)(2,1)S(1)} %fusion.29), channel_id=1, source_target_pairs={{0,2},{1,3},{2,0},{3,1},{4,6},{5,7},{6,4},{7,5},{8,10},{9,11},{10,... | collective-permute-start | bytes 786440 | tf_op jit(solution)/shard_map/ppermute | solution.py:24
  95.6 11.0 %copy-start.4 = (bf16[512,256]{1,0:T(8,128)(2,1)}, bf16[512,256]{1,0:T(8,128)(2,1)S(1)}, u32[]{:S(2)}) copy-start(bf16[512,256]{1,0:T(8,128)(2,1)S(1)} %collective-permute-done.14) | copy-start | bytes 786436
  95.6 6.8 %collective-permute-start.16 = (bf16[1,512,256]{2,1,0:T(8,128)(2,1)S(1)}, bf16[1,512,256]{2,1,0:T(8,128)(2,1)}, u32[]{:S(2)}, u32[]{:S(2)}) collective-permute-start(bf16[1,512,256]{2,1,0:T(8,128)(2,1)S(1)} %bitcast.246), channel_id=1, source_target_pairs={{0,2},{1,3},{2,0},{3,1},{4,6},{5,7},{6,4},{7,5},{8,10},{9,11},{10,... | collective-permute-start | bytes 786440 | tf_op jit(solution)/shard_map/ppermute | solution.py:24
  96.4 12.8 %collective-permute-start.12 = (bf16[512,256]{1,0:T(8,128)(2,1)S(1)}, bf16[512,256]{1,0:T(8,128)(2,1)}, u32[]{:S(2)}, u32[]{:S(2)}) collective-permute-start(bf16[512,256]{1,0:T(8,128)(2,1)S(1)} %fusion.29), channel_id=1, source_target_pairs={{0,1},{1,0},{2,3},{3,2},{4,5},{5,4},{6,7},{7,6},{8,9},{9,8},{10,11... | collective-permute-start | bytes 786440 | tf_op jit(solution)/shard_map/ppermute | solution.py:24
  98.0 8.8 %collective-permute-start.15 = (bf16[2,512,256]{2,1,0:T(8,128)(2,1)}, bf16[2,512,256]{2,1,0:T(8,128)(2,1)}, u32[]{:S(2)}, u32[]{:S(2)}) collective-permute-start(bf16[2,512,256]{2,1,0:T(8,128)(2,1)} %pad_maximum_fusion.2), channel_id=1, source_target_pairs={{0,1},{1,0},{2,3},{3,2},{4,5},{5,4},{6,7},{7,6},{8,9},{9,8},{10,11... | collective-permute-start | bytes 1572872 | tf_op jit(solution)/shard_map/ppermute | solution.py:24
  102.4 8.3 %collective-permute-start.17 = (bf16[1,512,256]{2,1,0:T(8,128)(2,1)}, bf16[1,512,256]{2,1,0:T(8,128)(2,1)}, u32[]{:S(2)}, u32[]{:S(2)}) collective-permute-start(bf16[1,512,256]{2,1,0:T(8,128)(2,1)} %collective-permute-done.16), channel_id=1, source_target_pairs={{0,1},{1,0},{2,3},{3,2},{4,5},{5,4},{6,7},{7,6},{8,9},{9,8},{10,11... | collective-permute-start | bytes 786440 | tf_op jit(solution)/shard_map/ppermute | solution.py:24
  112.6 14.8 %collective-permute-start.20 = (bf16[512,256]{1,0:T(8,128)(2,1)S(1)}, bf16[512,256]{1,0:T(8,128)(2,1)}, u32[]{:S(2)}, u32[]{:S(2)}) collective-permute-start(bf16[512,256]{1,0:T(8,128)(2,1)S(1)} %get-tuple-element.8), channel_id=1, source_target_pairs={{0,4},{1,5},{2,6},{3,7},{4,0},{5,1},{6,2},{7,3},{8,12},{9,13},{10,... | collective-permute-start | bytes 786440 | tf_op jit(solution)/shard_map/ppermute | solution.py:24
  115.1 12.9 %collective-permute-start.19 = (bf16[512,256]{1,0:T(8,128)(2,1)S(1)}, bf16[512,256]{1,0:T(8,128)(2,1)}, u32[]{:S(2)}, u32[]{:S(2)}) collective-permute-start(bf16[512,256]{1,0:T(8,128)(2,1)S(1)} %get-tuple-element.8), channel_id=1, source_target_pairs={{0,2},{1,3},{2,0},{3,1},{4,6},{5,7},{6,4},{7,5},{8,10},{9,11},{10,... | collective-permute-start | bytes 786440 | tf_op jit(solution)/shard_map/ppermute | solution.py:24
  116.6 16.0 %collective-permute-start.18 = (bf16[512,256]{1,0:T(8,128)(2,1)S(1)}, bf16[512,256]{1,0:T(8,128)(2,1)}, u32[]{:S(2)}, u32[]{:S(2)}) collective-permute-start(bf16[512,256]{1,0:T(8,128)(2,1)S(1)} %get-tuple-element.8), channel_id=1, source_target_pairs={{0,1},{1,0},{2,3},{3,2},{4,5},{5,4},{6,7},{7,6},{8,9},{9,8},{10,11... | collective-permute-start | bytes 786440 | tf_op jit(solution)/shard_map/ppermute | solution.py:24
  118.2 20.3 %all-to-all-start.3 = ((bf16[4,512,256]{2,1,0:T(8,128)(2,1)}), bf16[4,512,256]{2,1,0:T(8,128)(2,1)S(1)}, u32[]{:S(2)}, u32[]{:S(2)}) async-start(bf16[4,512,256]{2,1,0:T(8,128)(2,1)} %broadcast_in_dim.20), calls=%async_computation.3 | async-start | bytes 2097152 | tf_op jit(solution)/shard_map/all_to_all | solution.py:28
  127.5 7.4 %collective-permute-start.22 = (bf16[1,512,256]{2,1,0:T(8,128)(2,1)}, bf16[1,512,256]{2,1,0:T(8,128)(2,1)}, u32[]{:S(2)}, u32[]{:S(2)}) collective-permute-start(bf16[1,512,256]{2,1,0:T(8,128)(2,1)} %bitcast.47), channel_id=1, source_target_pairs={{0,2},{1,3},{2,0},{3,1},{4,6},{5,7},{6,4},{7,5},{8,10},{9,11},{10,... | collective-permute-start | bytes 786440 | tf_op jit(solution)/shard_map/ppermute | solution.py:24
  129.9 15.7 %collective-permute-start.21 = (bf16[2,512,256]{2,1,0:T(8,128)(2,1)}, bf16[2,512,256]{2,1,0:T(8,128)(2,1)}, u32[]{:S(2)}, u32[]{:S(2)}) collective-permute-start(bf16[2,512,256]{2,1,0:T(8,128)(2,1)} %pad_maximum_fusion.3), channel_id=1, source_target_pairs={{0,1},{1,0},{2,3},{3,2},{4,5},{5,4},{6,7},{7,6},{8,9},{9,8},{10,11... | collective-permute-start | bytes 1572872 | tf_op jit(solution)/shard_map/ppermute | solution.py:24
  134.9 18.0 %collective-permute-start.23 = (bf16[1,512,256]{2,1,0:T(8,128)(2,1)}, bf16[1,512,256]{2,1,0:T(8,128)(2,1)}, u32[]{:S(2)}, u32[]{:S(2)}) collective-permute-start(bf16[1,512,256]{2,1,0:T(8,128)(2,1)} %collective-permute-done.22), channel_id=1, source_target_pairs={{0,1},{1,0},{2,3},{3,2},{4,5},{5,4},{6,7},{7,6},{8,9},{9,8},{10,11... | collective-permute-start | bytes 786440 | tf_op jit(solution)/shard_map/ppermute | solution.py:24
  138.5 1.0 copy-start.1
  142.9 1.2 copy-start.5
  149.1 1.0 copy-start.6
  149.1 1.2 copy-start.7
  149.1 1.3 copy-start.10
  151.7 1.3 copy-start.8

commit v6 on v4

--- a/solution.py
+++ b/solution.py
@@ -25,15 +25,14 @@
 
 
 def exchange(xb, n_row, n_col):
-    col_pieces = [xb] + [xor_permute(xb, "row", n_row, t) for t in range(1, n_row)]
     chips = n_col // 2
     same = {0: xb}
-    for s in [1] + list(range(2, chips, 2)):
+    for s in sorted(range(2, chips, 2), reverse=True) + [1]:
         same[s] = xor_permute(xb, "col", n_col, 2 * s)
-    partner_own = xor_permute(xb, "col", n_col, 1)
-    first = sorted(s for s in same if s != 0)
+    col_pieces = [xb] + [xor_permute(xb, "row", n_row, t) for t in range(1, n_row)]
+    first = sorted(same)
     relay_first = xor_permute(jnp.stack([same[s] for s in first]), "col", n_col, 1)
-    other = {0: partner_own}
+    other = {}
     for i, s in enumerate(first):
         other[s] = relay_first[i]
     forward = list(range(2, chips, 2))

time: 125 us -> 124 us (level)
  matrix products: 34.5 us -> 28.5 us
  waiting for transfers between devices: 37.7 us -> 43.1 us
  other arithmetic: 8.29 us -> 6.66 us
    dot_general x48, matrix products: 34.5 us -> 28.5 us  [contract(): part = jnp.dot(piece, k_blocks[s], preferred_element_type=jnp.float32)]
    ppermute x36 -> x32, waiting for transfers between devices: 37.7 us -> 43.1 us  [xor_permute(): return lax.ppermute(x, axis, perm=[(i, i ^ s) for i in range(size)])]
    another operation x4, other arithmetic: 4.41 us -> 2.52 us  [exchange(): return (row_pieces, jnp.stack(col_pieces))]
    unnamed x25 -> x33, local copies, waits for them, and re-layouts: 2.49 us -> 3.57 us
    ppermute x36 -> x32, starting transfers between devices: 35.3 us -> 35.3 us  [xor_permute(): return lax.ppermute(x, axis, perm=[(i, i ^ s) for i in range(size)])]
  transfers between devices with their start and end apart: 36 -> 32, of which waited for: 10 -> 11; matrix products, arithmetic and copies ran while one was open for 35% -> 30% of each run, Pallas kernels for 0% -> 0%
where the time goes in v6:
time: 124 us; the launch traced here: 123 us
  waiting for transfers between devices  43.1 us (35%)
  starting transfers between devices  35.3 us (28%)
  matrix products  28.5 us (23%)
  local copies, waits for them, and re-layouts  8.68 us (7%)
  other arithmetic  6.66 us (5%)
    ppermute x32, waiting for transfers between devices, xor_permute(): return lax.ppermute(x, axis, perm=[(i, i ^ s) for i in range(size)])  43.1 us
    ppermute x32, starting transfers between devices, xor_permute(): return lax.ppermute(x, axis, perm=[(i, i ^ s) for i in range(size)])  35.3 us
    dot_general x48, matrix products, contract(): part = jnp.dot(piece, k_blocks[s], preferred_element_type=jnp.float32)  28.5 us
    gather x4, local copies, waits for them, and re-layouts, ordered_k_blocks(): return jnp.take(split, index, axis=0)  4.9 us
    unnamed x33, local copies, waits for them, and re-layouts  3.57 us
    another operation x4, other arithmetic, exchange(): jnp.stack([same[s] for s in first])  3.31 us
    another operation x4, other arithmetic, exchange(): return (row_pieces, jnp.stack(col_pieces))  2.52 us
  transfers between devices with their start and end apart: 32, of which 11 were waited for; matrix products, arithmetic and copies ran while one was open for 30% of the time, Pallas kernels for 0%

profile of v6, /device:TPU:1, one launch (start us, length us, event | category | flops | bytes accessed | tf_op | source)
XLA Modules:
  0.0 123.0 jit_solution(9782014817749061599)
XLA Ops:
  1.2 3.2 %collective-permute-start.4 = (bf16[512,256]{1,0:T(8,128)(2,1)S(1)}, bf16[512,256]{1,0:T(8,128)(2,1)S(1)}, u32[]{:S(2)}, u32[]{:S(2)}) collective-permute-start(bf16[512,256]{1,0:T(8,128)(2,1)S(1)} %fusion.28), channel_id=1, source_target_pairs={{0,4},{1,5},{2,6},{3,7},{4,0},{5,1},{6,2},{7,3},{8,12},{9,13},{10,... | collective-permute-start | bytes 786440 | tf_op jit(solution)/shard_map/ppermute | solution.py:24
  4.4 1.3 %collective-permute-start.3 = (bf16[512,256]{1,0:T(8,128)(2,1)S(1)}, bf16[512,256]{1,0:T(8,128)(2,1)S(1)}, u32[]{:S(2)}, u32[]{:S(2)}) collective-permute-start(bf16[512,256]{1,0:T(8,128)(2,1)S(1)} %fusion.28), channel_id=1, source_target_pairs={{0,2},{1,3},{2,0},{3,1},{4,6},{5,7},{6,4},{7,5},{8,10},{9,11},{10,... | collective-permute-start | bytes 786440 | tf_op jit(solution)/shard_map/ppermute | solution.py:24
  5.7 2.2 %collective-permute-start.2 = (bf16[512,256]{1,0:T(8,128)(2,1)S(1)}, bf16[512,256]{1,0:T(8,128)(2,1)S(1)}, u32[]{:S(2)}, u32[]{:S(2)}) collective-permute-start(bf16[512,256]{1,0:T(8,128)(2,1)S(1)} %fusion.28), channel_id=1, source_target_pairs={{0,24},{8,16},{16,8},{24,0},{1,25},{9,17},{17,9},{25,1},{2,26},{10... | collective-permute-start | bytes 786440 | tf_op jit(solution)/shard_map/ppermute | solution.py:24
  8.3 7.7 %collective-permute-done.4 = bf16[512,256]{1,0:T(8,128)(2,1)S(1)} collective-permute-done((bf16[512,256]{1,0:T(8,128)(2,1)S(1)}, bf16[512,256]{1,0:T(8,128)(2,1)S(1)}, u32[]{:S(2)}, u32[]{:S(2)}) %collective-permute-start.4) | collective-permute-done | bytes 262176 | tf_op jit(solution)/shard_map/ppermute | solution.py:24
  16.1 1.1 collective-permute-start.6
  19.0 1.4 %collective-permute-done.1 = bf16[512,256]{1,0:T(8,128)(2,1)S(1)} collective-permute-done((bf16[512,256]{1,0:T(8,128)(2,1)S(1)}, bf16[512,256]{1,0:T(8,128)(2,1)S(1)}, u32[]{:S(2)}, u32[]{:S(2)}) %collective-permute-start.1) | collective-permute-done | bytes 262176 | tf_op jit(solution)/shard_map/ppermute | solution.py:24
  22.7 2.2 %collective-permute-start.7 = (bf16[1,512,256]{2,1,0:T(8,128)(2,1)}, bf16[1,512,256]{2,1,0:T(8,128)(2,1)S(1)}, u32[]{:S(2)}, u32[]{:S(2)}) collective-permute-start(bf16[1,512,256]{2,1,0:T(8,128)(2,1)} %collective-permute-done.6), channel_id=1, source_target_pairs={{0,1},{1,0},{2,3},{3,2},{4,5},{5,4},{6,7},{7,6},{8,9},{9,8},{10,11... | collective-permute-start | bytes 786440 | tf_op jit(solution)/shard_map/ppermute | solution.py:24
  24.9 1.2 fusion.54
  26.1 1.2 fusion.59
  27.2 1.2 fusion.57
  28.4 1.2 convolution_add_fusion.17
  30.9 1.9 %collective-permute-start.15 = (bf16[512,256]{1,0:T(8,128)(2,1)S(1)}, bf16[512,256]{1,0:T(8,128)(2,1)S(1)}, u32[]{:S(2)}, u32[]{:S(2)}) collective-permute-start(bf16[512,256]{1,0:T(8,128)(2,1)S(1)} %get-tuple-element.8), channel_id=1, source_target_pairs={{0,24},{8,16},{16,8},{24,0},{1,25},{9,17},{17,9},{25,1},{2,26},{10... | collective-permute-start | bytes 786440 | tf_op jit(solution)/shard_map/ppermute | solution.py:24
  33.6 2.8 %collective-permute-start.9 = (bf16[512,256]{1,0:T(8,128)(2,1)S(1)}, bf16[512,256]{1,0:T(8,128)(2,1)}, u32[]{:S(2)}, u32[]{:S(2)}) collective-permute-start(bf16[512,256]{1,0:T(8,128)(2,1)S(1)} %get-tuple-element.8), channel_id=1, source_target_pairs={{0,4},{1,5},{2,6},{3,7},{4,0},{5,1},{6,2},{7,3},{8,12},{9,13},{10,... | collective-permute-start | bytes 786440 | tf_op jit(solution)/shard_map/ppermute | solution.py:24
  36.3 1.5 %collective-permute-start.8 = (bf16[512,256]{1,0:T(8,128)(2,1)S(1)}, bf16[512,256]{1,0:T(8,128)(2,1)}, u32[]{:S(2)}, u32[]{:S(2)}) collective-permute-start(bf16[512,256]{1,0:T(8,128)(2,1)S(1)} %get-tuple-element.8), channel_id=1, source_target_pairs={{0,2},{1,3},{2,0},{3,1},{4,6},{5,7},{6,4},{7,5},{8,10},{9,11},{10,... | collective-permute-start | bytes 786440 | tf_op jit(solution)/shard_map/ppermute | solution.py:24
  38.8 1.1 collective-permute-done.15
  39.9 5.9 %collective-permute-done.14 = bf16[512,256]{1,0:T(8,128)(2,1)S(1)} collective-permute-done((bf16[512,256]{1,0:T(8,128)(2,1)S(1)}, bf16[512,256]{1,0:T(8,128)(2,1)S(1)}, u32[]{:S(2)}, u32[]{:S(2)}) %collective-permute-start.14) | collective-permute-done | bytes 262176 | tf_op jit(solution)/shard_map/ppermute | solution.py:24
  45.8 1.1 pad_maximum_fusion.1
  46.9 1.8 %gather_fusion.1 = bf16[8,256,256]{2,1,0:T(8,128)(2,1)S(1)} fusion(bf16[8,256,256]{2,1,0:T(8,128)(2,1)} %bitcast.268, s32[1024]{0:T(1024)S(1)} %pad_clamp_fusion), kind=kCustom, calls=%fused_computation.1.clone | custom fusion | bytes 2097184 | tf_op jit(solution)/shard_map/jit(_take)/gather | solution.py:59
  49.0 1.2 collective-permute-start.11
  50.4 1.1 pad_maximum_fusion.5
  52.3 1.2 fusion.52
  53.5 1.2 fusion.58
  55.0 1.2 fusion.56
  56.1 1.2 convolution_add_fusion.11
  57.6 1.2 fusion.70
  60.9 1.3 %fusion.22 = f32[512,256]{1,0:T(8,128)S(1)} fusion(f32[512,256]{1,0:T(8,128)S(1)} %fusion.48, f32[512,256]{1,0:T(8,128)S(1)} %fusion.32, f32[512,256]{1,0:T(8,128)S(1)} %fusion.70, f32[512,256]{1,0:T(8,128)S(1)} %fusion.33, f32[512,256]{1,0:T(8,128)S(1)} %convolution_add_fusion.14, bf16[512,256]{1,0:T(8,128)(2,1)} %collective-permute-done.8, ...), kind=kOutput, calls=%fused_computation.40 | convolution fusion | flops 67764224 | bytes 3538944 | tf_op jit(solution)/shard_map/dot_general | solution.py:65
  62.5 3.2 %collective-permute-start.20 = (bf16[512,256]{1,0:T(8,128)(2,1)S(1)}, bf16[512,256]{1,0:T(8,128)(2,1)S(1)}, u32[]{:S(2)}, u32[]{:S(2)}) collective-permute-start(bf16[512,256]{1,0:T(8,128)(2,1)S(1)} %fusion.29), channel_id=1, source_target_pairs={{0,4},{1,5},{2,6},{3,7},{4,0},{5,1},{6,2},{7,3},{8,12},{9,13},{10,... | collective-permute-start | bytes 786440 | tf_op jit(solution)/shard_map/ppermute | solution.py:24
  65.6 1.4 %collective-permute-start.18 = (bf16[512,256]{1,0:T(8,128)(2,1)S(1)}, bf16[512,256]{1,0:T(8,128)(2,1)S(1)}, u32[]{:S(2)}, u32[]{:S(2)}) collective-permute-start(bf16[512,256]{1,0:T(8,128)(2,1)S(1)} %fusion.29), channel_id=1, source_target_pairs={{0,24},{8,16},{16,8},{24,0},{1,25},{9,17},{17,9},{25,1},{2,26},{10... | collective-permute-start | bytes 786440 | tf_op jit(solution)/shard_map/ppermute | solution.py:24
  67.0 1.0 collective-permute-start.17
  68.3 9.5 %collective-permute-done.20 = bf16[512,256]{1,0:T(8,128)(2,1)S(1)} collective-permute-done((bf16[512,256]{1,0:T(8,128)(2,1)S(1)}, bf16[512,256]{1,0:T(8,128)(2,1)S(1)}, u32[]{:S(2)}, u32[]{:S(2)}) %collective-permute-start.20) | collective-permute-done | bytes 262176 | tf_op jit(solution)/shard_map/ppermute | solution.py:24
  77.8 2.6 %collective-permute-done.17 = bf16[512,256]{1,0:T(8,128)(2,1)S(1)} collective-permute-done((bf16[512,256]{1,0:T(8,128)(2,1)S(1)}, bf16[512,256]{1,0:T(8,128)(2,1)S(1)}, u32[]{:S(2)}, u32[]{:S(2)}) %collective-permute-start.17) | collective-permute-done | bytes 262176 | tf_op jit(solution)/shard_map/ppermute | solution.py:24
  81.3 2.9 %collective-permute-start.21 = (bf16[3,512,256]{2,1,0:T(8,128)(2,1)S(1)}, bf16[3,512,256]{2,1,0:T(8,128)(2,1)S(1)}, u32[]{:S(2)}, u32[]{:S(2)}) collective-permute-start(bf16[3,512,256]{2,1,0:T(8,128)(2,1)S(1)} %pad_maximum_fusion.6), channel_id=1, source_target_pairs={{0,1},{1,0},{2,3},{3,2},{4,5},{5,4},{6,7},{7,6},{8,9},{9,8},{10,11... | collective-permute-start | bytes 2359304 | tf_op jit(solution)/shard_map/ppermute | solution.py:24
  84.8 1.6 %collective-permute-done.22 = bf16[1,512,256]{2,1,0:T(8,128)(2,1)} collective-permute-done((bf16[1,512,256]{2,1,0:T(8,128)(2,1)S(1)}, bf16[1,512,256]{2,1,0:T(8,128)(2,1)}, u32[]{:S(2)}, u32[]{:S(2)}) %collective-permute-start.22) | collective-permute-done | bytes 262176 | tf_op jit(solution)/shard_map/ppermute | solution.py:24
  86.4 1.9 %collective-permute-start.23 = (bf16[1,512,256]{2,1,0:T(8,128)(2,1)}, bf16[1,512,256]{2,1,0:T(8,128)(2,1)S(1)}, u32[]{:S(2)}, u32[]{:S(2)}) collective-permute-start(bf16[1,512,256]{2,1,0:T(8,128)(2,1)} %collective-permute-done.22), channel_id=1, source_target_pairs={{0,1},{1,0},{2,3},{3,2},{4,5},{5,4},{6,7},{7,6},{8,9},{9,8},{10,11... | collective-permute-start | bytes 786440 | tf_op jit(solution)/shard_map/ppermute | solution.py:24
  88.2 1.2 fusion.43
  91.9 1.3 %collective-permute-start.31 = (bf16[512,256]{1,0:T(8,128)(2,1)S(1)}, bf16[512,256]{1,0:T(8,128)(2,1)S(1)}, u32[]{:S(2)}, u32[]{:S(2)}) collective-permute-start(bf16[512,256]{1,0:T(8,128)(2,1)S(1)} %get-tuple-element.10), channel_id=1, source_target_pairs={{0,24},{8,16},{16,8},{24,0},{1,25},{9,17},{17,9},{25,1},{2,26},{10... | collective-permute-start | bytes 786440 | tf_op jit(solution)/shard_map/ppermute | solution.py:24
  93.2 1.1 collective-permute-start.30
  95.7 5.1 %collective-permute-done.31 = bf16[512,256]{1,0:T(8,128)(2,1)S(1)} collective-permute-done((bf16[512,256]{1,0:T(8,128)(2,1)S(1)}, bf16[512,256]{1,0:T(8,128)(2,1)S(1)}, u32[]{:S(2)}, u32[]{:S(2)}) %collective-permute-start.31) | collective-permute-done | bytes 262176 | tf_op jit(solution)/shard_map/ppermute | solution.py:24
  100.8 6.0 %collective-permute-done.30 = bf16[512,256]{1,0:T(8,128)(2,1)S(1)} collective-permute-done((bf16[512,256]{1,0:T(8,128)(2,1)S(1)}, bf16[512,256]{1,0:T(8,128)(2,1)S(1)}, u32[]{:S(2)}, u32[]{:S(2)}) %collective-permute-start.30) | collective-permute-done | bytes 262176 | tf_op jit(solution)/shard_map/ppermute | solution.py:24
  106.8 1.1 pad_maximum_fusion.3
  107.9 1.8 %gather_fusion.3 = bf16[8,256,256]{2,1,0:T(8,128)(2,1)S(1)} fusion(bf16[8,256,256]{2,1,0:T(8,128)(2,1)} %bitcast.266, s32[1024]{0:T(1024)S(1)} %pad_clamp_fusion), kind=kCustom, calls=%fused_computation.3.clone | custom fusion | bytes 2097184 | tf_op jit(solution)/shard_map/jit(_take)/gather | solution.py:59
  110.2 1.1 pad_maximum_fusion.7
  111.8 1.2 fusion.41
  114.9 1.2 fusion.74
  116.4 1.4 %collective-permute-done.27 = bf16[1,512,256]{2,1,0:T(8,128)(2,1)S(1)} collective-permute-done((bf16[1,512,256]{2,1,0:T(8,128)(2,1)}, bf16[1,512,256]{2,1,0:T(8,128)(2,1)S(1)}, u32[]{:S(2)}, u32[]{:S(2)}) %collective-permute-start.27) | collective-permute-done | bytes 262176 | tf_op jit(solution)/shard_map/ppermute | solution.py:24
  117.7 1.2 collective-permute-start.28
  120.7 1.3 %fusion.8 = f32[512,256]{1,0:T(8,128)S(1)} fusion(f32[512,256]{1,0:T(8,128)S(1)} %fusion.37, f32[512,256]{1,0:T(8,128)S(1)} %fusion.30, f32[512,256]{1,0:T(8,128)S(1)} %fusion.74, f32[512,256]{1,0:T(8,128)S(1)} %fusion.31, f32[512,256]{1,0:T(8,128)S(1)} %convolution_add_fusion.5, bf16[512,256]{1,0:T(8,128)(2,1)} %collective-permute-done.24, ...), kind=kOutput, calls=%fused_computation.17 | convolution fusion | flops 67764224 | bytes 3538944 | tf_op jit(solution)/shard_map/dot_general | solution.py:65
  122.0 1.0 bitcast_multiply_fusion
  (118 shorter events, 22.9 us)
Async XLA Ops:
  0.0 0.7 copy-start.15
  0.0 1.1 copy-start.14
  1.2 14.9 %collective-permute-start.4 = (bf16[512,256]{1,0:T(8,128)(2,1)S(1)}, bf16[512,256]{1,0:T(8,128)(2,1)S(1)}, u32[]{:S(2)}, u32[]{:S(2)}) collective-permute-start(bf16[512,256]{1,0:T(8,128)(2,1)S(1)} %fusion.28), channel_id=1, source_target_pairs={{0,4},{1,5},{2,6},{3,7},{4,0},{5,1},{6,2},{7,3},{8,12},{9,13},{10,... | collective-permute-start | bytes 786440 | tf_op jit(solution)/shard_map/ppermute | solution.py:24
  4.4 12.8 %collective-permute-start.3 = (bf16[512,256]{1,0:T(8,128)(2,1)S(1)}, bf16[512,256]{1,0:T(8,128)(2,1)S(1)}, u32[]{:S(2)}, u32[]{:S(2)}) collective-permute-start(bf16[512,256]{1,0:T(8,128)(2,1)S(1)} %fusion.28), channel_id=1, source_target_pairs={{0,2},{1,3},{2,0},{3,1},{4,6},{5,7},{6,4},{7,5},{8,10},{9,11},{10,... | collective-permute-start | bytes 786440 | tf_op jit(solution)/shard_map/ppermute | solution.py:24
  5.7 13.3 %collective-permute-start.2 = (bf16[512,256]{1,0:T(8,128)(2,1)S(1)}, bf16[512,256]{1,0:T(8,128)(2,1)S(1)}, u32[]{:S(2)}, u32[]{:S(2)}) collective-permute-start(bf16[512,256]{1,0:T(8,128)(2,1)S(1)} %fusion.28), channel_id=1, source_target_pairs={{0,24},{8,16},{16,8},{24,0},{1,25},{9,17},{17,9},{25,1},{2,26},{10... | collective-permute-start | bytes 786440 | tf_op jit(solution)/shard_map/ppermute | solution.py:24
  7.8 12.6 %collective-permute-start.1 = (bf16[512,256]{1,0:T(8,128)(2,1)S(1)}, bf16[512,256]{1,0:T(8,128)(2,1)S(1)}, u32[]{:S(2)}, u32[]{:S(2)}) collective-permute-start(bf16[512,256]{1,0:T(8,128)(2,1)S(1)} %fusion.28), channel_id=1, source_target_pairs={{0,16},{8,24},{16,0},{24,8},{1,17},{9,25},{17,1},{25,9},{2,18},{10... | collective-permute-start | bytes 786440 | tf_op jit(solution)/shard_map/ppermute | solution.py:24
  8.0 12.4 %collective-permute-start = (bf16[512,256]{1,0:T(8,128)(2,1)S(1)}, bf16[512,256]{1,0:T(8,128)(2,1)S(1)}, u32[]{:S(2)}, u32[]{:S(2)}) collective-permute-start(bf16[512,256]{1,0:T(8,128)(2,1)S(1)} %fusion.28), channel_id=1, source_target_pairs={{0,8},{8,0},{16,24},{24,16},{1,9},{9,1},{17,25},{25,17},{2,10},{10... | collective-permute-start | bytes 786440 | tf_op jit(solution)/shard_map/ppermute | solution.py:24
  16.1 5.5 %copy-start.2 = (bf16[512,256]{1,0:T(8,128)(2,1)}, bf16[512,256]{1,0:T(8,128)(2,1)S(1)}, u32[]{:S(2)}) copy-start(bf16[512,256]{1,0:T(8,128)(2,1)S(1)} %collective-permute-done.4) | copy-start | bytes 786436
  16.1 6.6 %collective-permute-start.6 = (bf16[1,512,256]{2,1,0:T(8,128)(2,1)S(1)}, bf16[1,512,256]{2,1,0:T(8,128)(2,1)}, u32[]{:S(2)}, u32[]{:S(2)}) collective-permute-start(bf16[1,512,256]{2,1,0:T(8,128)(2,1)S(1)} %bitcast.275), channel_id=1, source_target_pairs={{0,2},{1,3},{2,0},{3,1},{4,6},{5,7},{6,4},{7,5},{8,10},{9,11},{10,... | collective-permute-start | bytes 786440 | tf_op jit(solution)/shard_map/ppermute | solution.py:24
  18.2 7.9 %collective-permute-start.5 = (bf16[3,512,256]{2,1,0:T(8,128)(2,1)}, bf16[3,512,256]{2,1,0:T(8,128)(2,1)}, u32[]{:S(2)}, u32[]{:S(2)}) collective-permute-start(bf16[3,512,256]{2,1,0:T(8,128)(2,1)} %pad_maximum_fusion.4), channel_id=1, source_target_pairs={{0,1},{1,0},{2,3},{3,2},{4,5},{5,4},{6,7},{7,6},{8,9},{9,8},{10,11... | collective-permute-start | bytes 2359304 | tf_op jit(solution)/shard_map/ppermute | solution.py:24
  22.7 7.2 %collective-permute-start.7 = (bf16[1,512,256]{2,1,0:T(8,128)(2,1)}, bf16[1,512,256]{2,1,0:T(8,128)(2,1)S(1)}, u32[]{:S(2)}, u32[]{:S(2)}) collective-permute-start(bf16[1,512,256]{2,1,0:T(8,128)(2,1)} %collective-permute-done.6), channel_id=1, source_target_pairs={{0,1},{1,0},{2,3},{3,2},{4,5},{5,4},{6,7},{7,6},{8,9},{9,8},{10,11... | collective-permute-start | bytes 786440 | tf_op jit(solution)/shard_map/ppermute | solution.py:24
  29.9 1.0 copy-start.12
  30.9 9.0 %collective-permute-start.15 = (bf16[512,256]{1,0:T(8,128)(2,1)S(1)}, bf16[512,256]{1,0:T(8,128)(2,1)S(1)}, u32[]{:S(2)}, u32[]{:S(2)}) collective-permute-start(bf16[512,256]{1,0:T(8,128)(2,1)S(1)} %get-tuple-element.8), channel_id=1, source_target_pairs={{0,24},{8,16},{16,8},{24,0},{1,25},{9,17},{17,9},{25,1},{2,26},{10... | collective-permute-start | bytes 786440 | tf_op jit(solution)/shard_map/ppermute | solution.py:24
  32.8 13.0 %collective-permute-start.14 = (bf16[512,256]{1,0:T(8,128)(2,1)S(1)}, bf16[512,256]{1,0:T(8,128)(2,1)S(1)}, u32[]{:S(2)}, u32[]{:S(2)}) collective-permute-start(bf16[512,256]{1,0:T(8,128)(2,1)S(1)} %get-tuple-element.8), channel_id=1, source_target_pairs={{0,16},{8,24},{16,0},{24,8},{1,17},{9,25},{17,1},{25,9},{2,18},{10... | collective-permute-start | bytes 786440 | tf_op jit(solution)/shard_map/ppermute | solution.py:24
  33.1 12.7 %collective-permute-start.13 = (bf16[512,256]{1,0:T(8,128)(2,1)S(1)}, bf16[512,256]{1,0:T(8,128)(2,1)S(1)}, u32[]{:S(2)}, u32[]{:S(2)}) collective-permute-start(bf16[512,256]{1,0:T(8,128)(2,1)S(1)} %get-tuple-element.8), channel_id=1, source_target_pairs={{0,8},{8,0},{16,24},{24,16},{1,9},{9,1},{17,25},{25,17},{2,10},{10... | collective-permute-start | bytes 786440 | tf_op jit(solution)/shard_map/ppermute | solution.py:24
  33.6 15.4 %collective-permute-start.9 = (bf16[512,256]{1,0:T(8,128)(2,1)S(1)}, bf16[512,256]{1,0:T(8,128)(2,1)}, u32[]{:S(2)}, u32[]{:S(2)}) collective-permute-start(bf16[512,256]{1,0:T(8,128)(2,1)S(1)} %get-tuple-element.8), channel_id=1, source_target_pairs={{0,4},{1,5},{2,6},{3,7},{4,0},{5,1},{6,2},{7,3},{8,12},{9,13},{10,... | collective-permute-start | bytes 786440 | tf_op jit(solution)/shard_map/ppermute | solution.py:24
  36.3 14.0 %collective-permute-start.8 = (bf16[512,256]{1,0:T(8,128)(2,1)S(1)}, bf16[512,256]{1,0:T(8,128)(2,1)}, u32[]{:S(2)}, u32[]{:S(2)}) collective-permute-start(bf16[512,256]{1,0:T(8,128)(2,1)S(1)} %get-tuple-element.8), channel_id=1, source_target_pairs={{0,2},{1,3},{2,0},{3,1},{4,6},{5,7},{6,4},{7,5},{8,10},{9,11},{10,... | collective-permute-start | bytes 786440 | tf_op jit(solution)/shard_map/ppermute | solution.py:24
  49.0 10.1 %collective-permute-start.11 = (bf16[1,512,256]{2,1,0:T(8,128)(2,1)}, bf16[1,512,256]{2,1,0:T(8,128)(2,1)S(1)}, u32[]{:S(2)}, u32[]{:S(2)}) collective-permute-start(bf16[1,512,256]{2,1,0:T(8,128)(2,1)} %bitcast.23), channel_id=1, source_target_pairs={{0,2},{1,3},{2,0},{3,1},{4,6},{5,7},{6,4},{7,5},{8,10},{9,11},{10,... | collective-permute-start | bytes 786440 | tf_op jit(solution)/shard_map/ppermute | solution.py:24
  51.5 7.9 %collective-permute-start.10 = (bf16[3,512,256]{2,1,0:T(8,128)(2,1)S(1)}, bf16[3,512,256]{2,1,0:T(8,128)(2,1)S(1)}, u32[]{:S(2)}, u32[]{:S(2)}) collective-permute-start(bf16[3,512,256]{2,1,0:T(8,128)(2,1)S(1)} %pad_maximum_fusion.5), channel_id=1, source_target_pairs={{0,1},{1,0},{2,3},{3,2},{4,5},{5,4},{6,7},{7,6},{8,9},{9,8},{10,11... | collective-permute-start | bytes 2359304 | tf_op jit(solution)/shard_map/ppermute | solution.py:24
  53.5 1.2 %copy-start.3 = (bf16[512,256]{1,0:T(8,128)(2,1)S(1)}, bf16[512,256]{1,0:T(8,128)(2,1)}, u32[]{:S(2)}) copy-start(bf16[512,256]{1,0:T(8,128)(2,1)} %copy-done.2) | copy-start | bytes 786436
  57.6 1.2 copy-start.13
  59.1 3.1 %collective-permute-start.12 = (bf16[1,512,256]{2,1,0:T(8,128)(2,1)S(1)}, bf16[1,512,256]{2,1,0:T(8,128)(2,1)S(1)}, u32[]{:S(2)}, u32[]{:S(2)}) collective-permute-start(bf16[1,512,256]{2,1,0:T(8,128)(2,1)S(1)} %collective-permute-done.11), channel_id=1, source_target_pairs={{0,1},{1,0},{2,3},{3,2},{4,5},{5,4},{6,7},{7,6},{8,9},{9,8},{10,11... | collective-permute-start | bytes 786440 | tf_op jit(solution)/shard_map/ppermute | solution.py:24
  59.6 1.0 copy-start.9
  60.9 1.3 %copy-start.7 = (f32[512,256]{1,0:T(8,128)S(1)}, f32[512,256]{1,0:T(8,128)}, u32[]{:S(2)}) copy-start(f32[512,256]{1,0:T(8,128)} %get-tuple-element.9) | copy-start | bytes 1572868
  62.5 15.4 %collective-permute-start.20 = (bf16[512,256]{1,0:T(8,128)(2,1)S(1)}, bf16[512,256]{1,0:T(8,128)(2,1)S(1)}, u32[]{:S(2)}, u32[]{:S(2)}) collective-permute-start(bf16[512,256]{1,0:T(8,128)(2,1)S(1)} %fusion.29), channel_id=1, source_target_pairs={{0,4},{1,5},{2,6},{3,7},{4,0},{5,1},{6,2},{7,3},{8,12},{9,13},{10,... | collective-permute-start | bytes 786440 | tf_op jit(solution)/shard_map/ppermute | solution.py:24
  65.6 12.2 %collective-permute-start.18 = (bf16[512,256]{1,0:T(8,128)(2,1)S(1)}, bf16[512,256]{1,0:T(8,128)(2,1)S(1)}, u32[]{:S(2)}, u32[]{:S(2)}) collective-permute-start(bf16[512,256]{1,0:T(8,128)(2,1)S(1)} %fusion.29), channel_id=1, source_target_pairs={{0,24},{8,16},{16,8},{24,0},{1,25},{9,17},{17,9},{25,1},{2,26},{10... | collective-permute-start | bytes 786440 | tf_op jit(solution)/shard_map/ppermute | solution.py:24
  67.0 13.4 %collective-permute-start.17 = (bf16[512,256]{1,0:T(8,128)(2,1)S(1)}, bf16[512,256]{1,0:T(8,128)(2,1)S(1)}, u32[]{:S(2)}, u32[]{:S(2)}) collective-permute-start(bf16[512,256]{1,0:T(8,128)(2,1)S(1)} %fusion.29), channel_id=1, source_target_pairs={{0,16},{8,24},{16,0},{24,8},{1,17},{9,25},{17,1},{25,9},{2,18},{10... | collective-permute-start | bytes 786440 | tf_op jit(solution)/shard_map/ppermute | solution.py:24
  68.0 12.3 %collective-permute-start.16 = (bf16[512,256]{1,0:T(8,128)(2,1)S(1)}, bf16[512,256]{1,0:T(8,128)(2,1)S(1)}, u32[]{:S(2)}, u32[]{:S(2)}) collective-permute-start(bf16[512,256]{1,0:T(8,128)(2,1)S(1)} %fusion.29), channel_id=1, source_target_pairs={{0,8},{8,0},{16,24},{24,16},{1,9},{9,1},{17,25},{25,17},{2,10},{10... | collective-permute-start | bytes 786440 | tf_op jit(solution)/shard_map/ppermute | solution.py:24
  68.3 12.9 %collective-permute-start.19 = (bf16[512,256]{1,0:T(8,128)(2,1)S(1)}, bf16[512,256]{1,0:T(8,128)(2,1)S(1)}, u32[]{:S(2)}, u32[]{:S(2)}) collective-permute-start(bf16[512,256]{1,0:T(8,128)(2,1)S(1)} %fusion.29), channel_id=1, source_target_pairs={{0,2},{1,3},{2,0},{3,1},{4,6},{5,7},{6,4},{7,5},{8,10},{9,11},{10,... | collective-permute-start | bytes 786440 | tf_op jit(solution)/shard_map/ppermute | solution.py:24
  77.8 8.5 %collective-permute-start.22 = (bf16[1,512,256]{2,1,0:T(8,128)(2,1)S(1)}, bf16[1,512,256]{2,1,0:T(8,128)(2,1)}, u32[]{:S(2)}, u32[]{:S(2)}) collective-permute-start(bf16[1,512,256]{2,1,0:T(8,128)(2,1)S(1)} %bitcast.277), channel_id=1, source_target_pairs={{0,2},{1,3},{2,0},{3,1},{4,6},{5,7},{6,4},{7,5},{8,10},{9,11},{10,... | collective-permute-start | bytes 786440 | tf_op jit(solution)/shard_map/ppermute | solution.py:24
  81.1 9.4 %copy-start.4 = (bf16[512,256]{1,0:T(8,128)(2,1)}, bf16[512,256]{1,0:T(8,128)(2,1)S(1)}, u32[]{:S(2)}) copy-start(bf16[512,256]{1,0:T(8,128)(2,1)S(1)} %collective-permute-done.19) | copy-start | bytes 786436
  81.3 8.2 %collective-permute-start.21 = (bf16[3,512,256]{2,1,0:T(8,128)(2,1)S(1)}, bf16[3,512,256]{2,1,0:T(8,128)(2,1)S(1)}, u32[]{:S(2)}, u32[]{:S(2)}) collective-permute-start(bf16[3,512,256]{2,1,0:T(8,128)(2,1)S(1)} %pad_maximum_fusion.6), channel_id=1, source_target_pairs={{0,1},{1,0},{2,3},{3,2},{4,5},{5,4},{6,7},{7,6},{8,9},{9,8},{10,11... | collective-permute-start | bytes 2359304 | tf_op jit(solution)/shard_map/ppermute | solution.py:24
  86.4 4.5 %collective-permute-start.23 = (bf16[1,512,256]{2,1,0:T(8,128)(2,1)}, bf16[1,512,256]{2,1,0:T(8,128)(2,1)S(1)}, u32[]{:S(2)}, u32[]{:S(2)}) collective-permute-start(bf16[1,512,256]{2,1,0:T(8,128)(2,1)} %collective-permute-done.22), channel_id=1, source_target_pairs={{0,1},{1,0},{2,3},{3,2},{4,5},{5,4},{6,7},{7,6},{8,9},{9,8},{10,11... | collective-permute-start | bytes 786440 | tf_op jit(solution)/shard_map/ppermute | solution.py:24
  89.4 0.9 copy-start
  90.8 1.0 copy-start.10
  91.9 8.9 %collective-permute-start.31 = (bf16[512,256]{1,0:T(8,128)(2,1)S(1)}, bf16[512,256]{1,0:T(8,128)(2,1)S(1)}, u32[]{:S(2)}, u32[]{:S(2)}) collective-permute-start(bf16[512,256]{1,0:T(8,128)(2,1)S(1)} %get-tuple-element.10), channel_id=1, source_target_pairs={{0,24},{8,16},{16,8},{24,0},{1,25},{9,17},{17,9},{25,1},{2,26},{10... | collective-permute-start | bytes 786440 | tf_op jit(solution)/shard_map/ppermute | solution.py:24
  93.2 13.6 %collective-permute-start.30 = (bf16[512,256]{1,0:T(8,128)(2,1)S(1)}, bf16[512,256]{1,0:T(8,128)(2,1)S(1)}, u32[]{:S(2)}, u32[]{:S(2)}) collective-permute-start(bf16[512,256]{1,0:T(8,128)(2,1)S(1)} %get-tuple-element.10), channel_id=1, source_target_pairs={{0,16},{8,24},{16,0},{24,8},{1,17},{9,25},{17,1},{25,9},{2,18},{10... | collective-permute-start | bytes 786440 | tf_op jit(solution)/shard_map/ppermute | solution.py:24
  94.3 12.5 %collective-permute-start.29 = (bf16[512,256]{1,0:T(8,128)(2,1)S(1)}, bf16[512,256]{1,0:T(8,128)(2,1)S(1)}, u32[]{:S(2)}, u32[]{:S(2)}) collective-permute-start(bf16[512,256]{1,0:T(8,128)(2,1)S(1)} %get-tuple-element.10), channel_id=1, source_target_pairs={{0,8},{8,0},{16,24},{24,16},{1,9},{9,1},{17,25},{25,17},{2,10},{10... | collective-permute-start | bytes 786440 | tf_op jit(solution)/shard_map/ppermute | solution.py:24
  94.5 15.4 %collective-permute-start.25 = (bf16[512,256]{1,0:T(8,128)(2,1)S(1)}, bf16[512,256]{1,0:T(8,128)(2,1)}, u32[]{:S(2)}, u32[]{:S(2)}) collective-permute-start(bf16[512,256]{1,0:T(8,128)(2,1)S(1)} %get-tuple-element.10), channel_id=1, source_target_pairs={{0,4},{1,5},{2,6},{3,7},{4,0},{5,1},{6,2},{7,3},{8,12},{9,13},{10,... | collective-permute-start | bytes 786440 | tf_op jit(solution)/shard_map/ppermute | solution.py:24
  94.5 15.7 %collective-permute-start.24 = (bf16[512,256]{1,0:T(8,128)(2,1)S(1)}, bf16[512,256]{1,0:T(8,128)(2,1)}, u32[]{:S(2)}, u32[]{:S(2)}) collective-permute-start(bf16[512,256]{1,0:T(8,128)(2,1)S(1)} %get-tuple-element.10), channel_id=1, source_target_pairs={{0,2},{1,3},{2,0},{3,1},{4,6},{5,7},{6,4},{7,5},{8,10},{9,11},{10,... | collective-permute-start | bytes 786440 | tf_op jit(solution)/shard_map/ppermute | solution.py:24
  109.9 7.8 %collective-permute-start.27 = (bf16[1,512,256]{2,1,0:T(8,128)(2,1)}, bf16[1,512,256]{2,1,0:T(8,128)(2,1)S(1)}, u32[]{:S(2)}, u32[]{:S(2)}) collective-permute-start(bf16[1,512,256]{2,1,0:T(8,128)(2,1)} %bitcast.63), channel_id=1, source_target_pairs={{0,2},{1,3},{2,0},{3,1},{4,6},{5,7},{6,4},{7,5},{8,10},{9,11},{10,... | collective-permute-start | bytes 786440 | tf_op jit(solution)/shard_map/ppermute | solution.py:24
  111.4 1.6 %copy-start.1 = (bf16[3,512,256]{2,1,0:T(8,128)(2,1)S(1)}, bf16[3,512,256]{2,1,0:T(8,128)(2,1)}, u32[]{:S(2)}) copy-start(bf16[3,512,256]{2,1,0:T(8,128)(2,1)} %copy-done) | copy-start | bytes 2359300
  111.4 7.8 %collective-permute-start.26 = (bf16[3,512,256]{2,1,0:T(8,128)(2,1)S(1)}, bf16[3,512,256]{2,1,0:T(8,128)(2,1)S(1)}, u32[]{:S(2)}, u32[]{:S(2)}) collective-permute-start(bf16[3,512,256]{2,1,0:T(8,128)(2,1)S(1)} %pad_maximum_fusion.7), channel_id=1, source_target_pairs={{0,1},{1,0},{2,3},{3,2},{4,5},{5,4},{6,7},{7,6},{8,9},{9,8},{10,11... | collective-permute-start | bytes 2359304 | tf_op jit(solution)/shard_map/ppermute | solution.py:24
  113.7 1.0 copy-start.5
  114.9 1.2 %copy-start.11 = (bf16[1,512,256]{2,1,0:T(8,128)(2,1)S(1)}, bf16[1,512,256]{2,1,0:T(8,128)(2,1)}, u32[]{:S(2)}) copy-start(bf16[1,512,256]{2,1,0:T(8,128)(2,1)} %copy-done.10) | copy-start | bytes 786436
  117.7 4.2 %collective-permute-start.28 = (bf16[1,512,256]{2,1,0:T(8,128)(2,1)S(1)}, bf16[1,512,256]{2,1,0:T(8,128)(2,1)S(1)}, u32[]{:S(2)}, u32[]{:S(2)}) collective-permute-start(bf16[1,512,256]{2,1,0:T(8,128)(2,1)S(1)} %collective-permute-done.27), channel_id=1, source_target_pairs={{0,1},{1,0},{2,3},{3,2},{4,5},{5,4},{6,7},{7,6},{8,9},{9,8},{10,11... | collective-permute-start | bytes 786440 | tf_op jit(solution)/shard_map/ppermute | solution.py:24
  119.4 1.0 copy-start.8
  120.7 1.3 %copy-start.6 = (f32[512,256]{1,0:T(8,128)S(1)}, f32[512,256]{1,0:T(8,128)}, u32[]{:S(2)}) copy-start(f32[512,256]{1,0:T(8,128)} %get-tuple-element.11) | copy-start | bytes 1572868

commit v7 on v6

--- a/solution.py
+++ b/solution.py
@@ -26,22 +26,28 @@
 
 def exchange(xb, n_row, n_col):
     chips = n_col // 2
+    half = xb.shape[1] // 2
+    parts = (xb[:, :half], xb[:, half:])
+    forward = list(range(2, chips, 2))
     same = {0: xb}
-    for s in sorted(range(2, chips, 2), reverse=True) + [1]:
-        same[s] = xor_permute(xb, "col", n_col, 2 * s)
+    for s in sorted(forward, reverse=True):
+        same[s] = tuple(xor_permute(p, "col", n_col, 2 * s) for p in parts)
+    same[1] = xor_permute(xb, "col", n_col, 2)
     col_pieces = [xb] + [xor_permute(xb, "row", n_row, t) for t in range(1, n_row)]
-    first = sorted(same)
-    relay_first = xor_permute(jnp.stack([same[s] for s in first]), "col", n_col, 1)
-    other = {}
-    for i, s in enumerate(first):
-        other[s] = relay_first[i]
-    forward = list(range(2, chips, 2))
+    relay_first = xor_permute(jnp.stack([xb, same[1]]), "col", n_col, 1)
+    other = {0: relay_first[0], 1: relay_first[1]}
     if forward:
-        sent = xor_permute(jnp.stack([same[s] for s in forward]), "col", n_col, 2)
-        relay_sent = xor_permute(sent, "col", n_col, 1)
+        relay_halves = xor_permute(
+            jnp.stack([p for s in forward for p in same[s]]), "col", n_col, 1
+        )
+        sent = [
+            xor_permute(jnp.stack([same[s][h] for s in forward]), "col", n_col, 2) for h in (0, 1)
+        ]
+        relay_sent = xor_permute(jnp.stack(sent), "col", n_col, 1)
         for i, s in enumerate(forward):
-            same[s ^ 1] = sent[i]
-            other[s ^ 1] = relay_sent[i]
+            other[s] = (relay_halves[2 * i], relay_halves[2 * i + 1])
+            same[s ^ 1] = (sent[0][i], sent[1][i])
+            other[s ^ 1] = (relay_sent[0, i], relay_sent[1, i])
     row_pieces = []
     for s in range(chips):
         row_pieces.append(same[s])
@@ -62,8 +68,16 @@
 def contract(row_pieces, k_blocks):
     total = None
     for s, piece in enumerate(row_pieces):
-        part = jnp.dot(piece, k_blocks[s], preferred_element_type=jnp.float32)
-        total = part if total is None else total + part
+        if isinstance(piece, tuple):
+            half = piece[0].shape[1]
+            parts = [
+                jnp.dot(piece[0], k_blocks[s, :half], preferred_element_type=jnp.float32),
+                jnp.dot(piece[1], k_blocks[s, half:], preferred_element_type=jnp.float32),
+            ]
+        else:
+            parts = [jnp.dot(piece, k_blocks[s], preferred_element_type=jnp.float32)]
+        for part in parts:
+            total = part if total is None else total + part
     return total
 
 

time: 124 us -> 186 us (1.50)
  matrix products: 28.5 us -> 53.1 us
  starting transfers between devices: 35.3 us -> 59.3 us
  other arithmetic: 6.66 us -> 13.6 us
  local copies, waits for them, and re-layouts: 8.68 us -> 14.2 us
    dot_general x48 -> x72, matrix products: 28.5 us -> 53.1 us  [the longest x24 19.2 us: contract(): jnp.dot(piece[0], k_blocks[s, :half], preferred_element_type=jnp.float32)]
    ppermute x32 -> x44, starting transfers between devices: 35.3 us -> 59.3 us  [xor_permute(): return lax.ppermute(x, axis, perm=[(i, i ^ s) for i in range(size)])]
    another operation x4 -> x12, other arithmetic: 3.31 us -> 10.2 us  [the longest x4 3.89 us: exchange(): jnp.stack([p for s in forward for p in same[s]])]
    unnamed x33 -> x55, local copies, waits for them, and re-layouts: 3.57 us -> 8.97 us
    ppermute x32 -> x44, waiting for transfers between devices: 43.1 us -> 43.3 us  [xor_permute(): return lax.ppermute(x, axis, perm=[(i, i ^ s) for i in range(size)])]
  transfers between devices with their start and end apart: 32 -> 44, of which waited for: 11 -> 14; matrix products, arithmetic and copies ran while one was open for 30% -> 33% of each run, Pallas kernels for 0% -> 0%
where the time goes in v7:
time: 186 us; the launch traced here: 184 us
  starting transfers between devices  59.3 us (32%)
  matrix products  53.1 us (29%)
  waiting for transfers between devices  43.3 us (23%)
  local copies, waits for them, and re-layouts  14.2 us (8%)
  other arithmetic  13.6 us (7%)
    ppermute x44, starting transfers between devices, xor_permute(): return lax.ppermute(x, axis, perm=[(i, i ^ s) for i in range(size)])  59.3 us
    ppermute x44, waiting for transfers between devices, xor_permute(): return lax.ppermute(x, axis, perm=[(i, i ^ s) for i in range(size)])  43.3 us
    dot_general x24, matrix products, contract(): jnp.dot(piece[0], k_blocks[s, :half], preferred_element_type=jnp.float32)  19.2 us
    dot_general x24, matrix products, contract(): jnp.dot(piece[1], k_blocks[s, half:], preferred_element_type=jnp.float32)  17.3 us
    dot_general x24, matrix products, contract(): parts = [jnp.dot(piece, k_blocks[s], preferred_element_type=jnp.float32)]  16.7 us
    unnamed x55, local copies, waits for them, and re-layouts  8.97 us
    gather x4, local copies, waits for them, and re-layouts, ordered_k_blocks(): return jnp.take(split, index, axis=0)  4.9 us
    another operation x4, other arithmetic, exchange(): jnp.stack([p for s in forward for p in same[s]])  3.89 us
  transfers between devices with their start and end apart: 44, of which 14 were waited for; matrix products, arithmetic and copies ran while one was open for 33% of the time, Pallas kernels for 0%

profile of v7, /device:TPU:1, one launch (start us, length us, event | category | flops | bytes accessed | tf_op | source)
XLA Modules:
  0.0 184.4 jit_solution(6280084476918474538)
XLA Ops:
  1.2 3.2 %collective-permute-start.6 = (bf16[512,128]{1,0:T(8,128)(2,1)S(1)}, bf16[512,128]{1,0:T(8,128)(2,1)S(1)}, u32[]{:S(2)}, u32[]{:S(2)}) collective-permute-start(bf16[512,128]{1,0:T(8,128)(2,1)S(1)} %get-tuple-element.15), channel_id=1, source_target_pairs={{0,4},{1,5},{2,6},{3,7},{4,0},{5,1},{6,2},{7,3},{8,12},{9,13},{10,... | collective-permute-start | bytes 393224 | tf_op jit(solution)/shard_map/ppermute | solution.py:24
  4.5 2.2 %collective-permute-start.2 = (bf16[512,256]{1,0:T(8,128)(2,1)S(1)}, bf16[512,256]{1,0:T(8,128)(2,1)S(1)}, u32[]{:S(2)}, u32[]{:S(2)}) collective-permute-start(bf16[512,256]{1,0:T(8,128)(2,1)S(1)} %fusion.58), channel_id=1, source_target_pairs={{0,24},{8,16},{16,8},{24,0},{1,25},{9,17},{17,9},{25,1},{2,26},{10... | collective-permute-start | bytes 786440 | tf_op jit(solution)/shard_map/ppermute | solution.py:24
  6.9 1.3 collective-permute-start.3
  8.2 5.1 %collective-permute-done.6 = bf16[512,128]{1,0:T(8,128)(2,1)S(1)} collective-permute-done((bf16[512,128]{1,0:T(8,128)(2,1)S(1)}, bf16[512,128]{1,0:T(8,128)(2,1)S(1)}, u32[]{:S(2)}, u32[]{:S(2)}) %collective-permute-start.6) | collective-permute-done | bytes 131104 | tf_op jit(solution)/shard_map/ppermute | solution.py:24
  13.2 1.2 collective-permute-start.9
  14.5 1.6 collective-permute-done.5
  16.1 1.2 collective-permute-start.8
  17.3 2.9 %collective-permute-done.9 = bf16[1,512,128]{2,1,0:T(8,128)(2,1)S(1)} collective-permute-done((bf16[1,512,128]{2,1,0:T(8,128)(2,1)S(1)}, bf16[1,512,128]{2,1,0:T(8,128)(2,1)S(1)}, u32[]{:S(2)}, u32[]{:S(2)}) %collective-permute-start.9) | collective-permute-done | bytes 131104 | tf_op jit(solution)/shard_map/ppermute | solution.py:24
  21.8 1.2 collective-permute-done.8
  23.0 2.6 %collective-permute-start.7 = (bf16[2,512,128]{2,1,0:T(8,128)(2,1)}, bf16[2,512,128]{2,1,0:T(8,128)(2,1)}, u32[]{:S(2)}, u32[]{:S(2)}) collective-permute-start(bf16[2,512,128]{2,1,0:T(8,128)(2,1)} %pad_maximum_fusion.8), channel_id=1, source_target_pairs={{0,1},{1,0},{2,3},{3,2},{4,5},{5,4},{6,7},{7,6},{8,9},{9,8},{10,11... | collective-permute-start | bytes 786440 | tf_op jit(solution)/shard_map/ppermute | solution.py:24
  34.9 1.2 fusion.63
  36.1 1.2 convolution_add_fusion.11
  37.3 1.3 fusion.139
  38.6 2.1 %collective-permute-start.21 = (bf16[512,256]{1,0:T(8,128)(2,1)S(1)}, bf16[512,256]{1,0:T(8,128)(2,1)S(1)}, u32[]{:S(2)}, u32[]{:S(2)}) collective-permute-start(bf16[512,256]{1,0:T(8,128)(2,1)S(1)} %get-tuple-element.16), channel_id=1, source_target_pairs={{0,24},{8,16},{16,8},{24,0},{1,25},{9,17},{17,9},{25,1},{2,26},{10... | collective-permute-start | bytes 786440 | tf_op jit(solution)/shard_map/ppermute | solution.py:24
  41.3 4.6 %collective-permute-start.14 = (bf16[512,128]{1,0:T(8,128)(2,1)S(1)}, bf16[512,128]{1,0:T(8,128)(2,1)S(1)}, u32[]{:S(2)}, u32[]{:S(2)}) collective-permute-start(bf16[512,128]{1,0:T(8,128)(2,1)S(1)} %get-tuple-element.13), channel_id=1, source_target_pairs={{0,4},{1,5},{2,6},{3,7},{4,0},{5,1},{6,2},{7,3},{8,12},{9,13},{10,... | collective-permute-start | bytes 393224 | tf_op jit(solution)/shard_map/ppermute | solution.py:24
  47.0 2.2 %collective-permute-done.14 = bf16[512,128]{1,0:T(8,128)(2,1)S(1)} collective-permute-done((bf16[512,128]{1,0:T(8,128)(2,1)S(1)}, bf16[512,128]{1,0:T(8,128)(2,1)S(1)}, u32[]{:S(2)}, u32[]{:S(2)}) %collective-permute-start.14) | collective-permute-done | bytes 131104 | tf_op jit(solution)/shard_map/ppermute | solution.py:24
  49.3 3.1 %collective-permute-start.13 = (bf16[512,128]{1,0:T(8,128)(2,1)S(1)}, bf16[512,128]{1,0:T(8,128)(2,1)S(1)}, u32[]{:S(2)}, u32[]{:S(2)}) collective-permute-start(bf16[512,128]{1,0:T(8,128)(2,1)S(1)} %get-tuple-element.12), channel_id=1, source_target_pairs={{0,4},{1,5},{2,6},{3,7},{4,0},{5,1},{6,2},{7,3},{8,12},{9,13},{10,... | collective-permute-start | bytes 393224 | tf_op jit(solution)/shard_map/ppermute | solution.py:24
  53.4 4.8 %collective-permute-done.13 = bf16[512,128]{1,0:T(8,128)(2,1)S(1)} collective-permute-done((bf16[512,128]{1,0:T(8,128)(2,1)S(1)}, bf16[512,128]{1,0:T(8,128)(2,1)S(1)}, u32[]{:S(2)}, u32[]{:S(2)}) %collective-permute-start.13) | collective-permute-done | bytes 131104 | tf_op jit(solution)/shard_map/ppermute | solution.py:24
  59.9 2.1 %collective-permute-done.17 = bf16[1,512,128]{2,1,0:T(8,128)(2,1)S(1)} collective-permute-done((bf16[1,512,128]{2,1,0:T(8,128)(2,1)S(1)}, bf16[1,512,128]{2,1,0:T(8,128)(2,1)S(1)}, u32[]{:S(2)}, u32[]{:S(2)}) %collective-permute-start.17) | collective-permute-done | bytes 131104 | tf_op jit(solution)/shard_map/ppermute | solution.py:24
  63.3 3.9 %collective-permute-done.16 = bf16[1,512,128]{2,1,0:T(8,128)(2,1)S(1)} collective-permute-done((bf16[1,512,128]{2,1,0:T(8,128)(2,1)S(1)}, bf16[1,512,128]{2,1,0:T(8,128)(2,1)S(1)}, u32[]{:S(2)}, u32[]{:S(2)}) %collective-permute-start.16) | collective-permute-done | bytes 131104 | tf_op jit(solution)/shard_map/ppermute | solution.py:24
  67.3 5.6 %collective-permute-start.15 = (bf16[2,512,128]{2,1,0:T(8,128)(2,1)}, bf16[2,512,128]{2,1,0:T(8,128)(2,1)}, u32[]{:S(2)}, u32[]{:S(2)}) collective-permute-start(bf16[2,512,128]{2,1,0:T(8,128)(2,1)} %pad_maximum_fusion.10), channel_id=1, source_target_pairs={{0,1},{1,0},{2,3},{3,2},{4,5},{5,4},{6,7},{7,6},{8,9},{9,8},{10,11... | collective-permute-start | bytes 786440 | tf_op jit(solution)/shard_map/ppermute | solution.py:24
  75.8 1.8 gather_fusion.1
  86.3 1.2 fusion.62
  87.5 1.2 convolution_add_fusion.7
  91.4 1.2 fusion.72
  92.6 1.2 fusion.73
  95.3 1.5 fusion.59
  96.9 2.0 %collective-permute-start.24 = (bf16[512,256]{1,0:T(8,128)(2,1)S(1)}, bf16[512,256]{1,0:T(8,128)(2,1)S(1)}, u32[]{:S(2)}, u32[]{:S(2)}) collective-permute-start(bf16[512,256]{1,0:T(8,128)(2,1)S(1)} %fusion.59), channel_id=1, source_target_pairs={{0,24},{8,16},{16,8},{24,0},{1,25},{9,17},{17,9},{25,1},{2,26},{10... | collective-permute-start | bytes 786440 | tf_op jit(solution)/shard_map/ppermute | solution.py:24
  100.5 1.5 collective-permute-start.27
  102.0 9.1 %collective-permute-done.28 = bf16[512,128]{1,0:T(8,128)(2,1)S(1)} collective-permute-done((bf16[512,128]{1,0:T(8,128)(2,1)S(1)}, bf16[512,128]{1,0:T(8,128)(2,1)S(1)}, u32[]{:S(2)}, u32[]{:S(2)}) %collective-permute-start.28) | collective-permute-done | bytes 131104 | tf_op jit(solution)/shard_map/ppermute | solution.py:24
  111.2 2.8 %collective-permute-done.27 = bf16[512,128]{1,0:T(8,128)(2,1)S(1)} collective-permute-done((bf16[512,128]{1,0:T(8,128)(2,1)S(1)}, bf16[512,128]{1,0:T(8,128)(2,1)S(1)}, u32[]{:S(2)}, u32[]{:S(2)}) %collective-permute-start.27) | collective-permute-done | bytes 131104 | tf_op jit(solution)/shard_map/ppermute | solution.py:24
  114.7 1.4 collective-permute-start.30
  116.2 1.5 collective-permute-start.29
  118.8 3.1 %collective-permute-start.26 = (bf16[2,512,256]{2,1,0:T(8,128)(2,1)S(1)}, bf16[2,512,256]{2,1,0:T(8,128)(2,1)S(1)}, u32[]{:S(2)}, u32[]{:S(2)}) collective-permute-start(bf16[2,512,256]{2,1,0:T(8,128)(2,1)S(1)} %pad_maximum_fusion.6), channel_id=1, source_target_pairs={{0,1},{1,0},{2,3},{3,2},{4,5},{5,4},{6,7},{7,6},{8,9},{9,8},{10,11... | collective-permute-start | bytes 1572872 | tf_op jit(solution)/shard_map/ppermute | solution.py:24
  122.7 1.9 %collective-permute-done.30 = bf16[1,512,128]{2,1,0:T(8,128)(2,1)} collective-permute-done((bf16[1,512,128]{2,1,0:T(8,128)(2,1)S(1)}, bf16[1,512,128]{2,1,0:T(8,128)(2,1)}, u32[]{:S(2)}, u32[]{:S(2)}) %collective-permute-start.30) | collective-permute-done | bytes 131104 | tf_op jit(solution)/shard_map/ppermute | solution.py:24
  125.4 1.8 collective-permute-start.32
  132.8 1.3 fusion.140
  134.0 1.9 %collective-permute-start.43 = (bf16[512,256]{1,0:T(8,128)(2,1)S(1)}, bf16[512,256]{1,0:T(8,128)(2,1)S(1)}, u32[]{:S(2)}, u32[]{:S(2)}) collective-permute-start(bf16[512,256]{1,0:T(8,128)(2,1)S(1)} %get-tuple-element.18), channel_id=1, source_target_pairs={{0,24},{8,16},{16,8},{24,0},{1,25},{9,17},{17,9},{25,1},{2,26},{10... | collective-permute-start | bytes 786440 | tf_op jit(solution)/shard_map/ppermute | solution.py:24
  136.8 2.0 %collective-permute-start.36 = (bf16[512,128]{1,0:T(8,128)(2,1)S(1)}, bf16[512,128]{1,0:T(8,128)(2,1)}, u32[]{:S(2)}, u32[]{:S(2)}) collective-permute-start(bf16[512,128]{1,0:T(8,128)(2,1)S(1)} %get-tuple-element.9), channel_id=1, source_target_pairs={{0,4},{1,5},{2,6},{3,7},{4,0},{5,1},{6,2},{7,3},{8,12},{9,13},{10,... | collective-permute-start | bytes 393224 | tf_op jit(solution)/shard_map/ppermute | solution.py:24
  139.8 4.8 %collective-permute-done.36 = bf16[512,128]{1,0:T(8,128)(2,1)} collective-permute-done((bf16[512,128]{1,0:T(8,128)(2,1)S(1)}, bf16[512,128]{1,0:T(8,128)(2,1)}, u32[]{:S(2)}, u32[]{:S(2)}) %collective-permute-start.36) | collective-permute-done | bytes 131104 | tf_op jit(solution)/shard_map/ppermute | solution.py:24
  144.7 3.2 %collective-permute-start.35 = (bf16[512,128]{1,0:T(8,128)(2,1)S(1)}, bf16[512,128]{1,0:T(8,128)(2,1)}, u32[]{:S(2)}, u32[]{:S(2)}) collective-permute-start(bf16[512,128]{1,0:T(8,128)(2,1)S(1)} %get-tuple-element.8), channel_id=1, source_target_pairs={{0,4},{1,5},{2,6},{3,7},{4,0},{5,1},{6,2},{7,3},{8,12},{9,13},{10,... | collective-permute-start | bytes 393224 | tf_op jit(solution)/shard_map/ppermute | solution.py:24
  147.9 1.9 %fusion.130 = f32[512,256]{1,0:T(8,128)} fusion(bf16[512,128]{1,0:T(8,128)(2,1)} %collective-permute-done.36, bf16[8,256,256]{2,1,0:T(8,128)(2,1)S(1)} %broadcast_select_fusion.1), kind=kOutput, calls=%fused_computation.241 | convolution fusion | flops 33554432 | bytes 720896 | tf_op jit(solution)/shard_map/dot_general | solution.py:75
  150.4 2.0 %collective-permute-start.39 = (bf16[1,512,128]{2,1,0:T(8,128)(2,1)}, bf16[1,512,128]{2,1,0:T(8,128)(2,1)}, u32[]{:S(2)}, u32[]{:S(2)}) collective-permute-start(bf16[1,512,128]{2,1,0:T(8,128)(2,1)} %bitcast.96), channel_id=1, source_target_pairs={{0,2},{1,3},{2,0},{3,1},{4,6},{5,7},{6,4},{7,5},{8,10},{9,11},{10,... | collective-permute-start | bytes 393224 | tf_op jit(solution)/shard_map/ppermute | solution.py:24
  152.4 1.7 pad_maximum_fusion.14
  154.1 1.9 %fusion.128 = f32[512,256]{1,0:T(8,128)} fusion(bf16[512,128]{1,0:T(8,128)(2,1)} %collective-permute-done.35, bf16[8,256,256]{2,1,0:T(8,128)(2,1)S(1)} %broadcast_select_fusion.1), kind=kOutput, calls=%fused_computation.239 | convolution fusion | flops 33554432 | bytes 720896 | tf_op jit(solution)/shard_map/dot_general | solution.py:74
  156.0 5.2 %collective-permute-start.37 = (bf16[2,512,128]{2,1,0:T(8,128)(2,1)}, bf16[2,512,128]{2,1,0:T(8,128)(2,1)}, u32[]{:S(2)}, u32[]{:S(2)}) collective-permute-start(bf16[2,512,128]{2,1,0:T(8,128)(2,1)} %pad_maximum_fusion.14), channel_id=1, source_target_pairs={{0,1},{1,0},{2,3},{3,2},{4,5},{5,4},{6,7},{7,6},{8,9},{9,8},{10,11... | collective-permute-start | bytes 786440 | tf_op jit(solution)/shard_map/ppermute | solution.py:24
  162.4 1.8 gather_fusion.3
  182.1 2.3 %bitcast_multiply_fusion = f32[512,256]{1,0:T(8,128)} fusion(f32[512,256]{1,0:T(8,128)S(1)} %copy-done.11, f32[64,8,2,128]{3,2,1,0:T(2,128)S(1)} %bitcast.373, f32[512,256]{1,0:T(8,128)S(1)} %fusion.8, f32[512,256]{1,0:T(8,128)S(1)} %fusion.67, f32[512,256]{1,0:T(8,128)S(1)} %fusion.68, f32[512,256]{1,0:T(8,128)S(1)} %fusion.76, ...), kind=kOutput, calls=%fused_computation.82 | convolution fusion | flops 68943872 | bytes 7733248 | tf_op jit(solution)/shard_map/dot_general | solution.py:78
  (200 shorter events, 65.3 us)
Async XLA Ops:
  1.2 12.0 %collective-permute-start.6 = (bf16[512,128]{1,0:T(8,128)(2,1)S(1)}, bf16[512,128]{1,0:T(8,128)(2,1)S(1)}, u32[]{:S(2)}, u32[]{:S(2)}) collective-permute-start(bf16[512,128]{1,0:T(8,128)(2,1)S(1)} %get-tuple-element.15), channel_id=1, source_target_pairs={{0,4},{1,5},{2,6},{3,7},{4,0},{5,1},{6,2},{7,3},{8,12},{9,13},{10,... | collective-permute-start | bytes 393224 | tf_op jit(solution)/shard_map/ppermute | solution.py:24
  4.4 11.7 %collective-permute-start.5 = (bf16[512,128]{1,0:T(8,128)(2,1)S(1)}, bf16[512,128]{1,0:T(8,128)(2,1)S(1)}, u32[]{:S(2)}, u32[]{:S(2)}) collective-permute-start(bf16[512,128]{1,0:T(8,128)(2,1)S(1)} %get-tuple-element.14), channel_id=1, source_target_pairs={{0,4},{1,5},{2,6},{3,7},{4,0},{5,1},{6,2},{7,3},{8,12},{9,13},{10,... | collective-permute-start | bytes 393224 | tf_op jit(solution)/shard_map/ppermute | solution.py:24
  4.5 22.8 %collective-permute-start.2 = (bf16[512,256]{1,0:T(8,128)(2,1)S(1)}, bf16[512,256]{1,0:T(8,128)(2,1)S(1)}, u32[]{:S(2)}, u32[]{:S(2)}) collective-permute-start(bf16[512,256]{1,0:T(8,128)(2,1)S(1)} %fusion.58), channel_id=1, source_target_pairs={{0,24},{8,16},{16,8},{24,0},{1,25},{9,17},{17,9},{25,1},{2,26},{10... | collective-permute-start | bytes 786440 | tf_op jit(solution)/shard_map/ppermute | solution.py:24
  6.6 21.1 %collective-permute-start.1 = (bf16[512,256]{1,0:T(8,128)(2,1)S(1)}, bf16[512,256]{1,0:T(8,128)(2,1)S(1)}, u32[]{:S(2)}, u32[]{:S(2)}) collective-permute-start(bf16[512,256]{1,0:T(8,128)(2,1)S(1)} %fusion.58), channel_id=1, source_target_pairs={{0,16},{8,24},{16,0},{24,8},{1,17},{9,25},{17,1},{25,9},{2,18},{10... | collective-permute-start | bytes 786440 | tf_op jit(solution)/shard_map/ppermute | solution.py:24
  6.9 19.5 %collective-permute-start.3 = (bf16[512,256]{1,0:T(8,128)(2,1)S(1)}, bf16[512,256]{1,0:T(8,128)(2,1)S(1)}, u32[]{:S(2)}, u32[]{:S(2)}) collective-permute-start(bf16[512,256]{1,0:T(8,128)(2,1)S(1)} %fusion.58), channel_id=1, source_target_pairs={{0,2},{1,3},{2,0},{3,1},{4,6},{5,7},{6,4},{7,5},{8,10},{9,11},{10,... | collective-permute-start | bytes 786440 | tf_op jit(solution)/shard_map/ppermute | solution.py:24
  13.2 7.0 %collective-permute-start.9 = (bf16[1,512,128]{2,1,0:T(8,128)(2,1)S(1)}, bf16[1,512,128]{2,1,0:T(8,128)(2,1)S(1)}, u32[]{:S(2)}, u32[]{:S(2)}) collective-permute-start(bf16[1,512,128]{2,1,0:T(8,128)(2,1)S(1)} %bitcast.388), channel_id=1, source_target_pairs={{0,2},{1,3},{2,0},{3,1},{4,6},{5,7},{6,4},{7,5},{8,10},{9,11},{10,... | collective-permute-start | bytes 393224 | tf_op jit(solution)/shard_map/ppermute | solution.py:24
  16.1 13.9 %copy-start.12 = (bf16[512,128]{1,0:T(8,128)(2,1)}, bf16[512,128]{1,0:T(8,128)(2,1)S(1)}, u32[]{:S(2)}) copy-start(bf16[512,128]{1,0:T(8,128)(2,1)S(1)} %collective-permute-done.5) | copy-start | bytes 393220
  16.1 6.9 %collective-permute-start.8 = (bf16[1,512,128]{2,1,0:T(8,128)(2,1)S(1)}, bf16[1,512,128]{2,1,0:T(8,128)(2,1)S(1)}, u32[]{:S(2)}, u32[]{:S(2)}) collective-permute-start(bf16[1,512,128]{2,1,0:T(8,128)(2,1)S(1)} %bitcast.390), channel_id=1, source_target_pairs={{0,2},{1,3},{2,0},{3,1},{4,6},{5,7},{6,4},{7,5},{8,10},{9,11},{10,... | collective-permute-start | bytes 393224 | tf_op jit(solution)/shard_map/ppermute | solution.py:24
  20.2 8.5 %copy-start.14 = (bf16[1,512,128]{2,1,0:T(8,128)(2,1)}, bf16[1,512,128]{2,1,0:T(8,128)(2,1)S(1)}, u32[]{:S(2)}) copy-start(bf16[1,512,128]{2,1,0:T(8,128)(2,1)S(1)} %collective-permute-done.9) | copy-start | bytes 393220
  20.2 7.5 %collective-permute-start = (bf16[512,256]{1,0:T(8,128)(2,1)S(1)}, bf16[512,256]{1,0:T(8,128)(2,1)S(1)}, u32[]{:S(2)}, u32[]{:S(2)}) collective-permute-start(bf16[512,256]{1,0:T(8,128)(2,1)S(1)} %fusion.58), channel_id=1, source_target_pairs={{0,8},{8,0},{16,24},{24,16},{1,9},{9,1},{17,25},{25,17},{2,10},{10... | collective-permute-start | bytes 786440 | tf_op jit(solution)/shard_map/ppermute | solution.py:24
  23.0 7.4 %collective-permute-start.7 = (bf16[2,512,128]{2,1,0:T(8,128)(2,1)}, bf16[2,512,128]{2,1,0:T(8,128)(2,1)}, u32[]{:S(2)}, u32[]{:S(2)}) collective-permute-start(bf16[2,512,128]{2,1,0:T(8,128)(2,1)} %pad_maximum_fusion.8), channel_id=1, source_target_pairs={{0,1},{1,0},{2,3},{3,2},{4,5},{5,4},{6,7},{7,6},{8,9},{9,8},{10,11... | collective-permute-start | bytes 786440 | tf_op jit(solution)/shard_map/ppermute | solution.py:24
  26.4 6.3 %collective-permute-start.10 = (bf16[2,1,512,128]{3,2,1,0:T(8,128)(2,1)}, bf16[2,1,512,128]{3,2,1,0:T(8,128)(2,1)}, u32[]{:S(2)}, u32[]{:S(2)}) collective-permute-start(bf16[2,1,512,128]{3,2,1,0:T(8,128)(2,1)} %pad_maximum_fusion.9), channel_id=1, source_target_pairs={{0,1},{1,0},{2,3},{3,2},{4,5},{5,4},{6,7},{7,6},{8,9},{9,8},{10,11... | collective-permute-start | bytes 786440 | tf_op jit(solution)/shard_map/ppermute | solution.py:24
  27.2 7.7 %collective-permute-start.4 = (bf16[2,512,256]{2,1,0:T(8,128)(2,1)}, bf16[2,512,256]{2,1,0:T(8,128)(2,1)}, u32[]{:S(2)}, u32[]{:S(2)}) collective-permute-start(bf16[2,512,256]{2,1,0:T(8,128)(2,1)} %pad_maximum_fusion.4), channel_id=1, source_target_pairs={{0,1},{1,0},{2,3},{3,2},{4,5},{5,4},{6,7},{7,6},{8,9},{9,8},{10,11... | collective-permute-start | bytes 1572872 | tf_op jit(solution)/shard_map/ppermute | solution.py:24
  38.6 36.0 %collective-permute-start.21 = (bf16[512,256]{1,0:T(8,128)(2,1)S(1)}, bf16[512,256]{1,0:T(8,128)(2,1)S(1)}, u32[]{:S(2)}, u32[]{:S(2)}) collective-permute-start(bf16[512,256]{1,0:T(8,128)(2,1)S(1)} %get-tuple-element.16), channel_id=1, source_target_pairs={{0,24},{8,16},{16,8},{24,0},{1,25},{9,17},{17,9},{25,1},{2,26},{10... | collective-permute-start | bytes 786440 | tf_op jit(solution)/shard_map/ppermute | solution.py:24
  40.7 33.9 %collective-permute-start.20 = (bf16[512,256]{1,0:T(8,128)(2,1)S(1)}, bf16[512,256]{1,0:T(8,128)(2,1)S(1)}, u32[]{:S(2)}, u32[]{:S(2)}) collective-permute-start(bf16[512,256]{1,0:T(8,128)(2,1)S(1)} %get-tuple-element.16), channel_id=1, source_target_pairs={{0,16},{8,24},{16,0},{24,8},{1,17},{9,25},{17,1},{25,9},{2,18},{10... | collective-permute-start | bytes 786440 | tf_op jit(solution)/shard_map/ppermute | solution.py:24
  40.9 33.8 %collective-permute-start.19 = (bf16[512,256]{1,0:T(8,128)(2,1)S(1)}, bf16[512,256]{1,0:T(8,128)(2,1)S(1)}, u32[]{:S(2)}, u32[]{:S(2)}) collective-permute-start(bf16[512,256]{1,0:T(8,128)(2,1)S(1)} %get-tuple-element.16), channel_id=1, source_target_pairs={{0,8},{8,0},{16,24},{24,16},{1,9},{9,1},{17,25},{25,17},{2,10},{10... | collective-permute-start | bytes 786440 | tf_op jit(solution)/shard_map/ppermute | solution.py:24
  41.3 36.8 %collective-permute-start.11 = (bf16[512,256]{1,0:T(8,128)(2,1)S(1)}, bf16[512,256]{1,0:T(8,128)(2,1)}, u32[]{:S(2)}, u32[]{:S(2)}) collective-permute-start(bf16[512,256]{1,0:T(8,128)(2,1)S(1)} %get-tuple-element.16), channel_id=1, source_target_pairs={{0,2},{1,3},{2,0},{3,1},{4,6},{5,7},{6,4},{7,5},{8,10},{9,11},{10,... | collective-permute-start | bytes 786440 | tf_op jit(solution)/shard_map/ppermute | solution.py:24
  41.3 7.9 %collective-permute-start.14 = (bf16[512,128]{1,0:T(8,128)(2,1)S(1)}, bf16[512,128]{1,0:T(8,128)(2,1)S(1)}, u32[]{:S(2)}, u32[]{:S(2)}) collective-permute-start(bf16[512,128]{1,0:T(8,128)(2,1)S(1)} %get-tuple-element.13), channel_id=1, source_target_pairs={{0,4},{1,5},{2,6},{3,7},{4,0},{5,1},{6,2},{7,3},{8,12},{9,13},{10,... | collective-permute-start | bytes 393224 | tf_op jit(solution)/shard_map/ppermute | solution.py:24
  49.3 8.9 %collective-permute-start.13 = (bf16[512,128]{1,0:T(8,128)(2,1)S(1)}, bf16[512,128]{1,0:T(8,128)(2,1)S(1)}, u32[]{:S(2)}, u32[]{:S(2)}) collective-permute-start(bf16[512,128]{1,0:T(8,128)(2,1)S(1)} %get-tuple-element.12), channel_id=1, source_target_pairs={{0,4},{1,5},{2,6},{3,7},{4,0},{5,1},{6,2},{7,3},{8,12},{9,13},{10,... | collective-permute-start | bytes 393224 | tf_op jit(solution)/shard_map/ppermute | solution.py:24
  58.2 3.8 %collective-permute-start.17 = (bf16[1,512,128]{2,1,0:T(8,128)(2,1)S(1)}, bf16[1,512,128]{2,1,0:T(8,128)(2,1)S(1)}, u32[]{:S(2)}, u32[]{:S(2)}) collective-permute-start(bf16[1,512,128]{2,1,0:T(8,128)(2,1)S(1)} %bitcast.399), channel_id=1, source_target_pairs={{0,2},{1,3},{2,0},{3,1},{4,6},{5,7},{6,4},{7,5},{8,10},{9,11},{10,... | collective-permute-start | bytes 393224 | tf_op jit(solution)/shard_map/ppermute | solution.py:24
  62.0 5.2 %collective-permute-start.16 = (bf16[1,512,128]{2,1,0:T(8,128)(2,1)S(1)}, bf16[1,512,128]{2,1,0:T(8,128)(2,1)S(1)}, u32[]{:S(2)}, u32[]{:S(2)}) collective-permute-start(bf16[1,512,128]{2,1,0:T(8,128)(2,1)S(1)} %bitcast.402), channel_id=1, source_target_pairs={{0,2},{1,3},{2,0},{3,1},{4,6},{5,7},{6,4},{7,5},{8,10},{9,11},{10,... | collective-permute-start | bytes 393224 | tf_op jit(solution)/shard_map/ppermute | solution.py:24
  67.3 21.9 %collective-permute-start.15 = (bf16[2,512,128]{2,1,0:T(8,128)(2,1)}, bf16[2,512,128]{2,1,0:T(8,128)(2,1)}, u32[]{:S(2)}, u32[]{:S(2)}) collective-permute-start(bf16[2,512,128]{2,1,0:T(8,128)(2,1)} %pad_maximum_fusion.10), channel_id=1, source_target_pairs={{0,1},{1,0},{2,3},{3,2},{4,5},{5,4},{6,7},{7,6},{8,9},{9,8},{10,11... | collective-permute-start | bytes 786440 | tf_op jit(solution)/shard_map/ppermute | solution.py:24
  74.6 16.8 %collective-permute-start.18 = (bf16[2,1,512,128]{3,2,1,0:T(8,128)(2,1)}, bf16[2,1,512,128]{3,2,1,0:T(8,128)(2,1)}, u32[]{:S(2)}, u32[]{:S(2)}) collective-permute-start(bf16[2,1,512,128]{3,2,1,0:T(8,128)(2,1)} %pad_maximum_fusion.11), channel_id=1, source_target_pairs={{0,1},{1,0},{2,3},{3,2},{4,5},{5,4},{6,7},{7,6},{8,9},{9,8},{10,11... | collective-permute-start | bytes 786440 | tf_op jit(solution)/shard_map/ppermute | solution.py:24
  79.0 14.7 %collective-permute-start.12 = (bf16[2,512,256]{2,1,0:T(8,128)(2,1)S(1)}, bf16[2,512,256]{2,1,0:T(8,128)(2,1)S(1)}, u32[]{:S(2)}, u32[]{:S(2)}) collective-permute-start(bf16[2,512,256]{2,1,0:T(8,128)(2,1)S(1)} %pad_maximum_fusion.5), channel_id=1, source_target_pairs={{0,1},{1,0},{2,3},{3,2},{4,5},{5,4},{6,7},{7,6},{8,9},{9,8},{10,11... | collective-permute-start | bytes 1572872 | tf_op jit(solution)/shard_map/ppermute | solution.py:24
  96.9 17.9 %collective-permute-start.24 = (bf16[512,256]{1,0:T(8,128)(2,1)S(1)}, bf16[512,256]{1,0:T(8,128)(2,1)S(1)}, u32[]{:S(2)}, u32[]{:S(2)}) collective-permute-start(bf16[512,256]{1,0:T(8,128)(2,1)S(1)} %fusion.59), channel_id=1, source_target_pairs={{0,24},{8,16},{16,8},{24,0},{1,25},{9,17},{17,9},{25,1},{2,26},{10... | collective-permute-start | bytes 786440 | tf_op jit(solution)/shard_map/ppermute | solution.py:24
  98.8 17.3 %collective-permute-start.23 = (bf16[512,256]{1,0:T(8,128)(2,1)S(1)}, bf16[512,256]{1,0:T(8,128)(2,1)S(1)}, u32[]{:S(2)}, u32[]{:S(2)}) collective-permute-start(bf16[512,256]{1,0:T(8,128)(2,1)S(1)} %fusion.59), channel_id=1, source_target_pairs={{0,16},{8,24},{16,0},{24,8},{1,17},{9,25},{17,1},{25,9},{2,18},{10... | collective-permute-start | bytes 786440 | tf_op jit(solution)/shard_map/ppermute | solution.py:24
  99.1 18.7 %collective-permute-start.22 = (bf16[512,256]{1,0:T(8,128)(2,1)S(1)}, bf16[512,256]{1,0:T(8,128)(2,1)S(1)}, u32[]{:S(2)}, u32[]{:S(2)}) collective-permute-start(bf16[512,256]{1,0:T(8,128)(2,1)S(1)} %fusion.59), channel_id=1, source_target_pairs={{0,8},{8,0},{16,24},{24,16},{1,9},{9,1},{17,25},{25,17},{2,10},{10... | collective-permute-start | bytes 786440 | tf_op jit(solution)/shard_map/ppermute | solution.py:24
  99.6 11.6 %collective-permute-start.28 = (bf16[512,128]{1,0:T(8,128)(2,1)S(1)}, bf16[512,128]{1,0:T(8,128)(2,1)S(1)}, u32[]{:S(2)}, u32[]{:S(2)}) collective-permute-start(bf16[512,128]{1,0:T(8,128)(2,1)S(1)} %get-tuple-element.11), channel_id=1, source_target_pairs={{0,4},{1,5},{2,6},{3,7},{4,0},{5,1},{6,2},{7,3},{8,12},{9,13},{10,... | collective-permute-start | bytes 393224 | tf_op jit(solution)/shard_map/ppermute | solution.py:24
  100.5 13.4 %collective-permute-start.27 = (bf16[512,128]{1,0:T(8,128)(2,1)S(1)}, bf16[512,128]{1,0:T(8,128)(2,1)S(1)}, u32[]{:S(2)}, u32[]{:S(2)}) collective-permute-start(bf16[512,128]{1,0:T(8,128)(2,1)S(1)} %get-tuple-element.10), channel_id=1, source_target_pairs={{0,4},{1,5},{2,6},{3,7},{4,0},{5,1},{6,2},{7,3},{8,12},{9,13},{10,... | collective-permute-start | bytes 393224 | tf_op jit(solution)/shard_map/ppermute | solution.py:24
  111.2 7.6 %collective-permute-start.25 = (bf16[512,256]{1,0:T(8,128)(2,1)S(1)}, bf16[512,256]{1,0:T(8,128)(2,1)S(1)}, u32[]{:S(2)}, u32[]{:S(2)}) collective-permute-start(bf16[512,256]{1,0:T(8,128)(2,1)S(1)} %fusion.59), channel_id=1, source_target_pairs={{0,2},{1,3},{2,0},{3,1},{4,6},{5,7},{6,4},{7,5},{8,10},{9,11},{10,... | collective-permute-start | bytes 786440 | tf_op jit(solution)/shard_map/ppermute | solution.py:24
  114.0 8.4 %copy-start.16 = (bf16[512,128]{1,0:T(8,128)(2,1)}, bf16[512,128]{1,0:T(8,128)(2,1)S(1)}, u32[]{:S(2)}) copy-start(bf16[512,128]{1,0:T(8,128)(2,1)S(1)} %collective-permute-done.27) | copy-start | bytes 393220
  114.0 8.6 %collective-permute-start.31 = (bf16[1,512,128]{2,1,0:T(8,128)(2,1)S(1)}, bf16[1,512,128]{2,1,0:T(8,128)(2,1)S(1)}, u32[]{:S(2)}, u32[]{:S(2)}) collective-permute-start(bf16[1,512,128]{2,1,0:T(8,128)(2,1)S(1)} %bitcast.393), channel_id=1, source_target_pairs={{0,2},{1,3},{2,0},{3,1},{4,6},{5,7},{6,4},{7,5},{8,10},{9,11},{10,... | collective-permute-start | bytes 393224 | tf_op jit(solution)/shard_map/ppermute | solution.py:24
  114.7 9.8 %collective-permute-start.30 = (bf16[1,512,128]{2,1,0:T(8,128)(2,1)S(1)}, bf16[1,512,128]{2,1,0:T(8,128)(2,1)}, u32[]{:S(2)}, u32[]{:S(2)}) collective-permute-start(bf16[1,512,128]{2,1,0:T(8,128)(2,1)S(1)} %bitcast.396), channel_id=1, source_target_pairs={{0,2},{1,3},{2,0},{3,1},{4,6},{5,7},{6,4},{7,5},{8,10},{9,11},{10,... | collective-permute-start | bytes 393224 | tf_op jit(solution)/shard_map/ppermute | solution.py:24
  116.2 12.4 %collective-permute-start.29 = (bf16[2,512,128]{2,1,0:T(8,128)(2,1)}, bf16[2,512,128]{2,1,0:T(8,128)(2,1)}, u32[]{:S(2)}, u32[]{:S(2)}) collective-permute-start(bf16[2,512,128]{2,1,0:T(8,128)(2,1)} %pad_maximum_fusion.12), channel_id=1, source_target_pairs={{0,1},{1,0},{2,3},{3,2},{4,5},{5,4},{6,7},{7,6},{8,9},{9,8},{10,11... | collective-permute-start | bytes 786440 | tf_op jit(solution)/shard_map/ppermute | solution.py:24
  118.8 12.9 %collective-permute-start.26 = (bf16[2,512,256]{2,1,0:T(8,128)(2,1)S(1)}, bf16[2,512,256]{2,1,0:T(8,128)(2,1)S(1)}, u32[]{:S(2)}, u32[]{:S(2)}) collective-permute-start(bf16[2,512,256]{2,1,0:T(8,128)(2,1)S(1)} %pad_maximum_fusion.6), channel_id=1, source_target_pairs={{0,1},{1,0},{2,3},{3,2},{4,5},{5,4},{6,7},{7,6},{8,9},{9,8},{10,11... | collective-permute-start | bytes 1572872 | tf_op jit(solution)/shard_map/ppermute | solution.py:24
  122.6 4.6 %copy-start.21 = (bf16[1,512,128]{2,1,0:T(8,128)(2,1)}, bf16[1,512,128]{2,1,0:T(8,128)(2,1)S(1)}, u32[]{:S(2)}) copy-start(bf16[1,512,128]{2,1,0:T(8,128)(2,1)S(1)} %collective-permute-done.31) | copy-start | bytes 393220
  125.4 5.4 %collective-permute-start.32 = (bf16[2,1,512,128]{3,2,1,0:T(8,128)(2,1)S(1)}, bf16[2,1,512,128]{3,2,1,0:T(8,128)(2,1)S(1)}, u32[]{:S(2)}, u32[]{:S(2)}) collective-permute-start(bf16[2,1,512,128]{3,2,1,0:T(8,128)(2,1)S(1)} %pad_maximum_fusion.13), channel_id=1, source_target_pairs={{0,1},{1,0},{2,3},{3,2},{4,5},{5,4},{6,7},{7,6},{8,9},{9,8},{10,11... | collective-permute-start | bytes 786440 | tf_op jit(solution)/shard_map/ppermute | solution.py:24
  134.0 22.0 %collective-permute-start.43 = (bf16[512,256]{1,0:T(8,128)(2,1)S(1)}, bf16[512,256]{1,0:T(8,128)(2,1)S(1)}, u32[]{:S(2)}, u32[]{:S(2)}) collective-permute-start(bf16[512,256]{1,0:T(8,128)(2,1)S(1)} %get-tuple-element.18), channel_id=1, source_target_pairs={{0,24},{8,16},{16,8},{24,0},{1,25},{9,17},{17,9},{25,1},{2,26},{10... | collective-permute-start | bytes 786440 | tf_op jit(solution)/shard_map/ppermute | solution.py:24
  136.0 20.1 %collective-permute-start.42 = (bf16[512,256]{1,0:T(8,128)(2,1)S(1)}, bf16[512,256]{1,0:T(8,128)(2,1)S(1)}, u32[]{:S(2)}, u32[]{:S(2)}) collective-permute-start(bf16[512,256]{1,0:T(8,128)(2,1)S(1)} %get-tuple-element.18), channel_id=1, source_target_pairs={{0,16},{8,24},{16,0},{24,8},{1,17},{9,25},{17,1},{25,9},{2,18},{10... | collective-permute-start | bytes 786440 | tf_op jit(solution)/shard_map/ppermute | solution.py:24
  136.2 25.1 %collective-permute-start.41 = (bf16[512,256]{1,0:T(8,128)(2,1)S(1)}, bf16[512,256]{1,0:T(8,128)(2,1)S(1)}, u32[]{:S(2)}, u32[]{:S(2)}) collective-permute-start(bf16[512,256]{1,0:T(8,128)(2,1)S(1)} %get-tuple-element.18), channel_id=1, source_target_pairs={{0,8},{8,0},{16,24},{24,16},{1,9},{9,1},{17,25},{25,17},{2,10},{10... | collective-permute-start | bytes 786440 | tf_op jit(solution)/shard_map/ppermute | solution.py:24
  136.7 27.9 %collective-permute-start.33 = (bf16[512,256]{1,0:T(8,128)(2,1)S(1)}, bf16[512,256]{1,0:T(8,128)(2,1)}, u32[]{:S(2)}, u32[]{:S(2)}) collective-permute-start(bf16[512,256]{1,0:T(8,128)(2,1)S(1)} %get-tuple-element.18), channel_id=1, source_target_pairs={{0,2},{1,3},{2,0},{3,1},{4,6},{5,7},{6,4},{7,5},{8,10},{9,11},{10,... | collective-permute-start | bytes 786440 | tf_op jit(solution)/shard_map/ppermute | solution.py:24
  136.8 7.9 %collective-permute-start.36 = (bf16[512,128]{1,0:T(8,128)(2,1)S(1)}, bf16[512,128]{1,0:T(8,128)(2,1)}, u32[]{:S(2)}, u32[]{:S(2)}) collective-permute-start(bf16[512,128]{1,0:T(8,128)(2,1)S(1)} %get-tuple-element.9), channel_id=1, source_target_pairs={{0,4},{1,5},{2,6},{3,7},{4,0},{5,1},{6,2},{7,3},{8,12},{9,13},{10,... | collective-permute-start | bytes 393224 | tf_op jit(solution)/shard_map/ppermute | solution.py:24
  144.7 5.7 %collective-permute-start.35 = (bf16[512,128]{1,0:T(8,128)(2,1)S(1)}, bf16[512,128]{1,0:T(8,128)(2,1)}, u32[]{:S(2)}, u32[]{:S(2)}) collective-permute-start(bf16[512,128]{1,0:T(8,128)(2,1)S(1)} %get-tuple-element.8), channel_id=1, source_target_pairs={{0,4},{1,5},{2,6},{3,7},{4,0},{5,1},{6,2},{7,3},{8,12},{9,13},{10,... | collective-permute-start | bytes 393224 | tf_op jit(solution)/shard_map/ppermute | solution.py:24
  150.4 23.0 %collective-permute-start.39 = (bf16[1,512,128]{2,1,0:T(8,128)(2,1)}, bf16[1,512,128]{2,1,0:T(8,128)(2,1)}, u32[]{:S(2)}, u32[]{:S(2)}) collective-permute-start(bf16[1,512,128]{2,1,0:T(8,128)(2,1)} %bitcast.96), channel_id=1, source_target_pairs={{0,2},{1,3},{2,0},{3,1},{4,6},{5,7},{6,4},{7,5},{8,10},{9,11},{10,... | collective-permute-start | bytes 393224 | tf_op jit(solution)/shard_map/ppermute | solution.py:24
  156.0 17.3 %collective-permute-start.38 = (bf16[1,512,128]{2,1,0:T(8,128)(2,1)}, bf16[1,512,128]{2,1,0:T(8,128)(2,1)}, u32[]{:S(2)}, u32[]{:S(2)}) collective-permute-start(bf16[1,512,128]{2,1,0:T(8,128)(2,1)} %bitcast.95), channel_id=1, source_target_pairs={{0,2},{1,3},{2,0},{3,1},{4,6},{5,7},{6,4},{7,5},{8,10},{9,11},{10,... | collective-permute-start | bytes 393224 | tf_op jit(solution)/shard_map/ppermute | solution.py:24
  156.0 21.1 %collective-permute-start.37 = (bf16[2,512,128]{2,1,0:T(8,128)(2,1)}, bf16[2,512,128]{2,1,0:T(8,128)(2,1)}, u32[]{:S(2)}, u32[]{:S(2)}) collective-permute-start(bf16[2,512,128]{2,1,0:T(8,128)(2,1)} %pad_maximum_fusion.14), channel_id=1, source_target_pairs={{0,1},{1,0},{2,3},{3,2},{4,5},{5,4},{6,7},{7,6},{8,9},{9,8},{10,11... | collective-permute-start | bytes 786440 | tf_op jit(solution)/shard_map/ppermute | solution.py:24
  165.7 14.2 %collective-permute-start.34 = (bf16[2,512,256]{2,1,0:T(8,128)(2,1)S(1)}, bf16[2,512,256]{2,1,0:T(8,128)(2,1)S(1)}, u32[]{:S(2)}, u32[]{:S(2)}) collective-permute-start(bf16[2,512,256]{2,1,0:T(8,128)(2,1)S(1)} %pad_maximum_fusion.7), channel_id=1, source_target_pairs={{0,1},{1,0},{2,3},{3,2},{4,5},{5,4},{6,7},{7,6},{8,9},{9,8},{10,11... | collective-permute-start | bytes 1572872 | tf_op jit(solution)/shard_map/ppermute | solution.py:24
  174.3 5.0 %collective-permute-start.40 = (bf16[2,1,512,128]{3,2,1,0:T(8,128)(2,1)S(1)}, bf16[2,1,512,128]{3,2,1,0:T(8,128)(2,1)S(1)}, u32[]{:S(2)}, u32[]{:S(2)}) collective-permute-start(bf16[2,1,512,128]{3,2,1,0:T(8,128)(2,1)S(1)} %pad_maximum_fusion.15), channel_id=1, source_target_pairs={{0,1},{1,0},{2,3},{3,2},{4,5},{5,4},{6,7},{7,6},{8,9},{9,8},{10,11... | collective-permute-start | bytes 786440 | tf_op jit(solution)/shard_map/ppermute | solution.py:24
  (23 other events, 28.2 us)

commit v8 on v6

--- a/solution.py
+++ b/solution.py
@@ -37,11 +37,12 @@
         other[s] = relay_first[i]
     forward = list(range(2, chips, 2))
     if forward:
-        sent = xor_permute(jnp.stack([same[s] for s in forward]), "col", n_col, 2)
-        relay_sent = xor_permute(sent, "col", n_col, 1)
+        held = jnp.stack([same[s] for s in forward])
+        sent = xor_permute(held, "col", n_col, 2)
+        sent_other = xor_permute(held, "col", n_col, 3)
         for i, s in enumerate(forward):
             same[s ^ 1] = sent[i]
-            other[s ^ 1] = relay_sent[i]
+            other[s ^ 1] = sent_other[i]
     row_pieces = []
     for s in range(chips):
         row_pieces.append(same[s])

time: 124 us -> 140 us (1.13)
  matrix products: 28.5 us -> 36.2 us
  waiting for transfers between devices: 43.1 us -> 47.3 us
  local copies, waits for them, and re-layouts: 8.68 us -> 11.6 us
    dot_general x48, matrix products: 28.5 us -> 36.2 us  [contract(): part = jnp.dot(piece, k_blocks[s], preferred_element_type=jnp.float32)]
    ppermute x32, waiting for transfers between devices: 43.1 us -> 47.3 us  [xor_permute(): return lax.ppermute(x, axis, perm=[(i, i ^ s) for i in range(size)])]
    unnamed x33 -> x27, local copies, waits for them, and re-layouts: 3.57 us -> 6.49 us
  transfers between devices with their start and end apart: 32 -> 32, of which waited for: 11 -> 10; matrix products, arithmetic and copies ran while one was open for 30% -> 26% of each run, Pallas kernels for 0% -> 0%
where the time goes in v8:
time: 140 us; the launch traced here: 139 us
  waiting for transfers between devices  47.3 us (34%)
  starting transfers between devices  36.6 us (26%)
  matrix products  36.2 us (26%)
  local copies, waits for them, and re-layouts  11.6 us (8%)
  other arithmetic  6.69 us (5%)
    ppermute x32, waiting for transfers between devices, xor_permute(): return lax.ppermute(x, axis, perm=[(i, i ^ s) for i in range(size)])  47.3 us
    ppermute x32, starting transfers between devices, xor_permute(): return lax.ppermute(x, axis, perm=[(i, i ^ s) for i in range(size)])  36.6 us
    dot_general x48, matrix products, contract(): part = jnp.dot(piece, k_blocks[s], preferred_element_type=jnp.float32)  36.2 us
    unnamed x27, local copies, waits for them, and re-layouts  6.49 us
    gather x4, local copies, waits for them, and re-layouts, ordered_k_blocks(): return jnp.take(split, index, axis=0)  4.9 us
    another operation x4, other arithmetic, exchange(): jnp.stack([same[s] for s in first])  3.32 us
  transfers between devices with their start and end apart: 32, of which 10 were waited for; matrix products, arithmetic and copies ran while one was open for 26% of the time, Pallas kernels for 0%

profile of v8, /device:TPU:1, one launch (start us, length us, event | category | flops | bytes accessed | tf_op | source)
XLA Modules:
  0.0 139.1 jit_solution(14357327172445109970)
XLA Ops:
  1.2 3.2 %collective-permute-start.4 = (bf16[512,256]{1,0:T(8,128)(2,1)S(1)}, bf16[512,256]{1,0:T(8,128)(2,1)S(1)}, u32[]{:S(2)}, u32[]{:S(2)}) collective-permute-start(bf16[512,256]{1,0:T(8,128)(2,1)S(1)} %fusion.34), channel_id=1, source_target_pairs={{0,4},{1,5},{2,6},{3,7},{4,0},{5,1},{6,2},{7,3},{8,12},{9,13},{10,... | collective-permute-start | bytes 786440 | tf_op jit(solution)/shard_map/ppermute | solution.py:24
  4.4 1.3 collective-permute-start.3
  5.7 2.2 %collective-permute-start.2 = (bf16[512,256]{1,0:T(8,128)(2,1)S(1)}, bf16[512,256]{1,0:T(8,128)(2,1)S(1)}, u32[]{:S(2)}, u32[]{:S(2)}) collective-permute-start(bf16[512,256]{1,0:T(8,128)(2,1)S(1)} %fusion.34), channel_id=1, source_target_pairs={{0,24},{8,16},{16,8},{24,0},{1,25},{9,17},{17,9},{25,1},{2,26},{10... | collective-permute-start | bytes 786440 | tf_op jit(solution)/shard_map/ppermute | solution.py:24
  8.3 7.7 %collective-permute-done.4 = bf16[512,256]{1,0:T(8,128)(2,1)S(1)} collective-permute-done((bf16[512,256]{1,0:T(8,128)(2,1)S(1)}, bf16[512,256]{1,0:T(8,128)(2,1)S(1)}, u32[]{:S(2)}, u32[]{:S(2)}) %collective-permute-start.4) | collective-permute-done | bytes 262176 | tf_op jit(solution)/shard_map/ppermute | solution.py:24
  16.1 1.5 %collective-permute-start.7 = (bf16[1,512,256]{2,1,0:T(8,128)(2,1)S(1)}, bf16[1,512,256]{2,1,0:T(8,128)(2,1)}, u32[]{:S(2)}, u32[]{:S(2)}) collective-permute-start(bf16[1,512,256]{2,1,0:T(8,128)(2,1)S(1)} %bitcast.271), channel_id=1, source_target_pairs={{0,3},{1,2},{2,1},{3,0},{4,7},{5,6},{6,5},{7,4},{8,11},{9,10},{10,... | collective-permute-start | bytes 786440 | tf_op jit(solution)/shard_map/ppermute | solution.py:24
  21.9 2.6 %collective-permute-done.7 = bf16[1,512,256]{2,1,0:T(8,128)(2,1)} collective-permute-done((bf16[1,512,256]{2,1,0:T(8,128)(2,1)S(1)}, bf16[1,512,256]{2,1,0:T(8,128)(2,1)}, u32[]{:S(2)}, u32[]{:S(2)}) %collective-permute-start.7) | collective-permute-done | bytes 262176 | tf_op jit(solution)/shard_map/ppermute | solution.py:24
  24.5 1.2 fusion.58
  25.7 4.7 %collective-permute-done.6 = bf16[1,512,256]{2,1,0:T(8,128)(2,1)} collective-permute-done((bf16[1,512,256]{2,1,0:T(8,128)(2,1)S(1)}, bf16[1,512,256]{2,1,0:T(8,128)(2,1)}, u32[]{:S(2)}, u32[]{:S(2)}) %collective-permute-start.6) | collective-permute-done | bytes 262176 | tf_op jit(solution)/shard_map/ppermute | solution.py:24
  30.4 1.2 fusion.62
  31.6 1.2 fusion.67
  32.7 1.2 fusion.65
  33.9 1.2 convolution_add_fusion.11
  36.2 1.9 %collective-permute-start.9 = (bf16[512,256]{1,0:T(8,128)(2,1)S(1)}, bf16[512,256]{1,0:T(8,128)(2,1)}, u32[]{:S(2)}, u32[]{:S(2)}) collective-permute-start(bf16[512,256]{1,0:T(8,128)(2,1)S(1)} %get-tuple-element.8), channel_id=1, source_target_pairs={{0,4},{1,5},{2,6},{3,7},{4,0},{5,1},{6,2},{7,3},{8,12},{9,13},{10,... | collective-permute-start | bytes 786440 | tf_op jit(solution)/shard_map/ppermute | solution.py:24
  38.1 2.2 %collective-permute-start.15 = (bf16[512,256]{1,0:T(8,128)(2,1)S(1)}, bf16[512,256]{1,0:T(8,128)(2,1)S(1)}, u32[]{:S(2)}, u32[]{:S(2)}) collective-permute-start(bf16[512,256]{1,0:T(8,128)(2,1)S(1)} %get-tuple-element.8), channel_id=1, source_target_pairs={{0,24},{8,16},{16,8},{24,0},{1,25},{9,17},{17,9},{25,1},{2,26},{10... | collective-permute-start | bytes 786440 | tf_op jit(solution)/shard_map/ppermute | solution.py:24
  40.7 2.3 %collective-permute-start.8 = (bf16[512,256]{1,0:T(8,128)(2,1)S(1)}, bf16[512,256]{1,0:T(8,128)(2,1)}, u32[]{:S(2)}, u32[]{:S(2)}) collective-permute-start(bf16[512,256]{1,0:T(8,128)(2,1)S(1)} %get-tuple-element.8), channel_id=1, source_target_pairs={{0,2},{1,3},{2,0},{3,1},{4,6},{5,7},{6,4},{7,5},{8,10},{9,11},{10,... | collective-permute-start | bytes 786440 | tf_op jit(solution)/shard_map/ppermute | solution.py:24
  44.1 6.5 %collective-permute-done.9 = bf16[512,256]{1,0:T(8,128)(2,1)} collective-permute-done((bf16[512,256]{1,0:T(8,128)(2,1)S(1)}, bf16[512,256]{1,0:T(8,128)(2,1)}, u32[]{:S(2)}, u32[]{:S(2)}) %collective-permute-start.9) | collective-permute-done | bytes 262176 | tf_op jit(solution)/shard_map/ppermute | solution.py:24
  51.3 1.7 %collective-permute-start.11 = (bf16[1,512,256]{2,1,0:T(8,128)(2,1)}, bf16[1,512,256]{2,1,0:T(8,128)(2,1)}, u32[]{:S(2)}, u32[]{:S(2)}) collective-permute-start(bf16[1,512,256]{2,1,0:T(8,128)(2,1)} %bitcast.23), channel_id=1, source_target_pairs={{0,2},{1,3},{2,0},{3,1},{4,6},{5,7},{6,4},{7,5},{8,10},{9,11},{10,... | collective-permute-start | bytes 786440 | tf_op jit(solution)/shard_map/ppermute | solution.py:24
  53.0 1.1 pad_maximum_fusion.1
  54.2 1.8 %gather_fusion.1 = bf16[8,256,256]{2,1,0:T(8,128)(2,1)S(1)} fusion(bf16[8,256,256]{2,1,0:T(8,128)(2,1)} %bitcast.264, s32[1024]{0:T(1024)S(1)} %pad_clamp_fusion), kind=kCustom, calls=%fused_computation.1.clone | custom fusion | bytes 2097184 | tf_op jit(solution)/shard_map/jit(_take)/gather | solution.py:60
  58.0 1.2 fusion.56
  59.2 1.2 fusion.60
  60.4 1.2 fusion.66
  61.8 1.2 fusion.64
  63.0 1.2 convolution_add_fusion.7
  64.5 1.2 fusion.78
  65.7 1.2 fusion.52
  66.9 1.2 fusion.54
  70.4 1.3 fusion.35
  71.7 1.7 %collective-permute-start.20 = (bf16[512,256]{1,0:T(8,128)(2,1)S(1)}, bf16[512,256]{1,0:T(8,128)(2,1)S(1)}, u32[]{:S(2)}, u32[]{:S(2)}) collective-permute-start(bf16[512,256]{1,0:T(8,128)(2,1)S(1)} %fusion.35), channel_id=1, source_target_pairs={{0,4},{1,5},{2,6},{3,7},{4,0},{5,1},{6,2},{7,3},{8,12},{9,13},{10,... | collective-permute-start | bytes 786440 | tf_op jit(solution)/shard_map/ppermute | solution.py:24
  73.4 2.2 %collective-permute-start.18 = (bf16[512,256]{1,0:T(8,128)(2,1)S(1)}, bf16[512,256]{1,0:T(8,128)(2,1)S(1)}, u32[]{:S(2)}, u32[]{:S(2)}) collective-permute-start(bf16[512,256]{1,0:T(8,128)(2,1)S(1)} %fusion.35), channel_id=1, source_target_pairs={{0,24},{8,16},{16,8},{24,0},{1,25},{9,17},{17,9},{25,1},{2,26},{10... | collective-permute-start | bytes 786440 | tf_op jit(solution)/shard_map/ppermute | solution.py:24
  76.0 1.3 collective-permute-start.19
  77.3 8.9 %collective-permute-done.20 = bf16[512,256]{1,0:T(8,128)(2,1)S(1)} collective-permute-done((bf16[512,256]{1,0:T(8,128)(2,1)S(1)}, bf16[512,256]{1,0:T(8,128)(2,1)S(1)}, u32[]{:S(2)}, u32[]{:S(2)}) %collective-permute-start.20) | collective-permute-done | bytes 262176 | tf_op jit(solution)/shard_map/ppermute | solution.py:24
  86.6 1.8 %collective-permute-start.22 = (bf16[1,512,256]{2,1,0:T(8,128)(2,1)S(1)}, bf16[1,512,256]{2,1,0:T(8,128)(2,1)}, u32[]{:S(2)}, u32[]{:S(2)}) collective-permute-start(bf16[1,512,256]{2,1,0:T(8,128)(2,1)S(1)} %bitcast.275), channel_id=1, source_target_pairs={{0,2},{1,3},{2,0},{3,1},{4,6},{5,7},{6,4},{7,5},{8,10},{9,11},{10,... | collective-permute-start | bytes 786440 | tf_op jit(solution)/shard_map/ppermute | solution.py:24
  90.8 4.1 %collective-permute-done.23 = bf16[1,512,256]{2,1,0:T(8,128)(2,1)} collective-permute-done((bf16[1,512,256]{2,1,0:T(8,128)(2,1)S(1)}, bf16[1,512,256]{2,1,0:T(8,128)(2,1)}, u32[]{:S(2)}, u32[]{:S(2)}) %collective-permute-start.23) | collective-permute-done | bytes 262176 | tf_op jit(solution)/shard_map/ppermute | solution.py:24
  95.0 1.2 fusion.46
  96.1 4.4 %collective-permute-done.22 = bf16[1,512,256]{2,1,0:T(8,128)(2,1)} collective-permute-done((bf16[1,512,256]{2,1,0:T(8,128)(2,1)S(1)}, bf16[1,512,256]{2,1,0:T(8,128)(2,1)}, u32[]{:S(2)}, u32[]{:S(2)}) %collective-permute-start.22) | collective-permute-done | bytes 262176 | tf_op jit(solution)/shard_map/ppermute | solution.py:24
  100.6 1.2 fusion.50
  105.7 1.9 %collective-permute-start.31 = (bf16[512,256]{1,0:T(8,128)(2,1)S(1)}, bf16[512,256]{1,0:T(8,128)(2,1)S(1)}, u32[]{:S(2)}, u32[]{:S(2)}) collective-permute-start(bf16[512,256]{1,0:T(8,128)(2,1)S(1)} %get-tuple-element.10), channel_id=1, source_target_pairs={{0,24},{8,16},{16,8},{24,0},{1,25},{9,17},{17,9},{25,1},{2,26},{10... | collective-permute-start | bytes 786440 | tf_op jit(solution)/shard_map/ppermute | solution.py:24
  108.4 2.3 %collective-permute-start.24 = (bf16[512,256]{1,0:T(8,128)(2,1)S(1)}, bf16[512,256]{1,0:T(8,128)(2,1)}, u32[]{:S(2)}, u32[]{:S(2)}) collective-permute-start(bf16[512,256]{1,0:T(8,128)(2,1)S(1)} %get-tuple-element.10), channel_id=1, source_target_pairs={{0,2},{1,3},{2,0},{3,1},{4,6},{5,7},{6,4},{7,5},{8,10},{9,11},{10,... | collective-permute-start | bytes 786440 | tf_op jit(solution)/shard_map/ppermute | solution.py:24
  111.7 7.2 %collective-permute-done.25 = bf16[512,256]{1,0:T(8,128)(2,1)} collective-permute-done((bf16[512,256]{1,0:T(8,128)(2,1)S(1)}, bf16[512,256]{1,0:T(8,128)(2,1)}, u32[]{:S(2)}, u32[]{:S(2)}) %collective-permute-start.25) | collective-permute-done | bytes 262176 | tf_op jit(solution)/shard_map/ppermute | solution.py:24
  119.0 2.5 %collective-permute-start.27 = (bf16[1,512,256]{2,1,0:T(8,128)(2,1)}, bf16[1,512,256]{2,1,0:T(8,128)(2,1)}, u32[]{:S(2)}, u32[]{:S(2)}) collective-permute-start(bf16[1,512,256]{2,1,0:T(8,128)(2,1)} %bitcast.63), channel_id=1, source_target_pairs={{0,2},{1,3},{2,0},{3,1},{4,6},{5,7},{6,4},{7,5},{8,10},{9,11},{10,... | collective-permute-start | bytes 786440 | tf_op jit(solution)/shard_map/ppermute | solution.py:24
  122.7 1.8 %gather_fusion.3 = bf16[8,256,256]{2,1,0:T(8,128)(2,1)S(1)} fusion(bf16[8,256,256]{2,1,0:T(8,128)(2,1)} %bitcast.262, s32[1024]{0:T(1024)S(1)} %pad_clamp_fusion), kind=kCustom, calls=%fused_computation.3.clone | custom fusion | bytes 2097184 | tf_op jit(solution)/shard_map/jit(_take)/gather | solution.py:60
  126.1 1.2 fusion.44
  127.4 1.2 fusion.48
  130.5 1.2 fusion.82
  131.7 1.2 fusion.40
  133.5 1.2 fusion.42
  137.0 2.1 %bitcast_multiply_fusion = f32[512,256]{1,0:T(8,128)} fusion(f32[512,256]{1,0:T(8,128)S(1)} %copy-done.9, f32[64,8,2,128]{3,2,1,0:T(2,128)S(1)} %bitcast.257, f32[512,256]{1,0:T(8,128)S(1)} %fusion.4, f32[512,256]{1,0:T(8,128)S(1)} %fusion.40, f32[512,256]{1,0:T(8,128)S(1)} %fusion.42, f32[512,256]{1,0:T(8,128)S(1)} %fusion.36, f32[512,256]{1,0:T(8,128)S(1)} %fusion.82, ...), kind=kOutput, calls=%fused_computation.62 | convolution fusion | flops 68419584 | bytes 5636096 | tf_op jit(solution)/shard_map/dot_general | solution.py:66
  (112 shorter events, 30.7 us)
Async XLA Ops:
  0.0 0.7 copy-start.12
  0.0 1.1 copy-start.11
  1.2 14.9 %collective-permute-start.4 = (bf16[512,256]{1,0:T(8,128)(2,1)S(1)}, bf16[512,256]{1,0:T(8,128)(2,1)S(1)}, u32[]{:S(2)}, u32[]{:S(2)}) collective-permute-start(bf16[512,256]{1,0:T(8,128)(2,1)S(1)} %fusion.34), channel_id=1, source_target_pairs={{0,4},{1,5},{2,6},{3,7},{4,0},{5,1},{6,2},{7,3},{8,12},{9,13},{10,... | collective-permute-start | bytes 786440 | tf_op jit(solution)/shard_map/ppermute | solution.py:24
  4.4 13.2 %collective-permute-start.3 = (bf16[512,256]{1,0:T(8,128)(2,1)S(1)}, bf16[512,256]{1,0:T(8,128)(2,1)S(1)}, u32[]{:S(2)}, u32[]{:S(2)}) collective-permute-start(bf16[512,256]{1,0:T(8,128)(2,1)S(1)} %fusion.34), channel_id=1, source_target_pairs={{0,2},{1,3},{2,0},{3,1},{4,6},{5,7},{6,4},{7,5},{8,10},{9,11},{10,... | collective-permute-start | bytes 786440 | tf_op jit(solution)/shard_map/ppermute | solution.py:24
  5.7 14.0 %collective-permute-start.2 = (bf16[512,256]{1,0:T(8,128)(2,1)S(1)}, bf16[512,256]{1,0:T(8,128)(2,1)S(1)}, u32[]{:S(2)}, u32[]{:S(2)}) collective-permute-start(bf16[512,256]{1,0:T(8,128)(2,1)S(1)} %fusion.34), channel_id=1, source_target_pairs={{0,24},{8,16},{16,8},{24,0},{1,25},{9,17},{17,9},{25,1},{2,26},{10... | collective-permute-start | bytes 786440 | tf_op jit(solution)/shard_map/ppermute | solution.py:24
  7.8 12.7 %collective-permute-start.1 = (bf16[512,256]{1,0:T(8,128)(2,1)S(1)}, bf16[512,256]{1,0:T(8,128)(2,1)S(1)}, u32[]{:S(2)}, u32[]{:S(2)}) collective-permute-start(bf16[512,256]{1,0:T(8,128)(2,1)S(1)} %fusion.34), channel_id=1, source_target_pairs={{0,16},{8,24},{16,0},{24,8},{1,17},{9,25},{17,1},{25,9},{2,18},{10... | collective-permute-start | bytes 786440 | tf_op jit(solution)/shard_map/ppermute | solution.py:24
  8.0 12.5 %collective-permute-start = (bf16[512,256]{1,0:T(8,128)(2,1)S(1)}, bf16[512,256]{1,0:T(8,128)(2,1)S(1)}, u32[]{:S(2)}, u32[]{:S(2)}) collective-permute-start(bf16[512,256]{1,0:T(8,128)(2,1)S(1)} %fusion.34), channel_id=1, source_target_pairs={{0,8},{8,0},{16,24},{24,16},{1,9},{9,1},{17,25},{25,17},{2,10},{10... | collective-permute-start | bytes 786440 | tf_op jit(solution)/shard_map/ppermute | solution.py:24
  16.1 5.6 %copy-start.2 = (bf16[512,256]{1,0:T(8,128)(2,1)}, bf16[512,256]{1,0:T(8,128)(2,1)S(1)}, u32[]{:S(2)}) copy-start(bf16[512,256]{1,0:T(8,128)(2,1)S(1)} %collective-permute-done.4) | copy-start | bytes 786436
  16.1 8.5 %collective-permute-start.7 = (bf16[1,512,256]{2,1,0:T(8,128)(2,1)S(1)}, bf16[1,512,256]{2,1,0:T(8,128)(2,1)}, u32[]{:S(2)}, u32[]{:S(2)}) collective-permute-start(bf16[1,512,256]{2,1,0:T(8,128)(2,1)S(1)} %bitcast.271), channel_id=1, source_target_pairs={{0,3},{1,2},{2,1},{3,0},{4,7},{5,6},{6,5},{7,4},{8,11},{9,10},{10,... | collective-permute-start | bytes 786440 | tf_op jit(solution)/shard_map/ppermute | solution.py:24
  17.6 12.8 %collective-permute-start.6 = (bf16[1,512,256]{2,1,0:T(8,128)(2,1)S(1)}, bf16[1,512,256]{2,1,0:T(8,128)(2,1)}, u32[]{:S(2)}, u32[]{:S(2)}) collective-permute-start(bf16[1,512,256]{2,1,0:T(8,128)(2,1)S(1)} %bitcast.272), channel_id=1, source_target_pairs={{0,2},{1,3},{2,0},{3,1},{4,6},{5,7},{6,4},{7,5},{8,10},{9,11},{10,... | collective-permute-start | bytes 786440 | tf_op jit(solution)/shard_map/ppermute | solution.py:24
  19.7 11.9 %collective-permute-start.5 = (bf16[3,512,256]{2,1,0:T(8,128)(2,1)}, bf16[3,512,256]{2,1,0:T(8,128)(2,1)}, u32[]{:S(2)}, u32[]{:S(2)}) collective-permute-start(bf16[3,512,256]{2,1,0:T(8,128)(2,1)} %pad_maximum_fusion.4), channel_id=1, source_target_pairs={{0,1},{1,0},{2,3},{3,2},{4,5},{5,4},{6,7},{7,6},{8,9},{9,8},{10,11... | collective-permute-start | bytes 2359304 | tf_op jit(solution)/shard_map/ppermute | solution.py:24
  36.2 14.3 %collective-permute-start.9 = (bf16[512,256]{1,0:T(8,128)(2,1)S(1)}, bf16[512,256]{1,0:T(8,128)(2,1)}, u32[]{:S(2)}, u32[]{:S(2)}) collective-permute-start(bf16[512,256]{1,0:T(8,128)(2,1)S(1)} %get-tuple-element.8), channel_id=1, source_target_pairs={{0,4},{1,5},{2,6},{3,7},{4,0},{5,1},{6,2},{7,3},{8,12},{9,13},{10,... | collective-permute-start | bytes 786440 | tf_op jit(solution)/shard_map/ppermute | solution.py:24
  38.1 13.3 %collective-permute-start.15 = (bf16[512,256]{1,0:T(8,128)(2,1)S(1)}, bf16[512,256]{1,0:T(8,128)(2,1)S(1)}, u32[]{:S(2)}, u32[]{:S(2)}) collective-permute-start(bf16[512,256]{1,0:T(8,128)(2,1)S(1)} %get-tuple-element.8), channel_id=1, source_target_pairs={{0,24},{8,16},{16,8},{24,0},{1,25},{9,17},{17,9},{25,1},{2,26},{10... | collective-permute-start | bytes 786440 | tf_op jit(solution)/shard_map/ppermute | solution.py:24
  40.3 12.8 %collective-permute-start.14 = (bf16[512,256]{1,0:T(8,128)(2,1)S(1)}, bf16[512,256]{1,0:T(8,128)(2,1)S(1)}, u32[]{:S(2)}, u32[]{:S(2)}) collective-permute-start(bf16[512,256]{1,0:T(8,128)(2,1)S(1)} %get-tuple-element.8), channel_id=1, source_target_pairs={{0,16},{8,24},{16,0},{24,8},{1,17},{9,25},{17,1},{25,9},{2,18},{10... | collective-permute-start | bytes 786440 | tf_op jit(solution)/shard_map/ppermute | solution.py:24
  40.5 12.5 %collective-permute-start.13 = (bf16[512,256]{1,0:T(8,128)(2,1)S(1)}, bf16[512,256]{1,0:T(8,128)(2,1)S(1)}, u32[]{:S(2)}, u32[]{:S(2)}) collective-permute-start(bf16[512,256]{1,0:T(8,128)(2,1)S(1)} %get-tuple-element.8), channel_id=1, source_target_pairs={{0,8},{8,0},{16,24},{24,16},{1,9},{9,1},{17,25},{25,17},{2,10},{10... | collective-permute-start | bytes 786440 | tf_op jit(solution)/shard_map/ppermute | solution.py:24
  40.7 15.7 %collective-permute-start.8 = (bf16[512,256]{1,0:T(8,128)(2,1)S(1)}, bf16[512,256]{1,0:T(8,128)(2,1)}, u32[]{:S(2)}, u32[]{:S(2)}) collective-permute-start(bf16[512,256]{1,0:T(8,128)(2,1)S(1)} %get-tuple-element.8), channel_id=1, source_target_pairs={{0,2},{1,3},{2,0},{3,1},{4,6},{5,7},{6,4},{7,5},{8,10},{9,11},{10,... | collective-permute-start | bytes 786440 | tf_op jit(solution)/shard_map/ppermute | solution.py:24
  50.6 15.1 %collective-permute-start.12 = (bf16[1,512,256]{2,1,0:T(8,128)(2,1)}, bf16[1,512,256]{2,1,0:T(8,128)(2,1)}, u32[]{:S(2)}, u32[]{:S(2)}) collective-permute-start(bf16[1,512,256]{2,1,0:T(8,128)(2,1)} %bitcast.23), channel_id=1, source_target_pairs={{0,3},{1,2},{2,1},{3,0},{4,7},{5,6},{6,5},{7,4},{8,11},{9,10},{10,... | collective-permute-start | bytes 786440 | tf_op jit(solution)/shard_map/ppermute | solution.py:24
  51.3 15.5 %collective-permute-start.11 = (bf16[1,512,256]{2,1,0:T(8,128)(2,1)}, bf16[1,512,256]{2,1,0:T(8,128)(2,1)}, u32[]{:S(2)}, u32[]{:S(2)}) collective-permute-start(bf16[1,512,256]{2,1,0:T(8,128)(2,1)} %bitcast.23), channel_id=1, source_target_pairs={{0,2},{1,3},{2,0},{3,1},{4,6},{5,7},{6,4},{7,5},{8,10},{9,11},{10,... | collective-permute-start | bytes 786440 | tf_op jit(solution)/shard_map/ppermute | solution.py:24
  57.6 10.5 %collective-permute-start.10 = (bf16[3,512,256]{2,1,0:T(8,128)(2,1)S(1)}, bf16[3,512,256]{2,1,0:T(8,128)(2,1)S(1)}, u32[]{:S(2)}, u32[]{:S(2)}) collective-permute-start(bf16[3,512,256]{2,1,0:T(8,128)(2,1)S(1)} %pad_maximum_fusion.5), channel_id=1, source_target_pairs={{0,1},{1,0},{2,3},{3,2},{4,5},{5,4},{6,7},{7,6},{8,9},{9,8},{10,11... | collective-permute-start | bytes 2359304 | tf_op jit(solution)/shard_map/ppermute | solution.py:24
  60.4 1.2 copy-start.3
  68.3 1.0 copy-start.8
  69.3 1.0 copy-start.10
  71.7 14.5 %collective-permute-start.20 = (bf16[512,256]{1,0:T(8,128)(2,1)S(1)}, bf16[512,256]{1,0:T(8,128)(2,1)S(1)}, u32[]{:S(2)}, u32[]{:S(2)}) collective-permute-start(bf16[512,256]{1,0:T(8,128)(2,1)S(1)} %fusion.35), channel_id=1, source_target_pairs={{0,4},{1,5},{2,6},{3,7},{4,0},{5,1},{6,2},{7,3},{8,12},{9,13},{10,... | collective-permute-start | bytes 786440 | tf_op jit(solution)/shard_map/ppermute | solution.py:24
  73.4 13.3 %collective-permute-start.18 = (bf16[512,256]{1,0:T(8,128)(2,1)S(1)}, bf16[512,256]{1,0:T(8,128)(2,1)S(1)}, u32[]{:S(2)}, u32[]{:S(2)}) collective-permute-start(bf16[512,256]{1,0:T(8,128)(2,1)S(1)} %fusion.35), channel_id=1, source_target_pairs={{0,24},{8,16},{16,8},{24,0},{1,25},{9,17},{17,9},{25,1},{2,26},{10... | collective-permute-start | bytes 786440 | tf_op jit(solution)/shard_map/ppermute | solution.py:24
  75.5 12.9 %collective-permute-start.17 = (bf16[512,256]{1,0:T(8,128)(2,1)S(1)}, bf16[512,256]{1,0:T(8,128)(2,1)S(1)}, u32[]{:S(2)}, u32[]{:S(2)}) collective-permute-start(bf16[512,256]{1,0:T(8,128)(2,1)S(1)} %fusion.35), channel_id=1, source_target_pairs={{0,16},{8,24},{16,0},{24,8},{1,17},{9,25},{17,1},{25,9},{2,18},{10... | collective-permute-start | bytes 786440 | tf_op jit(solution)/shard_map/ppermute | solution.py:24
  75.8 12.7 %collective-permute-start.16 = (bf16[512,256]{1,0:T(8,128)(2,1)S(1)}, bf16[512,256]{1,0:T(8,128)(2,1)S(1)}, u32[]{:S(2)}, u32[]{:S(2)}) collective-permute-start(bf16[512,256]{1,0:T(8,128)(2,1)S(1)} %fusion.35), channel_id=1, source_target_pairs={{0,8},{8,0},{16,24},{24,16},{1,9},{9,1},{17,25},{25,17},{2,10},{10... | collective-permute-start | bytes 786440 | tf_op jit(solution)/shard_map/ppermute | solution.py:24
  76.0 13.4 %collective-permute-start.19 = (bf16[512,256]{1,0:T(8,128)(2,1)S(1)}, bf16[512,256]{1,0:T(8,128)(2,1)S(1)}, u32[]{:S(2)}, u32[]{:S(2)}) collective-permute-start(bf16[512,256]{1,0:T(8,128)(2,1)S(1)} %fusion.35), channel_id=1, source_target_pairs={{0,2},{1,3},{2,0},{3,1},{4,6},{5,7},{6,4},{7,5},{8,10},{9,11},{10,... | collective-permute-start | bytes 786440 | tf_op jit(solution)/shard_map/ppermute | solution.py:24
  86.2 8.8 %collective-permute-start.23 = (bf16[1,512,256]{2,1,0:T(8,128)(2,1)S(1)}, bf16[1,512,256]{2,1,0:T(8,128)(2,1)}, u32[]{:S(2)}, u32[]{:S(2)}) collective-permute-start(bf16[1,512,256]{2,1,0:T(8,128)(2,1)S(1)} %bitcast.274), channel_id=1, source_target_pairs={{0,3},{1,2},{2,1},{3,0},{4,7},{5,6},{6,5},{7,4},{8,11},{9,10},{10,... | collective-permute-start | bytes 786440 | tf_op jit(solution)/shard_map/ppermute | solution.py:24
  86.6 13.9 %collective-permute-start.22 = (bf16[1,512,256]{2,1,0:T(8,128)(2,1)S(1)}, bf16[1,512,256]{2,1,0:T(8,128)(2,1)}, u32[]{:S(2)}, u32[]{:S(2)}) collective-permute-start(bf16[1,512,256]{2,1,0:T(8,128)(2,1)S(1)} %bitcast.275), channel_id=1, source_target_pairs={{0,2},{1,3},{2,0},{3,1},{4,6},{5,7},{6,4},{7,5},{8,10},{9,11},{10,... | collective-permute-start | bytes 786440 | tf_op jit(solution)/shard_map/ppermute | solution.py:24
  89.4 0.7 copy-start.4
  90.1 11.6 %collective-permute-start.21 = (bf16[3,512,256]{2,1,0:T(8,128)(2,1)S(1)}, bf16[3,512,256]{2,1,0:T(8,128)(2,1)S(1)}, u32[]{:S(2)}, u32[]{:S(2)}) collective-permute-start(bf16[3,512,256]{2,1,0:T(8,128)(2,1)S(1)} %pad_maximum_fusion.6), channel_id=1, source_target_pairs={{0,1},{1,0},{2,3},{3,2},{4,5},{5,4},{6,7},{7,6},{8,9},{9,8},{10,11... | collective-permute-start | bytes 2359304 | tf_op jit(solution)/shard_map/ppermute | solution.py:24
  101.8 0.9 copy-start
  102.6 0.9 copy-start.5
  104.7 14.2 %collective-permute-start.25 = (bf16[512,256]{1,0:T(8,128)(2,1)S(1)}, bf16[512,256]{1,0:T(8,128)(2,1)}, u32[]{:S(2)}, u32[]{:S(2)}) collective-permute-start(bf16[512,256]{1,0:T(8,128)(2,1)S(1)} %get-tuple-element.10), channel_id=1, source_target_pairs={{0,4},{1,5},{2,6},{3,7},{4,0},{5,1},{6,2},{7,3},{8,12},{9,13},{10,... | collective-permute-start | bytes 786440 | tf_op jit(solution)/shard_map/ppermute | solution.py:24
  105.7 13.3 %collective-permute-start.31 = (bf16[512,256]{1,0:T(8,128)(2,1)S(1)}, bf16[512,256]{1,0:T(8,128)(2,1)S(1)}, u32[]{:S(2)}, u32[]{:S(2)}) collective-permute-start(bf16[512,256]{1,0:T(8,128)(2,1)S(1)} %get-tuple-element.10), channel_id=1, source_target_pairs={{0,24},{8,16},{16,8},{24,0},{1,25},{9,17},{17,9},{25,1},{2,26},{10... | collective-permute-start | bytes 786440 | tf_op jit(solution)/shard_map/ppermute | solution.py:24
  107.7 13.8 %collective-permute-start.30 = (bf16[512,256]{1,0:T(8,128)(2,1)S(1)}, bf16[512,256]{1,0:T(8,128)(2,1)S(1)}, u32[]{:S(2)}, u32[]{:S(2)}) collective-permute-start(bf16[512,256]{1,0:T(8,128)(2,1)S(1)} %get-tuple-element.10), channel_id=1, source_target_pairs={{0,16},{8,24},{16,0},{24,8},{1,17},{9,25},{17,1},{25,9},{2,18},{10... | collective-permute-start | bytes 786440 | tf_op jit(solution)/shard_map/ppermute | solution.py:24
  108.1 13.4 %collective-permute-start.29 = (bf16[512,256]{1,0:T(8,128)(2,1)S(1)}, bf16[512,256]{1,0:T(8,128)(2,1)S(1)}, u32[]{:S(2)}, u32[]{:S(2)}) collective-permute-start(bf16[512,256]{1,0:T(8,128)(2,1)S(1)} %get-tuple-element.10), channel_id=1, source_target_pairs={{0,8},{8,0},{16,24},{24,16},{1,9},{9,1},{17,25},{25,17},{2,10},{10... | collective-permute-start | bytes 786440 | tf_op jit(solution)/shard_map/ppermute | solution.py:24
  108.4 16.5 %collective-permute-start.24 = (bf16[512,256]{1,0:T(8,128)(2,1)S(1)}, bf16[512,256]{1,0:T(8,128)(2,1)}, u32[]{:S(2)}, u32[]{:S(2)}) collective-permute-start(bf16[512,256]{1,0:T(8,128)(2,1)S(1)} %get-tuple-element.10), channel_id=1, source_target_pairs={{0,2},{1,3},{2,0},{3,1},{4,6},{5,7},{6,4},{7,5},{8,10},{9,11},{10,... | collective-permute-start | bytes 786440 | tf_op jit(solution)/shard_map/ppermute | solution.py:24
  118.9 12.7 %collective-permute-start.28 = (bf16[1,512,256]{2,1,0:T(8,128)(2,1)}, bf16[1,512,256]{2,1,0:T(8,128)(2,1)}, u32[]{:S(2)}, u32[]{:S(2)}) collective-permute-start(bf16[1,512,256]{2,1,0:T(8,128)(2,1)} %bitcast.63), channel_id=1, source_target_pairs={{0,3},{1,2},{2,1},{3,0},{4,7},{5,6},{6,5},{7,4},{8,11},{9,10},{10,... | collective-permute-start | bytes 786440 | tf_op jit(solution)/shard_map/ppermute | solution.py:24
  119.0 14.5 %collective-permute-start.27 = (bf16[1,512,256]{2,1,0:T(8,128)(2,1)}, bf16[1,512,256]{2,1,0:T(8,128)(2,1)}, u32[]{:S(2)}, u32[]{:S(2)}) collective-permute-start(bf16[1,512,256]{2,1,0:T(8,128)(2,1)} %bitcast.63), channel_id=1, source_target_pairs={{0,2},{1,3},{2,0},{3,1},{4,6},{5,7},{6,4},{7,5},{8,10},{9,11},{10,... | collective-permute-start | bytes 786440 | tf_op jit(solution)/shard_map/ppermute | solution.py:24
  126.0 2.5 %copy-start.1 = (bf16[3,512,256]{2,1,0:T(8,128)(2,1)S(1)}, bf16[3,512,256]{2,1,0:T(8,128)(2,1)}, u32[]{:S(2)}) copy-start(bf16[3,512,256]{2,1,0:T(8,128)(2,1)} %copy-done) | copy-start | bytes 2359300
  126.0 8.6 %collective-permute-start.26 = (bf16[3,512,256]{2,1,0:T(8,128)(2,1)S(1)}, bf16[3,512,256]{2,1,0:T(8,128)(2,1)S(1)}, u32[]{:S(2)}, u32[]{:S(2)}) collective-permute-start(bf16[3,512,256]{2,1,0:T(8,128)(2,1)S(1)} %pad_maximum_fusion.7), channel_id=1, source_target_pairs={{0,1},{1,0},{2,3},{3,2},{4,5},{5,4},{6,7},{7,6},{8,9},{9,8},{10,11... | collective-permute-start | bytes 2359304 | tf_op jit(solution)/shard_map/ppermute | solution.py:24
  129.2 1.0 copy-start.6
  134.9 1.0 copy-start.7
  135.9 1.0 copy-start.9

commit v9 on v6

v9 whole, which is shorter than its diff:
```python
import jax
import jax.numpy as jnp
from jax import lax
from jax.sharding import PartitionSpec as P

BS = 128
STEPS = 2


def allowed_blocks(pattern):
    count = pattern.shape[0]
    index = lax.iota(jnp.int32, count)
    eye = (index[:, None] == index[None, :]).astype(jnp.int32)
    return jnp.maximum(jnp.maximum(pattern, pattern.T), eye)


def apply_mask(values, blocks):
    row_blocks, col_blocks = blocks.shape
    shaped = values.reshape(row_blocks, BS, col_blocks, BS) * blocks[:, None, :, None]
    return shaped.reshape(row_blocks * BS, col_blocks * BS)


def xor_permute(x, axis, size, s):
    return lax.ppermute(x, axis, perm=[(i, i ^ s) for i in range(size)])


def exchange(xb, n_row, n_col):
    chips = n_col // 2
    same = {0: xb}
    for s in sorted(range(2, chips, 2), reverse=True) + [1]:
        same[s] = xor_permute(xb, "col", n_col, 2 * s)
    col_same = [xb] + [xor_permute(xb, "row", n_row, t) for t in range(1, n_row)]
    forward = list(range(2, chips, 2))
    if forward:
        sent = xor_permute(jnp.stack([same[s] for s in forward]), "col", n_col, 2)
        for i, s in enumerate(forward):
            same[s ^ 1] = sent[i]
    mine = jnp.stack(col_same)
    partner = xor_permute(mine, "col", n_col, 1)
    return [same[s] for s in range(chips)], mine, partner


def ordered_k_blocks(mine, partner, me_row, core, chip, chips):
    n_row, half, wide = mine.shape
    per = wide // half
    both = jnp.concatenate([mine, partner], axis=0)
    s = lax.iota(jnp.int32, chips)
    first = jnp.bitwise_xor(s, chip)[:, None] * per + lax.iota(jnp.int32, per)[None, :]
    index = jnp.bitwise_xor(first % 2, core) * n_row + jnp.bitwise_xor(first // 2, me_row)
    picked = jnp.take(both, index.reshape(-1), axis=0)
    return picked.reshape(chips, per * half, wide)


def contract(row_pieces, k_blocks):
    total = None
    for s, piece in enumerate(row_pieces):
        part = jnp.dot(piece, k_blocks[s], preferred_element_type=jnp.float32)
        total = part if total is None else total + part
    return total


def swap_halves(keep, give, core, n_col, axis):
    got = xor_permute(give, "col", n_col, 1)
    first = jnp.where(core == 0, keep, got)
    second = jnp.where(core == 0, got, keep)
    return jnp.concatenate([first, second], axis=axis)


def on_device(density, pattern):
    rows, cols = density.shape
    half = rows // 2
    wide = 2 * cols
    n_row = lax.axis_size("row")
    n_col = lax.axis_size("col")
    chips = n_col // 2
    me_row = lax.axis_index("row")
    me_col = lax.axis_index("col")
    core = me_col % 2
    chip = me_col // 2
    allowed = allowed_blocks(pattern)
    blocks = lax.dynamic_slice(
        allowed,
        ((me_row * rows + core * half) // BS, chip * wide // BS),
        (half // BS, wide // BS),
    ).astype(jnp.float32)
    rounded = density.astype(jnp.bfloat16)
    keep = lax.dynamic_slice_in_dim(rounded, core * half, half, axis=0)
    give = lax.dynamic_slice_in_dim(rounded, (1 - core) * half, half, axis=0)
    xb = apply_mask(swap_halves(keep, give, core, n_col, 1), blocks).astype(jnp.bfloat16)
    for step in range(STEPS):
        x_row, x_mine, x_partner = exchange(xb, n_row, n_col)
        x_k = ordered_k_blocks(x_mine, x_partner, me_row, core, chip, chips)
        square = apply_mask(contract(x_row, x_k), blocks)
        qb = square.astype(jnp.bfloat16)
        q_row, q_mine, q_partner = exchange(qb, n_row, n_col)
        q_k = ordered_k_blocks(q_mine, q_partner, me_row, core, chip, chips)
        jordan = contract(q_row, x_k) + contract(x_row, q_k)
        current = apply_mask(3.0 * square - jordan, blocks)
        xb = current.astype(jnp.bfloat16)
    keep = lax.dynamic_slice_in_dim(current, core * cols, cols, axis=1)
    give = lax.dynamic_slice_in_dim(current, (1 - core) * cols, cols, axis=1)
    return swap_halves(keep, give, core, n_col, 0)


def solution(mesh):
    placed = (P("row", "col"), P())
    return jax.shard_map(
        on_device, mesh=mesh, in_specs=placed, out_specs=P("row", "col"), check_vma=False
    )
```

time: 124 us -> 149 us (1.20)
  waiting for transfers between devices: 43.1 us -> 65 us
  local copies, waits for them, and re-layouts: 8.68 us -> 26.8 us
  starting transfers between devices: 35.3 us -> 24.8 us
  matrix products: 28.5 us -> 24.6 us
    ppermute x32 -> x30, waiting for transfers between devices: 43.1 us -> 65 us  [xor_permute(): return lax.ppermute(x, axis, perm=[(i, i ^ s) for i in range(size)])]
    ppermute x32 -> x30, starting transfers between devices: 35.3 us -> 24.8 us  [xor_permute(): return lax.ppermute(x, axis, perm=[(i, i ^ s) for i in range(size)])]
    unnamed x33 -> x35, local copies, waits for them, and re-layouts: 3.57 us -> 11 us
    concatenate x0 -> x4, local copies, waits for them, and re-layouts: none -> 5.45 us  [ordered_k_blocks(): both = jnp.concatenate([mine, partner], axis=0)]
    another operation x8 -> x4, other arithmetic: 5.83 us -> 0.53 us  [exchange(): mine = jnp.stack(col_same)]
    gather x4, local copies, waits for them, and re-layouts: 4.9 us -> 9.08 us  [ordered_k_blocks(): picked = jnp.take(both, index.reshape(-1), axis=0)]
    dot_general x48 -> x24, matrix products: 28.5 us -> 24.6 us  [contract(): part = jnp.dot(piece, k_blocks[s], preferred_element_type=jnp.float32)]
    convert_element_type x2 -> x5, other arithmetic: 0.15 us -> 2.83 us  [the longest x1 1.07 us: on_device(): rounded = density.astype(jnp.bfloat16)]
  transfers between devices with their start and end apart: 32 -> 30, of which waited for: 11 -> 13; matrix products, arithmetic and copies ran while one was open for 30% -> 20% of each run, Pallas kernels for 0% -> 0%
where the time goes in v9:
time: 149 us; the launch traced here: 148 us
  waiting for transfers between devices  65 us (44%)
  local copies, waits for them, and re-layouts  26.8 us (18%)
  starting transfers between devices  24.8 us (17%)
  matrix products  24.6 us (17%)
  other arithmetic  6.26 us (4%)
    ppermute x30, waiting for transfers between devices, xor_permute(): return lax.ppermute(x, axis, perm=[(i, i ^ s) for i in range(size)])  65 us
    ppermute x30, starting transfers between devices, xor_permute(): return lax.ppermute(x, axis, perm=[(i, i ^ s) for i in range(size)])  24.8 us
    dot_general x24, matrix products, contract(): part = jnp.dot(piece, k_blocks[s], preferred_element_type=jnp.float32)  24.6 us
    unnamed x35, local copies, waits for them, and re-layouts  11 us
    gather x4, local copies, waits for them, and re-layouts, ordered_k_blocks(): picked = jnp.take(both, index.reshape(-1), axis=0)  9.08 us
    concatenate x4, local copies, waits for them, and re-layouts, ordered_k_blocks(): both = jnp.concatenate([mine, partner], axis=0)  5.45 us
  transfers between devices with their start and end apart: 30, of which 13 were waited for; matrix products, arithmetic and copies ran while one was open for 20% of the time, Pallas kernels for 0%

profile of v9, /device:TPU:1, one launch (start us, length us, event | category | flops | bytes accessed | tf_op | source)
XLA Modules:
  0.0 148.0 jit_solution(12222976561859574852)
XLA Ops:
  0.0 1.1 convert_element_type.74
  4.0 3.6 %collective-permute-start.3 = (bf16[256,512]{1,0:T(8,128)(2,1)}, bf16[256,512]{1,0:T(8,128)(2,1)S(1)}, u32[]{:S(2)}, u32[]{:S(2)}) collective-permute-start(bf16[256,512]{1,0:T(8,128)(2,1)} %fusion.10), channel_id=1, source_target_pairs={{0,24},{8,16},{16,8},{24,0},{1,25},{9,17},{17,9},{25,1},{2,26},{10... | collective-permute-start | bytes 786440 | tf_op jit(solution)/shard_map/ppermute | solution.py:24
  8.1 2.6 %collective-permute-start.6 = (bf16[256,512]{1,0:T(8,128)(2,1)}, bf16[256,512]{1,0:T(8,128)(2,1)}, u32[]{:S(2)}, u32[]{:S(2)}) collective-permute-start(bf16[256,512]{1,0:T(8,128)(2,1)} %fusion.10), channel_id=1, source_target_pairs={{0,4},{1,5},{2,6},{3,7},{4,0},{5,1},{6,2},{7,3},{8,12},{9,13},{10,... | collective-permute-start | bytes 786440 | tf_op jit(solution)/shard_map/ppermute | solution.py:24
  10.7 1.3 collective-permute-start.5
  12.8 1.8 %collective-permute-done.3 = bf16[256,512]{1,0:T(8,128)(2,1)S(1)} collective-permute-done((bf16[256,512]{1,0:T(8,128)(2,1)}, bf16[256,512]{1,0:T(8,128)(2,1)S(1)}, u32[]{:S(2)}, u32[]{:S(2)}) %collective-permute-start.3) | collective-permute-done | bytes 262176 | tf_op jit(solution)/shard_map/ppermute | solution.py:24
  14.6 5.7 %collective-permute-done.2 = bf16[256,512]{1,0:T(8,128)(2,1)S(1)} collective-permute-done((bf16[256,512]{1,0:T(8,128)(2,1)}, bf16[256,512]{1,0:T(8,128)(2,1)S(1)}, u32[]{:S(2)}, u32[]{:S(2)}) %collective-permute-start.2) | collective-permute-done | bytes 262176 | tf_op jit(solution)/shard_map/ppermute | solution.py:24
  22.5 1.4 collective-permute-start.7
  23.9 1.7 %constant_dynamic-update-slice_fusion.3 = bf16[8,256,512]{2,1,0:T(8,128)(2,1)} fusion(bf16[8,256,512]{2,1,0:T(8,128)(2,1)} %get-tuple-element.14, bf16[256,512]{1,0:T(8,128)(2,1)} %copy-done.6), kind=kLoop, calls=%fused_computation.68 | loop fusion | bytes 524288
  27.0 2.3 %constant_dynamic-update-slice_fusion = bf16[8,256,512]{2,1,0:T(8,128)(2,1)} fusion(bf16[8,256,512]{2,1,0:T(8,128)(2,1)} %constant_dynamic-update-slice_fusion.1, bf16[4,256,512]{2,1,0:T(8,128)(2,1)} %collective-permute-done.4), kind=kLoop, calls=%fused_computation.65 | loop fusion | bytes 2097152 | tf_op jit(solution)/shard_map/concatenate | solution.py:46
  29.3 2.3 %gather_fusion = bf16[8,256,512]{2,1,0:T(8,128)(2,1)S(1)} fusion(bf16[8,256,512]{2,1,0:T(8,128)(2,1)} %constant_dynamic-update-slice_fusion, s32[1024]{0:T(1024)S(1)} %pad_clamp_fusion), kind=kCustom, calls=%fused_computation.clone | custom fusion | bytes 4194336 | tf_op jit(solution)/shard_map/jit(_take)/gather | solution.py:50
  32.3 1.2 fusion.26
  33.5 1.2 convolution_add_fusion.11
  34.8 2.1 %constant_dynamic-update-slice_fusion.9 = (bf16[8,256,512]{2,1,0:T(8,128)(2,1)}, bf16[256,512]{1,0:T(8,128)(2,1)S(1)}, f32[256,512]{1,0:T(8,128)}) fusion(f32[32,8,4,128]{3,2,1,0:T(4,128)S(1)} %bitcast.130, f32[256,512]{1,0:T(8,128)S(1)} %fusion.26, f32[256,512]{1,0:T(8,128)S(1)} %convolution_add_fusion.11, bf16[256,512]{1,0:T(8,128)(2,1)} %collective-permute-done.6, ...), kind=kOutput, calls=%fused_computation.74 | convolution fusion | flops 134742016 | bytes 3407872 | tf_op jit(solution)/shard_map/dot_general | solution.py:57
  36.9 3.1 %collective-permute-start.9 = (bf16[256,512]{1,0:T(8,128)(2,1)S(1)}, bf16[256,512]{1,0:T(8,128)(2,1)S(1)}, u32[]{:S(2)}, u32[]{:S(2)}) collective-permute-start(bf16[256,512]{1,0:T(8,128)(2,1)S(1)} %get-tuple-element.11), channel_id=1, source_target_pairs={{0,4},{1,5},{2,6},{3,7},{4,0},{5,1},{6,2},{7,3},{8,12},{9,13},{10,... | collective-permute-start | bytes 786440 | tf_op jit(solution)/shard_map/ppermute | solution.py:24
  40.0 2.2 %collective-permute-start.13 = (bf16[256,512]{1,0:T(8,128)(2,1)S(1)}, bf16[256,512]{1,0:T(8,128)(2,1)S(1)}, u32[]{:S(2)}, u32[]{:S(2)}) collective-permute-start(bf16[256,512]{1,0:T(8,128)(2,1)S(1)} %get-tuple-element.11), channel_id=1, source_target_pairs={{0,24},{8,16},{16,8},{24,0},{1,25},{9,17},{17,9},{25,1},{2,26},{10... | collective-permute-start | bytes 786440 | tf_op jit(solution)/shard_map/ppermute | solution.py:24
  43.0 9.2 %collective-permute-done.9 = bf16[256,512]{1,0:T(8,128)(2,1)S(1)} collective-permute-done((bf16[256,512]{1,0:T(8,128)(2,1)S(1)}, bf16[256,512]{1,0:T(8,128)(2,1)S(1)}, u32[]{:S(2)}, u32[]{:S(2)}) %collective-permute-start.9) | collective-permute-done | bytes 262176 | tf_op jit(solution)/shard_map/ppermute | solution.py:24
  52.2 2.6 %collective-permute-done.12 = bf16[256,512]{1,0:T(8,128)(2,1)S(1)} collective-permute-done((bf16[256,512]{1,0:T(8,128)(2,1)S(1)}, bf16[256,512]{1,0:T(8,128)(2,1)S(1)}, u32[]{:S(2)}, u32[]{:S(2)}) %collective-permute-start.12) | collective-permute-done | bytes 262176 | tf_op jit(solution)/shard_map/ppermute | solution.py:24
  57.8 1.1 convolution_add_fusion.9
  58.9 2.0 %collective-permute-done.10 = bf16[1,256,512]{2,1,0:T(8,128)(2,1)S(1)} collective-permute-done((bf16[1,256,512]{2,1,0:T(8,128)(2,1)S(1)}, bf16[1,256,512]{2,1,0:T(8,128)(2,1)S(1)}, u32[]{:S(2)}, u32[]{:S(2)}) %collective-permute-start.10) | collective-permute-done | bytes 262176 | tf_op jit(solution)/shard_map/ppermute | solution.py:24
  60.9 1.1 fusion.22
  62.0 1.1 constant_dynamic-update-slice_fusion.5
  63.0 2.3 %gather_fusion.1 = bf16[8,256,512]{2,1,0:T(8,128)(2,1)S(1)} fusion(bf16[8,256,512]{2,1,0:T(8,128)(2,1)} %constant_dynamic-update-slice_fusion.5, s32[1024]{0:T(1024)S(1)} %pad_clamp_fusion), kind=kCustom, calls=%fused_computation.1.clone | custom fusion | bytes 4194336 | tf_op jit(solution)/shard_map/jit(_take)/gather | solution.py:50
  66.0 1.2 fusion.24
  67.3 1.4 convolution_add_fusion.7
  68.7 1.3 fusion.5
  70.0 1.1 constant_dynamic-update-slice_fusion.14
  71.1 2.1 %collective-permute-start.17 = (bf16[256,512]{1,0:T(8,128)(2,1)S(1)}, bf16[256,512]{1,0:T(8,128)(2,1)S(1)}, u32[]{:S(2)}, u32[]{:S(2)}) collective-permute-start(bf16[256,512]{1,0:T(8,128)(2,1)S(1)} %get-tuple-element.9), channel_id=1, source_target_pairs={{0,24},{8,16},{16,8},{24,0},{1,25},{9,17},{17,9},{25,1},{2,26},{10... | collective-permute-start | bytes 786440 | tf_op jit(solution)/shard_map/ppermute | solution.py:24
  73.7 4.5 %collective-permute-done.17 = bf16[256,512]{1,0:T(8,128)(2,1)S(1)} collective-permute-done((bf16[256,512]{1,0:T(8,128)(2,1)S(1)}, bf16[256,512]{1,0:T(8,128)(2,1)S(1)}, u32[]{:S(2)}, u32[]{:S(2)}) %collective-permute-start.17) | collective-permute-done | bytes 262176 | tf_op jit(solution)/shard_map/ppermute | solution.py:24
  78.2 7.6 %collective-permute-done.16 = bf16[256,512]{1,0:T(8,128)(2,1)S(1)} collective-permute-done((bf16[256,512]{1,0:T(8,128)(2,1)S(1)}, bf16[256,512]{1,0:T(8,128)(2,1)S(1)}, u32[]{:S(2)}, u32[]{:S(2)}) %collective-permute-start.16) | collective-permute-done | bytes 262176 | tf_op jit(solution)/shard_map/ppermute | solution.py:24
  86.6 13.9 %collective-permute-done.20 = bf16[256,512]{1,0:T(8,128)(2,1)} collective-permute-done((bf16[256,512]{1,0:T(8,128)(2,1)S(1)}, bf16[256,512]{1,0:T(8,128)(2,1)}, u32[]{:S(2)}, u32[]{:S(2)}) %collective-permute-start.20) | collective-permute-done | bytes 262176 | tf_op jit(solution)/shard_map/ppermute | solution.py:24
  102.7 1.1 constant_dynamic-update-slice_fusion.10
  103.8 2.3 %gather_fusion.2 = bf16[8,256,512]{2,1,0:T(8,128)(2,1)S(1)} fusion(bf16[8,256,512]{2,1,0:T(8,128)(2,1)} %constant_dynamic-update-slice_fusion.10, s32[1024]{0:T(1024)S(1)} %pad_clamp_fusion), kind=kCustom, calls=%fused_computation.2.clone | custom fusion | bytes 4194336 | tf_op jit(solution)/shard_map/jit(_take)/gather | solution.py:50
  106.8 1.4 collective-permute-done.21
  108.2 1.2 fusion.20
  109.5 1.2 convolution_add_fusion.5
  110.7 2.1 %constant_dynamic-update-slice_fusion.19 = (bf16[8,256,512]{2,1,0:T(8,128)(2,1)}, bf16[256,512]{1,0:T(8,128)(2,1)S(1)}, f32[256,512]{1,0:T(8,128)}) fusion(f32[32,8,4,128]{3,2,1,0:T(4,128)S(1)} %bitcast.132, f32[256,512]{1,0:T(8,128)S(1)} %fusion.20, f32[256,512]{1,0:T(8,128)S(1)} %convolution_add_fusion.5, bf16[256,512]{1,0:T(8,128)(2,1)} %collective-permute-done.20, ...), kind=kOutput, calls=%fused_computation.84 | convolution fusion | flops 134742016 | bytes 3407872 | tf_op jit(solution)/shard_map/dot_general | solution.py:57
  112.9 1.4 collective-permute-start.27
  116.1 11.5 %collective-permute-done.23 = bf16[256,512]{1,0:T(8,128)(2,1)S(1)} collective-permute-done((bf16[256,512]{1,0:T(8,128)(2,1)S(1)}, bf16[256,512]{1,0:T(8,128)(2,1)S(1)}, u32[]{:S(2)}, u32[]{:S(2)}) %collective-permute-start.23) | collective-permute-done | bytes 262176 | tf_op jit(solution)/shard_map/ppermute | solution.py:24
  130.6 1.1 convolution_add_fusion.3
  131.7 3.2 %collective-permute-done.24 = bf16[1,256,512]{2,1,0:T(8,128)(2,1)S(1)} collective-permute-done((bf16[1,256,512]{2,1,0:T(8,128)(2,1)S(1)}, bf16[1,256,512]{2,1,0:T(8,128)(2,1)S(1)}, u32[]{:S(2)}, u32[]{:S(2)}) %collective-permute-start.24) | collective-permute-done | bytes 262176 | tf_op jit(solution)/shard_map/ppermute | solution.py:24
  134.9 1.1 fusion.16
  136.0 1.1 constant_dynamic-update-slice_fusion.15
  137.0 2.3 %gather_fusion.3 = bf16[8,256,512]{2,1,0:T(8,128)(2,1)S(1)} fusion(bf16[8,256,512]{2,1,0:T(8,128)(2,1)} %constant_dynamic-update-slice_fusion.15, s32[1024]{0:T(1024)S(1)} %pad_clamp_fusion), kind=kCustom, calls=%fused_computation.3.clone | custom fusion | bytes 4194336 | tf_op jit(solution)/shard_map/jit(_take)/gather | solution.py:50
  140.0 1.2 fusion.18
  141.3 1.4 convolution_add_fusion.1
  142.7 1.3 fusion
  144.4 1.5 %collective-permute-start.29 = (f32[256,256]{1,0:T(8,128)S(1)}, f32[256,256]{1,0:T(8,128)S(1)}, u32[]{:S(2)}, u32[]{:S(2)}) collective-permute-start(f32[256,256]{1,0:T(8,128)S(1)} %constant_dynamic-slice_fusion), channel_id=1, source_target_pairs={{0,1},{1,0},{2,3},{3,2},{4,5},{5,4},{6,7},{7,6},{8,9},{9,8},{10,11... | collective-permute-start | bytes 786440 | tf_op jit(solution)/shard_map/ppermute | solution.py:24
  145.9 1.2 collective-permute-done.29
  (110 shorter events, 23.9 us)
Async XLA Ops:
  1.1 1.9 %collective-permute-start = (bf16[256,256]{1,0:T(8,128)(2,1)S(1)}, bf16[256,256]{1,0:T(8,128)(2,1)S(1)}, u32[]{:S(2)}, u32[]{:S(2)}) collective-permute-start(bf16[256,256]{1,0:T(8,128)(2,1)S(1)} %constant_dynamic-slice_fusion.1), channel_id=1, source_target_pairs={{0,1},{1,0},{2,3},{3,2},{4,5},{5,4},{6,7},{7,6},{8,9},{9,8},{10,11... | collective-permute-start | bytes 393224 | tf_op jit(solution)/shard_map/ppermute | solution.py:24
  4.0 10.6 %collective-permute-start.3 = (bf16[256,512]{1,0:T(8,128)(2,1)}, bf16[256,512]{1,0:T(8,128)(2,1)S(1)}, u32[]{:S(2)}, u32[]{:S(2)}) collective-permute-start(bf16[256,512]{1,0:T(8,128)(2,1)} %fusion.10), channel_id=1, source_target_pairs={{0,24},{8,16},{16,8},{24,0},{1,25},{9,17},{17,9},{25,1},{2,26},{10... | collective-permute-start | bytes 786440 | tf_op jit(solution)/shard_map/ppermute | solution.py:24
  7.6 12.7 %collective-permute-start.2 = (bf16[256,512]{1,0:T(8,128)(2,1)}, bf16[256,512]{1,0:T(8,128)(2,1)S(1)}, u32[]{:S(2)}, u32[]{:S(2)}) collective-permute-start(bf16[256,512]{1,0:T(8,128)(2,1)} %fusion.10), channel_id=1, source_target_pairs={{0,16},{8,24},{16,0},{24,8},{1,17},{9,25},{17,1},{25,9},{2,18},{10... | collective-permute-start | bytes 786440 | tf_op jit(solution)/shard_map/ppermute | solution.py:24
  7.9 12.5 %collective-permute-start.1 = (bf16[256,512]{1,0:T(8,128)(2,1)}, bf16[256,512]{1,0:T(8,128)(2,1)S(1)}, u32[]{:S(2)}, u32[]{:S(2)}) collective-permute-start(bf16[256,512]{1,0:T(8,128)(2,1)} %fusion.10), channel_id=1, source_target_pairs={{0,8},{8,0},{16,24},{24,16},{1,9},{9,1},{17,25},{25,17},{2,10},{10... | collective-permute-start | bytes 786440 | tf_op jit(solution)/shard_map/ppermute | solution.py:24
  8.1 14.4 %collective-permute-start.6 = (bf16[256,512]{1,0:T(8,128)(2,1)}, bf16[256,512]{1,0:T(8,128)(2,1)}, u32[]{:S(2)}, u32[]{:S(2)}) collective-permute-start(bf16[256,512]{1,0:T(8,128)(2,1)} %fusion.10), channel_id=1, source_target_pairs={{0,4},{1,5},{2,6},{3,7},{4,0},{5,1},{6,2},{7,3},{8,12},{9,13},{10,... | collective-permute-start | bytes 786440 | tf_op jit(solution)/shard_map/ppermute | solution.py:24
  10.7 22.8 %collective-permute-start.5 = (bf16[256,512]{1,0:T(8,128)(2,1)}, bf16[256,512]{1,0:T(8,128)(2,1)}, u32[]{:S(2)}, u32[]{:S(2)}) collective-permute-start(bf16[256,512]{1,0:T(8,128)(2,1)} %fusion.10), channel_id=1, source_target_pairs={{0,2},{1,3},{2,0},{3,1},{4,6},{5,7},{6,4},{7,5},{8,10},{9,11},{10,... | collective-permute-start | bytes 786440 | tf_op jit(solution)/shard_map/ppermute | solution.py:24
  20.4 0.7 copy-start.6
  21.1 5.9 %collective-permute-start.4 = (bf16[4,256,512]{2,1,0:T(8,128)(2,1)S(1)}, bf16[4,256,512]{2,1,0:T(8,128)(2,1)}, u32[]{:S(2)}, u32[]{:S(2)}) collective-permute-start(bf16[4,256,512]{2,1,0:T(8,128)(2,1)S(1)} %pad_maximum_fusion), channel_id=1, source_target_pairs={{0,1},{1,0},{2,3},{3,2},{4,5},{5,4},{6,7},{7,6},{8,9},{9,8},{10,11... | collective-permute-start | bytes 3145736 | tf_op jit(solution)/shard_map/ppermute | solution.py:24
  22.5 9.8 %collective-permute-start.7 = (bf16[1,256,512]{2,1,0:T(8,128)(2,1)}, bf16[1,256,512]{2,1,0:T(8,128)(2,1)}, u32[]{:S(2)}, u32[]{:S(2)}) collective-permute-start(bf16[1,256,512]{2,1,0:T(8,128)(2,1)} %bitcast.9), channel_id=1, source_target_pairs={{0,2},{1,3},{2,0},{3,1},{4,6},{5,7},{6,4},{7,5},{8,10},{9,11},{10,... | collective-permute-start | bytes 786440 | tf_op jit(solution)/shard_map/ppermute | solution.py:24
  36.9 15.2 %collective-permute-start.9 = (bf16[256,512]{1,0:T(8,128)(2,1)S(1)}, bf16[256,512]{1,0:T(8,128)(2,1)S(1)}, u32[]{:S(2)}, u32[]{:S(2)}) collective-permute-start(bf16[256,512]{1,0:T(8,128)(2,1)S(1)} %get-tuple-element.11), channel_id=1, source_target_pairs={{0,4},{1,5},{2,6},{3,7},{4,0},{5,1},{6,2},{7,3},{8,12},{9,13},{10,... | collective-permute-start | bytes 786440 | tf_op jit(solution)/shard_map/ppermute | solution.py:24
  40.0 12.2 %collective-permute-start.13 = (bf16[256,512]{1,0:T(8,128)(2,1)S(1)}, bf16[256,512]{1,0:T(8,128)(2,1)S(1)}, u32[]{:S(2)}, u32[]{:S(2)}) collective-permute-start(bf16[256,512]{1,0:T(8,128)(2,1)S(1)} %get-tuple-element.11), channel_id=1, source_target_pairs={{0,24},{8,16},{16,8},{24,0},{1,25},{9,17},{17,9},{25,1},{2,26},{10... | collective-permute-start | bytes 786440 | tf_op jit(solution)/shard_map/ppermute | solution.py:24
  42.2 12.6 %collective-permute-start.12 = (bf16[256,512]{1,0:T(8,128)(2,1)S(1)}, bf16[256,512]{1,0:T(8,128)(2,1)S(1)}, u32[]{:S(2)}, u32[]{:S(2)}) collective-permute-start(bf16[256,512]{1,0:T(8,128)(2,1)S(1)} %get-tuple-element.11), channel_id=1, source_target_pairs={{0,16},{8,24},{16,0},{24,8},{1,17},{9,25},{17,1},{25,9},{2,18},{10... | collective-permute-start | bytes 786440 | tf_op jit(solution)/shard_map/ppermute | solution.py:24
  42.4 12.4 %collective-permute-start.11 = (bf16[256,512]{1,0:T(8,128)(2,1)S(1)}, bf16[256,512]{1,0:T(8,128)(2,1)S(1)}, u32[]{:S(2)}, u32[]{:S(2)}) collective-permute-start(bf16[256,512]{1,0:T(8,128)(2,1)S(1)} %get-tuple-element.11), channel_id=1, source_target_pairs={{0,8},{8,0},{16,24},{24,16},{1,9},{9,1},{17,25},{25,17},{2,10},{10... | collective-permute-start | bytes 786440 | tf_op jit(solution)/shard_map/ppermute | solution.py:24
  42.7 15.1 %collective-permute-start.8 = (bf16[256,512]{1,0:T(8,128)(2,1)S(1)}, bf16[256,512]{1,0:T(8,128)(2,1)S(1)}, u32[]{:S(2)}, u32[]{:S(2)}) collective-permute-start(bf16[256,512]{1,0:T(8,128)(2,1)S(1)} %get-tuple-element.11), channel_id=1, source_target_pairs={{0,2},{1,3},{2,0},{3,1},{4,6},{5,7},{6,4},{7,5},{8,10},{9,11},{10,... | collective-permute-start | bytes 786440 | tf_op jit(solution)/shard_map/ppermute | solution.py:24
  52.2 6.7 %copy-start.9 = (bf16[256,512]{1,0:T(8,128)(2,1)}, bf16[256,512]{1,0:T(8,128)(2,1)S(1)}, u32[]{:S(2)}) copy-start(bf16[256,512]{1,0:T(8,128)(2,1)S(1)} %collective-permute-done.9) | copy-start | bytes 786436
  52.2 8.7 %collective-permute-start.10 = (bf16[1,256,512]{2,1,0:T(8,128)(2,1)S(1)}, bf16[1,256,512]{2,1,0:T(8,128)(2,1)S(1)}, u32[]{:S(2)}, u32[]{:S(2)}) collective-permute-start(bf16[1,256,512]{2,1,0:T(8,128)(2,1)S(1)} %bitcast.178), channel_id=1, source_target_pairs={{0,2},{1,3},{2,0},{3,1},{4,6},{5,7},{6,4},{7,5},{8,10},{9,11},{10,... | collective-permute-start | bytes 786440 | tf_op jit(solution)/shard_map/ppermute | solution.py:24
  54.9 7.0 %collective-permute-start.14 = (bf16[4,256,512]{2,1,0:T(8,128)(2,1)S(1)}, bf16[4,256,512]{2,1,0:T(8,128)(2,1)S(1)}, u32[]{:S(2)}, u32[]{:S(2)}) collective-permute-start(bf16[4,256,512]{2,1,0:T(8,128)(2,1)S(1)} %pad_maximum_fusion.1), channel_id=1, source_target_pairs={{0,1},{1,0},{2,3},{3,2},{4,5},{5,4},{6,7},{7,6},{8,9},{9,8},{10,11... | collective-permute-start | bytes 3145736 | tf_op jit(solution)/shard_map/ppermute | solution.py:24
  67.3 2.7 %copy-start.1 = (f32[256,512]{1,0:T(8,128)S(1)}, f32[256,512]{1,0:T(8,128)}, u32[]{:S(2)}) copy-start(f32[256,512]{1,0:T(8,128)} %convolution_add_fusion.9) | copy-start | bytes 1572868
  67.3 2.7 %copy-start.3 = (f32[256,512]{1,0:T(8,128)S(1)}, f32[256,512]{1,0:T(8,128)}, u32[]{:S(2)}) copy-start(f32[256,512]{1,0:T(8,128)} %fusion.22) | copy-start | bytes 1572868
  67.3 2.7 %copy-start.5 = (f32[256,512]{1,0:T(8,128)S(1)}, f32[256,512]{1,0:T(8,128)}, u32[]{:S(2)}) copy-start(f32[256,512]{1,0:T(8,128)} %get-tuple-element.36) | copy-start | bytes 1572868
  67.3 2.7 %copy-start.10 = (bf16[256,512]{1,0:T(8,128)(2,1)S(1)}, bf16[256,512]{1,0:T(8,128)(2,1)}, u32[]{:S(2)}) copy-start(bf16[256,512]{1,0:T(8,128)(2,1)} %copy-done.9) | copy-start | bytes 786436
  71.1 7.1 %collective-permute-start.17 = (bf16[256,512]{1,0:T(8,128)(2,1)S(1)}, bf16[256,512]{1,0:T(8,128)(2,1)S(1)}, u32[]{:S(2)}, u32[]{:S(2)}) collective-permute-start(bf16[256,512]{1,0:T(8,128)(2,1)S(1)} %get-tuple-element.9), channel_id=1, source_target_pairs={{0,24},{8,16},{16,8},{24,0},{1,25},{9,17},{17,9},{25,1},{2,26},{10... | collective-permute-start | bytes 786440 | tf_op jit(solution)/shard_map/ppermute | solution.py:24
  73.2 12.6 %collective-permute-start.16 = (bf16[256,512]{1,0:T(8,128)(2,1)S(1)}, bf16[256,512]{1,0:T(8,128)(2,1)S(1)}, u32[]{:S(2)}, u32[]{:S(2)}) collective-permute-start(bf16[256,512]{1,0:T(8,128)(2,1)S(1)} %get-tuple-element.9), channel_id=1, source_target_pairs={{0,16},{8,24},{16,0},{24,8},{1,17},{9,25},{17,1},{25,9},{2,18},{10... | collective-permute-start | bytes 786440 | tf_op jit(solution)/shard_map/ppermute | solution.py:24
  73.4 12.3 %collective-permute-start.15 = (bf16[256,512]{1,0:T(8,128)(2,1)S(1)}, bf16[256,512]{1,0:T(8,128)(2,1)S(1)}, u32[]{:S(2)}, u32[]{:S(2)}) collective-permute-start(bf16[256,512]{1,0:T(8,128)(2,1)S(1)} %get-tuple-element.9), channel_id=1, source_target_pairs={{0,8},{8,0},{16,24},{24,16},{1,9},{9,1},{17,25},{25,17},{2,10},{10... | collective-permute-start | bytes 786440 | tf_op jit(solution)/shard_map/ppermute | solution.py:24
  85.9 16.8 %collective-permute-start.18 = (bf16[4,256,512]{2,1,0:T(8,128)(2,1)S(1)}, bf16[4,256,512]{2,1,0:T(8,128)(2,1)S(1)}, u32[]{:S(2)}, u32[]{:S(2)}) collective-permute-start(bf16[4,256,512]{2,1,0:T(8,128)(2,1)S(1)} %pad_maximum_fusion.2), channel_id=1, source_target_pairs={{0,1},{1,0},{2,3},{3,2},{4,5},{5,4},{6,7},{7,6},{8,9},{9,8},{10,11... | collective-permute-start | bytes 3145736 | tf_op jit(solution)/shard_map/ppermute | solution.py:24
  86.6 13.9 %collective-permute-start.20 = (bf16[256,512]{1,0:T(8,128)(2,1)S(1)}, bf16[256,512]{1,0:T(8,128)(2,1)}, u32[]{:S(2)}, u32[]{:S(2)}) collective-permute-start(bf16[256,512]{1,0:T(8,128)(2,1)S(1)} %get-tuple-element.9), channel_id=1, source_target_pairs={{0,4},{1,5},{2,6},{3,7},{4,0},{5,1},{6,2},{7,3},{8,12},{9,13},{10,... | collective-permute-start | bytes 786440 | tf_op jit(solution)/shard_map/ppermute | solution.py:24
  86.6 22.9 %collective-permute-start.19 = (bf16[256,512]{1,0:T(8,128)(2,1)S(1)}, bf16[256,512]{1,0:T(8,128)(2,1)}, u32[]{:S(2)}, u32[]{:S(2)}) collective-permute-start(bf16[256,512]{1,0:T(8,128)(2,1)S(1)} %get-tuple-element.9), channel_id=1, source_target_pairs={{0,2},{1,3},{2,0},{3,1},{4,6},{5,7},{6,4},{7,5},{8,10},{9,11},{10,... | collective-permute-start | bytes 786440 | tf_op jit(solution)/shard_map/ppermute | solution.py:24
  100.5 7.7 %collective-permute-start.21 = (bf16[1,256,512]{2,1,0:T(8,128)(2,1)}, bf16[1,256,512]{2,1,0:T(8,128)(2,1)}, u32[]{:S(2)}, u32[]{:S(2)}) collective-permute-start(bf16[1,256,512]{2,1,0:T(8,128)(2,1)} %bitcast.29), channel_id=1, source_target_pairs={{0,2},{1,3},{2,0},{3,1},{4,6},{5,7},{6,4},{7,5},{8,10},{9,11},{10,... | collective-permute-start | bytes 786440 | tf_op jit(solution)/shard_map/ppermute | solution.py:24
  112.9 14.8 %collective-permute-start.23 = (bf16[256,512]{1,0:T(8,128)(2,1)S(1)}, bf16[256,512]{1,0:T(8,128)(2,1)S(1)}, u32[]{:S(2)}, u32[]{:S(2)}) collective-permute-start(bf16[256,512]{1,0:T(8,128)(2,1)S(1)} %get-tuple-element.7), channel_id=1, source_target_pairs={{0,4},{1,5},{2,6},{3,7},{4,0},{5,1},{6,2},{7,3},{8,12},{9,13},{10,... | collective-permute-start | bytes 786440 | tf_op jit(solution)/shard_map/ppermute | solution.py:24
  112.9 14.8 %collective-permute-start.27 = (bf16[256,512]{1,0:T(8,128)(2,1)S(1)}, bf16[256,512]{1,0:T(8,128)(2,1)S(1)}, u32[]{:S(2)}, u32[]{:S(2)}) collective-permute-start(bf16[256,512]{1,0:T(8,128)(2,1)S(1)} %get-tuple-element.7), channel_id=1, source_target_pairs={{0,24},{8,16},{16,8},{24,0},{1,25},{9,17},{17,9},{25,1},{2,26},{10... | collective-permute-start | bytes 786440 | tf_op jit(solution)/shard_map/ppermute | solution.py:24
  114.2 13.4 %collective-permute-start.26 = (bf16[256,512]{1,0:T(8,128)(2,1)S(1)}, bf16[256,512]{1,0:T(8,128)(2,1)S(1)}, u32[]{:S(2)}, u32[]{:S(2)}) collective-permute-start(bf16[256,512]{1,0:T(8,128)(2,1)S(1)} %get-tuple-element.7), channel_id=1, source_target_pairs={{0,16},{8,24},{16,0},{24,8},{1,17},{9,25},{17,1},{25,9},{2,18},{10... | collective-permute-start | bytes 786440 | tf_op jit(solution)/shard_map/ppermute | solution.py:24
  115.3 12.4 %collective-permute-start.25 = (bf16[256,512]{1,0:T(8,128)(2,1)S(1)}, bf16[256,512]{1,0:T(8,128)(2,1)S(1)}, u32[]{:S(2)}, u32[]{:S(2)}) collective-permute-start(bf16[256,512]{1,0:T(8,128)(2,1)S(1)} %get-tuple-element.7), channel_id=1, source_target_pairs={{0,8},{8,0},{16,24},{24,16},{1,9},{9,1},{17,25},{25,17},{2,10},{10... | collective-permute-start | bytes 786440 | tf_op jit(solution)/shard_map/ppermute | solution.py:24
  115.5 15.1 %collective-permute-start.22 = (bf16[256,512]{1,0:T(8,128)(2,1)S(1)}, bf16[256,512]{1,0:T(8,128)(2,1)S(1)}, u32[]{:S(2)}, u32[]{:S(2)}) collective-permute-start(bf16[256,512]{1,0:T(8,128)(2,1)S(1)} %get-tuple-element.7), channel_id=1, source_target_pairs={{0,2},{1,3},{2,0},{3,1},{4,6},{5,7},{6,4},{7,5},{8,10},{9,11},{10,... | collective-permute-start | bytes 786440 | tf_op jit(solution)/shard_map/ppermute | solution.py:24
  127.6 4.1 %copy-start.7 = (bf16[256,512]{1,0:T(8,128)(2,1)}, bf16[256,512]{1,0:T(8,128)(2,1)S(1)}, u32[]{:S(2)}) copy-start(bf16[256,512]{1,0:T(8,128)(2,1)S(1)} %collective-permute-done.23) | copy-start | bytes 786436
  127.6 7.3 %collective-permute-start.24 = (bf16[1,256,512]{2,1,0:T(8,128)(2,1)S(1)}, bf16[1,256,512]{2,1,0:T(8,128)(2,1)S(1)}, u32[]{:S(2)}, u32[]{:S(2)}) collective-permute-start(bf16[1,256,512]{2,1,0:T(8,128)(2,1)S(1)} %bitcast.177), channel_id=1, source_target_pairs={{0,2},{1,3},{2,0},{3,1},{4,6},{5,7},{6,4},{7,5},{8,10},{9,11},{10,... | collective-permute-start | bytes 786440 | tf_op jit(solution)/shard_map/ppermute | solution.py:24
  127.8 8.2 %collective-permute-start.28 = (bf16[4,256,512]{2,1,0:T(8,128)(2,1)S(1)}, bf16[4,256,512]{2,1,0:T(8,128)(2,1)S(1)}, u32[]{:S(2)}, u32[]{:S(2)}) collective-permute-start(bf16[4,256,512]{2,1,0:T(8,128)(2,1)S(1)} %pad_maximum_fusion.3), channel_id=1, source_target_pairs={{0,1},{1,0},{2,3},{3,2},{4,5},{5,4},{6,7},{7,6},{8,9},{9,8},{10,11... | collective-permute-start | bytes 3145736 | tf_op jit(solution)/shard_map/ppermute | solution.py:24
  141.3 2.7 %copy-start = (f32[256,512]{1,0:T(8,128)S(1)}, f32[256,512]{1,0:T(8,128)}, u32[]{:S(2)}) copy-start(f32[256,512]{1,0:T(8,128)} %convolution_add_fusion.3) | copy-start | bytes 1572868
  141.3 2.7 %copy-start.2 = (f32[256,512]{1,0:T(8,128)S(1)}, f32[256,512]{1,0:T(8,128)}, u32[]{:S(2)}) copy-start(f32[256,512]{1,0:T(8,128)} %fusion.16) | copy-start | bytes 1572868
  141.3 2.7 %copy-start.4 = (f32[256,512]{1,0:T(8,128)S(1)}, f32[256,512]{1,0:T(8,128)}, u32[]{:S(2)}) copy-start(f32[256,512]{1,0:T(8,128)} %get-tuple-element.37) | copy-start | bytes 1572868
  141.3 2.7 %copy-start.8 = (bf16[256,512]{1,0:T(8,128)(2,1)S(1)}, bf16[256,512]{1,0:T(8,128)(2,1)}, u32[]{:S(2)}) copy-start(bf16[256,512]{1,0:T(8,128)(2,1)} %copy-done.7) | copy-start | bytes 786436
  144.4 2.7 %collective-permute-start.29 = (f32[256,256]{1,0:T(8,128)S(1)}, f32[256,256]{1,0:T(8,128)S(1)}, u32[]{:S(2)}, u32[]{:S(2)}) collective-permute-start(f32[256,256]{1,0:T(8,128)S(1)} %constant_dynamic-slice_fusion), channel_id=1, source_target_pairs={{0,1},{1,0},{2,3},{3,2},{4,5},{5,4},{6,7},{7,6},{8,9},{9,8},{10,11... | collective-permute-start | bytes 786440 | tf_op jit(solution)/shard_map/ppermute | solution.py:24

commit v10 on v7

--- a/solution.py
+++ b/solution.py
@@ -31,23 +31,27 @@
     forward = list(range(2, chips, 2))
     same = {0: xb}
     for s in sorted(forward, reverse=True):
-        same[s] = tuple(xor_permute(p, "col", n_col, 2 * s) for p in parts)
+        same[s] = [xor_permute(parts[0], "col", n_col, 2 * s)]
     same[1] = xor_permute(xb, "col", n_col, 2)
     col_pieces = [xb] + [xor_permute(xb, "row", n_row, t) for t in range(1, n_row)]
     relay_first = xor_permute(jnp.stack([xb, same[1]]), "col", n_col, 1)
     other = {0: relay_first[0], 1: relay_first[1]}
     if forward:
-        relay_halves = xor_permute(
-            jnp.stack([p for s in forward for p in same[s]]), "col", n_col, 1
-        )
+        for s in sorted(forward, reverse=True):
+            later, landed = lax.optimization_barrier((parts[1], same[s][0]))
+            same[s] = [landed, xor_permute(later, "col", n_col, 2 * s)]
         sent = [
             xor_permute(jnp.stack([same[s][h] for s in forward]), "col", n_col, 2) for h in (0, 1)
         ]
+        relay_halves = xor_permute(
+            jnp.stack([same[s][h] for s in forward for h in (0, 1)]), "col", n_col, 1
+        )
         relay_sent = xor_permute(jnp.stack(sent), "col", n_col, 1)
         for i, s in enumerate(forward):
             other[s] = (relay_halves[2 * i], relay_halves[2 * i + 1])
             same[s ^ 1] = (sent[0][i], sent[1][i])
             other[s ^ 1] = (relay_sent[0, i], relay_sent[1, i])
+            same[s] = tuple(same[s])
     row_pieces = []
     for s in range(chips):
         row_pieces.append(same[s])

time: 186 us -> 159 us (0.85)
  matrix products: 53.1 us -> 37.7 us
  waiting for transfers between devices: 43.3 us -> 32.6 us
  local copies, waits for them, and re-layouts: 14.2 us -> 18.4 us
  starting transfers between devices: 59.3 us -> 56.4 us
    ppermute x44, waiting for transfers between devices: 43.3 us -> 32.6 us  [xor_permute(): return lax.ppermute(x, axis, perm=[(i, i ^ s) for i in range(size)])]
    dot_general x24, matrix products: 19.2 us -> 11.9 us  [contract(): jnp.dot(piece[0], k_blocks[s, :half], preferred_element_type=jnp.float32)]
    dot_general x24, matrix products: 17.3 us -> 13 us  [contract(): jnp.dot(piece[1], k_blocks[s, half:], preferred_element_type=jnp.float32)]
    dot_general x24, matrix products: 16.7 us -> 12.8 us  [contract(): parts = [jnp.dot(piece, k_blocks[s], preferred_element_type=jnp.float32)]]
    unnamed x55 -> x65, local copies, waits for them, and re-layouts: 8.97 us -> 11.9 us
    ppermute x44, starting transfers between devices: 59.3 us -> 56.4 us  [xor_permute(): return lax.ppermute(x, axis, perm=[(i, i ^ s) for i in range(size)])]
  transfers between devices with their start and end apart: 44 -> 44, of which waited for: 14 -> 11; matrix products, arithmetic and copies ran while one was open for 33% -> 30% of each run, Pallas kernels for 0% -> 0%
where the time goes in v10:
time: 159 us; the launch traced here: 158 us
  starting transfers between devices  56.4 us (35%)
  matrix products  37.7 us (24%)
  waiting for transfers between devices  32.6 us (21%)
  local copies, waits for them, and re-layouts  18.4 us (12%)
  other arithmetic  11.8 us (7%)
    ppermute x44, starting transfers between devices, xor_permute(): return lax.ppermute(x, axis, perm=[(i, i ^ s) for i in range(size)])  56.4 us
    ppermute x44, waiting for transfers between devices, xor_permute(): return lax.ppermute(x, axis, perm=[(i, i ^ s) for i in range(size)])  32.6 us
    dot_general x24, matrix products, contract(): jnp.dot(piece[1], k_blocks[s, half:], preferred_element_type=jnp.float32)  13 us
    dot_general x24, matrix products, contract(): parts = [jnp.dot(piece, k_blocks[s], preferred_element_type=jnp.float32)]  12.8 us
    unnamed x65, local copies, waits for them, and re-layouts  11.9 us
    dot_general x24, matrix products, contract(): jnp.dot(piece[0], k_blocks[s, :half], preferred_element_type=jnp.float32)  11.9 us
    gather x4, local copies, waits for them, and re-layouts, ordered_k_blocks(): return jnp.take(split, index, axis=0)  4.9 us
    another operation x4, other arithmetic, exchange(): jnp.stack([same[s][h] for s in forward for h in (0, 1)])  3.41 us
  transfers between devices with their start and end apart: 44, of which 11 were waited for; matrix products, arithmetic and copies ran while one was open for 30% of the time, Pallas kernels for 0%

profile of v10, /device:TPU:1, one launch (start us, length us, event | category | flops | bytes accessed | tf_op | source)
XLA Modules:
  0.0 157.8 jit_solution(8704621062223990243)
XLA Ops:
  1.2 3.2 %collective-permute-start.5 = (bf16[512,128]{1,0:T(8,128)(2,1)S(1)}, bf16[512,128]{1,0:T(8,128)(2,1)S(1)}, u32[]{:S(2)}, u32[]{:S(2)}) collective-permute-start(bf16[512,128]{1,0:T(8,128)(2,1)S(1)} %get-tuple-element.30), channel_id=1, source_target_pairs={{0,4},{1,5},{2,6},{3,7},{4,0},{5,1},{6,2},{7,3},{8,12},{9,13},{10,... | collective-permute-start | bytes 393224 | tf_op jit(solution)/shard_map/ppermute | solution.py:24
  4.4 2.2 %collective-permute-start.2 = (bf16[512,256]{1,0:T(8,128)(2,1)S(1)}, bf16[512,256]{1,0:T(8,128)(2,1)S(1)}, u32[]{:S(2)}, u32[]{:S(2)}) collective-permute-start(bf16[512,256]{1,0:T(8,128)(2,1)S(1)} %fusion.58), channel_id=1, source_target_pairs={{0,24},{8,16},{16,8},{24,0},{1,25},{9,17},{17,9},{25,1},{2,26},{10... | collective-permute-start | bytes 786440 | tf_op jit(solution)/shard_map/ppermute | solution.py:24
  7.0 1.3 collective-permute-start.3
  8.3 2.1 %collective-permute-done.5 = bf16[512,128]{1,0:T(8,128)(2,1)S(1)} collective-permute-done((bf16[512,128]{1,0:T(8,128)(2,1)S(1)}, bf16[512,128]{1,0:T(8,128)(2,1)S(1)}, u32[]{:S(2)}, u32[]{:S(2)}) %collective-permute-start.5) | collective-permute-done | bytes 131104 | tf_op jit(solution)/shard_map/ppermute | solution.py:24
  10.5 4.8 %collective-permute-done.6 = bf16[512,128]{1,0:T(8,128)(2,1)S(1)} collective-permute-done((bf16[512,128]{1,0:T(8,128)(2,1)S(1)}, bf16[512,128]{1,0:T(8,128)(2,1)S(1)}, u32[]{:S(2)}, u32[]{:S(2)}) %collective-permute-start.6) | collective-permute-done | bytes 131104 | tf_op jit(solution)/shard_map/ppermute | solution.py:24
  15.2 3.9 %collective-permute-start.8 = (bf16[1,512,128]{2,1,0:T(8,128)(2,1)S(1)}, bf16[1,512,128]{2,1,0:T(8,128)(2,1)S(1)}, u32[]{:S(2)}, u32[]{:S(2)}) collective-permute-start(bf16[1,512,128]{2,1,0:T(8,128)(2,1)S(1)} %bitcast.388), channel_id=1, source_target_pairs={{0,2},{1,3},{2,0},{3,1},{4,6},{5,7},{6,4},{7,5},{8,10},{9,11},{10,... | collective-permute-start | bytes 393224 | tf_op jit(solution)/shard_map/ppermute | solution.py:24
  19.9 3.1 %collective-permute-start.7 = (bf16[2,512,128]{2,1,0:T(8,128)(2,1)}, bf16[2,512,128]{2,1,0:T(8,128)(2,1)}, u32[]{:S(2)}, u32[]{:S(2)}) collective-permute-start(bf16[2,512,128]{2,1,0:T(8,128)(2,1)} %pad_maximum_fusion.8), channel_id=1, source_target_pairs={{0,1},{1,0},{2,3},{3,2},{4,5},{5,4},{6,7},{7,6},{8,9},{9,8},{10,11... | collective-permute-start | bytes 786440 | tf_op jit(solution)/shard_map/ppermute | solution.py:24
  26.4 1.9 %collective-permute-start.10 = (bf16[2,1,512,128]{3,2,1,0:T(8,128)(2,1)S(1)}, bf16[2,1,512,128]{3,2,1,0:T(8,128)(2,1)S(1)}, u32[]{:S(2)}, u32[]{:S(2)}) collective-permute-start(bf16[2,1,512,128]{3,2,1,0:T(8,128)(2,1)S(1)} %pad_maximum_fusion.9), channel_id=1, source_target_pairs={{0,1},{1,0},{2,3},{3,2},{4,5},{5,4},{6,7},{7,6},{8,9},{9,8},{10,11... | collective-permute-start | bytes 786440 | tf_op jit(solution)/shard_map/ppermute | solution.py:24
  28.3 1.1 fusion.94
  29.5 1.1 fusion.105
  30.6 1.1 fusion.103
  33.7 1.3 fusion.139
  34.9 2.1 %collective-permute-start.21 = (bf16[512,256]{1,0:T(8,128)(2,1)S(1)}, bf16[512,256]{1,0:T(8,128)(2,1)S(1)}, u32[]{:S(2)}, u32[]{:S(2)}) collective-permute-start(bf16[512,256]{1,0:T(8,128)(2,1)S(1)} %get-tuple-element.32), channel_id=1, source_target_pairs={{0,24},{8,16},{16,8},{24,0},{1,25},{9,17},{17,9},{25,1},{2,26},{10... | collective-permute-start | bytes 786440 | tf_op jit(solution)/shard_map/ppermute | solution.py:24
  38.4 3.2 %collective-permute-start.13 = (bf16[512,128]{1,0:T(8,128)(2,1)S(1)}, bf16[512,128]{1,0:T(8,128)(2,1)S(1)}, u32[]{:S(2)}, u32[]{:S(2)}) collective-permute-start(bf16[512,128]{1,0:T(8,128)(2,1)S(1)} %get-tuple-element.28), channel_id=1, source_target_pairs={{0,4},{1,5},{2,6},{3,7},{4,0},{5,1},{6,2},{7,3},{8,12},{9,13},{10,... | collective-permute-start | bytes 393224 | tf_op jit(solution)/shard_map/ppermute | solution.py:24
  42.6 3.3 %collective-permute-done.13 = bf16[512,128]{1,0:T(8,128)(2,1)S(1)} collective-permute-done((bf16[512,128]{1,0:T(8,128)(2,1)S(1)}, bf16[512,128]{1,0:T(8,128)(2,1)S(1)}, u32[]{:S(2)}, u32[]{:S(2)}) %collective-permute-start.13) | collective-permute-done | bytes 131104 | tf_op jit(solution)/shard_map/ppermute | solution.py:24
  45.9 3.1 %collective-permute-start.14 = (bf16[512,128]{1,0:T(8,128)(2,1)S(1)}, bf16[512,128]{1,0:T(8,128)(2,1)}, u32[]{:S(2)}, u32[]{:S(2)}) collective-permute-start(bf16[512,128]{1,0:T(8,128)(2,1)S(1)} %get-tuple-element.17), channel_id=1, source_target_pairs={{0,4},{1,5},{2,6},{3,7},{4,0},{5,1},{6,2},{7,3},{8,12},{9,13},{10,... | collective-permute-start | bytes 393224 | tf_op jit(solution)/shard_map/ppermute | solution.py:24
  50.0 2.6 %collective-permute-done.14 = bf16[512,128]{1,0:T(8,128)(2,1)} collective-permute-done((bf16[512,128]{1,0:T(8,128)(2,1)S(1)}, bf16[512,128]{1,0:T(8,128)(2,1)}, u32[]{:S(2)}, u32[]{:S(2)}) %collective-permute-start.14) | collective-permute-done | bytes 131104 | tf_op jit(solution)/shard_map/ppermute | solution.py:24
  52.6 2.8 %collective-permute-start.16 = (bf16[1,512,128]{2,1,0:T(8,128)(2,1)S(1)}, bf16[1,512,128]{2,1,0:T(8,128)(2,1)S(1)}, u32[]{:S(2)}, u32[]{:S(2)}) collective-permute-start(bf16[1,512,128]{2,1,0:T(8,128)(2,1)S(1)} %bitcast.401), channel_id=1, source_target_pairs={{0,2},{1,3},{2,0},{3,1},{4,6},{5,7},{6,4},{7,5},{8,10},{9,11},{10,... | collective-permute-start | bytes 393224 | tf_op jit(solution)/shard_map/ppermute | solution.py:24
  55.4 1.9 %fusion.126 = f32[512,256]{1,0:T(8,128)} fusion(bf16[512,128]{1,0:T(8,128)(2,1)} %collective-permute-done.14, bf16[8,256,256]{2,1,0:T(8,128)(2,1)S(1)} %broadcast_select_fusion.3), kind=kOutput, calls=%fused_computation.237 | convolution fusion | flops 33554432 | bytes 720896 | tf_op jit(solution)/shard_map/dot_general | solution.py:79
  57.3 1.7 %pad_maximum_fusion.10 = bf16[2,512,128]{2,1,0:T(8,128)(2,1)} fusion(bf16[1,512,128]{2,1,0:T(8,128)(2,1)} %bitcast.36, bf16[1,512,128]{2,1,0:T(8,128)(2,1)S(1)} %bitcast.402), kind=kLoop, calls=%fused_computation.103 | loop fusion | flops 131072 | bytes 524288 | tf_op jit(solution)/shard_map/stack | solution.py:47
  60.2 3.8 %collective-permute-start.15 = (bf16[2,512,128]{2,1,0:T(8,128)(2,1)}, bf16[2,512,128]{2,1,0:T(8,128)(2,1)}, u32[]{:S(2)}, u32[]{:S(2)}) collective-permute-start(bf16[2,512,128]{2,1,0:T(8,128)(2,1)} %pad_maximum_fusion.10), channel_id=1, source_target_pairs={{0,1},{1,0},{2,3},{3,2},{4,5},{5,4},{6,7},{7,6},{8,9},{9,8},{10,11... | collective-permute-start | bytes 786440 | tf_op jit(solution)/shard_map/ppermute | solution.py:24
  64.1 1.1 pad_maximum_fusion.1
  65.2 1.8 %gather_fusion.1 = bf16[8,256,256]{2,1,0:T(8,128)(2,1)S(1)} fusion(bf16[8,256,256]{2,1,0:T(8,128)(2,1)} %bitcast.384, s32[1024]{0:T(1024)S(1)} %pad_clamp_fusion), kind=kCustom, calls=%fused_computation.1.clone | custom fusion | bytes 2097184 | tf_op jit(solution)/shard_map/jit(_take)/gather | solution.py:69
  69.3 1.1 fusion.92
  70.6 1.1 fusion.104
  71.8 1.1 fusion.102
  77.9 1.1 fusion.74
  79.1 1.1 fusion.75
  82.7 1.5 fusion.59
  84.2 2.3 %collective-permute-start.24 = (bf16[512,256]{1,0:T(8,128)(2,1)S(1)}, bf16[512,256]{1,0:T(8,128)(2,1)S(1)}, u32[]{:S(2)}, u32[]{:S(2)}) collective-permute-start(bf16[512,256]{1,0:T(8,128)(2,1)S(1)} %fusion.59), channel_id=1, source_target_pairs={{0,24},{8,16},{16,8},{24,0},{1,25},{9,17},{17,9},{25,1},{2,26},{10... | collective-permute-start | bytes 786440 | tf_op jit(solution)/shard_map/ppermute | solution.py:24
  87.6 1.8 %collective-permute-start.27 = (bf16[512,128]{1,0:T(8,128)(2,1)S(1)}, bf16[512,128]{1,0:T(8,128)(2,1)S(1)}, u32[]{:S(2)}, u32[]{:S(2)}) collective-permute-start(bf16[512,128]{1,0:T(8,128)(2,1)S(1)} %get-tuple-element.26), channel_id=1, source_target_pairs={{0,4},{1,5},{2,6},{3,7},{4,0},{5,1},{6,2},{7,3},{8,12},{9,13},{10,... | collective-permute-start | bytes 393224 | tf_op jit(solution)/shard_map/ppermute | solution.py:24
  89.9 6.9 %collective-permute-done.27 = bf16[512,128]{1,0:T(8,128)(2,1)S(1)} collective-permute-done((bf16[512,128]{1,0:T(8,128)(2,1)S(1)}, bf16[512,128]{1,0:T(8,128)(2,1)S(1)}, u32[]{:S(2)}, u32[]{:S(2)}) %collective-permute-start.27) | collective-permute-done | bytes 131104 | tf_op jit(solution)/shard_map/ppermute | solution.py:24
  97.8 1.2 collective-permute-done.23
  100.1 1.9 %collective-permute-start.26 = (bf16[2,512,256]{2,1,0:T(8,128)(2,1)S(1)}, bf16[2,512,256]{2,1,0:T(8,128)(2,1)S(1)}, u32[]{:S(2)}, u32[]{:S(2)}) collective-permute-start(bf16[2,512,256]{2,1,0:T(8,128)(2,1)S(1)} %pad_maximum_fusion.6), channel_id=1, source_target_pairs={{0,1},{1,0},{2,3},{3,2},{4,5},{5,4},{6,7},{7,6},{8,9},{9,8},{10,11... | collective-permute-start | bytes 1572872 | tf_op jit(solution)/shard_map/ppermute | solution.py:24
  102.5 2.7 %collective-permute-done.28 = bf16[512,128]{1,0:T(8,128)(2,1)S(1)} collective-permute-done((bf16[512,128]{1,0:T(8,128)(2,1)}, bf16[512,128]{1,0:T(8,128)(2,1)S(1)}, u32[]{:S(2)}, u32[]{:S(2)}) %collective-permute-start.28) | collective-permute-done | bytes 131104 | tf_op jit(solution)/shard_map/ppermute | solution.py:24
  106.3 3.4 %collective-permute-done.31 = bf16[1,512,128]{2,1,0:T(8,128)(2,1)S(1)} collective-permute-done((bf16[1,512,128]{2,1,0:T(8,128)(2,1)S(1)}, bf16[1,512,128]{2,1,0:T(8,128)(2,1)S(1)}, u32[]{:S(2)}, u32[]{:S(2)}) %collective-permute-start.31) | collective-permute-done | bytes 131104 | tf_op jit(solution)/shard_map/ppermute | solution.py:24
  109.7 1.5 collective-permute-start.32
  114.1 1.3 fusion.140
  115.4 2.2 %collective-permute-start.43 = (bf16[512,256]{1,0:T(8,128)(2,1)S(1)}, bf16[512,256]{1,0:T(8,128)(2,1)S(1)}, u32[]{:S(2)}, u32[]{:S(2)}) collective-permute-start(bf16[512,256]{1,0:T(8,128)(2,1)S(1)} %get-tuple-element.34), channel_id=1, source_target_pairs={{0,24},{8,16},{16,8},{24,0},{1,25},{9,17},{17,9},{25,1},{2,26},{10... | collective-permute-start | bytes 786440 | tf_op jit(solution)/shard_map/ppermute | solution.py:24
  118.7 1.5 collective-permute-start.35
  121.2 4.5 %collective-permute-done.35 = bf16[512,128]{1,0:T(8,128)(2,1)} collective-permute-done((bf16[512,128]{1,0:T(8,128)(2,1)S(1)}, bf16[512,128]{1,0:T(8,128)(2,1)}, u32[]{:S(2)}, u32[]{:S(2)}) %collective-permute-start.35) | collective-permute-done | bytes 131104 | tf_op jit(solution)/shard_map/ppermute | solution.py:24
  125.7 2.9 %collective-permute-start.36 = (bf16[512,128]{1,0:T(8,128)(2,1)}, bf16[512,128]{1,0:T(8,128)(2,1)}, u32[]{:S(2)}, u32[]{:S(2)}) collective-permute-start(bf16[512,128]{1,0:T(8,128)(2,1)} %get-tuple-element.21), channel_id=1, source_target_pairs={{0,4},{1,5},{2,6},{3,7},{4,0},{5,1},{6,2},{7,3},{8,12},{9,13},{10,... | collective-permute-start | bytes 393224 | tf_op jit(solution)/shard_map/ppermute | solution.py:24
  128.7 1.9 %fusion.128 = f32[512,256]{1,0:T(8,128)} fusion(bf16[512,128]{1,0:T(8,128)(2,1)} %collective-permute-done.35, bf16[8,256,256]{2,1,0:T(8,128)(2,1)S(1)} %broadcast_select_fusion.1), kind=kOutput, calls=%fused_computation.239 | convolution fusion | flops 33554432 | bytes 720896 | tf_op jit(solution)/shard_map/dot_general | solution.py:78
  130.6 1.1 pad_maximum_fusion.3
  131.7 1.8 %gather_fusion.3 = bf16[8,256,256]{2,1,0:T(8,128)(2,1)S(1)} fusion(bf16[8,256,256]{2,1,0:T(8,128)(2,1)} %bitcast.382, s32[1024]{0:T(1024)S(1)} %pad_clamp_fusion), kind=kCustom, calls=%fused_computation.3.clone | custom fusion | bytes 2097184 | tf_op jit(solution)/shard_map/jit(_take)/gather | solution.py:69
  136.0 2.9 %collective-permute-start.34 = (bf16[2,512,256]{2,1,0:T(8,128)(2,1)S(1)}, bf16[2,512,256]{2,1,0:T(8,128)(2,1)S(1)}, u32[]{:S(2)}, u32[]{:S(2)}) collective-permute-start(bf16[2,512,256]{2,1,0:T(8,128)(2,1)S(1)} %pad_maximum_fusion.7), channel_id=1, source_target_pairs={{0,1},{1,0},{2,3},{3,2},{4,5},{5,4},{6,7},{7,6},{8,9},{9,8},{10,11... | collective-permute-start | bytes 1572872 | tf_op jit(solution)/shard_map/ppermute | solution.py:24
  144.3 1.8 %collective-permute-start.39 = (bf16[1,512,128]{2,1,0:T(8,128)(2,1)}, bf16[1,512,128]{2,1,0:T(8,128)(2,1)S(1)}, u32[]{:S(2)}, u32[]{:S(2)}) collective-permute-start(bf16[1,512,128]{2,1,0:T(8,128)(2,1)} %bitcast.96), channel_id=1, source_target_pairs={{0,2},{1,3},{2,0},{3,1},{4,6},{5,7},{6,4},{7,5},{8,10},{9,11},{10,... | collective-permute-start | bytes 393224 | tf_op jit(solution)/shard_map/ppermute | solution.py:24
  155.6 2.3 %bitcast_multiply_fusion = f32[512,256]{1,0:T(8,128)} fusion(f32[512,256]{1,0:T(8,128)S(1)} %copy-done.11, f32[64,8,2,128]{3,2,1,0:T(2,128)S(1)} %bitcast.373, f32[512,256]{1,0:T(8,128)S(1)} %fusion.8, f32[512,256]{1,0:T(8,128)S(1)} %fusion.67, f32[512,256]{1,0:T(8,128)S(1)} %fusion.68, f32[512,256]{1,0:T(8,128)S(1)} %fusion.76, ...), kind=kOutput, calls=%fused_computation.82 | convolution fusion | flops 68943872 | bytes 7733248 | tf_op jit(solution)/shard_map/dot_general | solution.py:82
  (210 shorter events, 48.9 us)
Async XLA Ops:
  1.2 9.2 %collective-permute-start.5 = (bf16[512,128]{1,0:T(8,128)(2,1)S(1)}, bf16[512,128]{1,0:T(8,128)(2,1)S(1)}, u32[]{:S(2)}, u32[]{:S(2)}) collective-permute-start(bf16[512,128]{1,0:T(8,128)(2,1)S(1)} %get-tuple-element.30), channel_id=1, source_target_pairs={{0,4},{1,5},{2,6},{3,7},{4,0},{5,1},{6,2},{7,3},{8,12},{9,13},{10,... | collective-permute-start | bytes 393224 | tf_op jit(solution)/shard_map/ppermute | solution.py:24
  4.4 15.5 %collective-permute-start.2 = (bf16[512,256]{1,0:T(8,128)(2,1)S(1)}, bf16[512,256]{1,0:T(8,128)(2,1)S(1)}, u32[]{:S(2)}, u32[]{:S(2)}) collective-permute-start(bf16[512,256]{1,0:T(8,128)(2,1)S(1)} %fusion.58), channel_id=1, source_target_pairs={{0,24},{8,16},{16,8},{24,0},{1,25},{9,17},{17,9},{25,1},{2,26},{10... | collective-permute-start | bytes 786440 | tf_op jit(solution)/shard_map/ppermute | solution.py:24
  6.6 13.4 %collective-permute-start.1 = (bf16[512,256]{1,0:T(8,128)(2,1)S(1)}, bf16[512,256]{1,0:T(8,128)(2,1)S(1)}, u32[]{:S(2)}, u32[]{:S(2)}) collective-permute-start(bf16[512,256]{1,0:T(8,128)(2,1)S(1)} %fusion.58), channel_id=1, source_target_pairs={{0,16},{8,24},{16,0},{24,8},{1,17},{9,25},{17,1},{25,9},{2,18},{10... | collective-permute-start | bytes 786440 | tf_op jit(solution)/shard_map/ppermute | solution.py:24
  6.8 16.3 %collective-permute-start = (bf16[512,256]{1,0:T(8,128)(2,1)S(1)}, bf16[512,256]{1,0:T(8,128)(2,1)S(1)}, u32[]{:S(2)}, u32[]{:S(2)}) collective-permute-start(bf16[512,256]{1,0:T(8,128)(2,1)S(1)} %fusion.58), channel_id=1, source_target_pairs={{0,8},{8,0},{16,24},{24,16},{1,9},{9,1},{17,25},{25,17},{2,10},{10... | collective-permute-start | bytes 786440 | tf_op jit(solution)/shard_map/ppermute | solution.py:24
  7.0 17.4 %collective-permute-start.3 = (bf16[512,256]{1,0:T(8,128)(2,1)S(1)}, bf16[512,256]{1,0:T(8,128)(2,1)S(1)}, u32[]{:S(2)}, u32[]{:S(2)}) collective-permute-start(bf16[512,256]{1,0:T(8,128)(2,1)S(1)} %fusion.58), channel_id=1, source_target_pairs={{0,2},{1,3},{2,0},{3,1},{4,6},{5,7},{6,4},{7,5},{8,10},{9,11},{10,... | collective-permute-start | bytes 786440 | tf_op jit(solution)/shard_map/ppermute | solution.py:24
  10.4 4.8 %collective-permute-start.6 = (bf16[512,128]{1,0:T(8,128)(2,1)S(1)}, bf16[512,128]{1,0:T(8,128)(2,1)S(1)}, u32[]{:S(2)}, u32[]{:S(2)}) collective-permute-start(bf16[512,128]{1,0:T(8,128)(2,1)S(1)} %get-tuple-element.15), channel_id=1, source_target_pairs={{0,4},{1,5},{2,6},{3,7},{4,0},{5,1},{6,2},{7,3},{8,12},{9,13},{10,... | collective-permute-start | bytes 393224 | tf_op jit(solution)/shard_map/ppermute | solution.py:24
  15.2 9.4 %copy-start.12 = (bf16[512,128]{1,0:T(8,128)(2,1)}, bf16[512,128]{1,0:T(8,128)(2,1)S(1)}, u32[]{:S(2)}) copy-start(bf16[512,128]{1,0:T(8,128)(2,1)S(1)} %collective-permute-done.6) | copy-start | bytes 393220
  15.2 9.6 %collective-permute-start.8 = (bf16[1,512,128]{2,1,0:T(8,128)(2,1)S(1)}, bf16[1,512,128]{2,1,0:T(8,128)(2,1)S(1)}, u32[]{:S(2)}, u32[]{:S(2)}) collective-permute-start(bf16[1,512,128]{2,1,0:T(8,128)(2,1)S(1)} %bitcast.388), channel_id=1, source_target_pairs={{0,2},{1,3},{2,0},{3,1},{4,6},{5,7},{6,4},{7,5},{8,10},{9,11},{10,... | collective-permute-start | bytes 393224 | tf_op jit(solution)/shard_map/ppermute | solution.py:24
  19.9 5.1 %collective-permute-start.9 = (bf16[1,512,128]{2,1,0:T(8,128)(2,1)S(1)}, bf16[1,512,128]{2,1,0:T(8,128)(2,1)}, u32[]{:S(2)}, u32[]{:S(2)}) collective-permute-start(bf16[1,512,128]{2,1,0:T(8,128)(2,1)S(1)} %bitcast.391), channel_id=1, source_target_pairs={{0,2},{1,3},{2,0},{3,1},{4,6},{5,7},{6,4},{7,5},{8,10},{9,11},{10,... | collective-permute-start | bytes 393224 | tf_op jit(solution)/shard_map/ppermute | solution.py:24
  19.9 9.5 %collective-permute-start.7 = (bf16[2,512,128]{2,1,0:T(8,128)(2,1)}, bf16[2,512,128]{2,1,0:T(8,128)(2,1)}, u32[]{:S(2)}, u32[]{:S(2)}) collective-permute-start(bf16[2,512,128]{2,1,0:T(8,128)(2,1)} %pad_maximum_fusion.8), channel_id=1, source_target_pairs={{0,1},{1,0},{2,3},{3,2},{4,5},{5,4},{6,7},{7,6},{8,9},{9,8},{10,11... | collective-permute-start | bytes 786440 | tf_op jit(solution)/shard_map/ppermute | solution.py:24
  24.5 8.1 %collective-permute-start.4 = (bf16[2,512,256]{2,1,0:T(8,128)(2,1)S(1)}, bf16[2,512,256]{2,1,0:T(8,128)(2,1)S(1)}, u32[]{:S(2)}, u32[]{:S(2)}) collective-permute-start(bf16[2,512,256]{2,1,0:T(8,128)(2,1)S(1)} %pad_maximum_fusion.4), channel_id=1, source_target_pairs={{0,1},{1,0},{2,3},{3,2},{4,5},{5,4},{6,7},{7,6},{8,9},{9,8},{10,11... | collective-permute-start | bytes 1572872 | tf_op jit(solution)/shard_map/ppermute | solution.py:24
  26.4 5.3 %collective-permute-start.10 = (bf16[2,1,512,128]{3,2,1,0:T(8,128)(2,1)S(1)}, bf16[2,1,512,128]{3,2,1,0:T(8,128)(2,1)S(1)}, u32[]{:S(2)}, u32[]{:S(2)}) collective-permute-start(bf16[2,1,512,128]{3,2,1,0:T(8,128)(2,1)S(1)} %pad_maximum_fusion.9), channel_id=1, source_target_pairs={{0,1},{1,0},{2,3},{3,2},{4,5},{5,4},{6,7},{7,6},{8,9},{9,8},{10,11... | collective-permute-start | bytes 786440 | tf_op jit(solution)/shard_map/ppermute | solution.py:24
  34.9 25.3 %collective-permute-start.21 = (bf16[512,256]{1,0:T(8,128)(2,1)S(1)}, bf16[512,256]{1,0:T(8,128)(2,1)S(1)}, u32[]{:S(2)}, u32[]{:S(2)}) collective-permute-start(bf16[512,256]{1,0:T(8,128)(2,1)S(1)} %get-tuple-element.32), channel_id=1, source_target_pairs={{0,24},{8,16},{16,8},{24,0},{1,25},{9,17},{17,9},{25,1},{2,26},{10... | collective-permute-start | bytes 786440 | tf_op jit(solution)/shard_map/ppermute | solution.py:24
  37.1 27.0 %collective-permute-start.20 = (bf16[512,256]{1,0:T(8,128)(2,1)S(1)}, bf16[512,256]{1,0:T(8,128)(2,1)S(1)}, u32[]{:S(2)}, u32[]{:S(2)}) collective-permute-start(bf16[512,256]{1,0:T(8,128)(2,1)S(1)} %get-tuple-element.32), channel_id=1, source_target_pairs={{0,16},{8,24},{16,0},{24,8},{1,17},{9,25},{17,1},{25,9},{2,18},{10... | collective-permute-start | bytes 786440 | tf_op jit(solution)/shard_map/ppermute | solution.py:24
  37.3 26.8 %collective-permute-start.19 = (bf16[512,256]{1,0:T(8,128)(2,1)S(1)}, bf16[512,256]{1,0:T(8,128)(2,1)S(1)}, u32[]{:S(2)}, u32[]{:S(2)}) collective-permute-start(bf16[512,256]{1,0:T(8,128)(2,1)S(1)} %get-tuple-element.32), channel_id=1, source_target_pairs={{0,8},{8,0},{16,24},{24,16},{1,9},{9,1},{17,25},{25,17},{2,10},{10... | collective-permute-start | bytes 786440 | tf_op jit(solution)/shard_map/ppermute | solution.py:24
  37.6 30.1 %collective-permute-start.11 = (bf16[512,256]{1,0:T(8,128)(2,1)S(1)}, bf16[512,256]{1,0:T(8,128)(2,1)}, u32[]{:S(2)}, u32[]{:S(2)}) collective-permute-start(bf16[512,256]{1,0:T(8,128)(2,1)S(1)} %get-tuple-element.32), channel_id=1, source_target_pairs={{0,2},{1,3},{2,0},{3,1},{4,6},{5,7},{6,4},{7,5},{8,10},{9,11},{10,... | collective-permute-start | bytes 786440 | tf_op jit(solution)/shard_map/ppermute | solution.py:24
  38.4 7.6 %collective-permute-start.13 = (bf16[512,128]{1,0:T(8,128)(2,1)S(1)}, bf16[512,128]{1,0:T(8,128)(2,1)S(1)}, u32[]{:S(2)}, u32[]{:S(2)}) collective-permute-start(bf16[512,128]{1,0:T(8,128)(2,1)S(1)} %get-tuple-element.28), channel_id=1, source_target_pairs={{0,4},{1,5},{2,6},{3,7},{4,0},{5,1},{6,2},{7,3},{8,12},{9,13},{10,... | collective-permute-start | bytes 393224 | tf_op jit(solution)/shard_map/ppermute | solution.py:24
  45.9 6.7 %collective-permute-start.14 = (bf16[512,128]{1,0:T(8,128)(2,1)S(1)}, bf16[512,128]{1,0:T(8,128)(2,1)}, u32[]{:S(2)}, u32[]{:S(2)}) collective-permute-start(bf16[512,128]{1,0:T(8,128)(2,1)S(1)} %get-tuple-element.17), channel_id=1, source_target_pairs={{0,4},{1,5},{2,6},{3,7},{4,0},{5,1},{6,2},{7,3},{8,12},{9,13},{10,... | collective-permute-start | bytes 393224 | tf_op jit(solution)/shard_map/ppermute | solution.py:24
  52.6 6.4 %collective-permute-start.16 = (bf16[1,512,128]{2,1,0:T(8,128)(2,1)S(1)}, bf16[1,512,128]{2,1,0:T(8,128)(2,1)S(1)}, u32[]{:S(2)}, u32[]{:S(2)}) collective-permute-start(bf16[1,512,128]{2,1,0:T(8,128)(2,1)S(1)} %bitcast.401), channel_id=1, source_target_pairs={{0,2},{1,3},{2,0},{3,1},{4,6},{5,7},{6,4},{7,5},{8,10},{9,11},{10,... | collective-permute-start | bytes 393224 | tf_op jit(solution)/shard_map/ppermute | solution.py:24
  59.0 15.9 %collective-permute-start.17 = (bf16[1,512,128]{2,1,0:T(8,128)(2,1)}, bf16[1,512,128]{2,1,0:T(8,128)(2,1)}, u32[]{:S(2)}, u32[]{:S(2)}) collective-permute-start(bf16[1,512,128]{2,1,0:T(8,128)(2,1)} %bitcast.36), channel_id=1, source_target_pairs={{0,2},{1,3},{2,0},{3,1},{4,6},{5,7},{6,4},{7,5},{8,10},{9,11},{10,... | collective-permute-start | bytes 393224 | tf_op jit(solution)/shard_map/ppermute | solution.py:24
  60.2 17.7 %collective-permute-start.15 = (bf16[2,512,128]{2,1,0:T(8,128)(2,1)}, bf16[2,512,128]{2,1,0:T(8,128)(2,1)}, u32[]{:S(2)}, u32[]{:S(2)}) collective-permute-start(bf16[2,512,128]{2,1,0:T(8,128)(2,1)} %pad_maximum_fusion.10), channel_id=1, source_target_pairs={{0,1},{1,0},{2,3},{3,2},{4,5},{5,4},{6,7},{7,6},{8,9},{9,8},{10,11... | collective-permute-start | bytes 786440 | tf_op jit(solution)/shard_map/ppermute | solution.py:24
  68.7 11.9 %collective-permute-start.12 = (bf16[2,512,256]{2,1,0:T(8,128)(2,1)S(1)}, bf16[2,512,256]{2,1,0:T(8,128)(2,1)S(1)}, u32[]{:S(2)}, u32[]{:S(2)}) collective-permute-start(bf16[2,512,256]{2,1,0:T(8,128)(2,1)S(1)} %pad_maximum_fusion.5), channel_id=1, source_target_pairs={{0,1},{1,0},{2,3},{3,2},{4,5},{5,4},{6,7},{7,6},{8,9},{9,8},{10,11... | collective-permute-start | bytes 1572872 | tf_op jit(solution)/shard_map/ppermute | solution.py:24
  76.3 3.9 %collective-permute-start.18 = (bf16[2,1,512,128]{3,2,1,0:T(8,128)(2,1)S(1)}, bf16[2,1,512,128]{3,2,1,0:T(8,128)(2,1)S(1)}, u32[]{:S(2)}, u32[]{:S(2)}) collective-permute-start(bf16[2,1,512,128]{3,2,1,0:T(8,128)(2,1)S(1)} %pad_maximum_fusion.11), channel_id=1, source_target_pairs={{0,1},{1,0},{2,3},{3,2},{4,5},{5,4},{6,7},{7,6},{8,9},{9,8},{10,11... | collective-permute-start | bytes 786440 | tf_op jit(solution)/shard_map/ppermute | solution.py:24
  84.2 12.5 %collective-permute-start.24 = (bf16[512,256]{1,0:T(8,128)(2,1)S(1)}, bf16[512,256]{1,0:T(8,128)(2,1)S(1)}, u32[]{:S(2)}, u32[]{:S(2)}) collective-permute-start(bf16[512,256]{1,0:T(8,128)(2,1)S(1)} %fusion.59), channel_id=1, source_target_pairs={{0,24},{8,16},{16,8},{24,0},{1,25},{9,17},{17,9},{25,1},{2,26},{10... | collective-permute-start | bytes 786440 | tf_op jit(solution)/shard_map/ppermute | solution.py:24
  86.5 12.5 %collective-permute-start.23 = (bf16[512,256]{1,0:T(8,128)(2,1)S(1)}, bf16[512,256]{1,0:T(8,128)(2,1)S(1)}, u32[]{:S(2)}, u32[]{:S(2)}) collective-permute-start(bf16[512,256]{1,0:T(8,128)(2,1)S(1)} %fusion.59), channel_id=1, source_target_pairs={{0,16},{8,24},{16,0},{24,8},{1,17},{9,25},{17,1},{25,9},{2,18},{10... | collective-permute-start | bytes 786440 | tf_op jit(solution)/shard_map/ppermute | solution.py:24
  86.8 12.3 %collective-permute-start.22 = (bf16[512,256]{1,0:T(8,128)(2,1)S(1)}, bf16[512,256]{1,0:T(8,128)(2,1)S(1)}, u32[]{:S(2)}, u32[]{:S(2)}) collective-permute-start(bf16[512,256]{1,0:T(8,128)(2,1)S(1)} %fusion.59), channel_id=1, source_target_pairs={{0,8},{8,0},{16,24},{24,16},{1,9},{9,1},{17,25},{25,17},{2,10},{10... | collective-permute-start | bytes 786440 | tf_op jit(solution)/shard_map/ppermute | solution.py:24
  87.6 9.1 %collective-permute-start.27 = (bf16[512,128]{1,0:T(8,128)(2,1)S(1)}, bf16[512,128]{1,0:T(8,128)(2,1)S(1)}, u32[]{:S(2)}, u32[]{:S(2)}) collective-permute-start(bf16[512,128]{1,0:T(8,128)(2,1)S(1)} %get-tuple-element.26), channel_id=1, source_target_pairs={{0,4},{1,5},{2,6},{3,7},{4,0},{5,1},{6,2},{7,3},{8,12},{9,13},{10,... | collective-permute-start | bytes 393224 | tf_op jit(solution)/shard_map/ppermute | solution.py:24
  89.5 10.5 %collective-permute-start.25 = (bf16[512,256]{1,0:T(8,128)(2,1)S(1)}, bf16[512,256]{1,0:T(8,128)(2,1)S(1)}, u32[]{:S(2)}, u32[]{:S(2)}) collective-permute-start(bf16[512,256]{1,0:T(8,128)(2,1)S(1)} %fusion.59), channel_id=1, source_target_pairs={{0,2},{1,3},{2,0},{3,1},{4,6},{5,7},{6,4},{7,5},{8,10},{9,11},{10,... | collective-permute-start | bytes 786440 | tf_op jit(solution)/shard_map/ppermute | solution.py:24
  96.8 8.4 %copy-start.16 = (bf16[512,128]{1,0:T(8,128)(2,1)}, bf16[512,128]{1,0:T(8,128)(2,1)S(1)}, u32[]{:S(2)}) copy-start(bf16[512,128]{1,0:T(8,128)(2,1)S(1)} %collective-permute-done.27) | copy-start | bytes 393220
  96.8 8.4 %collective-permute-start.28 = (bf16[512,128]{1,0:T(8,128)(2,1)}, bf16[512,128]{1,0:T(8,128)(2,1)S(1)}, u32[]{:S(2)}, u32[]{:S(2)}) collective-permute-start(bf16[512,128]{1,0:T(8,128)(2,1)} %get-tuple-element.19), channel_id=1, source_target_pairs={{0,4},{1,5},{2,6},{3,7},{4,0},{5,1},{6,2},{7,3},{8,12},{9,13},{10,... | collective-permute-start | bytes 393224 | tf_op jit(solution)/shard_map/ppermute | solution.py:24
  96.8 9.3 %collective-permute-start.30 = (bf16[1,512,128]{2,1,0:T(8,128)(2,1)S(1)}, bf16[1,512,128]{2,1,0:T(8,128)(2,1)S(1)}, u32[]{:S(2)}, u32[]{:S(2)}) collective-permute-start(bf16[1,512,128]{2,1,0:T(8,128)(2,1)S(1)} %bitcast.395), channel_id=1, source_target_pairs={{0,2},{1,3},{2,0},{3,1},{4,6},{5,7},{6,4},{7,5},{8,10},{9,11},{10,... | collective-permute-start | bytes 393224 | tf_op jit(solution)/shard_map/ppermute | solution.py:24
  100.1 13.2 %collective-permute-start.26 = (bf16[2,512,256]{2,1,0:T(8,128)(2,1)S(1)}, bf16[2,512,256]{2,1,0:T(8,128)(2,1)S(1)}, u32[]{:S(2)}, u32[]{:S(2)}) collective-permute-start(bf16[2,512,256]{2,1,0:T(8,128)(2,1)S(1)} %pad_maximum_fusion.6), channel_id=1, source_target_pairs={{0,1},{1,0},{2,3},{3,2},{4,5},{5,4},{6,7},{7,6},{8,9},{9,8},{10,11... | collective-permute-start | bytes 1572872 | tf_op jit(solution)/shard_map/ppermute | solution.py:24
  105.2 4.5 %collective-permute-start.31 = (bf16[1,512,128]{2,1,0:T(8,128)(2,1)S(1)}, bf16[1,512,128]{2,1,0:T(8,128)(2,1)S(1)}, u32[]{:S(2)}, u32[]{:S(2)}) collective-permute-start(bf16[1,512,128]{2,1,0:T(8,128)(2,1)S(1)} %bitcast.393), channel_id=1, source_target_pairs={{0,2},{1,3},{2,0},{3,1},{4,6},{5,7},{6,4},{7,5},{8,10},{9,11},{10,... | collective-permute-start | bytes 393224 | tf_op jit(solution)/shard_map/ppermute | solution.py:24
  105.2 6.2 %collective-permute-start.29 = (bf16[2,512,128]{2,1,0:T(8,128)(2,1)S(1)}, bf16[2,512,128]{2,1,0:T(8,128)(2,1)S(1)}, u32[]{:S(2)}, u32[]{:S(2)}) collective-permute-start(bf16[2,512,128]{2,1,0:T(8,128)(2,1)S(1)} %pad_maximum_fusion.12), channel_id=1, source_target_pairs={{0,1},{1,0},{2,3},{3,2},{4,5},{5,4},{6,7},{7,6},{8,9},{9,8},{10,11... | collective-permute-start | bytes 786440 | tf_op jit(solution)/shard_map/ppermute | solution.py:24
  106.1 3.6 %copy-start.18 = (bf16[1,512,128]{2,1,0:T(8,128)(2,1)}, bf16[1,512,128]{2,1,0:T(8,128)(2,1)S(1)}, u32[]{:S(2)}) copy-start(bf16[1,512,128]{2,1,0:T(8,128)(2,1)S(1)} %collective-permute-done.30) | copy-start | bytes 393220
  109.7 2.6 %collective-permute-start.32 = (bf16[2,1,512,128]{3,2,1,0:T(8,128)(2,1)S(1)}, bf16[2,1,512,128]{3,2,1,0:T(8,128)(2,1)S(1)}, u32[]{:S(2)}, u32[]{:S(2)}) collective-permute-start(bf16[2,1,512,128]{3,2,1,0:T(8,128)(2,1)S(1)} %pad_maximum_fusion.13), channel_id=1, source_target_pairs={{0,1},{1,0},{2,3},{3,2},{4,5},{5,4},{6,7},{7,6},{8,9},{9,8},{10,11... | collective-permute-start | bytes 786440 | tf_op jit(solution)/shard_map/ppermute | solution.py:24
  115.4 15.2 %collective-permute-start.43 = (bf16[512,256]{1,0:T(8,128)(2,1)S(1)}, bf16[512,256]{1,0:T(8,128)(2,1)S(1)}, u32[]{:S(2)}, u32[]{:S(2)}) collective-permute-start(bf16[512,256]{1,0:T(8,128)(2,1)S(1)} %get-tuple-element.34), channel_id=1, source_target_pairs={{0,24},{8,16},{16,8},{24,0},{1,25},{9,17},{17,9},{25,1},{2,26},{10... | collective-permute-start | bytes 786440 | tf_op jit(solution)/shard_map/ppermute | solution.py:24
  117.5 13.0 %collective-permute-start.42 = (bf16[512,256]{1,0:T(8,128)(2,1)S(1)}, bf16[512,256]{1,0:T(8,128)(2,1)S(1)}, u32[]{:S(2)}, u32[]{:S(2)}) collective-permute-start(bf16[512,256]{1,0:T(8,128)(2,1)S(1)} %get-tuple-element.34), channel_id=1, source_target_pairs={{0,16},{8,24},{16,0},{24,8},{1,17},{9,25},{17,1},{25,9},{2,18},{10... | collective-permute-start | bytes 786440 | tf_op jit(solution)/shard_map/ppermute | solution.py:24
  117.8 12.8 %collective-permute-start.41 = (bf16[512,256]{1,0:T(8,128)(2,1)S(1)}, bf16[512,256]{1,0:T(8,128)(2,1)S(1)}, u32[]{:S(2)}, u32[]{:S(2)}) collective-permute-start(bf16[512,256]{1,0:T(8,128)(2,1)S(1)} %get-tuple-element.34), channel_id=1, source_target_pairs={{0,8},{8,0},{16,24},{24,16},{1,9},{9,1},{17,25},{25,17},{2,10},{10... | collective-permute-start | bytes 786440 | tf_op jit(solution)/shard_map/ppermute | solution.py:24
  118.7 16.2 %collective-permute-start.33 = (bf16[512,256]{1,0:T(8,128)(2,1)S(1)}, bf16[512,256]{1,0:T(8,128)(2,1)}, u32[]{:S(2)}, u32[]{:S(2)}) collective-permute-start(bf16[512,256]{1,0:T(8,128)(2,1)S(1)} %get-tuple-element.34), channel_id=1, source_target_pairs={{0,2},{1,3},{2,0},{3,1},{4,6},{5,7},{6,4},{7,5},{8,10},{9,11},{10,... | collective-permute-start | bytes 786440 | tf_op jit(solution)/shard_map/ppermute | solution.py:24
  118.7 7.1 %collective-permute-start.35 = (bf16[512,128]{1,0:T(8,128)(2,1)S(1)}, bf16[512,128]{1,0:T(8,128)(2,1)}, u32[]{:S(2)}, u32[]{:S(2)}) collective-permute-start(bf16[512,128]{1,0:T(8,128)(2,1)S(1)} %get-tuple-element.24), channel_id=1, source_target_pairs={{0,4},{1,5},{2,6},{3,7},{4,0},{5,1},{6,2},{7,3},{8,12},{9,13},{10,... | collective-permute-start | bytes 393224 | tf_op jit(solution)/shard_map/ppermute | solution.py:24
  125.7 18.5 %collective-permute-start.36 = (bf16[512,128]{1,0:T(8,128)(2,1)}, bf16[512,128]{1,0:T(8,128)(2,1)}, u32[]{:S(2)}, u32[]{:S(2)}) collective-permute-start(bf16[512,128]{1,0:T(8,128)(2,1)} %get-tuple-element.21), channel_id=1, source_target_pairs={{0,4},{1,5},{2,6},{3,7},{4,0},{5,1},{6,2},{7,3},{8,12},{9,13},{10,... | collective-permute-start | bytes 393224 | tf_op jit(solution)/shard_map/ppermute | solution.py:24
  130.6 18.0 %collective-permute-start.38 = (bf16[1,512,128]{2,1,0:T(8,128)(2,1)}, bf16[1,512,128]{2,1,0:T(8,128)(2,1)}, u32[]{:S(2)}, u32[]{:S(2)}) collective-permute-start(bf16[1,512,128]{2,1,0:T(8,128)(2,1)} %bitcast.95), channel_id=1, source_target_pairs={{0,2},{1,3},{2,0},{3,1},{4,6},{5,7},{6,4},{7,5},{8,10},{9,11},{10,... | collective-permute-start | bytes 393224 | tf_op jit(solution)/shard_map/ppermute | solution.py:24
  134.9 4.0 %copy-start.27 = (bf16[2,1,512,128]{3,2,1,0:T(8,128)(2,1)S(1)}, bf16[2,1,512,128]{3,2,1,0:T(8,128)(2,1)}, u32[]{:S(2)}) copy-start(bf16[2,1,512,128]{3,2,1,0:T(8,128)(2,1)} %copy-done.26) | copy-start | bytes 786436
  136.0 17.4 %collective-permute-start.34 = (bf16[2,512,256]{2,1,0:T(8,128)(2,1)S(1)}, bf16[2,512,256]{2,1,0:T(8,128)(2,1)S(1)}, u32[]{:S(2)}, u32[]{:S(2)}) collective-permute-start(bf16[2,512,256]{2,1,0:T(8,128)(2,1)S(1)} %pad_maximum_fusion.7), channel_id=1, source_target_pairs={{0,1},{1,0},{2,3},{3,2},{4,5},{5,4},{6,7},{7,6},{8,9},{9,8},{10,11... | collective-permute-start | bytes 1572872 | tf_op jit(solution)/shard_map/ppermute | solution.py:24
  144.3 5.8 %collective-permute-start.39 = (bf16[1,512,128]{2,1,0:T(8,128)(2,1)}, bf16[1,512,128]{2,1,0:T(8,128)(2,1)S(1)}, u32[]{:S(2)}, u32[]{:S(2)}) collective-permute-start(bf16[1,512,128]{2,1,0:T(8,128)(2,1)} %bitcast.96), channel_id=1, source_target_pairs={{0,2},{1,3},{2,0},{3,1},{4,6},{5,7},{6,4},{7,5},{8,10},{9,11},{10,... | collective-permute-start | bytes 393224 | tf_op jit(solution)/shard_map/ppermute | solution.py:24
  147.1 4.9 %collective-permute-start.37 = (bf16[2,512,128]{2,1,0:T(8,128)(2,1)S(1)}, bf16[2,512,128]{2,1,0:T(8,128)(2,1)S(1)}, u32[]{:S(2)}, u32[]{:S(2)}) collective-permute-start(bf16[2,512,128]{2,1,0:T(8,128)(2,1)S(1)} %pad_maximum_fusion.14), channel_id=1, source_target_pairs={{0,1},{1,0},{2,3},{3,2},{4,5},{5,4},{6,7},{7,6},{8,9},{9,8},{10,11... | collective-permute-start | bytes 786440 | tf_op jit(solution)/shard_map/ppermute | solution.py:24
  151.0 1.9 %collective-permute-start.40 = (bf16[2,1,512,128]{3,2,1,0:T(8,128)(2,1)S(1)}, bf16[2,1,512,128]{3,2,1,0:T(8,128)(2,1)S(1)}, u32[]{:S(2)}, u32[]{:S(2)}) collective-permute-start(bf16[2,1,512,128]{3,2,1,0:T(8,128)(2,1)S(1)} %pad_maximum_fusion.15), channel_id=1, source_target_pairs={{0,1},{1,0},{2,3},{3,2},{4,5},{5,4},{6,7},{7,6},{8,9},{9,8},{10,11... | collective-permute-start | bytes 786440 | tf_op jit(solution)/shard_map/ppermute | solution.py:24
  (28 other events, 28.0 us)

commit v11 on v6

--- a/solution.py
+++ b/solution.py
@@ -29,7 +29,10 @@
     same = {0: xb}
     for s in sorted(range(2, chips, 2), reverse=True) + [1]:
         same[s] = xor_permute(xb, "col", n_col, 2 * s)
-    col_pieces = [xb] + [xor_permute(xb, "row", n_row, t) for t in range(1, n_row)]
+    col_pieces = [xb]
+    for t in range(1, n_row):
+        low = t & -t
+        col_pieces.append(xor_permute(col_pieces[t ^ low], "row", n_row, low))
     first = sorted(same)
     relay_first = xor_permute(jnp.stack([same[s] for s in first]), "col", n_col, 1)
     other = {}

time: 124 us -> 145 us (1.17)
  matrix products: 28.5 us -> 41.5 us
  starting transfers between devices: 35.3 us -> 39 us
  other arithmetic: 6.66 us -> 9.36 us
  waiting for transfers between devices: 43.1 us -> 44.6 us
    dot_general x48, matrix products: 28.5 us -> 41.5 us  [contract(): part = jnp.dot(piece, k_blocks[s], preferred_element_type=jnp.float32)]
    ppermute x32, starting transfers between devices: 35.3 us -> 39 us  [xor_permute(): return lax.ppermute(x, axis, perm=[(i, i ^ s) for i in range(size)])]
    another operation x4, other arithmetic: 3.31 us -> 6.02 us  [exchange(): jnp.stack([same[s] for s in first])]
    ppermute x32, waiting for transfers between devices: 43.1 us -> 44.6 us  [xor_permute(): return lax.ppermute(x, axis, perm=[(i, i ^ s) for i in range(size)])]
  transfers between devices with their start and end apart: 32 -> 32, of which waited for: 11 -> 11; matrix products, arithmetic and copies ran while one was open for 30% -> 36% of each run, Pallas kernels for 0% -> 0%
where the time goes in v11:
time: 145 us; the launch traced here: 144 us
  waiting for transfers between devices  44.6 us (31%)
  matrix products  41.5 us (29%)
  starting transfers between devices  39 us (27%)
  other arithmetic  9.36 us (6%)
  local copies, waits for them, and re-layouts  8.76 us (6%)
    ppermute x32, waiting for transfers between devices, xor_permute(): return lax.ppermute(x, axis, perm=[(i, i ^ s) for i in range(size)])  44.6 us
    dot_general x48, matrix products, contract(): part = jnp.dot(piece, k_blocks[s], preferred_element_type=jnp.float32)  41.5 us
    ppermute x32, starting transfers between devices, xor_permute(): return lax.ppermute(x, axis, perm=[(i, i ^ s) for i in range(size)])  39 us
    another operation x4, other arithmetic, exchange(): jnp.stack([same[s] for s in first])  6.02 us
    gather x4, local copies, waits for them, and re-layouts, ordered_k_blocks(): return jnp.take(split, index, axis=0)  4.9 us
    unnamed x33, local copies, waits for them, and re-layouts  3.65 us
  transfers between devices with their start and end apart: 32, of which 11 were waited for; matrix products, arithmetic and copies ran while one was open for 36% of the time, Pallas kernels for 0%

profile of v11, /device:TPU:1, one launch (start us, length us, event | category | flops | bytes accessed | tf_op | source)
XLA Modules:
  0.0 143.9 jit_solution(14631205907430708358)
XLA Ops:
  1.2 2.1 %collective-permute-start.1 = (bf16[512,256]{1,0:T(8,128)(2,1)S(1)}, bf16[512,256]{1,0:T(8,128)(2,1)S(1)}, u32[]{:S(2)}, u32[]{:S(2)}) collective-permute-start(bf16[512,256]{1,0:T(8,128)(2,1)S(1)} %fusion.28), channel_id=1, source_target_pairs={{0,16},{8,24},{16,0},{24,8},{1,17},{9,25},{17,1},{25,9},{2,18},{10... | collective-permute-start | bytes 786440 | tf_op jit(solution)/shard_map/ppermute | solution.py:24
  3.3 2.3 %collective-permute-start.4 = (bf16[512,256]{1,0:T(8,128)(2,1)S(1)}, bf16[512,256]{1,0:T(8,128)(2,1)S(1)}, u32[]{:S(2)}, u32[]{:S(2)}) collective-permute-start(bf16[512,256]{1,0:T(8,128)(2,1)S(1)} %fusion.28), channel_id=1, source_target_pairs={{0,4},{1,5},{2,6},{3,7},{4,0},{5,1},{6,2},{7,3},{8,12},{9,13},{10,... | collective-permute-start | bytes 786440 | tf_op jit(solution)/shard_map/ppermute | solution.py:24
  5.6 1.3 collective-permute-start.3
  6.9 1.2 collective-permute-start
  8.1 1.2 collective-permute-done.1
  10.5 6.5 %collective-permute-done.4 = bf16[512,256]{1,0:T(8,128)(2,1)S(1)} collective-permute-done((bf16[512,256]{1,0:T(8,128)(2,1)S(1)}, bf16[512,256]{1,0:T(8,128)(2,1)S(1)}, u32[]{:S(2)}, u32[]{:S(2)}) %collective-permute-start.4) | collective-permute-done | bytes 262176 | tf_op jit(solution)/shard_map/ppermute | solution.py:24
  17.0 1.4 collective-permute-start.6
  21.1 2.5 %collective-permute-done.6 = bf16[1,512,256]{2,1,0:T(8,128)(2,1)} collective-permute-done((bf16[1,512,256]{2,1,0:T(8,128)(2,1)S(1)}, bf16[1,512,256]{2,1,0:T(8,128)(2,1)}, u32[]{:S(2)}, u32[]{:S(2)}) %collective-permute-start.6) | collective-permute-done | bytes 262176 | tf_op jit(solution)/shard_map/ppermute | solution.py:24
  23.6 2.2 %collective-permute-start.7 = (bf16[1,512,256]{2,1,0:T(8,128)(2,1)}, bf16[1,512,256]{2,1,0:T(8,128)(2,1)S(1)}, u32[]{:S(2)}, u32[]{:S(2)}) collective-permute-start(bf16[1,512,256]{2,1,0:T(8,128)(2,1)} %collective-permute-done.6), channel_id=1, source_target_pairs={{0,1},{1,0},{2,3},{3,2},{4,5},{5,4},{6,7},{7,6},{8,9},{9,8},{10,11... | collective-permute-start | bytes 786440 | tf_op jit(solution)/shard_map/ppermute | solution.py:24
  29.8 1.2 convolution_add_fusion.17
  32.3 3.1 %collective-permute-start.9 = (bf16[512,256]{1,0:T(8,128)(2,1)S(1)}, bf16[512,256]{1,0:T(8,128)(2,1)}, u32[]{:S(2)}, u32[]{:S(2)}) collective-permute-start(bf16[512,256]{1,0:T(8,128)(2,1)S(1)} %get-tuple-element.8), channel_id=1, source_target_pairs={{0,4},{1,5},{2,6},{3,7},{4,0},{5,1},{6,2},{7,3},{8,12},{9,13},{10,... | collective-permute-start | bytes 786440 | tf_op jit(solution)/shard_map/ppermute | solution.py:24
  35.6 1.5 %collective-permute-start.8 = (bf16[512,256]{1,0:T(8,128)(2,1)S(1)}, bf16[512,256]{1,0:T(8,128)(2,1)S(1)}, u32[]{:S(2)}, u32[]{:S(2)}) collective-permute-start(bf16[512,256]{1,0:T(8,128)(2,1)S(1)} %get-tuple-element.8), channel_id=1, source_target_pairs={{0,2},{1,3},{2,0},{3,1},{4,6},{5,7},{6,4},{7,5},{8,10},{9,11},{10,... | collective-permute-start | bytes 786440 | tf_op jit(solution)/shard_map/ppermute | solution.py:24
  37.1 1.2 collective-permute-start.13
  39.3 8.5 %collective-permute-done.9 = bf16[512,256]{1,0:T(8,128)(2,1)} collective-permute-done((bf16[512,256]{1,0:T(8,128)(2,1)S(1)}, bf16[512,256]{1,0:T(8,128)(2,1)}, u32[]{:S(2)}, u32[]{:S(2)}) %collective-permute-start.9) | collective-permute-done | bytes 262176 | tf_op jit(solution)/shard_map/ppermute | solution.py:24
  48.3 1.2 collective-permute-start.15
  49.5 2.0 %pad_maximum_fusion.5 = bf16[3,512,256]{2,1,0:T(8,128)(2,1)} fusion(bf16[1,512,256]{2,1,0:T(8,128)(2,1)} %bitcast.23, bf16[1,512,256]{2,1,0:T(8,128)(2,1)S(1)} %bitcast.281, bf16[1,512,256]{2,1,0:T(8,128)(2,1)S(1)} %bitcast.270), kind=kLoop, calls=%fused_computation.59 | loop fusion | flops 786432 | bytes 1572864 | tf_op jit(solution)/shard_map/stack | solution.py:37
  52.5 2.0 %fusion.70 = f32[512,256]{1,0:T(8,128)} fusion(bf16[512,256]{1,0:T(8,128)(2,1)} %collective-permute-done.9, bf16[8,256,256]{2,1,0:T(8,128)(2,1)S(1)} %broadcast_select_fusion.3), kind=kOutput, calls=%fused_computation.147 | convolution fusion | flops 67108864 | bytes 917504 | tf_op jit(solution)/shard_map/dot_general | solution.py:68
  56.6 1.8 %gather_fusion.1 = bf16[8,256,256]{2,1,0:T(8,128)(2,1)S(1)} fusion(bf16[8,256,256]{2,1,0:T(8,128)(2,1)} %bitcast.267, s32[1024]{0:T(1024)S(1)} %pad_clamp_fusion), kind=kCustom, calls=%fused_computation.1.clone | custom fusion | bytes 2097184 | tf_op jit(solution)/shard_map/jit(_take)/gather | solution.py:62
  61.4 1.2 fusion.56
  62.6 1.2 convolution_add_fusion.11
  63.8 1.6 %collective-permute-start.12 = (bf16[1,512,256]{2,1,0:T(8,128)(2,1)}, bf16[1,512,256]{2,1,0:T(8,128)(2,1)S(1)}, u32[]{:S(2)}, u32[]{:S(2)}) collective-permute-start(bf16[1,512,256]{2,1,0:T(8,128)(2,1)} %collective-permute-done.11), channel_id=1, source_target_pairs={{0,1},{1,0},{2,3},{3,2},{4,5},{5,4},{6,7},{7,6},{8,9},{9,8},{10,11... | collective-permute-start | bytes 786440 | tf_op jit(solution)/shard_map/ppermute | solution.py:24
  65.4 1.2 fusion.48
  68.9 1.2 fusion.33
  70.2 1.2 convolution_add_fusion.14
  73.1 3.2 %collective-permute-start.20 = (bf16[512,256]{1,0:T(8,128)(2,1)S(1)}, bf16[512,256]{1,0:T(8,128)(2,1)S(1)}, u32[]{:S(2)}, u32[]{:S(2)}) collective-permute-start(bf16[512,256]{1,0:T(8,128)(2,1)S(1)} %fusion.29), channel_id=1, source_target_pairs={{0,4},{1,5},{2,6},{3,7},{4,0},{5,1},{6,2},{7,3},{8,12},{9,13},{10,... | collective-permute-start | bytes 786440 | tf_op jit(solution)/shard_map/ppermute | solution.py:24
  76.3 1.2 collective-permute-start.16
  77.5 3.2 %collective-permute-done.17 = bf16[512,256]{1,0:T(8,128)(2,1)S(1)} collective-permute-done((bf16[512,256]{1,0:T(8,128)(2,1)S(1)}, bf16[512,256]{1,0:T(8,128)(2,1)S(1)}, u32[]{:S(2)}, u32[]{:S(2)}) %collective-permute-start.17) | collective-permute-done | bytes 262176 | tf_op jit(solution)/shard_map/ppermute | solution.py:24
  80.8 1.2 collective-permute-start.18
  82.0 6.7 %collective-permute-done.20 = bf16[512,256]{1,0:T(8,128)(2,1)S(1)} collective-permute-done((bf16[512,256]{1,0:T(8,128)(2,1)S(1)}, bf16[512,256]{1,0:T(8,128)(2,1)S(1)}, u32[]{:S(2)}, u32[]{:S(2)}) %collective-permute-start.20) | collective-permute-done | bytes 262176 | tf_op jit(solution)/shard_map/ppermute | solution.py:24
  90.1 1.4 %collective-permute-start.21 = (bf16[3,512,256]{2,1,0:T(8,128)(2,1)}, bf16[3,512,256]{2,1,0:T(8,128)(2,1)}, u32[]{:S(2)}, u32[]{:S(2)}) collective-permute-start(bf16[3,512,256]{2,1,0:T(8,128)(2,1)} %pad_maximum_fusion.6), channel_id=1, source_target_pairs={{0,1},{1,0},{2,3},{3,2},{4,5},{5,4},{6,7},{7,6},{8,9},{9,8},{10,11... | collective-permute-start | bytes 2359304 | tf_op jit(solution)/shard_map/ppermute | solution.py:24
  92.5 3.6 %collective-permute-done.22 = bf16[1,512,256]{2,1,0:T(8,128)(2,1)} collective-permute-done((bf16[1,512,256]{2,1,0:T(8,128)(2,1)S(1)}, bf16[1,512,256]{2,1,0:T(8,128)(2,1)}, u32[]{:S(2)}, u32[]{:S(2)}) %collective-permute-start.22) | collective-permute-done | bytes 262176 | tf_op jit(solution)/shard_map/ppermute | solution.py:24
  96.1 1.3 collective-permute-start.23
  101.5 1.2 convolution_add_fusion.8
  104.3 1.2 collective-permute-start.30
  105.5 1.4 %collective-permute-start.24 = (bf16[512,256]{1,0:T(8,128)(2,1)S(1)}, bf16[512,256]{1,0:T(8,128)(2,1)S(1)}, u32[]{:S(2)}, u32[]{:S(2)}) collective-permute-start(bf16[512,256]{1,0:T(8,128)(2,1)S(1)} %get-tuple-element.10), channel_id=1, source_target_pairs={{0,2},{1,3},{2,0},{3,1},{4,6},{5,7},{6,4},{7,5},{8,10},{9,11},{10,... | collective-permute-start | bytes 786440 | tf_op jit(solution)/shard_map/ppermute | solution.py:24
  107.0 1.2 collective-permute-start.29
  109.2 9.4 %collective-permute-done.25 = bf16[512,256]{1,0:T(8,128)(2,1)} collective-permute-done((bf16[512,256]{1,0:T(8,128)(2,1)S(1)}, bf16[512,256]{1,0:T(8,128)(2,1)}, u32[]{:S(2)}, u32[]{:S(2)}) %collective-permute-start.25) | collective-permute-done | bytes 262176 | tf_op jit(solution)/shard_map/ppermute | solution.py:24
  118.6 1.2 collective-permute-start.31
  119.8 2.0 %pad_maximum_fusion.7 = bf16[3,512,256]{2,1,0:T(8,128)(2,1)} fusion(bf16[1,512,256]{2,1,0:T(8,128)(2,1)} %bitcast.63, bf16[1,512,256]{2,1,0:T(8,128)(2,1)S(1)} %bitcast.280, bf16[1,512,256]{2,1,0:T(8,128)(2,1)S(1)} %bitcast.272), kind=kLoop, calls=%fused_computation.61 | loop fusion | flops 786432 | bytes 1572864 | tf_op jit(solution)/shard_map/stack | solution.py:37
  122.7 2.0 %fusion.74 = f32[512,256]{1,0:T(8,128)} fusion(bf16[512,256]{1,0:T(8,128)(2,1)} %collective-permute-done.25, bf16[8,256,256]{2,1,0:T(8,128)(2,1)S(1)} %broadcast_select_fusion.1), kind=kOutput, calls=%fused_computation.151 | convolution fusion | flops 67108864 | bytes 917504 | tf_op jit(solution)/shard_map/dot_general | solution.py:68
  124.7 1.5 %collective-permute-done.31 = bf16[512,256]{1,0:T(8,128)(2,1)S(1)} collective-permute-done((bf16[512,256]{1,0:T(8,128)(2,1)S(1)}, bf16[512,256]{1,0:T(8,128)(2,1)S(1)}, u32[]{:S(2)}, u32[]{:S(2)}) %collective-permute-start.31) | collective-permute-done | bytes 262176 | tf_op jit(solution)/shard_map/ppermute | solution.py:24
  127.2 1.8 %gather_fusion.3 = bf16[8,256,256]{2,1,0:T(8,128)(2,1)S(1)} fusion(bf16[8,256,256]{2,1,0:T(8,128)(2,1)} %bitcast.266, s32[1024]{0:T(1024)S(1)} %pad_clamp_fusion), kind=kCustom, calls=%fused_computation.3.clone | custom fusion | bytes 2097184 | tf_op jit(solution)/shard_map/jit(_take)/gather | solution.py:62
  129.5 1.2 fusion.41
  133.2 1.2 convolution_add_fusion.2
  134.4 1.3 collective-permute-start.28
  135.7 1.2 fusion.37
  139.3 1.2 fusion.31
  140.6 1.2 convolution_add_fusion.5
  (118 shorter events, 40.1 us)
Async XLA Ops:
  0.0 0.7 copy-start.15
  0.0 1.1 copy-start.14
  1.2 8.2 %collective-permute-start.1 = (bf16[512,256]{1,0:T(8,128)(2,1)S(1)}, bf16[512,256]{1,0:T(8,128)(2,1)S(1)}, u32[]{:S(2)}, u32[]{:S(2)}) collective-permute-start(bf16[512,256]{1,0:T(8,128)(2,1)S(1)} %fusion.28), channel_id=1, source_target_pairs={{0,16},{8,24},{16,0},{24,8},{1,17},{9,25},{17,1},{25,9},{2,18},{10... | collective-permute-start | bytes 786440 | tf_op jit(solution)/shard_map/ppermute | solution.py:24
  3.3 13.7 %collective-permute-start.4 = (bf16[512,256]{1,0:T(8,128)(2,1)S(1)}, bf16[512,256]{1,0:T(8,128)(2,1)S(1)}, u32[]{:S(2)}, u32[]{:S(2)}) collective-permute-start(bf16[512,256]{1,0:T(8,128)(2,1)S(1)} %fusion.28), channel_id=1, source_target_pairs={{0,4},{1,5},{2,6},{3,7},{4,0},{5,1},{6,2},{7,3},{8,12},{9,13},{10,... | collective-permute-start | bytes 786440 | tf_op jit(solution)/shard_map/ppermute | solution.py:24
  5.6 12.8 %collective-permute-start.3 = (bf16[512,256]{1,0:T(8,128)(2,1)S(1)}, bf16[512,256]{1,0:T(8,128)(2,1)S(1)}, u32[]{:S(2)}, u32[]{:S(2)}) collective-permute-start(bf16[512,256]{1,0:T(8,128)(2,1)S(1)} %fusion.28), channel_id=1, source_target_pairs={{0,2},{1,3},{2,0},{3,1},{4,6},{5,7},{6,4},{7,5},{8,10},{9,11},{10,... | collective-permute-start | bytes 786440 | tf_op jit(solution)/shard_map/ppermute | solution.py:24
  6.9 13.3 %collective-permute-start = (bf16[512,256]{1,0:T(8,128)(2,1)S(1)}, bf16[512,256]{1,0:T(8,128)(2,1)S(1)}, u32[]{:S(2)}, u32[]{:S(2)}) collective-permute-start(bf16[512,256]{1,0:T(8,128)(2,1)S(1)} %fusion.28), channel_id=1, source_target_pairs={{0,8},{8,0},{16,24},{24,16},{1,9},{9,1},{17,25},{25,17},{2,10},{10... | collective-permute-start | bytes 786440 | tf_op jit(solution)/shard_map/ppermute | solution.py:24
  9.3 10.9 %collective-permute-start.2 = (bf16[512,256]{1,0:T(8,128)(2,1)S(1)}, bf16[512,256]{1,0:T(8,128)(2,1)S(1)}, u32[]{:S(2)}, u32[]{:S(2)}) collective-permute-start(bf16[512,256]{1,0:T(8,128)(2,1)S(1)} %collective-permute-done.1), channel_id=1, source_target_pairs={{0,8},{8,0},{16,24},{24,16},{1,9},{9,1},{17,25},{25,17},{2,10},{10... | collective-permute-start | bytes 786440 | tf_op jit(solution)/shard_map/ppermute | solution.py:24
  17.0 6.6 %collective-permute-start.6 = (bf16[1,512,256]{2,1,0:T(8,128)(2,1)S(1)}, bf16[1,512,256]{2,1,0:T(8,128)(2,1)}, u32[]{:S(2)}, u32[]{:S(2)}) collective-permute-start(bf16[1,512,256]{2,1,0:T(8,128)(2,1)S(1)} %bitcast.276), channel_id=1, source_target_pairs={{0,2},{1,3},{2,0},{3,1},{4,6},{5,7},{6,4},{7,5},{8,10},{9,11},{10,... | collective-permute-start | bytes 786440 | tf_op jit(solution)/shard_map/ppermute | solution.py:24
  19.4 8.0 %collective-permute-start.5 = (bf16[3,512,256]{2,1,0:T(8,128)(2,1)}, bf16[3,512,256]{2,1,0:T(8,128)(2,1)}, u32[]{:S(2)}, u32[]{:S(2)}) collective-permute-start(bf16[3,512,256]{2,1,0:T(8,128)(2,1)} %pad_maximum_fusion.4), channel_id=1, source_target_pairs={{0,1},{1,0},{2,3},{3,2},{4,5},{5,4},{6,7},{7,6},{8,9},{9,8},{10,11... | collective-permute-start | bytes 2359304 | tf_op jit(solution)/shard_map/ppermute | solution.py:24
  23.6 7.7 %collective-permute-start.7 = (bf16[1,512,256]{2,1,0:T(8,128)(2,1)}, bf16[1,512,256]{2,1,0:T(8,128)(2,1)S(1)}, u32[]{:S(2)}, u32[]{:S(2)}) collective-permute-start(bf16[1,512,256]{2,1,0:T(8,128)(2,1)} %collective-permute-done.6), channel_id=1, source_target_pairs={{0,1},{1,0},{2,3},{3,2},{4,5},{5,4},{6,7},{7,6},{8,9},{9,8},{10,11... | collective-permute-start | bytes 786440 | tf_op jit(solution)/shard_map/ppermute | solution.py:24
  31.3 1.0 copy-start.8
  32.3 15.5 %collective-permute-start.9 = (bf16[512,256]{1,0:T(8,128)(2,1)S(1)}, bf16[512,256]{1,0:T(8,128)(2,1)}, u32[]{:S(2)}, u32[]{:S(2)}) collective-permute-start(bf16[512,256]{1,0:T(8,128)(2,1)S(1)} %get-tuple-element.8), channel_id=1, source_target_pairs={{0,4},{1,5},{2,6},{3,7},{4,0},{5,1},{6,2},{7,3},{8,12},{9,13},{10,... | collective-permute-start | bytes 786440 | tf_op jit(solution)/shard_map/ppermute | solution.py:24
  35.4 12.9 %collective-permute-start.14 = (bf16[512,256]{1,0:T(8,128)(2,1)S(1)}, bf16[512,256]{1,0:T(8,128)(2,1)S(1)}, u32[]{:S(2)}, u32[]{:S(2)}) collective-permute-start(bf16[512,256]{1,0:T(8,128)(2,1)S(1)} %get-tuple-element.8), channel_id=1, source_target_pairs={{0,16},{8,24},{16,0},{24,8},{1,17},{9,25},{17,1},{25,9},{2,18},{10... | collective-permute-start | bytes 786440 | tf_op jit(solution)/shard_map/ppermute | solution.py:24
  35.6 13.9 %collective-permute-start.8 = (bf16[512,256]{1,0:T(8,128)(2,1)S(1)}, bf16[512,256]{1,0:T(8,128)(2,1)S(1)}, u32[]{:S(2)}, u32[]{:S(2)}) collective-permute-start(bf16[512,256]{1,0:T(8,128)(2,1)S(1)} %get-tuple-element.8), channel_id=1, source_target_pairs={{0,2},{1,3},{2,0},{3,1},{4,6},{5,7},{6,4},{7,5},{8,10},{9,11},{10,... | collective-permute-start | bytes 786440 | tf_op jit(solution)/shard_map/ppermute | solution.py:24
  37.1 17.5 %collective-permute-start.13 = (bf16[512,256]{1,0:T(8,128)(2,1)S(1)}, bf16[512,256]{1,0:T(8,128)(2,1)S(1)}, u32[]{:S(2)}, u32[]{:S(2)}) collective-permute-start(bf16[512,256]{1,0:T(8,128)(2,1)S(1)} %get-tuple-element.8), channel_id=1, source_target_pairs={{0,8},{8,0},{16,24},{24,16},{1,9},{9,1},{17,25},{25,17},{2,10},{10... | collective-permute-start | bytes 786440 | tf_op jit(solution)/shard_map/ppermute | solution.py:24
  47.8 15.9 %collective-permute-start.11 = (bf16[1,512,256]{2,1,0:T(8,128)(2,1)}, bf16[1,512,256]{2,1,0:T(8,128)(2,1)}, u32[]{:S(2)}, u32[]{:S(2)}) collective-permute-start(bf16[1,512,256]{2,1,0:T(8,128)(2,1)} %bitcast.23), channel_id=1, source_target_pairs={{0,2},{1,3},{2,0},{3,1},{4,6},{5,7},{6,4},{7,5},{8,10},{9,11},{10,... | collective-permute-start | bytes 786440 | tf_op jit(solution)/shard_map/ppermute | solution.py:24
  48.3 7.2 %collective-permute-start.15 = (bf16[512,256]{1,0:T(8,128)(2,1)S(1)}, bf16[512,256]{1,0:T(8,128)(2,1)S(1)}, u32[]{:S(2)}, u32[]{:S(2)}) collective-permute-start(bf16[512,256]{1,0:T(8,128)(2,1)S(1)} %collective-permute-done.14), channel_id=1, source_target_pairs={{0,8},{8,0},{16,24},{24,16},{1,9},{9,1},{17,25},{25,17},{2,10},{10... | collective-permute-start | bytes 786440 | tf_op jit(solution)/shard_map/ppermute | solution.py:24
  49.5 2.0 %copy-start.12 = (bf16[512,256]{1,0:T(8,128)(2,1)}, bf16[512,256]{1,0:T(8,128)(2,1)S(1)}, u32[]{:S(2)}) copy-start(bf16[512,256]{1,0:T(8,128)(2,1)S(1)} %collective-permute-done.8) | copy-start | bytes 786436
  51.5 16.2 %collective-permute-start.10 = (bf16[3,512,256]{2,1,0:T(8,128)(2,1)}, bf16[3,512,256]{2,1,0:T(8,128)(2,1)}, u32[]{:S(2)}, u32[]{:S(2)}) collective-permute-start(bf16[3,512,256]{2,1,0:T(8,128)(2,1)} %pad_maximum_fusion.5), channel_id=1, source_target_pairs={{0,1},{1,0},{2,3},{3,2},{4,5},{5,4},{6,7},{7,6},{8,9},{9,8},{10,11... | collective-permute-start | bytes 2359304 | tf_op jit(solution)/shard_map/ppermute | solution.py:24
  63.8 8.0 %collective-permute-start.12 = (bf16[1,512,256]{2,1,0:T(8,128)(2,1)}, bf16[1,512,256]{2,1,0:T(8,128)(2,1)S(1)}, u32[]{:S(2)}, u32[]{:S(2)}) collective-permute-start(bf16[1,512,256]{2,1,0:T(8,128)(2,1)} %collective-permute-done.11), channel_id=1, source_target_pairs={{0,1},{1,0},{2,3},{3,2},{4,5},{5,4},{6,7},{7,6},{8,9},{9,8},{10,11... | collective-permute-start | bytes 786440 | tf_op jit(solution)/shard_map/ppermute | solution.py:24
  66.5 1.0 copy-start.9
  68.9 1.2 copy-start.5
  70.2 1.3 copy-start.1
  70.2 1.3 copy-start.13
  71.5 1.0 copy-start.3
  72.8 8.0 %collective-permute-start.17 = (bf16[512,256]{1,0:T(8,128)(2,1)S(1)}, bf16[512,256]{1,0:T(8,128)(2,1)S(1)}, u32[]{:S(2)}, u32[]{:S(2)}) collective-permute-start(bf16[512,256]{1,0:T(8,128)(2,1)S(1)} %fusion.29), channel_id=1, source_target_pairs={{0,16},{8,24},{16,0},{24,8},{1,17},{9,25},{17,1},{25,9},{2,18},{10... | collective-permute-start | bytes 786440 | tf_op jit(solution)/shard_map/ppermute | solution.py:24
  73.1 15.5 %collective-permute-start.20 = (bf16[512,256]{1,0:T(8,128)(2,1)S(1)}, bf16[512,256]{1,0:T(8,128)(2,1)S(1)}, u32[]{:S(2)}, u32[]{:S(2)}) collective-permute-start(bf16[512,256]{1,0:T(8,128)(2,1)S(1)} %fusion.29), channel_id=1, source_target_pairs={{0,4},{1,5},{2,6},{3,7},{4,0},{5,1},{6,2},{7,3},{8,12},{9,13},{10,... | collective-permute-start | bytes 786440 | tf_op jit(solution)/shard_map/ppermute | solution.py:24
  76.3 12.8 %collective-permute-start.19 = (bf16[512,256]{1,0:T(8,128)(2,1)S(1)}, bf16[512,256]{1,0:T(8,128)(2,1)S(1)}, u32[]{:S(2)}, u32[]{:S(2)}) collective-permute-start(bf16[512,256]{1,0:T(8,128)(2,1)S(1)} %fusion.29), channel_id=1, source_target_pairs={{0,2},{1,3},{2,0},{3,1},{4,6},{5,7},{6,4},{7,5},{8,10},{9,11},{10,... | collective-permute-start | bytes 786440 | tf_op jit(solution)/shard_map/ppermute | solution.py:24
  76.3 15.2 %collective-permute-start.16 = (bf16[512,256]{1,0:T(8,128)(2,1)S(1)}, bf16[512,256]{1,0:T(8,128)(2,1)S(1)}, u32[]{:S(2)}, u32[]{:S(2)}) collective-permute-start(bf16[512,256]{1,0:T(8,128)(2,1)S(1)} %fusion.29), channel_id=1, source_target_pairs={{0,8},{8,0},{16,24},{24,16},{1,9},{9,1},{17,25},{25,17},{2,10},{10... | collective-permute-start | bytes 786440 | tf_op jit(solution)/shard_map/ppermute | solution.py:24
  80.8 10.8 %collective-permute-start.18 = (bf16[512,256]{1,0:T(8,128)(2,1)S(1)}, bf16[512,256]{1,0:T(8,128)(2,1)S(1)}, u32[]{:S(2)}, u32[]{:S(2)}) collective-permute-start(bf16[512,256]{1,0:T(8,128)(2,1)S(1)} %collective-permute-done.17), channel_id=1, source_target_pairs={{0,8},{8,0},{16,24},{24,16},{1,9},{9,1},{17,25},{25,17},{2,10},{10... | collective-permute-start | bytes 786440 | tf_op jit(solution)/shard_map/ppermute | solution.py:24
  88.6 7.5 %collective-permute-start.22 = (bf16[1,512,256]{2,1,0:T(8,128)(2,1)S(1)}, bf16[1,512,256]{2,1,0:T(8,128)(2,1)}, u32[]{:S(2)}, u32[]{:S(2)}) collective-permute-start(bf16[1,512,256]{2,1,0:T(8,128)(2,1)S(1)} %bitcast.278), channel_id=1, source_target_pairs={{0,2},{1,3},{2,0},{3,1},{4,6},{5,7},{6,4},{7,5},{8,10},{9,11},{10,... | collective-permute-start | bytes 786440 | tf_op jit(solution)/shard_map/ppermute | solution.py:24
  90.1 9.0 %collective-permute-start.21 = (bf16[3,512,256]{2,1,0:T(8,128)(2,1)}, bf16[3,512,256]{2,1,0:T(8,128)(2,1)}, u32[]{:S(2)}, u32[]{:S(2)}) collective-permute-start(bf16[3,512,256]{2,1,0:T(8,128)(2,1)} %pad_maximum_fusion.6), channel_id=1, source_target_pairs={{0,1},{1,0},{2,3},{3,2},{4,5},{5,4},{6,7},{7,6},{8,9},{9,8},{10,11... | collective-permute-start | bytes 2359304 | tf_op jit(solution)/shard_map/ppermute | solution.py:24
  96.1 6.8 %collective-permute-start.23 = (bf16[1,512,256]{2,1,0:T(8,128)(2,1)}, bf16[1,512,256]{2,1,0:T(8,128)(2,1)S(1)}, u32[]{:S(2)}, u32[]{:S(2)}) collective-permute-start(bf16[1,512,256]{2,1,0:T(8,128)(2,1)} %collective-permute-done.22), channel_id=1, source_target_pairs={{0,1},{1,0},{2,3},{3,2},{4,5},{5,4},{6,7},{7,6},{8,9},{9,8},{10,11... | collective-permute-start | bytes 786440 | tf_op jit(solution)/shard_map/ppermute | solution.py:24
  102.9 1.0 copy-start.6
  104.0 14.7 %collective-permute-start.25 = (bf16[512,256]{1,0:T(8,128)(2,1)S(1)}, bf16[512,256]{1,0:T(8,128)(2,1)}, u32[]{:S(2)}, u32[]{:S(2)}) collective-permute-start(bf16[512,256]{1,0:T(8,128)(2,1)S(1)} %get-tuple-element.10), channel_id=1, source_target_pairs={{0,4},{1,5},{2,6},{3,7},{4,0},{5,1},{6,2},{7,3},{8,12},{9,13},{10,... | collective-permute-start | bytes 786440 | tf_op jit(solution)/shard_map/ppermute | solution.py:24
  104.3 14.3 %collective-permute-start.30 = (bf16[512,256]{1,0:T(8,128)(2,1)S(1)}, bf16[512,256]{1,0:T(8,128)(2,1)S(1)}, u32[]{:S(2)}, u32[]{:S(2)}) collective-permute-start(bf16[512,256]{1,0:T(8,128)(2,1)S(1)} %get-tuple-element.10), channel_id=1, source_target_pairs={{0,16},{8,24},{16,0},{24,8},{1,17},{9,25},{17,1},{25,9},{2,18},{10... | collective-permute-start | bytes 786440 | tf_op jit(solution)/shard_map/ppermute | solution.py:24
  105.5 14.3 %collective-permute-start.24 = (bf16[512,256]{1,0:T(8,128)(2,1)S(1)}, bf16[512,256]{1,0:T(8,128)(2,1)S(1)}, u32[]{:S(2)}, u32[]{:S(2)}) collective-permute-start(bf16[512,256]{1,0:T(8,128)(2,1)S(1)} %get-tuple-element.10), channel_id=1, source_target_pairs={{0,2},{1,3},{2,0},{3,1},{4,6},{5,7},{6,4},{7,5},{8,10},{9,11},{10,... | collective-permute-start | bytes 786440 | tf_op jit(solution)/shard_map/ppermute | solution.py:24
  107.0 17.7 %collective-permute-start.29 = (bf16[512,256]{1,0:T(8,128)(2,1)S(1)}, bf16[512,256]{1,0:T(8,128)(2,1)S(1)}, u32[]{:S(2)}, u32[]{:S(2)}) collective-permute-start(bf16[512,256]{1,0:T(8,128)(2,1)S(1)} %get-tuple-element.10), channel_id=1, source_target_pairs={{0,8},{8,0},{16,24},{24,16},{1,9},{9,1},{17,25},{25,17},{2,10},{10... | collective-permute-start | bytes 786440 | tf_op jit(solution)/shard_map/ppermute | solution.py:24
  118.6 15.8 %collective-permute-start.27 = (bf16[1,512,256]{2,1,0:T(8,128)(2,1)}, bf16[1,512,256]{2,1,0:T(8,128)(2,1)}, u32[]{:S(2)}, u32[]{:S(2)}) collective-permute-start(bf16[1,512,256]{2,1,0:T(8,128)(2,1)} %bitcast.63), channel_id=1, source_target_pairs={{0,2},{1,3},{2,0},{3,1},{4,6},{5,7},{6,4},{7,5},{8,10},{9,11},{10,... | collective-permute-start | bytes 786440 | tf_op jit(solution)/shard_map/ppermute | solution.py:24
  118.6 7.5 %collective-permute-start.31 = (bf16[512,256]{1,0:T(8,128)(2,1)S(1)}, bf16[512,256]{1,0:T(8,128)(2,1)S(1)}, u32[]{:S(2)}, u32[]{:S(2)}) collective-permute-start(bf16[512,256]{1,0:T(8,128)(2,1)S(1)} %collective-permute-done.30), channel_id=1, source_target_pairs={{0,8},{8,0},{16,24},{24,16},{1,9},{9,1},{17,25},{25,17},{2,10},{10... | collective-permute-start | bytes 786440 | tf_op jit(solution)/shard_map/ppermute | solution.py:24
  119.8 2.0 %copy-start.10 = (bf16[512,256]{1,0:T(8,128)(2,1)}, bf16[512,256]{1,0:T(8,128)(2,1)S(1)}, u32[]{:S(2)}) copy-start(bf16[512,256]{1,0:T(8,128)(2,1)S(1)} %collective-permute-done.24) | copy-start | bytes 786436
  121.9 16.2 %collective-permute-start.26 = (bf16[3,512,256]{2,1,0:T(8,128)(2,1)}, bf16[3,512,256]{2,1,0:T(8,128)(2,1)}, u32[]{:S(2)}, u32[]{:S(2)}) collective-permute-start(bf16[3,512,256]{2,1,0:T(8,128)(2,1)} %pad_maximum_fusion.7), channel_id=1, source_target_pairs={{0,1},{1,0},{2,3},{3,2},{4,5},{5,4},{6,7},{7,6},{8,9},{9,8},{10,11... | collective-permute-start | bytes 2359304 | tf_op jit(solution)/shard_map/ppermute | solution.py:24
  134.4 7.7 %collective-permute-start.28 = (bf16[1,512,256]{2,1,0:T(8,128)(2,1)}, bf16[1,512,256]{2,1,0:T(8,128)(2,1)S(1)}, u32[]{:S(2)}, u32[]{:S(2)}) collective-permute-start(bf16[1,512,256]{2,1,0:T(8,128)(2,1)} %collective-permute-done.27), channel_id=1, source_target_pairs={{0,1},{1,0},{2,3},{3,2},{4,5},{5,4},{6,7},{7,6},{8,9},{9,8},{10,11... | collective-permute-start | bytes 786440 | tf_op jit(solution)/shard_map/ppermute | solution.py:24
  136.9 1.0 copy-start.7
  139.3 1.2 copy-start.4
  140.5 1.3 copy-start
  140.6 1.3 copy-start.11
  141.8 1.0 copy-start.2

commit v12 on v6

--- a/solution.py
+++ b/solution.py
@@ -30,12 +30,16 @@
     for s in sorted(range(2, chips, 2), reverse=True) + [1]:
         same[s] = xor_permute(xb, "col", n_col, 2 * s)
     col_pieces = [xb] + [xor_permute(xb, "row", n_row, t) for t in range(1, n_row)]
-    first = sorted(same)
-    relay_first = xor_permute(jnp.stack([same[s] for s in first]), "col", n_col, 1)
+    forward = list(range(2, chips, 2))
+    early = [0, 1]
     other = {}
-    for i, s in enumerate(first):
-        other[s] = relay_first[i]
-    forward = list(range(2, chips, 2))
+    relay_early = xor_permute(jnp.stack([same[s] for s in early]), "col", n_col, 1)
+    for i, s in enumerate(early):
+        other[s] = relay_early[i]
+    if forward:
+        relay_late = xor_permute(jnp.stack([same[s] for s in forward]), "col", n_col, 1)
+        for i, s in enumerate(forward):
+            other[s] = relay_late[i]
     if forward:
         sent = xor_permute(jnp.stack([same[s] for s in forward]), "col", n_col, 2)
         relay_sent = xor_permute(sent, "col", n_col, 1)

time: 124 us -> 126 us (1.016)
  local copies, waits for them, and re-layouts: 8.68 us -> 11.6 us
  starting transfers between devices: 35.3 us -> 32.5 us
  matrix products: 28.5 us -> 30.3 us
    unnamed x33 -> x37, local copies, waits for them, and re-layouts: 3.57 us -> 6.5 us
    ppermute x32 -> x36, starting transfers between devices: 35.3 us -> 32.5 us  [xor_permute(): return lax.ppermute(x, axis, perm=[(i, i ^ s) for i in range(size)])]
    dot_general x48, matrix products: 28.5 us -> 30.3 us  [contract(): part = jnp.dot(piece, k_blocks[s], preferred_element_type=jnp.float32)]
    ppermute x32 -> x36, waiting for transfers between devices: 43.1 us -> 44 us  [xor_permute(): return lax.ppermute(x, axis, perm=[(i, i ^ s) for i in range(size)])]
  transfers between devices with their start and end apart: 32 -> 36, of which waited for: 11 -> 10; matrix products, arithmetic and copies ran while one was open for 30% -> 30% of each run, Pallas kernels for 0% -> 0%
where the time goes in v12:
time: 126 us; the launch traced here: 125 us
  waiting for transfers between devices  44 us (35%)
  starting transfers between devices  32.5 us (26%)
  matrix products  30.3 us (24%)
  local copies, waits for them, and re-layouts  11.6 us (9%)
  other arithmetic  5.47 us (4%)
    ppermute x36, waiting for transfers between devices, xor_permute(): return lax.ppermute(x, axis, perm=[(i, i ^ s) for i in range(size)])  44 us
    ppermute x36, starting transfers between devices, xor_permute(): return lax.ppermute(x, axis, perm=[(i, i ^ s) for i in range(size)])  32.5 us
    dot_general x48, matrix products, contract(): part = jnp.dot(piece, k_blocks[s], preferred_element_type=jnp.float32)  30.3 us
    unnamed x37, local copies, waits for them, and re-layouts  6.5 us
    gather x4, local copies, waits for them, and re-layouts, ordered_k_blocks(): return jnp.take(split, index, axis=0)  4.9 us
    another operation x4, other arithmetic, exchange(): return (row_pieces, jnp.stack(col_pieces))  2.54 us
  transfers between devices with their start and end apart: 36, of which 10 were waited for; matrix products, arithmetic and copies ran while one was open for 30% of the time, Pallas kernels for 0%

profile of v12, /device:TPU:1, one launch (start us, length us, event | category | flops | bytes accessed | tf_op | source)
XLA Modules:
  0.0 124.6 jit_solution(818154150479392659)
XLA Ops:
  1.2 3.2 %collective-permute-start.5 = (bf16[512,256]{1,0:T(8,128)(2,1)S(1)}, bf16[512,256]{1,0:T(8,128)(2,1)S(1)}, u32[]{:S(2)}, u32[]{:S(2)}) collective-permute-start(bf16[512,256]{1,0:T(8,128)(2,1)S(1)} %fusion.28), channel_id=1, source_target_pairs={{0,4},{1,5},{2,6},{3,7},{4,0},{5,1},{6,2},{7,3},{8,12},{9,13},{10,... | collective-permute-start | bytes 786440 | tf_op jit(solution)/shard_map/ppermute | solution.py:24
  4.4 2.2 %collective-permute-start.2 = (bf16[512,256]{1,0:T(8,128)(2,1)S(1)}, bf16[512,256]{1,0:T(8,128)(2,1)S(1)}, u32[]{:S(2)}, u32[]{:S(2)}) collective-permute-start(bf16[512,256]{1,0:T(8,128)(2,1)S(1)} %fusion.28), channel_id=1, source_target_pairs={{0,24},{8,16},{16,8},{24,0},{1,25},{9,17},{17,9},{25,1},{2,26},{10... | collective-permute-start | bytes 786440 | tf_op jit(solution)/shard_map/ppermute | solution.py:24
  7.0 1.3 %collective-permute-start.3 = (bf16[512,256]{1,0:T(8,128)(2,1)S(1)}, bf16[512,256]{1,0:T(8,128)(2,1)S(1)}, u32[]{:S(2)}, u32[]{:S(2)}) collective-permute-start(bf16[512,256]{1,0:T(8,128)(2,1)S(1)} %fusion.28), channel_id=1, source_target_pairs={{0,2},{1,3},{2,0},{3,1},{4,6},{5,7},{6,4},{7,5},{8,10},{9,11},{10,... | collective-permute-start | bytes 786440 | tf_op jit(solution)/shard_map/ppermute | solution.py:24
  8.3 7.7 %collective-permute-done.5 = bf16[512,256]{1,0:T(8,128)(2,1)S(1)} collective-permute-done((bf16[512,256]{1,0:T(8,128)(2,1)S(1)}, bf16[512,256]{1,0:T(8,128)(2,1)S(1)}, u32[]{:S(2)}, u32[]{:S(2)}) %collective-permute-start.5) | collective-permute-done | bytes 262176 | tf_op jit(solution)/shard_map/ppermute | solution.py:24
  16.1 1.2 collective-permute-start.7
  18.0 1.1 collective-permute-done.1
  21.5 3.1 %collective-permute-done.7 = bf16[1,512,256]{2,1,0:T(8,128)(2,1)} collective-permute-done((bf16[1,512,256]{2,1,0:T(8,128)(2,1)S(1)}, bf16[1,512,256]{2,1,0:T(8,128)(2,1)}, u32[]{:S(2)}, u32[]{:S(2)}) %collective-permute-start.7) | collective-permute-done | bytes 262176 | tf_op jit(solution)/shard_map/ppermute | solution.py:24
  24.6 1.4 %collective-permute-start.8 = (bf16[1,512,256]{2,1,0:T(8,128)(2,1)}, bf16[1,512,256]{2,1,0:T(8,128)(2,1)S(1)}, u32[]{:S(2)}, u32[]{:S(2)}) collective-permute-start(bf16[1,512,256]{2,1,0:T(8,128)(2,1)} %collective-permute-done.7), channel_id=1, source_target_pairs={{0,1},{1,0},{2,3},{3,2},{4,5},{5,4},{6,7},{7,6},{8,9},{9,8},{10,11... | collective-permute-start | bytes 786440 | tf_op jit(solution)/shard_map/ppermute | solution.py:24
  25.9 1.2 fusion.60
  27.1 1.2 fusion.64
  29.6 1.0 fusion.85
  30.6 1.8 %collective-permute-start.11 = (bf16[512,256]{1,0:T(8,128)(2,1)S(1)}, bf16[512,256]{1,0:T(8,128)(2,1)}, u32[]{:S(2)}, u32[]{:S(2)}) collective-permute-start(bf16[512,256]{1,0:T(8,128)(2,1)S(1)} %get-tuple-element.8), channel_id=1, source_target_pairs={{0,4},{1,5},{2,6},{3,7},{4,0},{5,1},{6,2},{7,3},{8,12},{9,13},{10,... | collective-permute-start | bytes 786440 | tf_op jit(solution)/shard_map/ppermute | solution.py:24
  32.4 2.2 %collective-permute-start.17 = (bf16[512,256]{1,0:T(8,128)(2,1)S(1)}, bf16[512,256]{1,0:T(8,128)(2,1)S(1)}, u32[]{:S(2)}, u32[]{:S(2)}) collective-permute-start(bf16[512,256]{1,0:T(8,128)(2,1)S(1)} %get-tuple-element.8), channel_id=1, source_target_pairs={{0,24},{8,16},{16,8},{24,0},{1,25},{9,17},{17,9},{25,1},{2,26},{10... | collective-permute-start | bytes 786440 | tf_op jit(solution)/shard_map/ppermute | solution.py:24
  35.1 1.5 %collective-permute-start.9 = (bf16[512,256]{1,0:T(8,128)(2,1)S(1)}, bf16[512,256]{1,0:T(8,128)(2,1)}, u32[]{:S(2)}, u32[]{:S(2)}) collective-permute-start(bf16[512,256]{1,0:T(8,128)(2,1)S(1)} %get-tuple-element.8), channel_id=1, source_target_pairs={{0,2},{1,3},{2,0},{3,1},{4,6},{5,7},{6,4},{7,5},{8,10},{9,11},{10,... | collective-permute-start | bytes 786440 | tf_op jit(solution)/shard_map/ppermute | solution.py:24
  36.5 1.0 fusion.74
  37.6 7.7 %collective-permute-done.11 = bf16[512,256]{1,0:T(8,128)(2,1)} collective-permute-done((bf16[512,256]{1,0:T(8,128)(2,1)S(1)}, bf16[512,256]{1,0:T(8,128)(2,1)}, u32[]{:S(2)}, u32[]{:S(2)}) %collective-permute-start.11) | collective-permute-done | bytes 262176 | tf_op jit(solution)/shard_map/ppermute | solution.py:24
  46.1 1.2 collective-permute-done.16
  47.3 1.1 pad_maximum_fusion.1
  48.4 1.8 %gather_fusion.1 = bf16[8,256,256]{2,1,0:T(8,128)(2,1)S(1)} fusion(bf16[8,256,256]{2,1,0:T(8,128)(2,1)} %bitcast.270, s32[1024]{0:T(1024)S(1)} %pad_clamp_fusion), kind=kCustom, calls=%fused_computation.1.clone | custom fusion | bytes 2097184 | tf_op jit(solution)/shard_map/jit(_take)/gather | solution.py:63
  52.2 1.2 fusion.58
  53.4 1.2 fusion.62
  57.3 1.2 fusion.76
  58.6 1.2 fusion.52
  59.8 1.2 fusion.54
  62.2 1.3 %fusion.22 = f32[512,256]{1,0:T(8,128)S(1)} fusion(f32[512,256]{1,0:T(8,128)S(1)} %fusion.52, f32[512,256]{1,0:T(8,128)S(1)} %fusion.54, f32[512,256]{1,0:T(8,128)S(1)} %fusion.76, f32[512,256]{1,0:T(8,128)S(1)} %fusion.31, f32[512,256]{1,0:T(8,128)S(1)} %convolution_add_fusion.14, bf16[512,256]{1,0:T(8,128)(2,1)} %collective-permute-done.9, ...), kind=kOutput, calls=%fused_computation.40 | convolution fusion | flops 67764224 | bytes 3538944 | tf_op jit(solution)/shard_map/dot_general | solution.py:69
  63.8 2.1 %collective-permute-start.23 = (bf16[512,256]{1,0:T(8,128)(2,1)S(1)}, bf16[512,256]{1,0:T(8,128)(2,1)S(1)}, u32[]{:S(2)}, u32[]{:S(2)}) collective-permute-start(bf16[512,256]{1,0:T(8,128)(2,1)S(1)} %fusion.29), channel_id=1, source_target_pairs={{0,4},{1,5},{2,6},{3,7},{4,0},{5,1},{6,2},{7,3},{8,12},{9,13},{10,... | collective-permute-start | bytes 786440 | tf_op jit(solution)/shard_map/ppermute | solution.py:24
  66.0 2.2 %collective-permute-start.20 = (bf16[512,256]{1,0:T(8,128)(2,1)S(1)}, bf16[512,256]{1,0:T(8,128)(2,1)S(1)}, u32[]{:S(2)}, u32[]{:S(2)}) collective-permute-start(bf16[512,256]{1,0:T(8,128)(2,1)S(1)} %fusion.29), channel_id=1, source_target_pairs={{0,24},{8,16},{16,8},{24,0},{1,25},{9,17},{17,9},{25,1},{2,26},{10... | collective-permute-start | bytes 786440 | tf_op jit(solution)/shard_map/ppermute | solution.py:24
  68.6 9.2 %collective-permute-done.23 = bf16[512,256]{1,0:T(8,128)(2,1)S(1)} collective-permute-done((bf16[512,256]{1,0:T(8,128)(2,1)S(1)}, bf16[512,256]{1,0:T(8,128)(2,1)S(1)}, u32[]{:S(2)}, u32[]{:S(2)}) %collective-permute-start.23) | collective-permute-done | bytes 262176 | tf_op jit(solution)/shard_map/ppermute | solution.py:24
  77.8 1.5 %collective-permute-start.24 = (bf16[1,512,256]{2,1,0:T(8,128)(2,1)S(1)}, bf16[1,512,256]{2,1,0:T(8,128)(2,1)}, u32[]{:S(2)}, u32[]{:S(2)}) collective-permute-start(bf16[1,512,256]{2,1,0:T(8,128)(2,1)S(1)} %bitcast.281), channel_id=1, source_target_pairs={{0,1},{1,0},{2,3},{3,2},{4,5},{5,4},{6,7},{7,6},{8,9},{9,8},{10,11... | collective-permute-start | bytes 786440 | tf_op jit(solution)/shard_map/ppermute | solution.py:24
  79.3 1.4 %collective-permute-done.19 = bf16[512,256]{1,0:T(8,128)(2,1)S(1)} collective-permute-done((bf16[512,256]{1,0:T(8,128)(2,1)S(1)}, bf16[512,256]{1,0:T(8,128)(2,1)S(1)}, u32[]{:S(2)}, u32[]{:S(2)}) %collective-permute-start.19) | collective-permute-done | bytes 262176 | tf_op jit(solution)/shard_map/ppermute | solution.py:24
  82.8 3.0 %collective-permute-done.25 = bf16[1,512,256]{2,1,0:T(8,128)(2,1)} collective-permute-done((bf16[1,512,256]{2,1,0:T(8,128)(2,1)S(1)}, bf16[1,512,256]{2,1,0:T(8,128)(2,1)}, u32[]{:S(2)}, u32[]{:S(2)}) %collective-permute-start.25) | collective-permute-done | bytes 262176 | tf_op jit(solution)/shard_map/ppermute | solution.py:24
  85.8 1.6 %collective-permute-start.26 = (bf16[1,512,256]{2,1,0:T(8,128)(2,1)}, bf16[1,512,256]{2,1,0:T(8,128)(2,1)S(1)}, u32[]{:S(2)}, u32[]{:S(2)}) collective-permute-start(bf16[1,512,256]{2,1,0:T(8,128)(2,1)} %collective-permute-done.25), channel_id=1, source_target_pairs={{0,1},{1,0},{2,3},{3,2},{4,5},{5,4},{6,7},{7,6},{8,9},{9,8},{10,11... | collective-permute-start | bytes 786440 | tf_op jit(solution)/shard_map/ppermute | solution.py:24
  87.4 1.2 fusion.43
  88.6 1.2 fusion.47
  91.1 1.0 fusion.86
  92.1 2.7 %collective-permute-start.35 = (bf16[512,256]{1,0:T(8,128)(2,1)S(1)}, bf16[512,256]{1,0:T(8,128)(2,1)S(1)}, u32[]{:S(2)}, u32[]{:S(2)}) collective-permute-start(bf16[512,256]{1,0:T(8,128)(2,1)S(1)} %get-tuple-element.10), channel_id=1, source_target_pairs={{0,24},{8,16},{16,8},{24,0},{1,25},{9,17},{17,9},{25,1},{2,26},{10... | collective-permute-start | bytes 786440 | tf_op jit(solution)/shard_map/ppermute | solution.py:24
  95.2 1.1 collective-permute-start.27
  96.2 1.0 fusion.78
  97.2 8.8 %collective-permute-done.29 = bf16[512,256]{1,0:T(8,128)(2,1)} collective-permute-done((bf16[512,256]{1,0:T(8,128)(2,1)S(1)}, bf16[512,256]{1,0:T(8,128)(2,1)}, u32[]{:S(2)}, u32[]{:S(2)}) %collective-permute-start.29) | collective-permute-done | bytes 262176 | tf_op jit(solution)/shard_map/ppermute | solution.py:24
  107.3 1.1 pad_maximum_fusion.3
  108.5 1.8 %gather_fusion.3 = bf16[8,256,256]{2,1,0:T(8,128)(2,1)S(1)} fusion(bf16[8,256,256]{2,1,0:T(8,128)(2,1)} %bitcast.268, s32[1024]{0:T(1024)S(1)} %pad_clamp_fusion), kind=kCustom, calls=%fused_computation.3.clone | custom fusion | bytes 2097184 | tf_op jit(solution)/shard_map/jit(_take)/gather | solution.py:63
  112.1 1.2 fusion.41
  113.3 1.2 fusion.45
  117.2 1.2 fusion.80
  118.6 1.2 fusion.35
  119.8 1.2 fusion.37
  122.3 1.3 %fusion.8 = f32[512,256]{1,0:T(8,128)S(1)} fusion(f32[512,256]{1,0:T(8,128)S(1)} %fusion.35, f32[512,256]{1,0:T(8,128)S(1)} %fusion.37, f32[512,256]{1,0:T(8,128)S(1)} %fusion.80, f32[512,256]{1,0:T(8,128)S(1)} %fusion.30, f32[512,256]{1,0:T(8,128)S(1)} %convolution_add_fusion.5, bf16[512,256]{1,0:T(8,128)(2,1)} %collective-permute-done.27, ...), kind=kOutput, calls=%fused_computation.17 | convolution fusion | flops 67764224 | bytes 3538944 | tf_op jit(solution)/shard_map/dot_general | solution.py:69
  123.6 1.0 bitcast_multiply_fusion
  (130 shorter events, 24.9 us)
Async XLA Ops:
  0.0 1.1 copy-start.16
  1.2 14.9 %collective-permute-start.5 = (bf16[512,256]{1,0:T(8,128)(2,1)S(1)}, bf16[512,256]{1,0:T(8,128)(2,1)S(1)}, u32[]{:S(2)}, u32[]{:S(2)}) collective-permute-start(bf16[512,256]{1,0:T(8,128)(2,1)S(1)} %fusion.28), channel_id=1, source_target_pairs={{0,4},{1,5},{2,6},{3,7},{4,0},{5,1},{6,2},{7,3},{8,12},{9,13},{10,... | collective-permute-start | bytes 786440 | tf_op jit(solution)/shard_map/ppermute | solution.py:24
  4.4 12.9 %collective-permute-start.2 = (bf16[512,256]{1,0:T(8,128)(2,1)S(1)}, bf16[512,256]{1,0:T(8,128)(2,1)S(1)}, u32[]{:S(2)}, u32[]{:S(2)}) collective-permute-start(bf16[512,256]{1,0:T(8,128)(2,1)S(1)} %fusion.28), channel_id=1, source_target_pairs={{0,24},{8,16},{16,8},{24,0},{1,25},{9,17},{17,9},{25,1},{2,26},{10... | collective-permute-start | bytes 786440 | tf_op jit(solution)/shard_map/ppermute | solution.py:24
  6.5 12.6 %collective-permute-start.1 = (bf16[512,256]{1,0:T(8,128)(2,1)S(1)}, bf16[512,256]{1,0:T(8,128)(2,1)S(1)}, u32[]{:S(2)}, u32[]{:S(2)}) collective-permute-start(bf16[512,256]{1,0:T(8,128)(2,1)S(1)} %fusion.28), channel_id=1, source_target_pairs={{0,16},{8,24},{16,0},{24,8},{1,17},{9,25},{17,1},{25,9},{2,18},{10... | collective-permute-start | bytes 786440 | tf_op jit(solution)/shard_map/ppermute | solution.py:24
  6.8 12.4 %collective-permute-start = (bf16[512,256]{1,0:T(8,128)(2,1)S(1)}, bf16[512,256]{1,0:T(8,128)(2,1)S(1)}, u32[]{:S(2)}, u32[]{:S(2)}) collective-permute-start(bf16[512,256]{1,0:T(8,128)(2,1)S(1)} %fusion.28), channel_id=1, source_target_pairs={{0,8},{8,0},{16,24},{24,16},{1,9},{9,1},{17,25},{25,17},{2,10},{10... | collective-permute-start | bytes 786440 | tf_op jit(solution)/shard_map/ppermute | solution.py:24
  7.0 13.3 %collective-permute-start.3 = (bf16[512,256]{1,0:T(8,128)(2,1)S(1)}, bf16[512,256]{1,0:T(8,128)(2,1)S(1)}, u32[]{:S(2)}, u32[]{:S(2)}) collective-permute-start(bf16[512,256]{1,0:T(8,128)(2,1)S(1)} %fusion.28), channel_id=1, source_target_pairs={{0,2},{1,3},{2,0},{3,1},{4,6},{5,7},{6,4},{7,5},{8,10},{9,11},{10,... | collective-permute-start | bytes 786440 | tf_op jit(solution)/shard_map/ppermute | solution.py:24
  16.1 5.2 %copy-start.8 = (bf16[512,256]{1,0:T(8,128)(2,1)}, bf16[512,256]{1,0:T(8,128)(2,1)S(1)}, u32[]{:S(2)}) copy-start(bf16[512,256]{1,0:T(8,128)(2,1)S(1)} %collective-permute-done.5) | copy-start | bytes 786436
  16.1 8.5 %collective-permute-start.7 = (bf16[1,512,256]{2,1,0:T(8,128)(2,1)S(1)}, bf16[1,512,256]{2,1,0:T(8,128)(2,1)}, u32[]{:S(2)}, u32[]{:S(2)}) collective-permute-start(bf16[1,512,256]{2,1,0:T(8,128)(2,1)S(1)} %bitcast.278), channel_id=1, source_target_pairs={{0,2},{1,3},{2,0},{3,1},{4,6},{5,7},{6,4},{7,5},{8,10},{9,11},{10,... | collective-permute-start | bytes 786440 | tf_op jit(solution)/shard_map/ppermute | solution.py:24
  17.2 9.8 %collective-permute-start.6 = (bf16[1,512,256]{2,1,0:T(8,128)(2,1)S(1)}, bf16[1,512,256]{2,1,0:T(8,128)(2,1)}, u32[]{:S(2)}, u32[]{:S(2)}) collective-permute-start(bf16[1,512,256]{2,1,0:T(8,128)(2,1)S(1)} %bitcast.279), channel_id=1, source_target_pairs={{0,1},{1,0},{2,3},{3,2},{4,5},{5,4},{6,7},{7,6},{8,9},{9,8},{10,11... | collective-permute-start | bytes 786440 | tf_op jit(solution)/shard_map/ppermute | solution.py:24
  20.3 7.9 %collective-permute-start.4 = (bf16[2,512,256]{2,1,0:T(8,128)(2,1)S(1)}, bf16[2,512,256]{2,1,0:T(8,128)(2,1)S(1)}, u32[]{:S(2)}, u32[]{:S(2)}) collective-permute-start(bf16[2,512,256]{2,1,0:T(8,128)(2,1)S(1)} %pad_maximum_fusion.4), channel_id=1, source_target_pairs={{0,1},{1,0},{2,3},{3,2},{4,5},{5,4},{6,7},{7,6},{8,9},{9,8},{10,11... | collective-permute-start | bytes 1572872 | tf_op jit(solution)/shard_map/ppermute | solution.py:24
  24.6 5.0 %collective-permute-start.8 = (bf16[1,512,256]{2,1,0:T(8,128)(2,1)}, bf16[1,512,256]{2,1,0:T(8,128)(2,1)S(1)}, u32[]{:S(2)}, u32[]{:S(2)}) collective-permute-start(bf16[1,512,256]{2,1,0:T(8,128)(2,1)} %collective-permute-done.7), channel_id=1, source_target_pairs={{0,1},{1,0},{2,3},{3,2},{4,5},{5,4},{6,7},{7,6},{8,9},{9,8},{10,11... | collective-permute-start | bytes 786440 | tf_op jit(solution)/shard_map/ppermute | solution.py:24
  29.6 1.0 copy-start.14
  30.6 14.6 %collective-permute-start.11 = (bf16[512,256]{1,0:T(8,128)(2,1)S(1)}, bf16[512,256]{1,0:T(8,128)(2,1)}, u32[]{:S(2)}, u32[]{:S(2)}) collective-permute-start(bf16[512,256]{1,0:T(8,128)(2,1)S(1)} %get-tuple-element.8), channel_id=1, source_target_pairs={{0,4},{1,5},{2,6},{3,7},{4,0},{5,1},{6,2},{7,3},{8,12},{9,13},{10,... | collective-permute-start | bytes 786440 | tf_op jit(solution)/shard_map/ppermute | solution.py:24
  32.4 12.9 %collective-permute-start.17 = (bf16[512,256]{1,0:T(8,128)(2,1)S(1)}, bf16[512,256]{1,0:T(8,128)(2,1)S(1)}, u32[]{:S(2)}, u32[]{:S(2)}) collective-permute-start(bf16[512,256]{1,0:T(8,128)(2,1)S(1)} %get-tuple-element.8), channel_id=1, source_target_pairs={{0,24},{8,16},{16,8},{24,0},{1,25},{9,17},{17,9},{25,1},{2,26},{10... | collective-permute-start | bytes 786440 | tf_op jit(solution)/shard_map/ppermute | solution.py:24
  34.6 12.7 %collective-permute-start.16 = (bf16[512,256]{1,0:T(8,128)(2,1)S(1)}, bf16[512,256]{1,0:T(8,128)(2,1)S(1)}, u32[]{:S(2)}, u32[]{:S(2)}) collective-permute-start(bf16[512,256]{1,0:T(8,128)(2,1)S(1)} %get-tuple-element.8), channel_id=1, source_target_pairs={{0,16},{8,24},{16,0},{24,8},{1,17},{9,25},{17,1},{25,9},{2,18},{10... | collective-permute-start | bytes 786440 | tf_op jit(solution)/shard_map/ppermute | solution.py:24
  34.8 12.5 %collective-permute-start.15 = (bf16[512,256]{1,0:T(8,128)(2,1)S(1)}, bf16[512,256]{1,0:T(8,128)(2,1)S(1)}, u32[]{:S(2)}, u32[]{:S(2)}) collective-permute-start(bf16[512,256]{1,0:T(8,128)(2,1)S(1)} %get-tuple-element.8), channel_id=1, source_target_pairs={{0,8},{8,0},{16,24},{24,16},{1,9},{9,1},{17,25},{25,17},{2,10},{10... | collective-permute-start | bytes 786440 | tf_op jit(solution)/shard_map/ppermute | solution.py:24
  35.1 15.6 %collective-permute-start.9 = (bf16[512,256]{1,0:T(8,128)(2,1)S(1)}, bf16[512,256]{1,0:T(8,128)(2,1)}, u32[]{:S(2)}, u32[]{:S(2)}) collective-permute-start(bf16[512,256]{1,0:T(8,128)(2,1)S(1)} %get-tuple-element.8), channel_id=1, source_target_pairs={{0,2},{1,3},{2,0},{3,1},{4,6},{5,7},{6,4},{7,5},{8,10},{9,11},{10,... | collective-permute-start | bytes 786440 | tf_op jit(solution)/shard_map/ppermute | solution.py:24
  45.2 13.3 %collective-permute-start.13 = (bf16[1,512,256]{2,1,0:T(8,128)(2,1)}, bf16[1,512,256]{2,1,0:T(8,128)(2,1)}, u32[]{:S(2)}, u32[]{:S(2)}) collective-permute-start(bf16[1,512,256]{2,1,0:T(8,128)(2,1)} %bitcast.25), channel_id=1, source_target_pairs={{0,2},{1,3},{2,0},{3,1},{4,6},{5,7},{6,4},{7,5},{8,10},{9,11},{10,... | collective-permute-start | bytes 786440 | tf_op jit(solution)/shard_map/ppermute | solution.py:24
  45.4 14.4 %collective-permute-start.12 = (bf16[1,512,256]{2,1,0:T(8,128)(2,1)}, bf16[1,512,256]{2,1,0:T(8,128)(2,1)}, u32[]{:S(2)}, u32[]{:S(2)}) collective-permute-start(bf16[1,512,256]{2,1,0:T(8,128)(2,1)} %bitcast.25), channel_id=1, source_target_pairs={{0,1},{1,0},{2,3},{3,2},{4,5},{5,4},{6,7},{7,6},{8,9},{9,8},{10,11... | collective-permute-start | bytes 786440 | tf_op jit(solution)/shard_map/ppermute | solution.py:24
  51.7 9.3 %collective-permute-start.10 = (bf16[2,512,256]{2,1,0:T(8,128)(2,1)S(1)}, bf16[2,512,256]{2,1,0:T(8,128)(2,1)S(1)}, u32[]{:S(2)}, u32[]{:S(2)}) collective-permute-start(bf16[2,512,256]{2,1,0:T(8,128)(2,1)S(1)} %pad_maximum_fusion.5), channel_id=1, source_target_pairs={{0,1},{1,0},{2,3},{3,2},{4,5},{5,4},{6,7},{7,6},{8,9},{9,8},{10,11... | collective-permute-start | bytes 1572872 | tf_op jit(solution)/shard_map/ppermute | solution.py:24
  53.4 1.2 copy-start.9
  54.6 1.0 copy-start.5
  58.5 5.0 %collective-permute-start.14 = (bf16[1,512,256]{2,1,0:T(8,128)(2,1)}, bf16[1,512,256]{2,1,0:T(8,128)(2,1)S(1)}, u32[]{:S(2)}, u32[]{:S(2)}) collective-permute-start(bf16[1,512,256]{2,1,0:T(8,128)(2,1)} %collective-permute-done.13), channel_id=1, source_target_pairs={{0,1},{1,0},{2,3},{3,2},{4,5},{5,4},{6,7},{7,6},{8,9},{9,8},{10,11... | collective-permute-start | bytes 786440 | tf_op jit(solution)/shard_map/ppermute | solution.py:24
  61.0 1.0 copy-start.7
  62.2 1.3 %copy-start.1 = (f32[512,256]{1,0:T(8,128)S(1)}, f32[512,256]{1,0:T(8,128)}, u32[]{:S(2)}) copy-start(f32[512,256]{1,0:T(8,128)} %get-tuple-element.9) | copy-start | bytes 1572868
  63.8 14.0 %collective-permute-start.23 = (bf16[512,256]{1,0:T(8,128)(2,1)S(1)}, bf16[512,256]{1,0:T(8,128)(2,1)S(1)}, u32[]{:S(2)}, u32[]{:S(2)}) collective-permute-start(bf16[512,256]{1,0:T(8,128)(2,1)S(1)} %fusion.29), channel_id=1, source_target_pairs={{0,4},{1,5},{2,6},{3,7},{4,0},{5,1},{6,2},{7,3},{8,12},{9,13},{10,... | collective-permute-start | bytes 786440 | tf_op jit(solution)/shard_map/ppermute | solution.py:24
  66.0 11.9 %collective-permute-start.20 = (bf16[512,256]{1,0:T(8,128)(2,1)S(1)}, bf16[512,256]{1,0:T(8,128)(2,1)S(1)}, u32[]{:S(2)}, u32[]{:S(2)}) collective-permute-start(bf16[512,256]{1,0:T(8,128)(2,1)S(1)} %fusion.29), channel_id=1, source_target_pairs={{0,24},{8,16},{16,8},{24,0},{1,25},{9,17},{17,9},{25,1},{2,26},{10... | collective-permute-start | bytes 786440 | tf_op jit(solution)/shard_map/ppermute | solution.py:24
  68.1 12.6 %collective-permute-start.19 = (bf16[512,256]{1,0:T(8,128)(2,1)S(1)}, bf16[512,256]{1,0:T(8,128)(2,1)S(1)}, u32[]{:S(2)}, u32[]{:S(2)}) collective-permute-start(bf16[512,256]{1,0:T(8,128)(2,1)S(1)} %fusion.29), channel_id=1, source_target_pairs={{0,16},{8,24},{16,0},{24,8},{1,17},{9,25},{17,1},{25,9},{2,18},{10... | collective-permute-start | bytes 786440 | tf_op jit(solution)/shard_map/ppermute | solution.py:24
  68.3 12.4 %collective-permute-start.18 = (bf16[512,256]{1,0:T(8,128)(2,1)S(1)}, bf16[512,256]{1,0:T(8,128)(2,1)S(1)}, u32[]{:S(2)}, u32[]{:S(2)}) collective-permute-start(bf16[512,256]{1,0:T(8,128)(2,1)S(1)} %fusion.29), channel_id=1, source_target_pairs={{0,8},{8,0},{16,24},{24,16},{1,9},{9,1},{17,25},{25,17},{2,10},{10... | collective-permute-start | bytes 786440 | tf_op jit(solution)/shard_map/ppermute | solution.py:24
  68.6 13.3 %collective-permute-start.21 = (bf16[512,256]{1,0:T(8,128)(2,1)S(1)}, bf16[512,256]{1,0:T(8,128)(2,1)S(1)}, u32[]{:S(2)}, u32[]{:S(2)}) collective-permute-start(bf16[512,256]{1,0:T(8,128)(2,1)S(1)} %fusion.29), channel_id=1, source_target_pairs={{0,2},{1,3},{2,0},{3,1},{4,6},{5,7},{6,4},{7,5},{8,10},{9,11},{10,... | collective-permute-start | bytes 786440 | tf_op jit(solution)/shard_map/ppermute | solution.py:24
  77.8 4.7 %copy-start.10 = (bf16[512,256]{1,0:T(8,128)(2,1)}, bf16[512,256]{1,0:T(8,128)(2,1)S(1)}, u32[]{:S(2)}) copy-start(bf16[512,256]{1,0:T(8,128)(2,1)S(1)} %collective-permute-done.23) | copy-start | bytes 786436
  77.8 8.0 %collective-permute-start.25 = (bf16[1,512,256]{2,1,0:T(8,128)(2,1)S(1)}, bf16[1,512,256]{2,1,0:T(8,128)(2,1)}, u32[]{:S(2)}, u32[]{:S(2)}) collective-permute-start(bf16[1,512,256]{2,1,0:T(8,128)(2,1)S(1)} %bitcast.280), channel_id=1, source_target_pairs={{0,2},{1,3},{2,0},{3,1},{4,6},{5,7},{6,4},{7,5},{8,10},{9,11},{10,... | collective-permute-start | bytes 786440 | tf_op jit(solution)/shard_map/ppermute | solution.py:24
  77.8 10.7 %collective-permute-start.24 = (bf16[1,512,256]{2,1,0:T(8,128)(2,1)S(1)}, bf16[1,512,256]{2,1,0:T(8,128)(2,1)}, u32[]{:S(2)}, u32[]{:S(2)}) collective-permute-start(bf16[1,512,256]{2,1,0:T(8,128)(2,1)S(1)} %bitcast.281), channel_id=1, source_target_pairs={{0,1},{1,0},{2,3},{3,2},{4,5},{5,4},{6,7},{7,6},{8,9},{9,8},{10,11... | collective-permute-start | bytes 786440 | tf_op jit(solution)/shard_map/ppermute | solution.py:24
  81.9 7.8 %collective-permute-start.22 = (bf16[2,512,256]{2,1,0:T(8,128)(2,1)S(1)}, bf16[2,512,256]{2,1,0:T(8,128)(2,1)S(1)}, u32[]{:S(2)}, u32[]{:S(2)}) collective-permute-start(bf16[2,512,256]{2,1,0:T(8,128)(2,1)S(1)} %pad_maximum_fusion.6), channel_id=1, source_target_pairs={{0,1},{1,0},{2,3},{3,2},{4,5},{5,4},{6,7},{7,6},{8,9},{9,8},{10,11... | collective-permute-start | bytes 1572872 | tf_op jit(solution)/shard_map/ppermute | solution.py:24
  85.8 5.2 %collective-permute-start.26 = (bf16[1,512,256]{2,1,0:T(8,128)(2,1)}, bf16[1,512,256]{2,1,0:T(8,128)(2,1)S(1)}, u32[]{:S(2)}, u32[]{:S(2)}) collective-permute-start(bf16[1,512,256]{2,1,0:T(8,128)(2,1)} %collective-permute-done.25), channel_id=1, source_target_pairs={{0,1},{1,0},{2,3},{3,2},{4,5},{5,4},{6,7},{7,6},{8,9},{9,8},{10,11... | collective-permute-start | bytes 786440 | tf_op jit(solution)/shard_map/ppermute | solution.py:24
  92.1 13.9 %collective-permute-start.29 = (bf16[512,256]{1,0:T(8,128)(2,1)S(1)}, bf16[512,256]{1,0:T(8,128)(2,1)}, u32[]{:S(2)}, u32[]{:S(2)}) collective-permute-start(bf16[512,256]{1,0:T(8,128)(2,1)S(1)} %get-tuple-element.10), channel_id=1, source_target_pairs={{0,4},{1,5},{2,6},{3,7},{4,0},{5,1},{6,2},{7,3},{8,12},{9,13},{10,... | collective-permute-start | bytes 786440 | tf_op jit(solution)/shard_map/ppermute | solution.py:24
  92.1 13.9 %collective-permute-start.35 = (bf16[512,256]{1,0:T(8,128)(2,1)S(1)}, bf16[512,256]{1,0:T(8,128)(2,1)S(1)}, u32[]{:S(2)}, u32[]{:S(2)}) collective-permute-start(bf16[512,256]{1,0:T(8,128)(2,1)S(1)} %get-tuple-element.10), channel_id=1, source_target_pairs={{0,24},{8,16},{16,8},{24,0},{1,25},{9,17},{17,9},{25,1},{2,26},{10... | collective-permute-start | bytes 786440 | tf_op jit(solution)/shard_map/ppermute | solution.py:24
  94.8 12.5 %collective-permute-start.34 = (bf16[512,256]{1,0:T(8,128)(2,1)S(1)}, bf16[512,256]{1,0:T(8,128)(2,1)S(1)}, u32[]{:S(2)}, u32[]{:S(2)}) collective-permute-start(bf16[512,256]{1,0:T(8,128)(2,1)S(1)} %get-tuple-element.10), channel_id=1, source_target_pairs={{0,16},{8,24},{16,0},{24,8},{1,17},{9,25},{17,1},{25,9},{2,18},{10... | collective-permute-start | bytes 786440 | tf_op jit(solution)/shard_map/ppermute | solution.py:24
  94.8 12.5 %collective-permute-start.33 = (bf16[512,256]{1,0:T(8,128)(2,1)S(1)}, bf16[512,256]{1,0:T(8,128)(2,1)S(1)}, u32[]{:S(2)}, u32[]{:S(2)}) collective-permute-start(bf16[512,256]{1,0:T(8,128)(2,1)S(1)} %get-tuple-element.10), channel_id=1, source_target_pairs={{0,8},{8,0},{16,24},{24,16},{1,9},{9,1},{17,25},{25,17},{2,10},{10... | collective-permute-start | bytes 786440 | tf_op jit(solution)/shard_map/ppermute | solution.py:24
  95.2 15.5 %collective-permute-start.27 = (bf16[512,256]{1,0:T(8,128)(2,1)S(1)}, bf16[512,256]{1,0:T(8,128)(2,1)}, u32[]{:S(2)}, u32[]{:S(2)}) collective-permute-start(bf16[512,256]{1,0:T(8,128)(2,1)S(1)} %get-tuple-element.10), channel_id=1, source_target_pairs={{0,2},{1,3},{2,0},{3,1},{4,6},{5,7},{6,4},{7,5},{8,10},{9,11},{10,... | collective-permute-start | bytes 786440 | tf_op jit(solution)/shard_map/ppermute | solution.py:24
  106.1 12.3 %collective-permute-start.31 = (bf16[1,512,256]{2,1,0:T(8,128)(2,1)}, bf16[1,512,256]{2,1,0:T(8,128)(2,1)}, u32[]{:S(2)}, u32[]{:S(2)}) collective-permute-start(bf16[1,512,256]{2,1,0:T(8,128)(2,1)} %bitcast.65), channel_id=1, source_target_pairs={{0,2},{1,3},{2,0},{3,1},{4,6},{5,7},{6,4},{7,5},{8,10},{9,11},{10,... | collective-permute-start | bytes 786440 | tf_op jit(solution)/shard_map/ppermute | solution.py:24
  106.1 13.8 %collective-permute-start.30 = (bf16[1,512,256]{2,1,0:T(8,128)(2,1)}, bf16[1,512,256]{2,1,0:T(8,128)(2,1)}, u32[]{:S(2)}, u32[]{:S(2)}) collective-permute-start(bf16[1,512,256]{2,1,0:T(8,128)(2,1)} %bitcast.65), channel_id=1, source_target_pairs={{0,1},{1,0},{2,3},{3,2},{4,5},{5,4},{6,7},{7,6},{8,9},{9,8},{10,11... | collective-permute-start | bytes 786440 | tf_op jit(solution)/shard_map/ppermute | solution.py:24
  111.7 9.3 %collective-permute-start.28 = (bf16[2,512,256]{2,1,0:T(8,128)(2,1)S(1)}, bf16[2,512,256]{2,1,0:T(8,128)(2,1)S(1)}, u32[]{:S(2)}, u32[]{:S(2)}) collective-permute-start(bf16[2,512,256]{2,1,0:T(8,128)(2,1)S(1)} %pad_maximum_fusion.7), channel_id=1, source_target_pairs={{0,1},{1,0},{2,3},{3,2},{4,5},{5,4},{6,7},{7,6},{8,9},{9,8},{10,11... | collective-permute-start | bytes 1572872 | tf_op jit(solution)/shard_map/ppermute | solution.py:24
  113.3 1.2 copy-start.11
  114.5 1.0 copy-start.3
  118.4 5.2 %collective-permute-start.32 = (bf16[1,512,256]{2,1,0:T(8,128)(2,1)}, bf16[1,512,256]{2,1,0:T(8,128)(2,1)S(1)}, u32[]{:S(2)}, u32[]{:S(2)}) collective-permute-start(bf16[1,512,256]{2,1,0:T(8,128)(2,1)} %collective-permute-done.31), channel_id=1, source_target_pairs={{0,1},{1,0},{2,3},{3,2},{4,5},{5,4},{6,7},{7,6},{8,9},{9,8},{10,11... | collective-permute-start | bytes 786440 | tf_op jit(solution)/shard_map/ppermute | solution.py:24
  121.0 1.0 copy-start.6
  122.3 1.3 %copy-start = (f32[512,256]{1,0:T(8,128)S(1)}, f32[512,256]{1,0:T(8,128)}, u32[]{:S(2)}) copy-start(f32[512,256]{1,0:T(8,128)} %get-tuple-element.11) | copy-start | bytes 1572868
  (6 other events, 5.2 us)

commit v13 on v6

--- a/solution.py
+++ b/solution.py
@@ -29,13 +29,20 @@
     same = {0: xb}
     for s in sorted(range(2, chips, 2), reverse=True) + [1]:
         same[s] = xor_permute(xb, "col", n_col, 2 * s)
-    col_pieces = [xb] + [xor_permute(xb, "row", n_row, t) for t in range(1, n_row)]
+    col_pieces = [xb] + [xor_permute(xb, "row", n_row, t) for t in range(1, n_row) if t & (t - 1) == 0]
+    forward = list(range(2, chips, 2))
+    if forward:
+        later, same[forward[0]] = lax.optimization_barrier((xb, same[forward[0]]))
+    else:
+        later = xb
+    for t in range(3, n_row):
+        if t & (t - 1):
+            col_pieces.insert(t, xor_permute(later, "row", n_row, t))
     first = sorted(same)
     relay_first = xor_permute(jnp.stack([same[s] for s in first]), "col", n_col, 1)
     other = {}
     for i, s in enumerate(first):
         other[s] = relay_first[i]
-    forward = list(range(2, chips, 2))
     if forward:
         sent = xor_permute(jnp.stack([same[s] for s in forward]), "col", n_col, 2)
         relay_sent = xor_permute(sent, "col", n_col, 1)

time: 124 us -> 147 us (1.19)
  matrix products: 28.5 us -> 41.5 us
  waiting for transfers between devices: 43.1 us -> 46.8 us
  starting transfers between devices: 35.3 us -> 38.8 us
  other arithmetic: 6.66 us -> 9.37 us
    dot_general x48, matrix products: 28.5 us -> 41.5 us  [contract(): part = jnp.dot(piece, k_blocks[s], preferred_element_type=jnp.float32)]
    ppermute x32, waiting for transfers between devices: 43.1 us -> 46.8 us  [xor_permute(): return lax.ppermute(x, axis, perm=[(i, i ^ s) for i in range(size)])]
    ppermute x32, starting transfers between devices: 35.3 us -> 38.8 us  [xor_permute(): return lax.ppermute(x, axis, perm=[(i, i ^ s) for i in range(size)])]
    another operation x4, other arithmetic: 3.31 us -> 6.02 us  [exchange(): jnp.stack([same[s] for s in first])]
  transfers between devices with their start and end apart: 32 -> 32, of which waited for: 11 -> 8; matrix products, arithmetic and copies ran while one was open for 30% -> 36% of each run, Pallas kernels for 0% -> 0%
where the time goes in v13:
time: 147 us; the launch traced here: 146 us
  waiting for transfers between devices  46.8 us (32%)
  matrix products  41.5 us (28%)
  starting transfers between devices  38.8 us (26%)
  other arithmetic  9.37 us (6%)
  local copies, waits for them, and re-layouts  8.77 us (6%)
    ppermute x32, waiting for transfers between devices, xor_permute(): return lax.ppermute(x, axis, perm=[(i, i ^ s) for i in range(size)])  46.8 us
    dot_general x48, matrix products, contract(): part = jnp.dot(piece, k_blocks[s], preferred_element_type=jnp.float32)  41.5 us
    ppermute x32, starting transfers between devices, xor_permute(): return lax.ppermute(x, axis, perm=[(i, i ^ s) for i in range(size)])  38.8 us
    another operation x4, other arithmetic, exchange(): jnp.stack([same[s] for s in first])  6.02 us
    gather x4, local copies, waits for them, and re-layouts, ordered_k_blocks(): return jnp.take(split, index, axis=0)  4.9 us
    unnamed x33, local copies, waits for them, and re-layouts  3.66 us
  transfers between devices with their start and end apart: 32, of which 8 were waited for; matrix products, arithmetic and copies ran while one was open for 36% of the time, Pallas kernels for 0%

profile of v13, /device:TPU:1, one launch (start us, length us, event | category | flops | bytes accessed | tf_op | source)
XLA Modules:
  0.0 145.9 jit_solution(6898231550848754348)
XLA Ops:
  1.2 3.2 %collective-permute-start.2 = (bf16[512,256]{1,0:T(8,128)(2,1)S(1)}, bf16[512,256]{1,0:T(8,128)(2,1)S(1)}, u32[]{:S(2)}, u32[]{:S(2)}) collective-permute-start(bf16[512,256]{1,0:T(8,128)(2,1)S(1)} %fusion.28), channel_id=1, source_target_pairs={{0,4},{1,5},{2,6},{3,7},{4,0},{5,1},{6,2},{7,3},{8,12},{9,13},{10,... | collective-permute-start | bytes 786440 | tf_op jit(solution)/shard_map/ppermute | solution.py:24
  4.4 1.3 collective-permute-start.4
  5.7 1.2 collective-permute-start.1
  6.9 1.2 collective-permute-start
  8.1 7.9 %collective-permute-done.2 = bf16[512,256]{1,0:T(8,128)(2,1)S(1)} collective-permute-done((bf16[512,256]{1,0:T(8,128)(2,1)S(1)}, bf16[512,256]{1,0:T(8,128)(2,1)S(1)}, u32[]{:S(2)}, u32[]{:S(2)}) %collective-permute-start.2) | collective-permute-done | bytes 262176 | tf_op jit(solution)/shard_map/ppermute | solution.py:24
  16.1 1.9 %collective-permute-start.3 = (bf16[512,256]{1,0:T(8,128)(2,1)S(1)}, bf16[512,256]{1,0:T(8,128)(2,1)S(1)}, u32[]{:S(2)}, u32[]{:S(2)}) collective-permute-start(bf16[512,256]{1,0:T(8,128)(2,1)S(1)} %fusion.28), channel_id=1, source_target_pairs={{0,24},{8,16},{16,8},{24,0},{1,25},{9,17},{17,9},{25,1},{2,26},{10... | collective-permute-start | bytes 786440 | tf_op jit(solution)/shard_map/ppermute | solution.py:24
  18.0 1.4 collective-permute-start.6
  21.5 2.0 %collective-permute-done.3 = bf16[512,256]{1,0:T(8,128)(2,1)S(1)} collective-permute-done((bf16[512,256]{1,0:T(8,128)(2,1)S(1)}, bf16[512,256]{1,0:T(8,128)(2,1)S(1)}, u32[]{:S(2)}, u32[]{:S(2)}) %collective-permute-start.3) | collective-permute-done | bytes 262176 | tf_op jit(solution)/shard_map/ppermute | solution.py:24
  24.4 2.5 %collective-permute-start.7 = (bf16[1,512,256]{2,1,0:T(8,128)(2,1)}, bf16[1,512,256]{2,1,0:T(8,128)(2,1)S(1)}, u32[]{:S(2)}, u32[]{:S(2)}) collective-permute-start(bf16[1,512,256]{2,1,0:T(8,128)(2,1)} %collective-permute-done.6), channel_id=1, source_target_pairs={{0,1},{1,0},{2,3},{3,2},{4,5},{5,4},{6,7},{7,6},{8,9},{9,8},{10,11... | collective-permute-start | bytes 786440 | tf_op jit(solution)/shard_map/ppermute | solution.py:24
  27.3 1.2 fusion.54
  29.7 1.2 fusion.57
  30.9 1.2 convolution_add_fusion.17
  33.4 3.0 %collective-permute-start.9 = (bf16[512,256]{1,0:T(8,128)(2,1)S(1)}, bf16[512,256]{1,0:T(8,128)(2,1)}, u32[]{:S(2)}, u32[]{:S(2)}) collective-permute-start(bf16[512,256]{1,0:T(8,128)(2,1)S(1)} %get-tuple-element.17), channel_id=1, source_target_pairs={{0,4},{1,5},{2,6},{3,7},{4,0},{5,1},{6,2},{7,3},{8,12},{9,13},{10,... | collective-permute-start | bytes 786440 | tf_op jit(solution)/shard_map/ppermute | solution.py:24
  36.4 1.5 %collective-permute-start.8 = (bf16[512,256]{1,0:T(8,128)(2,1)S(1)}, bf16[512,256]{1,0:T(8,128)(2,1)S(1)}, u32[]{:S(2)}, u32[]{:S(2)}) collective-permute-start(bf16[512,256]{1,0:T(8,128)(2,1)S(1)} %get-tuple-element.17), channel_id=1, source_target_pairs={{0,2},{1,3},{2,0},{3,1},{4,6},{5,7},{6,4},{7,5},{8,10},{9,11},{10,... | collective-permute-start | bytes 786440 | tf_op jit(solution)/shard_map/ppermute | solution.py:24
  38.6 1.2 collective-permute-start.13
  40.9 8.0 %collective-permute-done.9 = bf16[512,256]{1,0:T(8,128)(2,1)} collective-permute-done((bf16[512,256]{1,0:T(8,128)(2,1)S(1)}, bf16[512,256]{1,0:T(8,128)(2,1)}, u32[]{:S(2)}, u32[]{:S(2)}) %collective-permute-start.9) | collective-permute-done | bytes 262176 | tf_op jit(solution)/shard_map/ppermute | solution.py:24
  49.7 2.0 %pad_maximum_fusion.5 = bf16[3,512,256]{2,1,0:T(8,128)(2,1)} fusion(bf16[1,512,256]{2,1,0:T(8,128)(2,1)} %bitcast.23, bf16[1,512,256]{2,1,0:T(8,128)(2,1)S(1)} %bitcast.281, bf16[1,512,256]{2,1,0:T(8,128)(2,1)S(1)} %bitcast.270), kind=kLoop, calls=%fused_computation.59 | loop fusion | flops 786432 | bytes 1572864 | tf_op jit(solution)/shard_map/stack | solution.py:42
  52.9 2.0 %fusion.70 = f32[512,256]{1,0:T(8,128)} fusion(bf16[512,256]{1,0:T(8,128)(2,1)} %collective-permute-done.9, bf16[8,256,256]{2,1,0:T(8,128)(2,1)S(1)} %broadcast_select_fusion.3), kind=kOutput, calls=%fused_computation.147 | convolution fusion | flops 67108864 | bytes 917504 | tf_op jit(solution)/shard_map/dot_general | solution.py:72
  54.9 2.1 %collective-permute-done.15 = bf16[512,256]{1,0:T(8,128)(2,1)S(1)} collective-permute-done((bf16[512,256]{1,0:T(8,128)(2,1)S(1)}, bf16[512,256]{1,0:T(8,128)(2,1)S(1)}, u32[]{:S(2)}, u32[]{:S(2)}) %collective-permute-start.15) | collective-permute-done | bytes 262176 | tf_op jit(solution)/shard_map/ppermute | solution.py:24
  58.1 1.8 %gather_fusion.1 = bf16[8,256,256]{2,1,0:T(8,128)(2,1)S(1)} fusion(bf16[8,256,256]{2,1,0:T(8,128)(2,1)} %bitcast.267, s32[1024]{0:T(1024)S(1)} %pad_clamp_fusion), kind=kCustom, calls=%fused_computation.1.clone | custom fusion | bytes 2097184 | tf_op jit(solution)/shard_map/jit(_take)/gather | solution.py:66
  60.6 1.2 fusion.52
  62.9 1.2 fusion.56
  64.1 1.2 convolution_add_fusion.11
  65.3 1.6 %collective-permute-start.12 = (bf16[1,512,256]{2,1,0:T(8,128)(2,1)}, bf16[1,512,256]{2,1,0:T(8,128)(2,1)S(1)}, u32[]{:S(2)}, u32[]{:S(2)}) collective-permute-start(bf16[1,512,256]{2,1,0:T(8,128)(2,1)} %collective-permute-done.11), channel_id=1, source_target_pairs={{0,1},{1,0},{2,3},{3,2},{4,5},{5,4},{6,7},{7,6},{8,9},{9,8},{10,11... | collective-permute-start | bytes 786440 | tf_op jit(solution)/shard_map/ppermute | solution.py:24
  66.9 1.2 fusion.48
  70.4 1.2 fusion.33
  71.7 1.2 convolution_add_fusion.14
  74.3 3.6 %collective-permute-start.20 = (bf16[512,256]{1,0:T(8,128)(2,1)S(1)}, bf16[512,256]{1,0:T(8,128)(2,1)S(1)}, u32[]{:S(2)}, u32[]{:S(2)}) collective-permute-start(bf16[512,256]{1,0:T(8,128)(2,1)S(1)} %fusion.29), channel_id=1, source_target_pairs={{0,2},{1,3},{2,0},{3,1},{4,6},{5,7},{6,4},{7,5},{8,10},{9,11},{10,... | collective-permute-start | bytes 786440 | tf_op jit(solution)/shard_map/ppermute | solution.py:24
  78.5 10.3 %collective-permute-done.18 = bf16[512,256]{1,0:T(8,128)(2,1)S(1)} collective-permute-done((bf16[512,256]{1,0:T(8,128)(2,1)S(1)}, bf16[512,256]{1,0:T(8,128)(2,1)S(1)}, u32[]{:S(2)}, u32[]{:S(2)}) %collective-permute-start.18) | collective-permute-done | bytes 262176 | tf_op jit(solution)/shard_map/ppermute | solution.py:24
  91.8 4.9 %collective-permute-done.19 = bf16[512,256]{1,0:T(8,128)(2,1)S(1)} collective-permute-done((bf16[512,256]{1,0:T(8,128)(2,1)S(1)}, bf16[512,256]{1,0:T(8,128)(2,1)S(1)}, u32[]{:S(2)}, u32[]{:S(2)}) %collective-permute-start.19) | collective-permute-done | bytes 262176 | tf_op jit(solution)/shard_map/ppermute | solution.py:24
  97.6 1.8 %collective-permute-start.23 = (bf16[1,512,256]{2,1,0:T(8,128)(2,1)}, bf16[1,512,256]{2,1,0:T(8,128)(2,1)S(1)}, u32[]{:S(2)}, u32[]{:S(2)}) collective-permute-start(bf16[1,512,256]{2,1,0:T(8,128)(2,1)} %collective-permute-done.22), channel_id=1, source_target_pairs={{0,1},{1,0},{2,3},{3,2},{4,5},{5,4},{6,7},{7,6},{8,9},{9,8},{10,11... | collective-permute-start | bytes 786440 | tf_op jit(solution)/shard_map/ppermute | solution.py:24
  101.1 1.2 fusion.63
  103.4 1.2 convolution_add_fusion.8
  105.9 1.5 %collective-permute-start.24 = (bf16[512,256]{1,0:T(8,128)(2,1)S(1)}, bf16[512,256]{1,0:T(8,128)(2,1)S(1)}, u32[]{:S(2)}, u32[]{:S(2)}) collective-permute-start(bf16[512,256]{1,0:T(8,128)(2,1)S(1)} %get-tuple-element.21), channel_id=1, source_target_pairs={{0,2},{1,3},{2,0},{3,1},{4,6},{5,7},{6,4},{7,5},{8,10},{9,11},{10,... | collective-permute-start | bytes 786440 | tf_op jit(solution)/shard_map/ppermute | solution.py:24
  108.0 1.2 collective-permute-start.29
  110.2 9.5 %collective-permute-done.25 = bf16[512,256]{1,0:T(8,128)(2,1)} collective-permute-done((bf16[512,256]{1,0:T(8,128)(2,1)S(1)}, bf16[512,256]{1,0:T(8,128)(2,1)}, u32[]{:S(2)}, u32[]{:S(2)}) %collective-permute-start.25) | collective-permute-done | bytes 262176 | tf_op jit(solution)/shard_map/ppermute | solution.py:24
  119.8 1.5 collective-permute-start.31
  121.2 2.0 %pad_maximum_fusion.7 = bf16[3,512,256]{2,1,0:T(8,128)(2,1)} fusion(bf16[1,512,256]{2,1,0:T(8,128)(2,1)} %bitcast.63, bf16[1,512,256]{2,1,0:T(8,128)(2,1)S(1)} %bitcast.280, bf16[1,512,256]{2,1,0:T(8,128)(2,1)S(1)} %bitcast.272), kind=kLoop, calls=%fused_computation.61 | loop fusion | flops 786432 | bytes 1572864 | tf_op jit(solution)/shard_map/stack | solution.py:42
  124.0 2.0 %fusion.74 = f32[512,256]{1,0:T(8,128)} fusion(bf16[512,256]{1,0:T(8,128)(2,1)} %collective-permute-done.25, bf16[8,256,256]{2,1,0:T(8,128)(2,1)S(1)} %broadcast_select_fusion.1), kind=kOutput, calls=%fused_computation.151 | convolution fusion | flops 67108864 | bytes 917504 | tf_op jit(solution)/shard_map/dot_general | solution.py:72
  126.0 2.0 %collective-permute-done.31 = bf16[512,256]{1,0:T(8,128)(2,1)S(1)} collective-permute-done((bf16[512,256]{1,0:T(8,128)(2,1)S(1)}, bf16[512,256]{1,0:T(8,128)(2,1)S(1)}, u32[]{:S(2)}, u32[]{:S(2)}) %collective-permute-start.31) | collective-permute-done | bytes 262176 | tf_op jit(solution)/shard_map/ppermute | solution.py:24
  129.2 1.8 %gather_fusion.3 = bf16[8,256,256]{2,1,0:T(8,128)(2,1)S(1)} fusion(bf16[8,256,256]{2,1,0:T(8,128)(2,1)} %bitcast.266, s32[1024]{0:T(1024)S(1)} %pad_clamp_fusion), kind=kCustom, calls=%fused_computation.3.clone | custom fusion | bytes 2097184 | tf_op jit(solution)/shard_map/jit(_take)/gather | solution.py:66
  131.6 1.2 fusion.41
  132.8 1.2 fusion.62
  135.2 1.2 convolution_add_fusion.2
  136.4 1.4 collective-permute-start.28
  137.8 1.2 fusion.37
  141.3 1.2 fusion.31
  142.6 1.2 convolution_add_fusion.5
  (118 shorter events, 35.5 us)
Async XLA Ops:
  0.0 0.7 copy-start.15
  0.0 1.1 copy-start.14
  1.2 14.9 %collective-permute-start.2 = (bf16[512,256]{1,0:T(8,128)(2,1)S(1)}, bf16[512,256]{1,0:T(8,128)(2,1)S(1)}, u32[]{:S(2)}, u32[]{:S(2)}) collective-permute-start(bf16[512,256]{1,0:T(8,128)(2,1)S(1)} %fusion.28), channel_id=1, source_target_pairs={{0,4},{1,5},{2,6},{3,7},{4,0},{5,1},{6,2},{7,3},{8,12},{9,13},{10,... | collective-permute-start | bytes 786440 | tf_op jit(solution)/shard_map/ppermute | solution.py:24
  4.4 15.1 %collective-permute-start.4 = (bf16[512,256]{1,0:T(8,128)(2,1)S(1)}, bf16[512,256]{1,0:T(8,128)(2,1)S(1)}, u32[]{:S(2)}, u32[]{:S(2)}) collective-permute-start(bf16[512,256]{1,0:T(8,128)(2,1)S(1)} %fusion.28), channel_id=1, source_target_pairs={{0,2},{1,3},{2,0},{3,1},{4,6},{5,7},{6,4},{7,5},{8,10},{9,11},{10,... | collective-permute-start | bytes 786440 | tf_op jit(solution)/shard_map/ppermute | solution.py:24
  5.7 15.8 %collective-permute-start.1 = (bf16[512,256]{1,0:T(8,128)(2,1)S(1)}, bf16[512,256]{1,0:T(8,128)(2,1)S(1)}, u32[]{:S(2)}, u32[]{:S(2)}) collective-permute-start(bf16[512,256]{1,0:T(8,128)(2,1)S(1)} %fusion.28), channel_id=1, source_target_pairs={{0,16},{8,24},{16,0},{24,8},{1,17},{9,25},{17,1},{25,9},{2,18},{10... | collective-permute-start | bytes 786440 | tf_op jit(solution)/shard_map/ppermute | solution.py:24
  6.9 14.6 %collective-permute-start = (bf16[512,256]{1,0:T(8,128)(2,1)S(1)}, bf16[512,256]{1,0:T(8,128)(2,1)S(1)}, u32[]{:S(2)}, u32[]{:S(2)}) collective-permute-start(bf16[512,256]{1,0:T(8,128)(2,1)S(1)} %fusion.28), channel_id=1, source_target_pairs={{0,8},{8,0},{16,24},{24,16},{1,9},{9,1},{17,25},{25,17},{2,10},{10... | collective-permute-start | bytes 786440 | tf_op jit(solution)/shard_map/ppermute | solution.py:24
  16.1 7.4 %collective-permute-start.3 = (bf16[512,256]{1,0:T(8,128)(2,1)S(1)}, bf16[512,256]{1,0:T(8,128)(2,1)S(1)}, u32[]{:S(2)}, u32[]{:S(2)}) collective-permute-start(bf16[512,256]{1,0:T(8,128)(2,1)S(1)} %fusion.28), channel_id=1, source_target_pairs={{0,24},{8,16},{16,8},{24,0},{1,25},{9,17},{17,9},{25,1},{2,26},{10... | collective-permute-start | bytes 786440 | tf_op jit(solution)/shard_map/ppermute | solution.py:24
  18.0 6.4 %collective-permute-start.6 = (bf16[1,512,256]{2,1,0:T(8,128)(2,1)S(1)}, bf16[1,512,256]{2,1,0:T(8,128)(2,1)}, u32[]{:S(2)}, u32[]{:S(2)}) collective-permute-start(bf16[1,512,256]{2,1,0:T(8,128)(2,1)S(1)} %bitcast.276), channel_id=1, source_target_pairs={{0,2},{1,3},{2,0},{3,1},{4,6},{5,7},{6,4},{7,5},{8,10},{9,11},{10,... | collective-permute-start | bytes 786440 | tf_op jit(solution)/shard_map/ppermute | solution.py:24
  20.4 8.1 %collective-permute-start.5 = (bf16[3,512,256]{2,1,0:T(8,128)(2,1)}, bf16[3,512,256]{2,1,0:T(8,128)(2,1)}, u32[]{:S(2)}, u32[]{:S(2)}) collective-permute-start(bf16[3,512,256]{2,1,0:T(8,128)(2,1)} %pad_maximum_fusion.4), channel_id=1, source_target_pairs={{0,1},{1,0},{2,3},{3,2},{4,5},{5,4},{6,7},{7,6},{8,9},{9,8},{10,11... | collective-permute-start | bytes 2359304 | tf_op jit(solution)/shard_map/ppermute | solution.py:24
  24.4 7.9 %collective-permute-start.7 = (bf16[1,512,256]{2,1,0:T(8,128)(2,1)}, bf16[1,512,256]{2,1,0:T(8,128)(2,1)S(1)}, u32[]{:S(2)}, u32[]{:S(2)}) collective-permute-start(bf16[1,512,256]{2,1,0:T(8,128)(2,1)} %collective-permute-done.6), channel_id=1, source_target_pairs={{0,1},{1,0},{2,3},{3,2},{4,5},{5,4},{6,7},{7,6},{8,9},{9,8},{10,11... | collective-permute-start | bytes 786440 | tf_op jit(solution)/shard_map/ppermute | solution.py:24
  32.4 1.0 copy-start.8
  33.4 15.5 %collective-permute-start.9 = (bf16[512,256]{1,0:T(8,128)(2,1)S(1)}, bf16[512,256]{1,0:T(8,128)(2,1)}, u32[]{:S(2)}, u32[]{:S(2)}) collective-permute-start(bf16[512,256]{1,0:T(8,128)(2,1)S(1)} %get-tuple-element.17), channel_id=1, source_target_pairs={{0,4},{1,5},{2,6},{3,7},{4,0},{5,1},{6,2},{7,3},{8,12},{9,13},{10,... | collective-permute-start | bytes 786440 | tf_op jit(solution)/shard_map/ppermute | solution.py:24
  36.4 13.3 %collective-permute-start.8 = (bf16[512,256]{1,0:T(8,128)(2,1)S(1)}, bf16[512,256]{1,0:T(8,128)(2,1)S(1)}, u32[]{:S(2)}, u32[]{:S(2)}) collective-permute-start(bf16[512,256]{1,0:T(8,128)(2,1)S(1)} %get-tuple-element.17), channel_id=1, source_target_pairs={{0,2},{1,3},{2,0},{3,1},{4,6},{5,7},{6,4},{7,5},{8,10},{9,11},{10,... | collective-permute-start | bytes 786440 | tf_op jit(solution)/shard_map/ppermute | solution.py:24
  37.9 17.0 %collective-permute-start.14 = (bf16[512,256]{1,0:T(8,128)(2,1)S(1)}, bf16[512,256]{1,0:T(8,128)(2,1)S(1)}, u32[]{:S(2)}, u32[]{:S(2)}) collective-permute-start(bf16[512,256]{1,0:T(8,128)(2,1)S(1)} %get-tuple-element.17), channel_id=1, source_target_pairs={{0,16},{8,24},{16,0},{24,8},{1,17},{9,25},{17,1},{25,9},{2,18},{10... | collective-permute-start | bytes 786440 | tf_op jit(solution)/shard_map/ppermute | solution.py:24
  38.6 16.2 %collective-permute-start.13 = (bf16[512,256]{1,0:T(8,128)(2,1)S(1)}, bf16[512,256]{1,0:T(8,128)(2,1)S(1)}, u32[]{:S(2)}, u32[]{:S(2)}) collective-permute-start(bf16[512,256]{1,0:T(8,128)(2,1)S(1)} %get-tuple-element.17), channel_id=1, source_target_pairs={{0,8},{8,0},{16,24},{24,16},{1,9},{9,1},{17,25},{25,17},{2,10},{10... | collective-permute-start | bytes 786440 | tf_op jit(solution)/shard_map/ppermute | solution.py:24
  48.9 8.1 %collective-permute-start.15 = (bf16[512,256]{1,0:T(8,128)(2,1)S(1)}, bf16[512,256]{1,0:T(8,128)(2,1)S(1)}, u32[]{:S(2)}, u32[]{:S(2)}) collective-permute-start(bf16[512,256]{1,0:T(8,128)(2,1)S(1)} %get-tuple-element.17), channel_id=1, source_target_pairs={{0,24},{8,16},{16,8},{24,0},{1,25},{9,17},{17,9},{25,1},{2,26},{10... | collective-permute-start | bytes 786440 | tf_op jit(solution)/shard_map/ppermute | solution.py:24
  49.7 15.6 %collective-permute-start.11 = (bf16[1,512,256]{2,1,0:T(8,128)(2,1)}, bf16[1,512,256]{2,1,0:T(8,128)(2,1)}, u32[]{:S(2)}, u32[]{:S(2)}) collective-permute-start(bf16[1,512,256]{2,1,0:T(8,128)(2,1)} %bitcast.23), channel_id=1, source_target_pairs={{0,2},{1,3},{2,0},{3,1},{4,6},{5,7},{6,4},{7,5},{8,10},{9,11},{10,... | collective-permute-start | bytes 786440 | tf_op jit(solution)/shard_map/ppermute | solution.py:24
  49.7 2.0 %copy-start.12 = (bf16[512,256]{1,0:T(8,128)(2,1)}, bf16[512,256]{1,0:T(8,128)(2,1)S(1)}, u32[]{:S(2)}) copy-start(bf16[512,256]{1,0:T(8,128)(2,1)S(1)} %collective-permute-done.8) | copy-start | bytes 786436
  51.7 17.5 %collective-permute-start.10 = (bf16[3,512,256]{2,1,0:T(8,128)(2,1)}, bf16[3,512,256]{2,1,0:T(8,128)(2,1)}, u32[]{:S(2)}, u32[]{:S(2)}) collective-permute-start(bf16[3,512,256]{2,1,0:T(8,128)(2,1)} %pad_maximum_fusion.5), channel_id=1, source_target_pairs={{0,1},{1,0},{2,3},{3,2},{4,5},{5,4},{6,7},{7,6},{8,9},{9,8},{10,11... | collective-permute-start | bytes 2359304 | tf_op jit(solution)/shard_map/ppermute | solution.py:24
  65.3 7.9 %collective-permute-start.12 = (bf16[1,512,256]{2,1,0:T(8,128)(2,1)}, bf16[1,512,256]{2,1,0:T(8,128)(2,1)S(1)}, u32[]{:S(2)}, u32[]{:S(2)}) collective-permute-start(bf16[1,512,256]{2,1,0:T(8,128)(2,1)} %collective-permute-done.11), channel_id=1, source_target_pairs={{0,1},{1,0},{2,3},{3,2},{4,5},{5,4},{6,7},{7,6},{8,9},{9,8},{10,11... | collective-permute-start | bytes 786440 | tf_op jit(solution)/shard_map/ppermute | solution.py:24
  68.0 1.0 copy-start.9
  70.4 1.2 copy-start.5
  71.7 1.3 copy-start.1
  71.7 1.3 copy-start.13
  72.9 1.0 copy-start.3
  74.2 14.6 %collective-permute-start.18 = (bf16[512,256]{1,0:T(8,128)(2,1)S(1)}, bf16[512,256]{1,0:T(8,128)(2,1)S(1)}, u32[]{:S(2)}, u32[]{:S(2)}) collective-permute-start(bf16[512,256]{1,0:T(8,128)(2,1)S(1)} %fusion.29), channel_id=1, source_target_pairs={{0,4},{1,5},{2,6},{3,7},{4,0},{5,1},{6,2},{7,3},{8,12},{9,13},{10,... | collective-permute-start | bytes 786440 | tf_op jit(solution)/shard_map/ppermute | solution.py:24
  74.3 15.3 %collective-permute-start.20 = (bf16[512,256]{1,0:T(8,128)(2,1)S(1)}, bf16[512,256]{1,0:T(8,128)(2,1)S(1)}, u32[]{:S(2)}, u32[]{:S(2)}) collective-permute-start(bf16[512,256]{1,0:T(8,128)(2,1)S(1)} %fusion.29), channel_id=1, source_target_pairs={{0,2},{1,3},{2,0},{3,1},{4,6},{5,7},{6,4},{7,5},{8,10},{9,11},{10,... | collective-permute-start | bytes 786440 | tf_op jit(solution)/shard_map/ppermute | solution.py:24
  78.0 13.8 %collective-permute-start.17 = (bf16[512,256]{1,0:T(8,128)(2,1)S(1)}, bf16[512,256]{1,0:T(8,128)(2,1)S(1)}, u32[]{:S(2)}, u32[]{:S(2)}) collective-permute-start(bf16[512,256]{1,0:T(8,128)(2,1)S(1)} %fusion.29), channel_id=1, source_target_pairs={{0,16},{8,24},{16,0},{24,8},{1,17},{9,25},{17,1},{25,9},{2,18},{10... | collective-permute-start | bytes 786440 | tf_op jit(solution)/shard_map/ppermute | solution.py:24
  78.2 13.6 %collective-permute-start.16 = (bf16[512,256]{1,0:T(8,128)(2,1)S(1)}, bf16[512,256]{1,0:T(8,128)(2,1)S(1)}, u32[]{:S(2)}, u32[]{:S(2)}) collective-permute-start(bf16[512,256]{1,0:T(8,128)(2,1)S(1)} %fusion.29), channel_id=1, source_target_pairs={{0,8},{8,0},{16,24},{24,16},{1,9},{9,1},{17,25},{25,17},{2,10},{10... | collective-permute-start | bytes 786440 | tf_op jit(solution)/shard_map/ppermute | solution.py:24
  88.8 7.9 %collective-permute-start.19 = (bf16[512,256]{1,0:T(8,128)(2,1)S(1)}, bf16[512,256]{1,0:T(8,128)(2,1)S(1)}, u32[]{:S(2)}, u32[]{:S(2)}) collective-permute-start(bf16[512,256]{1,0:T(8,128)(2,1)S(1)} %fusion.29), channel_id=1, source_target_pairs={{0,24},{8,16},{16,8},{24,0},{1,25},{9,17},{17,9},{25,1},{2,26},{10... | collective-permute-start | bytes 786440 | tf_op jit(solution)/shard_map/ppermute | solution.py:24
  89.6 8.0 %collective-permute-start.22 = (bf16[1,512,256]{2,1,0:T(8,128)(2,1)S(1)}, bf16[1,512,256]{2,1,0:T(8,128)(2,1)}, u32[]{:S(2)}, u32[]{:S(2)}) collective-permute-start(bf16[1,512,256]{2,1,0:T(8,128)(2,1)S(1)} %bitcast.278), channel_id=1, source_target_pairs={{0,2},{1,3},{2,0},{3,1},{4,6},{5,7},{6,4},{7,5},{8,10},{9,11},{10,... | collective-permute-start | bytes 786440 | tf_op jit(solution)/shard_map/ppermute | solution.py:24
  90.6 10.4 %collective-permute-start.21 = (bf16[3,512,256]{2,1,0:T(8,128)(2,1)}, bf16[3,512,256]{2,1,0:T(8,128)(2,1)}, u32[]{:S(2)}, u32[]{:S(2)}) collective-permute-start(bf16[3,512,256]{2,1,0:T(8,128)(2,1)} %pad_maximum_fusion.6), channel_id=1, source_target_pairs={{0,1},{1,0},{2,3},{3,2},{4,5},{5,4},{6,7},{7,6},{8,9},{9,8},{10,11... | collective-permute-start | bytes 2359304 | tf_op jit(solution)/shard_map/ppermute | solution.py:24
  97.6 7.3 %collective-permute-start.23 = (bf16[1,512,256]{2,1,0:T(8,128)(2,1)}, bf16[1,512,256]{2,1,0:T(8,128)(2,1)S(1)}, u32[]{:S(2)}, u32[]{:S(2)}) collective-permute-start(bf16[1,512,256]{2,1,0:T(8,128)(2,1)} %collective-permute-done.22), channel_id=1, source_target_pairs={{0,1},{1,0},{2,3},{3,2},{4,5},{5,4},{6,7},{7,6},{8,9},{9,8},{10,11... | collective-permute-start | bytes 786440 | tf_op jit(solution)/shard_map/ppermute | solution.py:24
  104.9 1.0 copy-start.6
  105.9 13.8 %collective-permute-start.25 = (bf16[512,256]{1,0:T(8,128)(2,1)S(1)}, bf16[512,256]{1,0:T(8,128)(2,1)}, u32[]{:S(2)}, u32[]{:S(2)}) collective-permute-start(bf16[512,256]{1,0:T(8,128)(2,1)S(1)} %get-tuple-element.21), channel_id=1, source_target_pairs={{0,4},{1,5},{2,6},{3,7},{4,0},{5,1},{6,2},{7,3},{8,12},{9,13},{10,... | collective-permute-start | bytes 786440 | tf_op jit(solution)/shard_map/ppermute | solution.py:24
  105.9 15.3 %collective-permute-start.24 = (bf16[512,256]{1,0:T(8,128)(2,1)S(1)}, bf16[512,256]{1,0:T(8,128)(2,1)S(1)}, u32[]{:S(2)}, u32[]{:S(2)}) collective-permute-start(bf16[512,256]{1,0:T(8,128)(2,1)S(1)} %get-tuple-element.21), channel_id=1, source_target_pairs={{0,2},{1,3},{2,0},{3,1},{4,6},{5,7},{6,4},{7,5},{8,10},{9,11},{10,... | collective-permute-start | bytes 786440 | tf_op jit(solution)/shard_map/ppermute | solution.py:24
  107.5 18.6 %collective-permute-start.30 = (bf16[512,256]{1,0:T(8,128)(2,1)S(1)}, bf16[512,256]{1,0:T(8,128)(2,1)S(1)}, u32[]{:S(2)}, u32[]{:S(2)}) collective-permute-start(bf16[512,256]{1,0:T(8,128)(2,1)S(1)} %get-tuple-element.21), channel_id=1, source_target_pairs={{0,16},{8,24},{16,0},{24,8},{1,17},{9,25},{17,1},{25,9},{2,18},{10... | collective-permute-start | bytes 786440 | tf_op jit(solution)/shard_map/ppermute | solution.py:24
  108.0 18.1 %collective-permute-start.29 = (bf16[512,256]{1,0:T(8,128)(2,1)S(1)}, bf16[512,256]{1,0:T(8,128)(2,1)S(1)}, u32[]{:S(2)}, u32[]{:S(2)}) collective-permute-start(bf16[512,256]{1,0:T(8,128)(2,1)S(1)} %get-tuple-element.21), channel_id=1, source_target_pairs={{0,8},{8,0},{16,24},{24,16},{1,9},{9,1},{17,25},{25,17},{2,10},{10... | collective-permute-start | bytes 786440 | tf_op jit(solution)/shard_map/ppermute | solution.py:24
  119.8 8.3 %collective-permute-start.31 = (bf16[512,256]{1,0:T(8,128)(2,1)S(1)}, bf16[512,256]{1,0:T(8,128)(2,1)S(1)}, u32[]{:S(2)}, u32[]{:S(2)}) collective-permute-start(bf16[512,256]{1,0:T(8,128)(2,1)S(1)} %get-tuple-element.21), channel_id=1, source_target_pairs={{0,24},{8,16},{16,8},{24,0},{1,25},{9,17},{17,9},{25,1},{2,26},{10... | collective-permute-start | bytes 786440 | tf_op jit(solution)/shard_map/ppermute | solution.py:24
  121.2 15.1 %collective-permute-start.27 = (bf16[1,512,256]{2,1,0:T(8,128)(2,1)}, bf16[1,512,256]{2,1,0:T(8,128)(2,1)}, u32[]{:S(2)}, u32[]{:S(2)}) collective-permute-start(bf16[1,512,256]{2,1,0:T(8,128)(2,1)} %bitcast.63), channel_id=1, source_target_pairs={{0,2},{1,3},{2,0},{3,1},{4,6},{5,7},{6,4},{7,5},{8,10},{9,11},{10,... | collective-permute-start | bytes 786440 | tf_op jit(solution)/shard_map/ppermute | solution.py:24
  121.2 2.0 %copy-start.10 = (bf16[512,256]{1,0:T(8,128)(2,1)}, bf16[512,256]{1,0:T(8,128)(2,1)S(1)}, u32[]{:S(2)}) copy-start(bf16[512,256]{1,0:T(8,128)(2,1)S(1)} %collective-permute-done.24) | copy-start | bytes 786436
  123.3 16.9 %collective-permute-start.26 = (bf16[3,512,256]{2,1,0:T(8,128)(2,1)}, bf16[3,512,256]{2,1,0:T(8,128)(2,1)}, u32[]{:S(2)}, u32[]{:S(2)}) collective-permute-start(bf16[3,512,256]{2,1,0:T(8,128)(2,1)} %pad_maximum_fusion.7), channel_id=1, source_target_pairs={{0,1},{1,0},{2,3},{3,2},{4,5},{5,4},{6,7},{7,6},{8,9},{9,8},{10,11... | collective-permute-start | bytes 2359304 | tf_op jit(solution)/shard_map/ppermute | solution.py:24
  136.4 7.8 %collective-permute-start.28 = (bf16[1,512,256]{2,1,0:T(8,128)(2,1)}, bf16[1,512,256]{2,1,0:T(8,128)(2,1)S(1)}, u32[]{:S(2)}, u32[]{:S(2)}) collective-permute-start(bf16[1,512,256]{2,1,0:T(8,128)(2,1)} %collective-permute-done.27), channel_id=1, source_target_pairs={{0,1},{1,0},{2,3},{3,2},{4,5},{5,4},{6,7},{7,6},{8,9},{9,8},{10,11... | collective-permute-start | bytes 786440 | tf_op jit(solution)/shard_map/ppermute | solution.py:24
  138.9 1.0 copy-start.7
  141.3 1.2 copy-start.4
  142.6 1.3 copy-start
  142.6 1.3 copy-start.11
  143.8 1.0 copy-start.2

commit v14 on v13

--- a/solution.py
+++ b/solution.py
@@ -31,10 +31,7 @@
         same[s] = xor_permute(xb, "col", n_col, 2 * s)
     col_pieces = [xb] + [xor_permute(xb, "row", n_row, t) for t in range(1, n_row) if t & (t - 1) == 0]
     forward = list(range(2, chips, 2))
-    if forward:
-        later, same[forward[0]] = lax.optimization_barrier((xb, same[forward[0]]))
-    else:
-        later = xb
+    later, same[1] = lax.optimization_barrier((xb, same[1]))
     for t in range(3, n_row):
         if t & (t - 1):
             col_pieces.insert(t, xor_permute(later, "row", n_row, t))

time: 147 us -> 141 us (0.959)
  waiting for transfers between devices: 46.8 us -> 39.9 us
    ppermute x32, waiting for transfers between devices: 46.8 us -> 39.9 us  [xor_permute(): return lax.ppermute(x, axis, perm=[(i, i ^ s) for i in range(size)])]
  transfers between devices with their start and end apart: 32 -> 32, of which waited for: 8 -> 8; matrix products, arithmetic and copies ran while one was open for 36% -> 37% of each run, Pallas kernels for 0% -> 0%
where the time goes in v14:
time: 141 us; the launch traced here: 140 us
  matrix products  41.5 us (29%)
  starting transfers between devices  40.1 us (28%)
  waiting for transfers between devices  39.9 us (28%)
  other arithmetic  9.24 us (7%)
  local copies, waits for them, and re-layouts  8.77 us (6%)
    dot_general x48, matrix products, contract(): part = jnp.dot(piece, k_blocks[s], preferred_element_type=jnp.float32)  41.5 us
    ppermute x32, starting transfers between devices, xor_permute(): return lax.ppermute(x, axis, perm=[(i, i ^ s) for i in range(size)])  40.1 us
    ppermute x32, waiting for transfers between devices, xor_permute(): return lax.ppermute(x, axis, perm=[(i, i ^ s) for i in range(size)])  39.9 us
    another operation x4, other arithmetic, exchange(): jnp.stack([same[s] for s in first])  5.89 us
    gather x4, local copies, waits for them, and re-layouts, ordered_k_blocks(): return jnp.take(split, index, axis=0)  4.9 us
    unnamed x33, local copies, waits for them, and re-layouts  3.66 us
  transfers between devices with their start and end apart: 32, of which 8 were waited for; matrix products, arithmetic and copies ran while one was open for 37% of the time, Pallas kernels for 0%

profile of v14, /device:TPU:1, one launch (start us, length us, event | category | flops | bytes accessed | tf_op | source)
XLA Modules:
  0.0 140.2 jit_solution(2415924995930365167)
XLA Ops:
  1.2 2.2 %collective-permute-start.2 = (bf16[512,256]{1,0:T(8,128)(2,1)S(1)}, bf16[512,256]{1,0:T(8,128)(2,1)S(1)}, u32[]{:S(2)}, u32[]{:S(2)}) collective-permute-start(bf16[512,256]{1,0:T(8,128)(2,1)S(1)} %fusion.28), channel_id=1, source_target_pairs={{0,2},{1,3},{2,0},{3,1},{4,6},{5,7},{6,4},{7,5},{8,10},{9,11},{10,... | collective-permute-start | bytes 786440 | tf_op jit(solution)/shard_map/ppermute | solution.py:24
  3.3 2.3 %collective-permute-start.4 = (bf16[512,256]{1,0:T(8,128)(2,1)S(1)}, bf16[512,256]{1,0:T(8,128)(2,1)S(1)}, u32[]{:S(2)}, u32[]{:S(2)}) collective-permute-start(bf16[512,256]{1,0:T(8,128)(2,1)S(1)} %fusion.28), channel_id=1, source_target_pairs={{0,4},{1,5},{2,6},{3,7},{4,0},{5,1},{6,2},{7,3},{8,12},{9,13},{10,... | collective-permute-start | bytes 786440 | tf_op jit(solution)/shard_map/ppermute | solution.py:24
  5.7 1.2 collective-permute-start.1
  6.9 1.2 collective-permute-start
  8.1 6.8 %collective-permute-done.2 = bf16[512,256]{1,0:T(8,128)(2,1)S(1)} collective-permute-done((bf16[512,256]{1,0:T(8,128)(2,1)S(1)}, bf16[512,256]{1,0:T(8,128)(2,1)S(1)}, u32[]{:S(2)}, u32[]{:S(2)}) %collective-permute-start.2) | collective-permute-done | bytes 262176 | tf_op jit(solution)/shard_map/ppermute | solution.py:24
  14.9 2.0 %collective-permute-start.3 = (bf16[512,256]{1,0:T(8,128)(2,1)S(1)}, bf16[512,256]{1,0:T(8,128)(2,1)S(1)}, u32[]{:S(2)}, u32[]{:S(2)}) collective-permute-start(bf16[512,256]{1,0:T(8,128)(2,1)S(1)} %fusion.28), channel_id=1, source_target_pairs={{0,24},{8,16},{16,8},{24,0},{1,25},{9,17},{17,9},{25,1},{2,26},{10... | collective-permute-start | bytes 786440 | tf_op jit(solution)/shard_map/ppermute | solution.py:24
  18.2 1.9 %collective-permute-start.5 = (bf16[3,512,256]{2,1,0:T(8,128)(2,1)}, bf16[3,512,256]{2,1,0:T(8,128)(2,1)}, u32[]{:S(2)}, u32[]{:S(2)}) collective-permute-start(bf16[3,512,256]{2,1,0:T(8,128)(2,1)} %pad_maximum_fusion.4), channel_id=1, source_target_pairs={{0,1},{1,0},{2,3},{3,2},{4,5},{5,4},{6,7},{7,6},{8,9},{9,8},{10,11... | collective-permute-start | bytes 2359304 | tf_op jit(solution)/shard_map/ppermute | solution.py:24
  20.1 2.3 %collective-permute-done.3 = bf16[512,256]{1,0:T(8,128)(2,1)S(1)} collective-permute-done((bf16[512,256]{1,0:T(8,128)(2,1)S(1)}, bf16[512,256]{1,0:T(8,128)(2,1)S(1)}, u32[]{:S(2)}, u32[]{:S(2)}) %collective-permute-start.3) | collective-permute-done | bytes 262176 | tf_op jit(solution)/shard_map/ppermute | solution.py:24
  23.3 2.5 %collective-permute-start.7 = (bf16[1,512,256]{2,1,0:T(8,128)(2,1)}, bf16[1,512,256]{2,1,0:T(8,128)(2,1)S(1)}, u32[]{:S(2)}, u32[]{:S(2)}) collective-permute-start(bf16[1,512,256]{2,1,0:T(8,128)(2,1)} %collective-permute-done.6), channel_id=1, source_target_pairs={{0,1},{1,0},{2,3},{3,2},{4,5},{5,4},{6,7},{7,6},{8,9},{9,8},{10,11... | collective-permute-start | bytes 786440 | tf_op jit(solution)/shard_map/ppermute | solution.py:24
  26.0 1.2 fusion.54
  27.5 1.2 fusion.59
  29.8 1.2 convolution_add_fusion.17
  32.5 2.3 %collective-permute-start.9 = (bf16[512,256]{1,0:T(8,128)(2,1)S(1)}, bf16[512,256]{1,0:T(8,128)(2,1)}, u32[]{:S(2)}, u32[]{:S(2)}) collective-permute-start(bf16[512,256]{1,0:T(8,128)(2,1)S(1)} %get-tuple-element.17), channel_id=1, source_target_pairs={{0,4},{1,5},{2,6},{3,7},{4,0},{5,1},{6,2},{7,3},{8,12},{9,13},{10,... | collective-permute-start | bytes 786440 | tf_op jit(solution)/shard_map/ppermute | solution.py:24
  35.6 1.2 collective-permute-start.13
  37.8 7.9 %collective-permute-done.8 = bf16[512,256]{1,0:T(8,128)(2,1)S(1)} collective-permute-done((bf16[512,256]{1,0:T(8,128)(2,1)S(1)}, bf16[512,256]{1,0:T(8,128)(2,1)S(1)}, u32[]{:S(2)}, u32[]{:S(2)}) %collective-permute-start.8) | collective-permute-done | bytes 262176 | tf_op jit(solution)/shard_map/ppermute | solution.py:24
  45.7 1.2 collective-permute-start.15
  47.1 2.0 %pad_maximum_fusion.5 = bf16[3,512,256]{2,1,0:T(8,128)(2,1)} fusion(bf16[1,512,256]{2,1,0:T(8,128)(2,1)} %bitcast.23, bf16[1,512,256]{2,1,0:T(8,128)(2,1)S(1)} %bitcast.281, bf16[1,512,256]{2,1,0:T(8,128)(2,1)S(1)} %bitcast.270), kind=kLoop, calls=%fused_computation.59 | loop fusion | flops 786432 | bytes 1572864 | tf_op jit(solution)/shard_map/stack | solution.py:39
  50.1 2.0 %fusion.70 = f32[512,256]{1,0:T(8,128)} fusion(bf16[512,256]{1,0:T(8,128)(2,1)} %collective-permute-done.9, bf16[8,256,256]{2,1,0:T(8,128)(2,1)S(1)} %broadcast_select_fusion.3), kind=kOutput, calls=%fused_computation.147 | convolution fusion | flops 67108864 | bytes 917504 | tf_op jit(solution)/shard_map/dot_general | solution.py:69
  52.2 1.6 %collective-permute-done.15 = bf16[512,256]{1,0:T(8,128)(2,1)S(1)} collective-permute-done((bf16[512,256]{1,0:T(8,128)(2,1)S(1)}, bf16[512,256]{1,0:T(8,128)(2,1)S(1)}, u32[]{:S(2)}, u32[]{:S(2)}) %collective-permute-start.15) | collective-permute-done | bytes 262176 | tf_op jit(solution)/shard_map/ppermute | solution.py:24
  54.9 1.8 %gather_fusion.1 = bf16[8,256,256]{2,1,0:T(8,128)(2,1)S(1)} fusion(bf16[8,256,256]{2,1,0:T(8,128)(2,1)} %bitcast.267, s32[1024]{0:T(1024)S(1)} %pad_clamp_fusion), kind=kCustom, calls=%fused_computation.1.clone | custom fusion | bytes 2097184 | tf_op jit(solution)/shard_map/jit(_take)/gather | solution.py:63
  57.1 1.2 fusion.52
  59.7 1.2 fusion.56
  60.9 1.2 convolution_add_fusion.11
  62.1 1.6 %collective-permute-start.12 = (bf16[1,512,256]{2,1,0:T(8,128)(2,1)}, bf16[1,512,256]{2,1,0:T(8,128)(2,1)S(1)}, u32[]{:S(2)}, u32[]{:S(2)}) collective-permute-start(bf16[1,512,256]{2,1,0:T(8,128)(2,1)} %collective-permute-done.11), channel_id=1, source_target_pairs={{0,1},{1,0},{2,3},{3,2},{4,5},{5,4},{6,7},{7,6},{8,9},{9,8},{10,11... | collective-permute-start | bytes 786440 | tf_op jit(solution)/shard_map/ppermute | solution.py:24
  67.2 1.2 fusion.33
  68.5 1.2 convolution_add_fusion.14
  71.2 1.7 %collective-permute-start.20 = (bf16[512,256]{1,0:T(8,128)(2,1)S(1)}, bf16[512,256]{1,0:T(8,128)(2,1)S(1)}, u32[]{:S(2)}, u32[]{:S(2)}) collective-permute-start(bf16[512,256]{1,0:T(8,128)(2,1)S(1)} %fusion.29), channel_id=1, source_target_pairs={{0,4},{1,5},{2,6},{3,7},{4,0},{5,1},{6,2},{7,3},{8,12},{9,13},{10,... | collective-permute-start | bytes 786440 | tf_op jit(solution)/shard_map/ppermute | solution.py:24
  72.9 1.2 collective-permute-start.17
  74.1 1.2 collective-permute-start.16
  75.3 8.4 %collective-permute-done.18 = bf16[512,256]{1,0:T(8,128)(2,1)S(1)} collective-permute-done((bf16[512,256]{1,0:T(8,128)(2,1)S(1)}, bf16[512,256]{1,0:T(8,128)(2,1)S(1)}, u32[]{:S(2)}, u32[]{:S(2)}) %collective-permute-start.18) | collective-permute-done | bytes 262176 | tf_op jit(solution)/shard_map/ppermute | solution.py:24
  83.8 1.9 %collective-permute-start.19 = (bf16[512,256]{1,0:T(8,128)(2,1)S(1)}, bf16[512,256]{1,0:T(8,128)(2,1)S(1)}, u32[]{:S(2)}, u32[]{:S(2)}) collective-permute-start(bf16[512,256]{1,0:T(8,128)(2,1)S(1)} %fusion.29), channel_id=1, source_target_pairs={{0,24},{8,16},{16,8},{24,0},{1,25},{9,17},{17,9},{25,1},{2,26},{10... | collective-permute-start | bytes 786440 | tf_op jit(solution)/shard_map/ppermute | solution.py:24
  87.7 3.9 %collective-permute-done.19 = bf16[512,256]{1,0:T(8,128)(2,1)S(1)} collective-permute-done((bf16[512,256]{1,0:T(8,128)(2,1)S(1)}, bf16[512,256]{1,0:T(8,128)(2,1)S(1)}, u32[]{:S(2)}, u32[]{:S(2)}) %collective-permute-start.19) | collective-permute-done | bytes 262176 | tf_op jit(solution)/shard_map/ppermute | solution.py:24
  92.6 1.9 %collective-permute-start.23 = (bf16[1,512,256]{2,1,0:T(8,128)(2,1)}, bf16[1,512,256]{2,1,0:T(8,128)(2,1)S(1)}, u32[]{:S(2)}, u32[]{:S(2)}) collective-permute-start(bf16[1,512,256]{2,1,0:T(8,128)(2,1)} %collective-permute-done.22), channel_id=1, source_target_pairs={{0,1},{1,0},{2,3},{3,2},{4,5},{5,4},{6,7},{7,6},{8,9},{9,8},{10,11... | collective-permute-start | bytes 786440 | tf_op jit(solution)/shard_map/ppermute | solution.py:24
  94.7 1.2 fusion.43
  98.5 1.2 convolution_add_fusion.8
  101.0 1.9 %collective-permute-start.25 = (bf16[512,256]{1,0:T(8,128)(2,1)S(1)}, bf16[512,256]{1,0:T(8,128)(2,1)}, u32[]{:S(2)}, u32[]{:S(2)}) collective-permute-start(bf16[512,256]{1,0:T(8,128)(2,1)S(1)} %get-tuple-element.21), channel_id=1, source_target_pairs={{0,4},{1,5},{2,6},{3,7},{4,0},{5,1},{6,2},{7,3},{8,12},{9,13},{10,... | collective-permute-start | bytes 786440 | tf_op jit(solution)/shard_map/ppermute | solution.py:24
  104.0 1.2 collective-permute-start.29
  106.2 7.8 %collective-permute-done.24 = bf16[512,256]{1,0:T(8,128)(2,1)S(1)} collective-permute-done((bf16[512,256]{1,0:T(8,128)(2,1)S(1)}, bf16[512,256]{1,0:T(8,128)(2,1)S(1)}, u32[]{:S(2)}, u32[]{:S(2)}) %collective-permute-start.24) | collective-permute-done | bytes 262176 | tf_op jit(solution)/shard_map/ppermute | solution.py:24
  114.0 2.0 %collective-permute-start.31 = (bf16[512,256]{1,0:T(8,128)(2,1)S(1)}, bf16[512,256]{1,0:T(8,128)(2,1)S(1)}, u32[]{:S(2)}, u32[]{:S(2)}) collective-permute-start(bf16[512,256]{1,0:T(8,128)(2,1)S(1)} %get-tuple-element.21), channel_id=1, source_target_pairs={{0,24},{8,16},{16,8},{24,0},{1,25},{9,17},{17,9},{25,1},{2,26},{10... | collective-permute-start | bytes 786440 | tf_op jit(solution)/shard_map/ppermute | solution.py:24
  116.0 2.0 %pad_maximum_fusion.7 = bf16[3,512,256]{2,1,0:T(8,128)(2,1)} fusion(bf16[1,512,256]{2,1,0:T(8,128)(2,1)} %bitcast.63, bf16[1,512,256]{2,1,0:T(8,128)(2,1)S(1)} %bitcast.280, bf16[1,512,256]{2,1,0:T(8,128)(2,1)S(1)} %bitcast.272), kind=kLoop, calls=%fused_computation.61 | loop fusion | flops 786432 | bytes 1572864 | tf_op jit(solution)/shard_map/stack | solution.py:39
  118.9 2.0 %fusion.74 = f32[512,256]{1,0:T(8,128)} fusion(bf16[512,256]{1,0:T(8,128)(2,1)} %collective-permute-done.25, bf16[8,256,256]{2,1,0:T(8,128)(2,1)S(1)} %broadcast_select_fusion.1), kind=kOutput, calls=%fused_computation.151 | convolution fusion | flops 67108864 | bytes 917504 | tf_op jit(solution)/shard_map/dot_general | solution.py:69
  123.2 1.8 %gather_fusion.3 = bf16[8,256,256]{2,1,0:T(8,128)(2,1)S(1)} fusion(bf16[8,256,256]{2,1,0:T(8,128)(2,1)} %bitcast.266, s32[1024]{0:T(1024)S(1)} %pad_clamp_fusion), kind=kCustom, calls=%fused_computation.3.clone | custom fusion | bytes 2097184 | tf_op jit(solution)/shard_map/jit(_take)/gather | solution.py:63
  125.5 1.2 fusion.41
  128.0 1.2 fusion.60
  129.2 1.2 convolution_add_fusion.2
  130.4 1.6 %collective-permute-start.28 = (bf16[1,512,256]{2,1,0:T(8,128)(2,1)}, bf16[1,512,256]{2,1,0:T(8,128)(2,1)S(1)}, u32[]{:S(2)}, u32[]{:S(2)}) collective-permute-start(bf16[1,512,256]{2,1,0:T(8,128)(2,1)} %collective-permute-done.27), channel_id=1, source_target_pairs={{0,1},{1,0},{2,3},{3,2},{4,5},{5,4},{6,7},{7,6},{8,9},{9,8},{10,11... | collective-permute-start | bytes 786440 | tf_op jit(solution)/shard_map/ppermute | solution.py:24
  135.6 1.2 fusion.31
  136.8 1.2 convolution_add_fusion.5
  (118 shorter events, 37.0 us)
Async XLA Ops:
  0.0 0.7 copy-start.15
  0.0 1.1 copy-start.14
  1.2 13.7 %collective-permute-start.2 = (bf16[512,256]{1,0:T(8,128)(2,1)S(1)}, bf16[512,256]{1,0:T(8,128)(2,1)S(1)}, u32[]{:S(2)}, u32[]{:S(2)}) collective-permute-start(bf16[512,256]{1,0:T(8,128)(2,1)S(1)} %fusion.28), channel_id=1, source_target_pairs={{0,2},{1,3},{2,0},{3,1},{4,6},{5,7},{6,4},{7,5},{8,10},{9,11},{10,... | collective-permute-start | bytes 786440 | tf_op jit(solution)/shard_map/ppermute | solution.py:24
  3.3 13.6 %collective-permute-start.4 = (bf16[512,256]{1,0:T(8,128)(2,1)S(1)}, bf16[512,256]{1,0:T(8,128)(2,1)S(1)}, u32[]{:S(2)}, u32[]{:S(2)}) collective-permute-start(bf16[512,256]{1,0:T(8,128)(2,1)S(1)} %fusion.28), channel_id=1, source_target_pairs={{0,4},{1,5},{2,6},{3,7},{4,0},{5,1},{6,2},{7,3},{8,12},{9,13},{10,... | collective-permute-start | bytes 786440 | tf_op jit(solution)/shard_map/ppermute | solution.py:24
  5.7 14.4 %collective-permute-start.1 = (bf16[512,256]{1,0:T(8,128)(2,1)S(1)}, bf16[512,256]{1,0:T(8,128)(2,1)S(1)}, u32[]{:S(2)}, u32[]{:S(2)}) collective-permute-start(bf16[512,256]{1,0:T(8,128)(2,1)S(1)} %fusion.28), channel_id=1, source_target_pairs={{0,16},{8,24},{16,0},{24,8},{1,17},{9,25},{17,1},{25,9},{2,18},{10... | collective-permute-start | bytes 786440 | tf_op jit(solution)/shard_map/ppermute | solution.py:24
  6.9 13.2 %collective-permute-start = (bf16[512,256]{1,0:T(8,128)(2,1)S(1)}, bf16[512,256]{1,0:T(8,128)(2,1)S(1)}, u32[]{:S(2)}, u32[]{:S(2)}) collective-permute-start(bf16[512,256]{1,0:T(8,128)(2,1)S(1)} %fusion.28), channel_id=1, source_target_pairs={{0,8},{8,0},{16,24},{24,16},{1,9},{9,1},{17,25},{25,17},{2,10},{10... | collective-permute-start | bytes 786440 | tf_op jit(solution)/shard_map/ppermute | solution.py:24
  14.9 7.5 %collective-permute-start.3 = (bf16[512,256]{1,0:T(8,128)(2,1)S(1)}, bf16[512,256]{1,0:T(8,128)(2,1)S(1)}, u32[]{:S(2)}, u32[]{:S(2)}) collective-permute-start(bf16[512,256]{1,0:T(8,128)(2,1)S(1)} %fusion.28), channel_id=1, source_target_pairs={{0,24},{8,16},{16,8},{24,0},{1,25},{9,17},{17,9},{25,1},{2,26},{10... | collective-permute-start | bytes 786440 | tf_op jit(solution)/shard_map/ppermute | solution.py:24
  16.9 6.3 %collective-permute-start.6 = (bf16[1,512,256]{2,1,0:T(8,128)(2,1)S(1)}, bf16[1,512,256]{2,1,0:T(8,128)(2,1)}, u32[]{:S(2)}, u32[]{:S(2)}) collective-permute-start(bf16[1,512,256]{2,1,0:T(8,128)(2,1)S(1)} %bitcast.276), channel_id=1, source_target_pairs={{0,2},{1,3},{2,0},{3,1},{4,6},{5,7},{6,4},{7,5},{8,10},{9,11},{10,... | collective-permute-start | bytes 786440 | tf_op jit(solution)/shard_map/ppermute | solution.py:24
  18.2 9.3 %collective-permute-start.5 = (bf16[3,512,256]{2,1,0:T(8,128)(2,1)}, bf16[3,512,256]{2,1,0:T(8,128)(2,1)}, u32[]{:S(2)}, u32[]{:S(2)}) collective-permute-start(bf16[3,512,256]{2,1,0:T(8,128)(2,1)} %pad_maximum_fusion.4), channel_id=1, source_target_pairs={{0,1},{1,0},{2,3},{3,2},{4,5},{5,4},{6,7},{7,6},{8,9},{9,8},{10,11... | collective-permute-start | bytes 2359304 | tf_op jit(solution)/shard_map/ppermute | solution.py:24
  23.3 8.0 %collective-permute-start.7 = (bf16[1,512,256]{2,1,0:T(8,128)(2,1)}, bf16[1,512,256]{2,1,0:T(8,128)(2,1)S(1)}, u32[]{:S(2)}, u32[]{:S(2)}) collective-permute-start(bf16[1,512,256]{2,1,0:T(8,128)(2,1)} %collective-permute-done.6), channel_id=1, source_target_pairs={{0,1},{1,0},{2,3},{3,2},{4,5},{5,4},{6,7},{7,6},{8,9},{9,8},{10,11... | collective-permute-start | bytes 786440 | tf_op jit(solution)/shard_map/ppermute | solution.py:24
  31.3 1.0 copy-start.8
  32.3 13.4 %collective-permute-start.8 = (bf16[512,256]{1,0:T(8,128)(2,1)S(1)}, bf16[512,256]{1,0:T(8,128)(2,1)S(1)}, u32[]{:S(2)}, u32[]{:S(2)}) collective-permute-start(bf16[512,256]{1,0:T(8,128)(2,1)S(1)} %get-tuple-element.17), channel_id=1, source_target_pairs={{0,2},{1,3},{2,0},{3,1},{4,6},{5,7},{6,4},{7,5},{8,10},{9,11},{10,... | collective-permute-start | bytes 786440 | tf_op jit(solution)/shard_map/ppermute | solution.py:24
  32.5 14.4 %collective-permute-start.9 = (bf16[512,256]{1,0:T(8,128)(2,1)S(1)}, bf16[512,256]{1,0:T(8,128)(2,1)}, u32[]{:S(2)}, u32[]{:S(2)}) collective-permute-start(bf16[512,256]{1,0:T(8,128)(2,1)S(1)} %get-tuple-element.17), channel_id=1, source_target_pairs={{0,4},{1,5},{2,6},{3,7},{4,0},{5,1},{6,2},{7,3},{8,12},{9,13},{10,... | collective-permute-start | bytes 786440 | tf_op jit(solution)/shard_map/ppermute | solution.py:24
  34.8 17.3 %collective-permute-start.14 = (bf16[512,256]{1,0:T(8,128)(2,1)S(1)}, bf16[512,256]{1,0:T(8,128)(2,1)S(1)}, u32[]{:S(2)}, u32[]{:S(2)}) collective-permute-start(bf16[512,256]{1,0:T(8,128)(2,1)S(1)} %get-tuple-element.17), channel_id=1, source_target_pairs={{0,16},{8,24},{16,0},{24,8},{1,17},{9,25},{17,1},{25,9},{2,18},{10... | collective-permute-start | bytes 786440 | tf_op jit(solution)/shard_map/ppermute | solution.py:24
  35.6 16.6 %collective-permute-start.13 = (bf16[512,256]{1,0:T(8,128)(2,1)S(1)}, bf16[512,256]{1,0:T(8,128)(2,1)S(1)}, u32[]{:S(2)}, u32[]{:S(2)}) collective-permute-start(bf16[512,256]{1,0:T(8,128)(2,1)S(1)} %get-tuple-element.17), channel_id=1, source_target_pairs={{0,8},{8,0},{16,24},{24,16},{1,9},{9,1},{17,25},{25,17},{2,10},{10... | collective-permute-start | bytes 786440 | tf_op jit(solution)/shard_map/ppermute | solution.py:24
  45.7 3.3 %copy-start.12 = (bf16[512,256]{1,0:T(8,128)(2,1)}, bf16[512,256]{1,0:T(8,128)(2,1)S(1)}, u32[]{:S(2)}) copy-start(bf16[512,256]{1,0:T(8,128)(2,1)S(1)} %collective-permute-done.8) | copy-start | bytes 786436
  45.7 8.1 %collective-permute-start.15 = (bf16[512,256]{1,0:T(8,128)(2,1)S(1)}, bf16[512,256]{1,0:T(8,128)(2,1)S(1)}, u32[]{:S(2)}, u32[]{:S(2)}) collective-permute-start(bf16[512,256]{1,0:T(8,128)(2,1)S(1)} %get-tuple-element.17), channel_id=1, source_target_pairs={{0,24},{8,16},{16,8},{24,0},{1,25},{9,17},{17,9},{25,1},{2,26},{10... | collective-permute-start | bytes 786440 | tf_op jit(solution)/shard_map/ppermute | solution.py:24
  46.9 15.2 %collective-permute-start.11 = (bf16[1,512,256]{2,1,0:T(8,128)(2,1)}, bf16[1,512,256]{2,1,0:T(8,128)(2,1)}, u32[]{:S(2)}, u32[]{:S(2)}) collective-permute-start(bf16[1,512,256]{2,1,0:T(8,128)(2,1)} %bitcast.23), channel_id=1, source_target_pairs={{0,2},{1,3},{2,0},{3,1},{4,6},{5,7},{6,4},{7,5},{8,10},{9,11},{10,... | collective-permute-start | bytes 786440 | tf_op jit(solution)/shard_map/ppermute | solution.py:24
  49.0 17.0 %collective-permute-start.10 = (bf16[3,512,256]{2,1,0:T(8,128)(2,1)}, bf16[3,512,256]{2,1,0:T(8,128)(2,1)}, u32[]{:S(2)}, u32[]{:S(2)}) collective-permute-start(bf16[3,512,256]{2,1,0:T(8,128)(2,1)} %pad_maximum_fusion.5), channel_id=1, source_target_pairs={{0,1},{1,0},{2,3},{3,2},{4,5},{5,4},{6,7},{7,6},{8,9},{9,8},{10,11... | collective-permute-start | bytes 2359304 | tf_op jit(solution)/shard_map/ppermute | solution.py:24
  62.1 8.0 %collective-permute-start.12 = (bf16[1,512,256]{2,1,0:T(8,128)(2,1)}, bf16[1,512,256]{2,1,0:T(8,128)(2,1)S(1)}, u32[]{:S(2)}, u32[]{:S(2)}) collective-permute-start(bf16[1,512,256]{2,1,0:T(8,128)(2,1)} %collective-permute-done.11), channel_id=1, source_target_pairs={{0,1},{1,0},{2,3},{3,2},{4,5},{5,4},{6,7},{7,6},{8,9},{9,8},{10,11... | collective-permute-start | bytes 786440 | tf_op jit(solution)/shard_map/ppermute | solution.py:24
  64.9 1.0 copy-start.9
  67.2 1.2 copy-start.5
  68.5 1.3 copy-start.1
  68.5 1.3 copy-start.13
  69.8 1.0 copy-start.3
  71.1 12.7 %collective-permute-start.18 = (bf16[512,256]{1,0:T(8,128)(2,1)S(1)}, bf16[512,256]{1,0:T(8,128)(2,1)S(1)}, u32[]{:S(2)}, u32[]{:S(2)}) collective-permute-start(bf16[512,256]{1,0:T(8,128)(2,1)S(1)} %fusion.29), channel_id=1, source_target_pairs={{0,2},{1,3},{2,0},{3,1},{4,6},{5,7},{6,4},{7,5},{8,10},{9,11},{10,... | collective-permute-start | bytes 786440 | tf_op jit(solution)/shard_map/ppermute | solution.py:24
  71.2 14.5 %collective-permute-start.20 = (bf16[512,256]{1,0:T(8,128)(2,1)S(1)}, bf16[512,256]{1,0:T(8,128)(2,1)S(1)}, u32[]{:S(2)}, u32[]{:S(2)}) collective-permute-start(bf16[512,256]{1,0:T(8,128)(2,1)S(1)} %fusion.29), channel_id=1, source_target_pairs={{0,4},{1,5},{2,6},{3,7},{4,0},{5,1},{6,2},{7,3},{8,12},{9,13},{10,... | collective-permute-start | bytes 786440 | tf_op jit(solution)/shard_map/ppermute | solution.py:24
  72.9 14.9 %collective-permute-start.17 = (bf16[512,256]{1,0:T(8,128)(2,1)S(1)}, bf16[512,256]{1,0:T(8,128)(2,1)S(1)}, u32[]{:S(2)}, u32[]{:S(2)}) collective-permute-start(bf16[512,256]{1,0:T(8,128)(2,1)S(1)} %fusion.29), channel_id=1, source_target_pairs={{0,16},{8,24},{16,0},{24,8},{1,17},{9,25},{17,1},{25,9},{2,18},{10... | collective-permute-start | bytes 786440 | tf_op jit(solution)/shard_map/ppermute | solution.py:24
  74.1 13.7 %collective-permute-start.16 = (bf16[512,256]{1,0:T(8,128)(2,1)S(1)}, bf16[512,256]{1,0:T(8,128)(2,1)S(1)}, u32[]{:S(2)}, u32[]{:S(2)}) collective-permute-start(bf16[512,256]{1,0:T(8,128)(2,1)S(1)} %fusion.29), channel_id=1, source_target_pairs={{0,8},{8,0},{16,24},{24,16},{1,9},{9,1},{17,25},{25,17},{2,10},{10... | collective-permute-start | bytes 786440 | tf_op jit(solution)/shard_map/ppermute | solution.py:24
  83.8 7.9 %collective-permute-start.19 = (bf16[512,256]{1,0:T(8,128)(2,1)S(1)}, bf16[512,256]{1,0:T(8,128)(2,1)S(1)}, u32[]{:S(2)}, u32[]{:S(2)}) collective-permute-start(bf16[512,256]{1,0:T(8,128)(2,1)S(1)} %fusion.29), channel_id=1, source_target_pairs={{0,24},{8,16},{16,8},{24,0},{1,25},{9,17},{17,9},{25,1},{2,26},{10... | collective-permute-start | bytes 786440 | tf_op jit(solution)/shard_map/ppermute | solution.py:24
  85.7 6.9 %collective-permute-start.22 = (bf16[1,512,256]{2,1,0:T(8,128)(2,1)S(1)}, bf16[1,512,256]{2,1,0:T(8,128)(2,1)}, u32[]{:S(2)}, u32[]{:S(2)}) collective-permute-start(bf16[1,512,256]{2,1,0:T(8,128)(2,1)S(1)} %bitcast.278), channel_id=1, source_target_pairs={{0,2},{1,3},{2,0},{3,1},{4,6},{5,7},{6,4},{7,5},{8,10},{9,11},{10,... | collective-permute-start | bytes 786440 | tf_op jit(solution)/shard_map/ppermute | solution.py:24
  86.7 9.5 %collective-permute-start.21 = (bf16[3,512,256]{2,1,0:T(8,128)(2,1)}, bf16[3,512,256]{2,1,0:T(8,128)(2,1)}, u32[]{:S(2)}, u32[]{:S(2)}) collective-permute-start(bf16[3,512,256]{2,1,0:T(8,128)(2,1)} %pad_maximum_fusion.6), channel_id=1, source_target_pairs={{0,1},{1,0},{2,3},{3,2},{4,5},{5,4},{6,7},{7,6},{8,9},{9,8},{10,11... | collective-permute-start | bytes 2359304 | tf_op jit(solution)/shard_map/ppermute | solution.py:24
  92.6 7.4 %collective-permute-start.23 = (bf16[1,512,256]{2,1,0:T(8,128)(2,1)}, bf16[1,512,256]{2,1,0:T(8,128)(2,1)S(1)}, u32[]{:S(2)}, u32[]{:S(2)}) collective-permute-start(bf16[1,512,256]{2,1,0:T(8,128)(2,1)} %collective-permute-done.22), channel_id=1, source_target_pairs={{0,1},{1,0},{2,3},{3,2},{4,5},{5,4},{6,7},{7,6},{8,9},{9,8},{10,11... | collective-permute-start | bytes 786440 | tf_op jit(solution)/shard_map/ppermute | solution.py:24
  100.0 1.0 copy-start.6
  101.0 13.0 %collective-permute-start.24 = (bf16[512,256]{1,0:T(8,128)(2,1)S(1)}, bf16[512,256]{1,0:T(8,128)(2,1)S(1)}, u32[]{:S(2)}, u32[]{:S(2)}) collective-permute-start(bf16[512,256]{1,0:T(8,128)(2,1)S(1)} %get-tuple-element.21), channel_id=1, source_target_pairs={{0,2},{1,3},{2,0},{3,1},{4,6},{5,7},{6,4},{7,5},{8,10},{9,11},{10,... | collective-permute-start | bytes 786440 | tf_op jit(solution)/shard_map/ppermute | solution.py:24
  101.0 15.0 %collective-permute-start.25 = (bf16[512,256]{1,0:T(8,128)(2,1)S(1)}, bf16[512,256]{1,0:T(8,128)(2,1)}, u32[]{:S(2)}, u32[]{:S(2)}) collective-permute-start(bf16[512,256]{1,0:T(8,128)(2,1)S(1)} %get-tuple-element.21), channel_id=1, source_target_pairs={{0,4},{1,5},{2,6},{3,7},{4,0},{5,1},{6,2},{7,3},{8,12},{9,13},{10,... | collective-permute-start | bytes 786440 | tf_op jit(solution)/shard_map/ppermute | solution.py:24
  103.0 18.0 %collective-permute-start.30 = (bf16[512,256]{1,0:T(8,128)(2,1)S(1)}, bf16[512,256]{1,0:T(8,128)(2,1)S(1)}, u32[]{:S(2)}, u32[]{:S(2)}) collective-permute-start(bf16[512,256]{1,0:T(8,128)(2,1)S(1)} %get-tuple-element.21), channel_id=1, source_target_pairs={{0,16},{8,24},{16,0},{24,8},{1,17},{9,25},{17,1},{25,9},{2,18},{10... | collective-permute-start | bytes 786440 | tf_op jit(solution)/shard_map/ppermute | solution.py:24
  104.0 17.0 %collective-permute-start.29 = (bf16[512,256]{1,0:T(8,128)(2,1)S(1)}, bf16[512,256]{1,0:T(8,128)(2,1)S(1)}, u32[]{:S(2)}, u32[]{:S(2)}) collective-permute-start(bf16[512,256]{1,0:T(8,128)(2,1)S(1)} %get-tuple-element.21), channel_id=1, source_target_pairs={{0,8},{8,0},{16,24},{24,16},{1,9},{9,1},{17,25},{25,17},{2,10},{10... | collective-permute-start | bytes 786440 | tf_op jit(solution)/shard_map/ppermute | solution.py:24
  114.0 4.0 %copy-start.10 = (bf16[512,256]{1,0:T(8,128)(2,1)}, bf16[512,256]{1,0:T(8,128)(2,1)S(1)}, u32[]{:S(2)}) copy-start(bf16[512,256]{1,0:T(8,128)(2,1)S(1)} %collective-permute-done.24) | copy-start | bytes 786436
  114.0 8.1 %collective-permute-start.31 = (bf16[512,256]{1,0:T(8,128)(2,1)S(1)}, bf16[512,256]{1,0:T(8,128)(2,1)S(1)}, u32[]{:S(2)}, u32[]{:S(2)}) collective-permute-start(bf16[512,256]{1,0:T(8,128)(2,1)S(1)} %get-tuple-element.21), channel_id=1, source_target_pairs={{0,24},{8,16},{16,8},{24,0},{1,25},{9,17},{17,9},{25,1},{2,26},{10... | collective-permute-start | bytes 786440 | tf_op jit(solution)/shard_map/ppermute | solution.py:24
  116.0 14.4 %collective-permute-start.27 = (bf16[1,512,256]{2,1,0:T(8,128)(2,1)}, bf16[1,512,256]{2,1,0:T(8,128)(2,1)}, u32[]{:S(2)}, u32[]{:S(2)}) collective-permute-start(bf16[1,512,256]{2,1,0:T(8,128)(2,1)} %bitcast.63), channel_id=1, source_target_pairs={{0,2},{1,3},{2,0},{3,1},{4,6},{5,7},{6,4},{7,5},{8,10},{9,11},{10,... | collective-permute-start | bytes 786440 | tf_op jit(solution)/shard_map/ppermute | solution.py:24
  118.0 16.4 %collective-permute-start.26 = (bf16[3,512,256]{2,1,0:T(8,128)(2,1)}, bf16[3,512,256]{2,1,0:T(8,128)(2,1)}, u32[]{:S(2)}, u32[]{:S(2)}) collective-permute-start(bf16[3,512,256]{2,1,0:T(8,128)(2,1)} %pad_maximum_fusion.7), channel_id=1, source_target_pairs={{0,1},{1,0},{2,3},{3,2},{4,5},{5,4},{6,7},{7,6},{8,9},{9,8},{10,11... | collective-permute-start | bytes 2359304 | tf_op jit(solution)/shard_map/ppermute | solution.py:24
  130.4 8.0 %collective-permute-start.28 = (bf16[1,512,256]{2,1,0:T(8,128)(2,1)}, bf16[1,512,256]{2,1,0:T(8,128)(2,1)S(1)}, u32[]{:S(2)}, u32[]{:S(2)}) collective-permute-start(bf16[1,512,256]{2,1,0:T(8,128)(2,1)} %collective-permute-done.27), channel_id=1, source_target_pairs={{0,1},{1,0},{2,3},{3,2},{4,5},{5,4},{6,7},{7,6},{8,9},{9,8},{10,11... | collective-permute-start | bytes 786440 | tf_op jit(solution)/shard_map/ppermute | solution.py:24
  133.2 1.0 copy-start.7
  135.6 1.2 copy-start.4
  136.8 1.3 copy-start
  136.8 1.3 copy-start.11
  138.1 1.0 copy-start.2

commit v15 on v6

--- a/solution.py
+++ b/solution.py
@@ -31,7 +31,7 @@
         same[s] = xor_permute(xb, "col", n_col, 2 * s)
     col_pieces = [xb] + [xor_permute(xb, "row", n_row, t) for t in range(1, n_row)]
     first = sorted(same)
-    relay_first = xor_permute(jnp.stack([same[s] for s in first]), "col", n_col, 1)
+    relay_first = xor_permute(tuple(same[s] for s in first), "col", n_col, 1)
     other = {}
     for i, s in enumerate(first):
         other[s] = relay_first[i]

time: 124 us -> 124 us (level)
  matrix products: 28.5 us -> 32 us
  local copies, waits for them, and re-layouts: 8.68 us -> 12.1 us
  other arithmetic: 6.66 us -> 3.39 us
  waiting for transfers between devices: 43.1 us -> 39.9 us
    dot_general x48, matrix products: 28.5 us -> 32 us  [contract(): part = jnp.dot(piece, k_blocks[s], preferred_element_type=jnp.float32)]
    unnamed x33 -> x37, local copies, waits for them, and re-layouts: 3.57 us -> 6.95 us
    another operation x4 -> x0, other arithmetic: 3.31 us -> none  [exchange(): jnp.stack([same[s] for s in first])]
    ppermute x32 -> x40, waiting for transfers between devices: 43.1 us -> 39.9 us  [xor_permute(): return lax.ppermute(x, axis, perm=[(i, i ^ s) for i in range(size)])]
    ppermute x32 -> x40, starting transfers between devices: 35.3 us -> 34.8 us  [xor_permute(): return lax.ppermute(x, axis, perm=[(i, i ^ s) for i in range(size)])]
  transfers between devices with their start and end apart: 32 -> 40, of which waited for: 11 -> 12; matrix products, arithmetic and copies ran while one was open for 30% -> 30% of each run, Pallas kernels for 0% -> 0%
where the time goes in v15:
time: 124 us; the launch traced here: 123 us
  waiting for transfers between devices  39.9 us (32%)
  starting transfers between devices  34.8 us (28%)
  matrix products  32 us (26%)
  local copies, waits for them, and re-layouts  12.1 us (10%)
  other arithmetic  3.39 us (3%)
    ppermute x40, waiting for transfers between devices, xor_permute(): return lax.ppermute(x, axis, perm=[(i, i ^ s) for i in range(size)])  39.9 us
    ppermute x40, starting transfers between devices, xor_permute(): return lax.ppermute(x, axis, perm=[(i, i ^ s) for i in range(size)])  34.8 us
    dot_general x48, matrix products, contract(): part = jnp.dot(piece, k_blocks[s], preferred_element_type=jnp.float32)  32 us
    unnamed x37, local copies, waits for them, and re-layouts  6.95 us
    gather x4, local copies, waits for them, and re-layouts, ordered_k_blocks(): return jnp.take(split, index, axis=0)  4.9 us
    another operation x4, other arithmetic, exchange(): return (row_pieces, jnp.stack(col_pieces))  2.56 us
  transfers between devices with their start and end apart: 40, of which 12 were waited for; matrix products, arithmetic and copies ran while one was open for 30% of the time, Pallas kernels for 0%

profile of v15, /device:TPU:1, one launch (start us, length us, event | category | flops | bytes accessed | tf_op | source)
XLA Modules:
  0.0 122.9 jit_solution(859366330091848676)
XLA Ops:
  1.2 3.2 %collective-permute-start.6 = (bf16[512,256]{1,0:T(8,128)(2,1)S(1)}, bf16[512,256]{1,0:T(8,128)(2,1)S(1)}, u32[]{:S(2)}, u32[]{:S(2)}) collective-permute-start(bf16[512,256]{1,0:T(8,128)(2,1)S(1)} %fusion.16), channel_id=1, source_target_pairs={{0,4},{1,5},{2,6},{3,7},{4,0},{5,1},{6,2},{7,3},{8,12},{9,13},{10,... | collective-permute-start | bytes 786440 | tf_op jit(solution)/shard_map/ppermute | solution.py:24
  4.4 2.2 %collective-permute-start.2 = (bf16[512,256]{1,0:T(8,128)(2,1)S(1)}, bf16[512,256]{1,0:T(8,128)(2,1)S(1)}, u32[]{:S(2)}, u32[]{:S(2)}) collective-permute-start(bf16[512,256]{1,0:T(8,128)(2,1)S(1)} %fusion.16), channel_id=1, source_target_pairs={{0,24},{8,16},{16,8},{24,0},{1,25},{9,17},{17,9},{25,1},{2,26},{10... | collective-permute-start | bytes 786440 | tf_op jit(solution)/shard_map/ppermute | solution.py:24
  7.0 1.3 %collective-permute-start.4 = (bf16[512,256]{1,0:T(8,128)(2,1)S(1)}, bf16[512,256]{1,0:T(8,128)(2,1)}, u32[]{:S(2)}, u32[]{:S(2)}) collective-permute-start(bf16[512,256]{1,0:T(8,128)(2,1)S(1)} %fusion.16), channel_id=1, source_target_pairs={{0,2},{1,3},{2,0},{3,1},{4,6},{5,7},{6,4},{7,5},{8,10},{9,11},{10,... | collective-permute-start | bytes 786440 | tf_op jit(solution)/shard_map/ppermute | solution.py:24
  8.3 7.7 %collective-permute-done.6 = bf16[512,256]{1,0:T(8,128)(2,1)S(1)} collective-permute-done((bf16[512,256]{1,0:T(8,128)(2,1)S(1)}, bf16[512,256]{1,0:T(8,128)(2,1)S(1)}, u32[]{:S(2)}, u32[]{:S(2)}) %collective-permute-start.6) | collective-permute-done | bytes 262176 | tf_op jit(solution)/shard_map/ppermute | solution.py:24
  16.1 1.3 %collective-permute-start.3 = (bf16[512,256]{1,0:T(8,128)(2,1)S(1)}, bf16[512,256]{1,0:T(8,128)(2,1)}, u32[]{:S(2)}, u32[]{:S(2)}) collective-permute-start(bf16[512,256]{1,0:T(8,128)(2,1)S(1)} %fusion.16), channel_id=1, source_target_pairs={{0,1},{1,0},{2,3},{3,2},{4,5},{5,4},{6,7},{7,6},{8,9},{9,8},{10,11... | collective-permute-start | bytes 786440 | tf_op jit(solution)/shard_map/ppermute | solution.py:24
  17.7 1.5 %collective-permute-done.1 = bf16[512,256]{1,0:T(8,128)(2,1)S(1)} collective-permute-done((bf16[512,256]{1,0:T(8,128)(2,1)S(1)}, bf16[512,256]{1,0:T(8,128)(2,1)S(1)}, u32[]{:S(2)}, u32[]{:S(2)}) %collective-permute-start.1) | collective-permute-done | bytes 262176 | tf_op jit(solution)/shard_map/ppermute | solution.py:24
  21.0 1.2 convolution_add_fusion.29
  22.2 1.2 convolution_add_fusion.28
  23.6 1.8 %collective-permute-done.8 = bf16[1,512,256]{2,1,0:T(8,128)(2,1)} collective-permute-done((bf16[1,512,256]{2,1,0:T(8,128)(2,1)S(1)}, bf16[1,512,256]{2,1,0:T(8,128)(2,1)}, u32[]{:S(2)}, u32[]{:S(2)}) %collective-permute-start.8) | collective-permute-done | bytes 262176 | tf_op jit(solution)/shard_map/ppermute | solution.py:24
  26.2 1.2 fusion.38
  29.8 2.2 %collective-permute-start.19 = (bf16[512,256]{1,0:T(8,128)(2,1)S(1)}, bf16[512,256]{1,0:T(8,128)(2,1)S(1)}, u32[]{:S(2)}, u32[]{:S(2)}) collective-permute-start(bf16[512,256]{1,0:T(8,128)(2,1)S(1)} %get-tuple-element.8), channel_id=1, source_target_pairs={{0,24},{8,16},{16,8},{24,0},{1,25},{9,17},{17,9},{25,1},{2,26},{10... | collective-permute-start | bytes 786440 | tf_op jit(solution)/shard_map/ppermute | solution.py:24
  32.5 2.1 %collective-permute-start.13 = (bf16[512,256]{1,0:T(8,128)(2,1)S(1)}, bf16[512,256]{1,0:T(8,128)(2,1)}, u32[]{:S(2)}, u32[]{:S(2)}) collective-permute-start(bf16[512,256]{1,0:T(8,128)(2,1)S(1)} %get-tuple-element.8), channel_id=1, source_target_pairs={{0,4},{1,5},{2,6},{3,7},{4,0},{5,1},{6,2},{7,3},{8,12},{9,13},{10,... | collective-permute-start | bytes 786440 | tf_op jit(solution)/shard_map/ppermute | solution.py:24
  34.6 1.5 %collective-permute-start.11 = (bf16[512,256]{1,0:T(8,128)(2,1)S(1)}, bf16[512,256]{1,0:T(8,128)(2,1)}, u32[]{:S(2)}, u32[]{:S(2)}) collective-permute-start(bf16[512,256]{1,0:T(8,128)(2,1)S(1)} %get-tuple-element.8), channel_id=1, source_target_pairs={{0,2},{1,3},{2,0},{3,1},{4,6},{5,7},{6,4},{7,5},{8,10},{9,11},{10,... | collective-permute-start | bytes 786440 | tf_op jit(solution)/shard_map/ppermute | solution.py:24
  37.0 1.7 %collective-permute-done.19 = bf16[512,256]{1,0:T(8,128)(2,1)S(1)} collective-permute-done((bf16[512,256]{1,0:T(8,128)(2,1)S(1)}, bf16[512,256]{1,0:T(8,128)(2,1)S(1)}, u32[]{:S(2)}, u32[]{:S(2)}) %collective-permute-start.19) | collective-permute-done | bytes 262176 | tf_op jit(solution)/shard_map/ppermute | solution.py:24
  38.7 1.2 collective-permute-start.10
  39.9 4.8 %collective-permute-done.18 = bf16[512,256]{1,0:T(8,128)(2,1)S(1)} collective-permute-done((bf16[512,256]{1,0:T(8,128)(2,1)S(1)}, bf16[512,256]{1,0:T(8,128)(2,1)S(1)}, u32[]{:S(2)}, u32[]{:S(2)}) %collective-permute-start.18) | collective-permute-done | bytes 262176 | tf_op jit(solution)/shard_map/ppermute | solution.py:24
  44.7 1.1 pad_maximum_fusion.1
  45.9 1.8 %gather_fusion.1 = bf16[8,256,256]{2,1,0:T(8,128)(2,1)S(1)} fusion(bf16[8,256,256]{2,1,0:T(8,128)(2,1)} %bitcast.236, s32[1024]{0:T(1024)S(1)} %pad_clamp_fusion), kind=kCustom, calls=%fused_computation.1.clone | custom fusion | bytes 2097184 | tf_op jit(solution)/shard_map/jit(_take)/gather | solution.py:59
  48.6 1.2 fusion.36
  50.8 1.2 convolution_add_fusion.19
  52.0 1.2 convolution_add_fusion.18
  56.1 1.2 convolution_add_fusion.24
  57.3 1.2 convolution_add_fusion.23
  58.5 1.2 fusion.46
  61.6 3.2 %collective-permute-start.26 = (bf16[512,256]{1,0:T(8,128)(2,1)S(1)}, bf16[512,256]{1,0:T(8,128)(2,1)S(1)}, u32[]{:S(2)}, u32[]{:S(2)}) collective-permute-start(bf16[512,256]{1,0:T(8,128)(2,1)S(1)} %fusion.17), channel_id=1, source_target_pairs={{0,4},{1,5},{2,6},{3,7},{4,0},{5,1},{6,2},{7,3},{8,12},{9,13},{10,... | collective-permute-start | bytes 786440 | tf_op jit(solution)/shard_map/ppermute | solution.py:24
  64.8 1.4 %collective-permute-start.22 = (bf16[512,256]{1,0:T(8,128)(2,1)S(1)}, bf16[512,256]{1,0:T(8,128)(2,1)S(1)}, u32[]{:S(2)}, u32[]{:S(2)}) collective-permute-start(bf16[512,256]{1,0:T(8,128)(2,1)S(1)} %fusion.17), channel_id=1, source_target_pairs={{0,24},{8,16},{16,8},{24,0},{1,25},{9,17},{17,9},{25,1},{2,26},{10... | collective-permute-start | bytes 786440 | tf_op jit(solution)/shard_map/ppermute | solution.py:24
  67.4 9.7 %collective-permute-done.26 = bf16[512,256]{1,0:T(8,128)(2,1)S(1)} collective-permute-done((bf16[512,256]{1,0:T(8,128)(2,1)S(1)}, bf16[512,256]{1,0:T(8,128)(2,1)S(1)}, u32[]{:S(2)}, u32[]{:S(2)}) %collective-permute-start.26) | collective-permute-done | bytes 262176 | tf_op jit(solution)/shard_map/ppermute | solution.py:24
  77.8 1.9 %collective-permute-done.21 = bf16[512,256]{1,0:T(8,128)(2,1)S(1)} collective-permute-done((bf16[512,256]{1,0:T(8,128)(2,1)S(1)}, bf16[512,256]{1,0:T(8,128)(2,1)S(1)}, u32[]{:S(2)}, u32[]{:S(2)}) %collective-permute-start.21) | collective-permute-done | bytes 262176 | tf_op jit(solution)/shard_map/ppermute | solution.py:24
  81.0 1.3 %collective-permute-start.25 = (bf16[512,256]{1,0:T(8,128)(2,1)}, bf16[512,256]{1,0:T(8,128)(2,1)S(1)}, u32[]{:S(2)}, u32[]{:S(2)}) collective-permute-start(bf16[512,256]{1,0:T(8,128)(2,1)} %collective-permute-done.24), channel_id=1, source_target_pairs={{0,1},{1,0},{2,3},{3,2},{4,5},{5,4},{6,7},{7,6},{8,9},{9,8},{10,11... | collective-permute-start | bytes 786440 | tf_op jit(solution)/shard_map/ppermute | solution.py:24
  82.6 1.2 convolution_add_fusion.14
  83.8 1.2 convolution_add_fusion.13
  85.2 1.1 collective-permute-done.28
  86.2 1.1 collective-permute-start.29
  87.3 1.2 fusion.27
  91.0 1.3 %collective-permute-start.39 = (bf16[512,256]{1,0:T(8,128)(2,1)S(1)}, bf16[512,256]{1,0:T(8,128)(2,1)S(1)}, u32[]{:S(2)}, u32[]{:S(2)}) collective-permute-start(bf16[512,256]{1,0:T(8,128)(2,1)S(1)} %get-tuple-element.10), channel_id=1, source_target_pairs={{0,24},{8,16},{16,8},{24,0},{1,25},{9,17},{17,9},{25,1},{2,26},{10... | collective-permute-start | bytes 786440 | tf_op jit(solution)/shard_map/ppermute | solution.py:24
  92.3 1.1 collective-permute-start.38
  93.8 1.5 %collective-permute-start.31 = (bf16[512,256]{1,0:T(8,128)(2,1)S(1)}, bf16[512,256]{1,0:T(8,128)(2,1)}, u32[]{:S(2)}, u32[]{:S(2)}) collective-permute-start(bf16[512,256]{1,0:T(8,128)(2,1)S(1)} %get-tuple-element.10), channel_id=1, source_target_pairs={{0,2},{1,3},{2,0},{3,1},{4,6},{5,7},{6,4},{7,5},{8,10},{9,11},{10,... | collective-permute-start | bytes 786440 | tf_op jit(solution)/shard_map/ppermute | solution.py:24
  96.3 3.5 %collective-permute-done.39 = bf16[512,256]{1,0:T(8,128)(2,1)S(1)} collective-permute-done((bf16[512,256]{1,0:T(8,128)(2,1)S(1)}, bf16[512,256]{1,0:T(8,128)(2,1)S(1)}, u32[]{:S(2)}, u32[]{:S(2)}) %collective-permute-start.39) | collective-permute-done | bytes 262176 | tf_op jit(solution)/shard_map/ppermute | solution.py:24
  99.8 1.2 collective-permute-start.30
  101.0 4.8 %collective-permute-done.38 = bf16[512,256]{1,0:T(8,128)(2,1)S(1)} collective-permute-done((bf16[512,256]{1,0:T(8,128)(2,1)S(1)}, bf16[512,256]{1,0:T(8,128)(2,1)S(1)}, u32[]{:S(2)}, u32[]{:S(2)}) %collective-permute-start.38) | collective-permute-done | bytes 262176 | tf_op jit(solution)/shard_map/ppermute | solution.py:24
  105.8 1.1 pad_maximum_fusion.3
  107.0 1.8 %gather_fusion.3 = bf16[8,256,256]{2,1,0:T(8,128)(2,1)S(1)} fusion(bf16[8,256,256]{2,1,0:T(8,128)(2,1)} %bitcast.234, s32[1024]{0:T(1024)S(1)} %pad_clamp_fusion), kind=kCustom, calls=%fused_computation.3.clone | custom fusion | bytes 2097184 | tf_op jit(solution)/shard_map/jit(_take)/gather | solution.py:59
  109.3 1.2 fusion.25
  111.2 1.2 convolution_add_fusion.4
  112.4 1.2 convolution_add_fusion.3
  116.6 1.2 convolution_add_fusion.9
  117.7 1.2 convolution_add_fusion.8
  118.9 1.2 fusion.50
  (134 shorter events, 29.7 us)
Async XLA Ops:
  0.0 1.1 copy-start.16
  1.2 14.9 %collective-permute-start.6 = (bf16[512,256]{1,0:T(8,128)(2,1)S(1)}, bf16[512,256]{1,0:T(8,128)(2,1)S(1)}, u32[]{:S(2)}, u32[]{:S(2)}) collective-permute-start(bf16[512,256]{1,0:T(8,128)(2,1)S(1)} %fusion.16), channel_id=1, source_target_pairs={{0,4},{1,5},{2,6},{3,7},{4,0},{5,1},{6,2},{7,3},{8,12},{9,13},{10,... | collective-permute-start | bytes 786440 | tf_op jit(solution)/shard_map/ppermute | solution.py:24
  4.4 13.0 %collective-permute-start.2 = (bf16[512,256]{1,0:T(8,128)(2,1)S(1)}, bf16[512,256]{1,0:T(8,128)(2,1)S(1)}, u32[]{:S(2)}, u32[]{:S(2)}) collective-permute-start(bf16[512,256]{1,0:T(8,128)(2,1)S(1)} %fusion.16), channel_id=1, source_target_pairs={{0,24},{8,16},{16,8},{24,0},{1,25},{9,17},{17,9},{25,1},{2,26},{10... | collective-permute-start | bytes 786440 | tf_op jit(solution)/shard_map/ppermute | solution.py:24
  6.5 12.7 %collective-permute-start.1 = (bf16[512,256]{1,0:T(8,128)(2,1)S(1)}, bf16[512,256]{1,0:T(8,128)(2,1)S(1)}, u32[]{:S(2)}, u32[]{:S(2)}) collective-permute-start(bf16[512,256]{1,0:T(8,128)(2,1)S(1)} %fusion.16), channel_id=1, source_target_pairs={{0,16},{8,24},{16,0},{24,8},{1,17},{9,25},{17,1},{25,9},{2,18},{10... | collective-permute-start | bytes 786440 | tf_op jit(solution)/shard_map/ppermute | solution.py:24
  6.8 12.5 %collective-permute-start = (bf16[512,256]{1,0:T(8,128)(2,1)S(1)}, bf16[512,256]{1,0:T(8,128)(2,1)S(1)}, u32[]{:S(2)}, u32[]{:S(2)}) collective-permute-start(bf16[512,256]{1,0:T(8,128)(2,1)S(1)} %fusion.16), channel_id=1, source_target_pairs={{0,8},{8,0},{16,24},{24,16},{1,9},{9,1},{17,25},{25,17},{2,10},{10... | collective-permute-start | bytes 786440 | tf_op jit(solution)/shard_map/ppermute | solution.py:24
  7.0 13.7 %collective-permute-start.4 = (bf16[512,256]{1,0:T(8,128)(2,1)S(1)}, bf16[512,256]{1,0:T(8,128)(2,1)}, u32[]{:S(2)}, u32[]{:S(2)}) collective-permute-start(bf16[512,256]{1,0:T(8,128)(2,1)S(1)} %fusion.16), channel_id=1, source_target_pairs={{0,2},{1,3},{2,0},{3,1},{4,6},{5,7},{6,4},{7,5},{8,10},{9,11},{10,... | collective-permute-start | bytes 786440 | tf_op jit(solution)/shard_map/ppermute | solution.py:24
  16.1 5.0 %collective-permute-start.3 = (bf16[512,256]{1,0:T(8,128)(2,1)S(1)}, bf16[512,256]{1,0:T(8,128)(2,1)}, u32[]{:S(2)}, u32[]{:S(2)}) collective-permute-start(bf16[512,256]{1,0:T(8,128)(2,1)S(1)} %fusion.16), channel_id=1, source_target_pairs={{0,1},{1,0},{2,3},{3,2},{4,5},{5,4},{6,7},{7,6},{8,9},{9,8},{10,11... | collective-permute-start | bytes 786440 | tf_op jit(solution)/shard_map/ppermute | solution.py:24
  17.3 8.0 %collective-permute-start.8 = (bf16[1,512,256]{2,1,0:T(8,128)(2,1)S(1)}, bf16[1,512,256]{2,1,0:T(8,128)(2,1)}, u32[]{:S(2)}, u32[]{:S(2)}) collective-permute-start(bf16[1,512,256]{2,1,0:T(8,128)(2,1)S(1)} %bitcast.242), channel_id=1, source_target_pairs={{0,2},{1,3},{2,0},{3,1},{4,6},{5,7},{6,4},{7,5},{8,10},{9,11},{10,... | collective-permute-start | bytes 786440 | tf_op jit(solution)/shard_map/ppermute | solution.py:24
  20.1 7.9 %collective-permute-start.7 = (bf16[512,256]{1,0:T(8,128)(2,1)S(1)}, bf16[512,256]{1,0:T(8,128)(2,1)S(1)}, u32[]{:S(2)}, u32[]{:S(2)}) collective-permute-start(bf16[512,256]{1,0:T(8,128)(2,1)S(1)} %collective-permute-done.6), channel_id=1, source_target_pairs={{0,1},{1,0},{2,3},{3,2},{4,5},{5,4},{6,7},{7,6},{8,9},{9,8},{10,11... | collective-permute-start | bytes 786440 | tf_op jit(solution)/shard_map/ppermute | solution.py:24
  20.7 6.7 %collective-permute-start.5 = (bf16[512,256]{1,0:T(8,128)(2,1)}, bf16[512,256]{1,0:T(8,128)(2,1)S(1)}, u32[]{:S(2)}, u32[]{:S(2)}) collective-permute-start(bf16[512,256]{1,0:T(8,128)(2,1)} %collective-permute-done.4), channel_id=1, source_target_pairs={{0,1},{1,0},{2,3},{3,2},{4,5},{5,4},{6,7},{7,6},{8,9},{9,8},{10,11... | collective-permute-start | bytes 786440 | tf_op jit(solution)/shard_map/ppermute | solution.py:24
  25.4 3.4 %collective-permute-start.9 = (bf16[1,512,256]{2,1,0:T(8,128)(2,1)}, bf16[1,512,256]{2,1,0:T(8,128)(2,1)S(1)}, u32[]{:S(2)}, u32[]{:S(2)}) collective-permute-start(bf16[1,512,256]{2,1,0:T(8,128)(2,1)} %collective-permute-done.8), channel_id=1, source_target_pairs={{0,1},{1,0},{2,3},{3,2},{4,5},{5,4},{6,7},{7,6},{8,9},{9,8},{10,11... | collective-permute-start | bytes 786440 | tf_op jit(solution)/shard_map/ppermute | solution.py:24
  29.8 8.9 %collective-permute-start.19 = (bf16[512,256]{1,0:T(8,128)(2,1)S(1)}, bf16[512,256]{1,0:T(8,128)(2,1)S(1)}, u32[]{:S(2)}, u32[]{:S(2)}) collective-permute-start(bf16[512,256]{1,0:T(8,128)(2,1)S(1)} %get-tuple-element.8), channel_id=1, source_target_pairs={{0,24},{8,16},{16,8},{24,0},{1,25},{9,17},{17,9},{25,1},{2,26},{10... | collective-permute-start | bytes 786440 | tf_op jit(solution)/shard_map/ppermute | solution.py:24
  32.0 12.7 %collective-permute-start.18 = (bf16[512,256]{1,0:T(8,128)(2,1)S(1)}, bf16[512,256]{1,0:T(8,128)(2,1)S(1)}, u32[]{:S(2)}, u32[]{:S(2)}) collective-permute-start(bf16[512,256]{1,0:T(8,128)(2,1)S(1)} %get-tuple-element.8), channel_id=1, source_target_pairs={{0,16},{8,24},{16,0},{24,8},{1,17},{9,25},{17,1},{25,9},{2,18},{10... | collective-permute-start | bytes 786440 | tf_op jit(solution)/shard_map/ppermute | solution.py:24
  32.3 12.4 %collective-permute-start.17 = (bf16[512,256]{1,0:T(8,128)(2,1)S(1)}, bf16[512,256]{1,0:T(8,128)(2,1)S(1)}, u32[]{:S(2)}, u32[]{:S(2)}) collective-permute-start(bf16[512,256]{1,0:T(8,128)(2,1)S(1)} %get-tuple-element.8), channel_id=1, source_target_pairs={{0,8},{8,0},{16,24},{24,16},{1,9},{9,1},{17,25},{25,17},{2,10},{10... | collective-permute-start | bytes 786440 | tf_op jit(solution)/shard_map/ppermute | solution.py:24
  32.5 15.6 %collective-permute-start.13 = (bf16[512,256]{1,0:T(8,128)(2,1)S(1)}, bf16[512,256]{1,0:T(8,128)(2,1)}, u32[]{:S(2)}, u32[]{:S(2)}) collective-permute-start(bf16[512,256]{1,0:T(8,128)(2,1)S(1)} %get-tuple-element.8), channel_id=1, source_target_pairs={{0,4},{1,5},{2,6},{3,7},{4,0},{5,1},{6,2},{7,3},{8,12},{9,13},{10,... | collective-permute-start | bytes 786440 | tf_op jit(solution)/shard_map/ppermute | solution.py:24
  34.6 18.6 %collective-permute-start.11 = (bf16[512,256]{1,0:T(8,128)(2,1)S(1)}, bf16[512,256]{1,0:T(8,128)(2,1)}, u32[]{:S(2)}, u32[]{:S(2)}) collective-permute-start(bf16[512,256]{1,0:T(8,128)(2,1)S(1)} %get-tuple-element.8), channel_id=1, source_target_pairs={{0,2},{1,3},{2,0},{3,1},{4,6},{5,7},{6,4},{7,5},{8,10},{9,11},{10,... | collective-permute-start | bytes 786440 | tf_op jit(solution)/shard_map/ppermute | solution.py:24
  38.7 16.6 %collective-permute-start.10 = (bf16[512,256]{1,0:T(8,128)(2,1)S(1)}, bf16[512,256]{1,0:T(8,128)(2,1)}, u32[]{:S(2)}, u32[]{:S(2)}) collective-permute-start(bf16[512,256]{1,0:T(8,128)(2,1)S(1)} %get-tuple-element.8), channel_id=1, source_target_pairs={{0,1},{1,0},{2,3},{3,2},{4,5},{5,4},{6,7},{7,6},{8,9},{9,8},{10,11... | collective-permute-start | bytes 786440 | tf_op jit(solution)/shard_map/ppermute | solution.py:24
  48.1 11.6 %collective-permute-start.15 = (bf16[1,512,256]{2,1,0:T(8,128)(2,1)}, bf16[1,512,256]{2,1,0:T(8,128)(2,1)S(1)}, u32[]{:S(2)}, u32[]{:S(2)}) collective-permute-start(bf16[1,512,256]{2,1,0:T(8,128)(2,1)} %bitcast.17), channel_id=1, source_target_pairs={{0,2},{1,3},{2,0},{3,1},{4,6},{5,7},{6,4},{7,5},{8,10},{9,11},{10,... | collective-permute-start | bytes 786440 | tf_op jit(solution)/shard_map/ppermute | solution.py:24
  50.0 10.3 %collective-permute-start.14 = (bf16[512,256]{1,0:T(8,128)(2,1)}, bf16[512,256]{1,0:T(8,128)(2,1)S(1)}, u32[]{:S(2)}, u32[]{:S(2)}) collective-permute-start(bf16[512,256]{1,0:T(8,128)(2,1)} %collective-permute-done.13), channel_id=1, source_target_pairs={{0,1},{1,0},{2,3},{3,2},{4,5},{5,4},{6,7},{7,6},{8,9},{9,8},{10,11... | collective-permute-start | bytes 786440 | tf_op jit(solution)/shard_map/ppermute | solution.py:24
  51.9 1.3 %copy-start.11 = (bf16[512,256]{1,0:T(8,128)(2,1)S(1)}, bf16[512,256]{1,0:T(8,128)(2,1)}, u32[]{:S(2)}) copy-start(bf16[512,256]{1,0:T(8,128)(2,1)} %copy-done.10) | copy-start | bytes 786436
  53.2 6.8 %collective-permute-start.12 = (bf16[512,256]{1,0:T(8,128)(2,1)}, bf16[512,256]{1,0:T(8,128)(2,1)S(1)}, u32[]{:S(2)}, u32[]{:S(2)}) collective-permute-start(bf16[512,256]{1,0:T(8,128)(2,1)} %collective-permute-done.11), channel_id=1, source_target_pairs={{0,1},{1,0},{2,3},{3,2},{4,5},{5,4},{6,7},{7,6},{8,9},{9,8},{10,11... | collective-permute-start | bytes 786440 | tf_op jit(solution)/shard_map/ppermute | solution.py:24
  55.1 1.0 copy-start.3
  59.7 1.6 %collective-permute-start.16 = (bf16[1,512,256]{2,1,0:T(8,128)(2,1)S(1)}, bf16[1,512,256]{2,1,0:T(8,128)(2,1)S(1)}, u32[]{:S(2)}, u32[]{:S(2)}) collective-permute-start(bf16[1,512,256]{2,1,0:T(8,128)(2,1)S(1)} %collective-permute-done.15), channel_id=1, source_target_pairs={{0,1},{1,0},{2,3},{3,2},{4,5},{5,4},{6,7},{7,6},{8,9},{9,8},{10,11... | collective-permute-start | bytes 786440 | tf_op jit(solution)/shard_map/ppermute | solution.py:24
  60.2 1.0 copy-start.1
  61.6 15.6 %collective-permute-start.26 = (bf16[512,256]{1,0:T(8,128)(2,1)S(1)}, bf16[512,256]{1,0:T(8,128)(2,1)S(1)}, u32[]{:S(2)}, u32[]{:S(2)}) collective-permute-start(bf16[512,256]{1,0:T(8,128)(2,1)S(1)} %fusion.17), channel_id=1, source_target_pairs={{0,4},{1,5},{2,6},{3,7},{4,0},{5,1},{6,2},{7,3},{8,12},{9,13},{10,... | collective-permute-start | bytes 786440 | tf_op jit(solution)/shard_map/ppermute | solution.py:24
  64.8 13.0 %collective-permute-start.22 = (bf16[512,256]{1,0:T(8,128)(2,1)S(1)}, bf16[512,256]{1,0:T(8,128)(2,1)S(1)}, u32[]{:S(2)}, u32[]{:S(2)}) collective-permute-start(bf16[512,256]{1,0:T(8,128)(2,1)S(1)} %fusion.17), channel_id=1, source_target_pairs={{0,24},{8,16},{16,8},{24,0},{1,25},{9,17},{17,9},{25,1},{2,26},{10... | collective-permute-start | bytes 786440 | tf_op jit(solution)/shard_map/ppermute | solution.py:24
  66.1 13.5 %collective-permute-start.21 = (bf16[512,256]{1,0:T(8,128)(2,1)S(1)}, bf16[512,256]{1,0:T(8,128)(2,1)S(1)}, u32[]{:S(2)}, u32[]{:S(2)}) collective-permute-start(bf16[512,256]{1,0:T(8,128)(2,1)S(1)} %fusion.17), channel_id=1, source_target_pairs={{0,16},{8,24},{16,0},{24,8},{1,17},{9,25},{17,1},{25,9},{2,18},{10... | collective-permute-start | bytes 786440 | tf_op jit(solution)/shard_map/ppermute | solution.py:24
  67.2 12.4 %collective-permute-start.20 = (bf16[512,256]{1,0:T(8,128)(2,1)S(1)}, bf16[512,256]{1,0:T(8,128)(2,1)S(1)}, u32[]{:S(2)}, u32[]{:S(2)}) collective-permute-start(bf16[512,256]{1,0:T(8,128)(2,1)S(1)} %fusion.17), channel_id=1, source_target_pairs={{0,8},{8,0},{16,24},{24,16},{1,9},{9,1},{17,25},{25,17},{2,10},{10... | collective-permute-start | bytes 786440 | tf_op jit(solution)/shard_map/ppermute | solution.py:24
  67.4 13.6 %collective-permute-start.24 = (bf16[512,256]{1,0:T(8,128)(2,1)S(1)}, bf16[512,256]{1,0:T(8,128)(2,1)}, u32[]{:S(2)}, u32[]{:S(2)}) collective-permute-start(bf16[512,256]{1,0:T(8,128)(2,1)S(1)} %fusion.17), channel_id=1, source_target_pairs={{0,2},{1,3},{2,0},{3,1},{4,6},{5,7},{6,4},{7,5},{8,10},{9,11},{10,... | collective-permute-start | bytes 786440 | tf_op jit(solution)/shard_map/ppermute | solution.py:24
  77.1 5.5 %collective-permute-start.23 = (bf16[512,256]{1,0:T(8,128)(2,1)S(1)}, bf16[512,256]{1,0:T(8,128)(2,1)}, u32[]{:S(2)}, u32[]{:S(2)}) collective-permute-start(bf16[512,256]{1,0:T(8,128)(2,1)S(1)} %fusion.17), channel_id=1, source_target_pairs={{0,1},{1,0},{2,3},{3,2},{4,5},{5,4},{6,7},{7,6},{8,9},{9,8},{10,11... | collective-permute-start | bytes 786440 | tf_op jit(solution)/shard_map/ppermute | solution.py:24
  77.7 8.5 %collective-permute-start.28 = (bf16[1,512,256]{2,1,0:T(8,128)(2,1)S(1)}, bf16[1,512,256]{2,1,0:T(8,128)(2,1)}, u32[]{:S(2)}, u32[]{:S(2)}) collective-permute-start(bf16[1,512,256]{2,1,0:T(8,128)(2,1)S(1)} %bitcast.243), channel_id=1, source_target_pairs={{0,2},{1,3},{2,0},{3,1},{4,6},{5,7},{6,4},{7,5},{8,10},{9,11},{10,... | collective-permute-start | bytes 786440 | tf_op jit(solution)/shard_map/ppermute | solution.py:24
  80.5 8.7 %collective-permute-start.27 = (bf16[512,256]{1,0:T(8,128)(2,1)S(1)}, bf16[512,256]{1,0:T(8,128)(2,1)S(1)}, u32[]{:S(2)}, u32[]{:S(2)}) collective-permute-start(bf16[512,256]{1,0:T(8,128)(2,1)S(1)} %collective-permute-done.26), channel_id=1, source_target_pairs={{0,1},{1,0},{2,3},{3,2},{4,5},{5,4},{6,7},{7,6},{8,9},{9,8},{10,11... | collective-permute-start | bytes 786440 | tf_op jit(solution)/shard_map/ppermute | solution.py:24
  81.0 7.5 %collective-permute-start.25 = (bf16[512,256]{1,0:T(8,128)(2,1)}, bf16[512,256]{1,0:T(8,128)(2,1)S(1)}, u32[]{:S(2)}, u32[]{:S(2)}) collective-permute-start(bf16[512,256]{1,0:T(8,128)(2,1)} %collective-permute-done.24), channel_id=1, source_target_pairs={{0,1},{1,0},{2,3},{3,2},{4,5},{5,4},{6,7},{7,6},{8,9},{9,8},{10,11... | collective-permute-start | bytes 786440 | tf_op jit(solution)/shard_map/ppermute | solution.py:24
  86.2 3.7 %collective-permute-start.29 = (bf16[1,512,256]{2,1,0:T(8,128)(2,1)}, bf16[1,512,256]{2,1,0:T(8,128)(2,1)S(1)}, u32[]{:S(2)}, u32[]{:S(2)}) collective-permute-start(bf16[1,512,256]{2,1,0:T(8,128)(2,1)} %collective-permute-done.28), channel_id=1, source_target_pairs={{0,1},{1,0},{2,3},{3,2},{4,5},{5,4},{6,7},{7,6},{8,9},{9,8},{10,11... | collective-permute-start | bytes 786440 | tf_op jit(solution)/shard_map/ppermute | solution.py:24
  89.9 1.0 copy-start.12
  91.0 8.9 %collective-permute-start.39 = (bf16[512,256]{1,0:T(8,128)(2,1)S(1)}, bf16[512,256]{1,0:T(8,128)(2,1)S(1)}, u32[]{:S(2)}, u32[]{:S(2)}) collective-permute-start(bf16[512,256]{1,0:T(8,128)(2,1)S(1)} %get-tuple-element.10), channel_id=1, source_target_pairs={{0,24},{8,16},{16,8},{24,0},{1,25},{9,17},{17,9},{25,1},{2,26},{10... | collective-permute-start | bytes 786440 | tf_op jit(solution)/shard_map/ppermute | solution.py:24
  92.3 13.6 %collective-permute-start.38 = (bf16[512,256]{1,0:T(8,128)(2,1)S(1)}, bf16[512,256]{1,0:T(8,128)(2,1)S(1)}, u32[]{:S(2)}, u32[]{:S(2)}) collective-permute-start(bf16[512,256]{1,0:T(8,128)(2,1)S(1)} %get-tuple-element.10), channel_id=1, source_target_pairs={{0,16},{8,24},{16,0},{24,8},{1,17},{9,25},{17,1},{25,9},{2,18},{10... | collective-permute-start | bytes 786440 | tf_op jit(solution)/shard_map/ppermute | solution.py:24
  93.4 12.4 %collective-permute-start.37 = (bf16[512,256]{1,0:T(8,128)(2,1)S(1)}, bf16[512,256]{1,0:T(8,128)(2,1)S(1)}, u32[]{:S(2)}, u32[]{:S(2)}) collective-permute-start(bf16[512,256]{1,0:T(8,128)(2,1)S(1)} %get-tuple-element.10), channel_id=1, source_target_pairs={{0,8},{8,0},{16,24},{24,16},{1,9},{9,1},{17,25},{25,17},{2,10},{10... | collective-permute-start | bytes 786440 | tf_op jit(solution)/shard_map/ppermute | solution.py:24
  93.6 15.6 %collective-permute-start.33 = (bf16[512,256]{1,0:T(8,128)(2,1)S(1)}, bf16[512,256]{1,0:T(8,128)(2,1)}, u32[]{:S(2)}, u32[]{:S(2)}) collective-permute-start(bf16[512,256]{1,0:T(8,128)(2,1)S(1)} %get-tuple-element.10), channel_id=1, source_target_pairs={{0,4},{1,5},{2,6},{3,7},{4,0},{5,1},{6,2},{7,3},{8,12},{9,13},{10,... | collective-permute-start | bytes 786440 | tf_op jit(solution)/shard_map/ppermute | solution.py:24
  93.8 19.8 %collective-permute-start.31 = (bf16[512,256]{1,0:T(8,128)(2,1)S(1)}, bf16[512,256]{1,0:T(8,128)(2,1)}, u32[]{:S(2)}, u32[]{:S(2)}) collective-permute-start(bf16[512,256]{1,0:T(8,128)(2,1)S(1)} %get-tuple-element.10), channel_id=1, source_target_pairs={{0,2},{1,3},{2,0},{3,1},{4,6},{5,7},{6,4},{7,5},{8,10},{9,11},{10,... | collective-permute-start | bytes 786440 | tf_op jit(solution)/shard_map/ppermute | solution.py:24
  99.8 15.9 %collective-permute-start.30 = (bf16[512,256]{1,0:T(8,128)(2,1)S(1)}, bf16[512,256]{1,0:T(8,128)(2,1)}, u32[]{:S(2)}, u32[]{:S(2)}) collective-permute-start(bf16[512,256]{1,0:T(8,128)(2,1)S(1)} %get-tuple-element.10), channel_id=1, source_target_pairs={{0,1},{1,0},{2,3},{3,2},{4,5},{5,4},{6,7},{7,6},{8,9},{9,8},{10,11... | collective-permute-start | bytes 786440 | tf_op jit(solution)/shard_map/ppermute | solution.py:24
  109.2 10.9 %collective-permute-start.35 = (bf16[1,512,256]{2,1,0:T(8,128)(2,1)}, bf16[1,512,256]{2,1,0:T(8,128)(2,1)S(1)}, u32[]{:S(2)}, u32[]{:S(2)}) collective-permute-start(bf16[1,512,256]{2,1,0:T(8,128)(2,1)} %bitcast.49), channel_id=1, source_target_pairs={{0,2},{1,3},{2,0},{3,1},{4,6},{5,7},{6,4},{7,5},{8,10},{9,11},{10,... | collective-permute-start | bytes 786440 | tf_op jit(solution)/shard_map/ppermute | solution.py:24
  110.7 10.1 %collective-permute-start.34 = (bf16[512,256]{1,0:T(8,128)(2,1)}, bf16[512,256]{1,0:T(8,128)(2,1)S(1)}, u32[]{:S(2)}, u32[]{:S(2)}) collective-permute-start(bf16[512,256]{1,0:T(8,128)(2,1)} %collective-permute-done.33), channel_id=1, source_target_pairs={{0,1},{1,0},{2,3},{3,2},{4,5},{5,4},{6,7},{7,6},{8,9},{9,8},{10,11... | collective-permute-start | bytes 786440 | tf_op jit(solution)/shard_map/ppermute | solution.py:24
  112.4 1.4 %copy-start.9 = (bf16[512,256]{1,0:T(8,128)(2,1)S(1)}, bf16[512,256]{1,0:T(8,128)(2,1)}, u32[]{:S(2)}) copy-start(bf16[512,256]{1,0:T(8,128)(2,1)} %copy-done.8) | copy-start | bytes 786436
  113.6 6.9 %collective-permute-start.32 = (bf16[512,256]{1,0:T(8,128)(2,1)}, bf16[512,256]{1,0:T(8,128)(2,1)S(1)}, u32[]{:S(2)}, u32[]{:S(2)}) collective-permute-start(bf16[512,256]{1,0:T(8,128)(2,1)} %collective-permute-done.31), channel_id=1, source_target_pairs={{0,1},{1,0},{2,3},{3,2},{4,5},{5,4},{6,7},{7,6},{8,9},{9,8},{10,11... | collective-permute-start | bytes 786440 | tf_op jit(solution)/shard_map/ppermute | solution.py:24
  115.5 1.0 copy-start.2
  120.1 1.6 %collective-permute-start.36 = (bf16[1,512,256]{2,1,0:T(8,128)(2,1)S(1)}, bf16[1,512,256]{2,1,0:T(8,128)(2,1)S(1)}, u32[]{:S(2)}, u32[]{:S(2)}) collective-permute-start(bf16[1,512,256]{2,1,0:T(8,128)(2,1)S(1)} %collective-permute-done.35), channel_id=1, source_target_pairs={{0,1},{1,0},{2,3},{3,2},{4,5},{5,4},{6,7},{7,6},{8,9},{9,8},{10,11... | collective-permute-start | bytes 786440 | tf_op jit(solution)/shard_map/ppermute | solution.py:24
  120.8 1.0 copy-start
  (10 other events, 8.4 us)
